TPU v7x, 256 devices: a whole 4x4x8 slice. The times are simulated.
256 devices in a mesh: lat: 8 (over x_lo, y), lon: 32 (over z, x_hi, core).
Axes of the slice: x: 4 (x_hi: 2, x_lo: 2; x = x_hi * 2 + x_lo), y: 4, z: 8, core: 2. Of those that a mesh axis runs over, the one named last changes fastest.
Arguments:
- features: bfloat16 [768, 1024, 256], P('lat', 'lon'), may hold values from -6 to 6
- quad_weights: float32 [768, 3, 129], P('lat'), may hold values from -6 to 6
- cycle_index: int32 [768, 3, 129], P('lat'), may hold values from 0 to 8
- widths: int32 [768], P('lat'), may hold values from 1 to 64, as said below
- mix_weight: bfloat16 [9, 256, 256], replicated, may hold values from -0.125 to 0.125
Outputs:
- mixed: bfloat16 [768, 1024, 256], P('lat', 'lon')
Inputs may be any that keep to these rules, and one draw needn't show every extreme that they name: Rows within 8 rows of either end of the grid have widths above 32; rows 0 and 767 have exactly 64. All other rows have widths of at most 16, which row 8 reaches.
All inputs are finite; a program needn't handle non-finite values.
Results may differ from a plain program's by a relative error of at most 0.0031.
Values may be sent and summed in bfloat16 or wider, within the bound.
No kernel may reach another device: no remote copies, remote signals or barrier semaphores. Data moves between devices by JAX's collectives and lax.ppermute only.
A program may use at most 128 MiB of HBM per device.

v0:
```python
import jax
import jax.numpy as jnp
from jax import lax
from jax.sharding import PartitionSpec as P

POLAR = 8


def shifted(block, axis, distance):
    devices = range(lax.axis_size(axis))
    route = [((i - distance) % len(devices), i) for i in devices]
    return lax.ppermute(block, axis, route)


def extended_2(value, sides, width):
    for axis, dim in sides:
        count, length = (lax.axis_size(axis), value.shape[dim])
        up = [(i, (i + 1) % count) for i in range(count - 1)]
        down = [(j, i) for i, j in up]
        last = lax.slice_in_dim(value, length - width, length, axis=dim)
        leading = lax.slice_in_dim(value, 0, width, axis=dim)
        before = lax.ppermute(last, axis, up)
        after = lax.ppermute(leading, axis, down)
        value = jnp.concatenate([before, value, after], axis=dim)
    return value


def basis_table(quad_weights, cycle_index, widths, count):
    offsets = jnp.arange(quad_weights.shape[2]) - quad_weights.shape[2] // 2
    inside = jnp.abs(offsets)[None, None, :] <= widths[:, None, None]
    member = cycle_index[:, None, :, :] == jnp.arange(count)[None, :, None, None]
    scale_row = 1.0 / jnp.sqrt(3.0 * (2.0 * widths.astype(jnp.float32) + 1.0))
    values = jnp.where(
        member & inside[:, None, :, :], quad_weights[:, None, :, :], jnp.float32(0.0)
    )
    return (values * scale_row[:, None, None, None]).astype(jnp.bfloat16)


def shift_table(length, columns):
    width_all = length - 1 + columns
    out_pos = jnp.arange(columns)[:, None, None]
    in_pos = jnp.arange(width_all)[None, :, None]
    offset = jnp.arange(length)[None, None, :]
    return (in_pos - out_pos == offset).astype(jnp.bfloat16)


def band_rows(extended, values, blocks, span_rows):
    length = values.shape[-1]
    columns = extended.shape[1] - (length - 1)
    table = shift_table(length, columns)

    def one_block(block_index):
        rows = lax.dynamic_slice_in_dim(extended, block_index * span_rows, span_rows + 2, 0)
        block_values = lax.dynamic_slice_in_dim(values, block_index * span_rows, span_rows, 0)
        total = None
        for offset_row in range(3):
            kernel = jnp.einsum(
                "nbt,jmt->nbjm",
                block_values[:, :, offset_row],
                table,
                preferred_element_type=jnp.float32,
            ).astype(jnp.bfloat16)
            term = jnp.einsum(
                "nbjm,nmc->nbjc",
                kernel,
                rows[offset_row : offset_row + span_rows],
                preferred_element_type=jnp.float32,
            )
            total = term if total is None else total + term
        return total.astype(jnp.bfloat16)

    result = lax.map(one_block, jnp.arange(blocks))
    return result.reshape((blocks * span_rows,) + result.shape[2:])


def extend_far(rows, reach, columns):
    hop_count = reach // columns
    western = []
    eastern = []
    for hop in range(1, hop_count + 1):
        western.insert(0, shifted(rows, "lon", hop))
        eastern.append(shifted(rows, "lon", -hop))
    return jnp.concatenate(western + [rows] + eastern, 1)


def body(features, quad_weights, cycle_index, widths, mix_weight):
    count = mix_weight.shape[0]
    lat_rows = features.shape[0]
    columns = features.shape[1]
    reach = quad_weights.shape[2] // 2
    basis_values = basis_table(quad_weights, cycle_index, widths, count)
    padded = extended_2(features, (("lat", 0),), 1)
    extended = extend_far(padded, reach, columns)
    conv = band_rows(extended, basis_values, lat_rows // POLAR, POLAR)
    mixing = jnp.einsum("nbjc,bcd->njd", conv, mix_weight, preferred_element_type=jnp.float32)
    return (features.astype(jnp.float32) + mixing).astype(jnp.bfloat16)


def solution(mesh):
    in_specs = (P("lat", "lon", None), P("lat", None, None), P("lat", None, None), P("lat"), P())
    out_specs = P("lat", "lon", None)
    return jax.shard_map(body, mesh=mesh, in_specs=in_specs, out_specs=out_specs, check_vma=False)
```

profile of v0, /device:TPU:2, one launch (start us, length us, event | category | flops | bytes accessed | tf_op | source)
XLA Modules:
  0.0 381.1 jit_solution(8221041683919122130)
XLA Ops:
  0.9 3.5 collective-permute-start
  4.3 4.5 %collective-permute-start.1 = (bf16[1,32,256]{2,1,0:T(8,128)(2,1)S(1)}, bf16[1,32,256]{2,1,0:T(8,128)(2,1)S(1)}, u32[]{:S(2)}, u32[]{:S(2)}) collective-permute-start(bf16[1,32,256]{2,1,0:T(8,128)(2,1)S(1)} %get-tuple-element.88), channel_id=1, source_target_pairs={{32,0},{64,32},{96,64},{128,96},{160,128},{192,160},{224,192},{33,... | collective-permute-start | bytes 49160 | tf_op jit(solution)/shard_map/ppermute | solution.py:23
  14.8 5.4 %collective-permute-start.4 = (bf16[98,32,256]{2,1,0:T(8,128)(2,1)}, bf16[98,32,256]{2,1,0:T(8,128)(2,1)}, u32[]{:S(2)}, u32[]{:S(2)}) collective-permute-start(bf16[98,32,256]{2,1,0:T(8,128)(2,1)} %constant_dynamic-update-slice_fusion), channel_id=1, source_target_pairs={{1,0},{2,1},{3,2},{4,3},{5,4},{6,5},{7,6},{8,7},{9,8},{10,9},{11,1... | collective-permute-start | bytes 4816904 | tf_op jit(solution)/shard_map/ppermute | solution.py:12
  20.8 3.2 collective-permute-start.5
  27.1 75.2 %collective-permute-done.2 = bf16[98,32,256]{2,1,0:T(8,128)(2,1)} collective-permute-done((bf16[98,32,256]{2,1,0:T(8,128)(2,1)}, bf16[98,32,256]{2,1,0:T(8,128)(2,1)}, u32[]{:S(2)}, u32[]{:S(2)}) %collective-permute-start.2) | collective-permute-done | bytes 1605664 | tf_op jit(solution)/shard_map/ppermute | solution.py:12
  107.5 16.2 %collective-permute-done.5 = bf16[98,32,256]{2,1,0:T(8,128)(2,1)S(1)} collective-permute-done((bf16[98,32,256]{2,1,0:T(8,128)(2,1)}, bf16[98,32,256]{2,1,0:T(8,128)(2,1)S(1)}, u32[]{:S(2)}, u32[]{:S(2)}) %collective-permute-start.5) | collective-permute-done | bytes 1605664 | tf_op jit(solution)/shard_map/ppermute | solution.py:12
  123.8 3.1 copy-done.1
  127.0 243.6 %while.12 = (s32[]{:T(128)}, bf16[12,8,9,32,256]{4,3,2,1,0:T(8,128)(2,1)}, s32[12]{0:T(128)S(1)}, bf16[96,9,3,129]{3,0,2,1:T(8,128)(2,1)}, bf16[98,160,256]{2,1,...) while((s32[]{:T(128)}, ...), condition=%wide.region_1.2_spmd.clone.clone, body=%wide.region_0.1_spmd.clone.clone.sunk | while | flops 857290752 | bytes 18101024 | solution.py:72
  128.2 3.8 fusion.42
  133.9 2.8 fusion.40
  136.7 2.9 fusion.41
  139.6 3.8 %fusion.44 = bf16[8,9,32,160]{3,0,2,1:T(8,128)(2,1)} fusion(s32[32,160]{1,0:T(8,128)} %get-tuple-element.158, bf16[96,9,3,129]{3,0,2,1:T(8,128)(2,1)} %get-tuple-element.156, s32[]{:T(128)S(6)} %select_n.18, s32[]{:T(128)S(6)} %add.72), kind=kOutput, calls=%fused_computation.4.clone.1 | convolution fusion | flops 96430080 | bytes 806920 | tf_op jit(solution)/shard_map/while/body/eval_jaxpr/nbt,jmt->nbjm/dot_general | solution.py:57
  143.5 3.8 fusion.45
  148.5 3.8 fusion.42
  154.2 2.8 fusion.40
  157.0 2.9 fusion.41
  159.9 3.8 %fusion.44 = bf16[8,9,32,160]{3,0,2,1:T(8,128)(2,1)} fusion(s32[32,160]{1,0:T(8,128)} %get-tuple-element.158, bf16[96,9,3,129]{3,0,2,1:T(8,128)(2,1)} %get-tuple-element.156, s32[]{:T(128)S(6)} %select_n.18, s32[]{:T(128)S(6)} %add.72), kind=kOutput, calls=%fused_computation.4.clone.1 | convolution fusion | flops 96430080 | bytes 806920 | tf_op jit(solution)/shard_map/while/body/eval_jaxpr/nbt,jmt->nbjm/dot_general | solution.py:57
  163.8 3.8 fusion.45
  168.8 3.8 fusion.42
  174.5 2.8 fusion.40
  177.3 2.9 fusion.41
  180.2 3.8 %fusion.44 = bf16[8,9,32,160]{3,0,2,1:T(8,128)(2,1)} fusion(s32[32,160]{1,0:T(8,128)} %get-tuple-element.158, bf16[96,9,3,129]{3,0,2,1:T(8,128)(2,1)} %get-tuple-element.156, s32[]{:T(128)S(6)} %select_n.18, s32[]{:T(128)S(6)} %add.72), kind=kOutput, calls=%fused_computation.4.clone.1 | convolution fusion | flops 96430080 | bytes 806920 | tf_op jit(solution)/shard_map/while/body/eval_jaxpr/nbt,jmt->nbjm/dot_general | solution.py:57
  184.1 3.8 fusion.45
  189.1 3.8 fusion.42
  194.8 2.8 fusion.40
  197.6 2.9 fusion.41
  200.5 3.8 %fusion.44 = bf16[8,9,32,160]{3,0,2,1:T(8,128)(2,1)} fusion(s32[32,160]{1,0:T(8,128)} %get-tuple-element.158, bf16[96,9,3,129]{3,0,2,1:T(8,128)(2,1)} %get-tuple-element.156, s32[]{:T(128)S(6)} %select_n.18, s32[]{:T(128)S(6)} %add.72), kind=kOutput, calls=%fused_computation.4.clone.1 | convolution fusion | flops 96430080 | bytes 806920 | tf_op jit(solution)/shard_map/while/body/eval_jaxpr/nbt,jmt->nbjm/dot_general | solution.py:57
  204.3 3.8 fusion.45
  209.4 3.8 fusion.42
  215.1 2.8 fusion.40
  217.9 2.9 fusion.41
  220.8 3.8 %fusion.44 = bf16[8,9,32,160]{3,0,2,1:T(8,128)(2,1)} fusion(s32[32,160]{1,0:T(8,128)} %get-tuple-element.158, bf16[96,9,3,129]{3,0,2,1:T(8,128)(2,1)} %get-tuple-element.156, s32[]{:T(128)S(6)} %select_n.18, s32[]{:T(128)S(6)} %add.72), kind=kOutput, calls=%fused_computation.4.clone.1 | convolution fusion | flops 96430080 | bytes 806920 | tf_op jit(solution)/shard_map/while/body/eval_jaxpr/nbt,jmt->nbjm/dot_general | solution.py:57
  224.6 3.8 %fusion.45 = bf16[12,8,9,32,256]{4,3,2,1,0:T(8,128)(2,1)} fusion(bf16[12,8,9,32,256]{4,3,2,1,0:T(8,128)(2,1)} %get-tuple-element.141, s32[]{:T(128)} %get-tuple-element.140, f32[8,9,32,256]{3,2,1,0:T(8,128)} %fusion.41, f32[8,9,32,256]{3,2,1,0:T(8,128)S(1)} %fusion.43, bf16[8,9,32,160]{3,0,2,1:T(8,128)(2,1)} %fusion.44, ...), kind=kOutput, calls=%fused_computation.15.clone.1 | convolution fusion | flops 190513152 | bytes 7733764 | tf_op jit(solution)/shard_map/while/body/eval_jaxpr/nbjm,nmc->nbjc/dot_general | solution.py:63
  229.7 3.8 fusion.42
  235.4 2.8 fusion.40
  238.2 2.9 fusion.41
  241.1 3.8 %fusion.44 = bf16[8,9,32,160]{3,0,2,1:T(8,128)(2,1)} fusion(s32[32,160]{1,0:T(8,128)} %get-tuple-element.158, bf16[96,9,3,129]{3,0,2,1:T(8,128)(2,1)} %get-tuple-element.156, s32[]{:T(128)S(6)} %select_n.18, s32[]{:T(128)S(6)} %add.72), kind=kOutput, calls=%fused_computation.4.clone.1 | convolution fusion | flops 96430080 | bytes 806920 | tf_op jit(solution)/shard_map/while/body/eval_jaxpr/nbt,jmt->nbjm/dot_general | solution.py:57
  245.0 3.8 %fusion.45 = bf16[12,8,9,32,256]{4,3,2,1,0:T(8,128)(2,1)} fusion(bf16[12,8,9,32,256]{4,3,2,1,0:T(8,128)(2,1)} %get-tuple-element.141, s32[]{:T(128)} %get-tuple-element.140, f32[8,9,32,256]{3,2,1,0:T(8,128)} %fusion.41, f32[8,9,32,256]{3,2,1,0:T(8,128)S(1)} %fusion.43, bf16[8,9,32,160]{3,0,2,1:T(8,128)(2,1)} %fusion.44, ...), kind=kOutput, calls=%fused_computation.15.clone.1 | convolution fusion | flops 190513152 | bytes 7733764 | tf_op jit(solution)/shard_map/while/body/eval_jaxpr/nbjm,nmc->nbjc/dot_general | solution.py:63
  250.1 3.8 fusion.42
  255.8 2.8 fusion.40
  258.5 2.9 fusion.41
  261.5 3.8 %fusion.44 = bf16[8,9,32,160]{3,0,2,1:T(8,128)(2,1)} fusion(s32[32,160]{1,0:T(8,128)} %get-tuple-element.158, bf16[96,9,3,129]{3,0,2,1:T(8,128)(2,1)} %get-tuple-element.156, s32[]{:T(128)S(6)} %select_n.18, s32[]{:T(128)S(6)} %add.72), kind=kOutput, calls=%fused_computation.4.clone.1 | convolution fusion | flops 96430080 | bytes 806920 | tf_op jit(solution)/shard_map/while/body/eval_jaxpr/nbt,jmt->nbjm/dot_general | solution.py:57
  265.3 3.8 fusion.45
  270.4 3.8 fusion.42
  278.8 2.9 fusion.41
  281.8 3.8 %fusion.44 = bf16[8,9,32,160]{3,0,2,1:T(8,128)(2,1)} fusion(s32[32,160]{1,0:T(8,128)} %get-tuple-element.158, bf16[96,9,3,129]{3,0,2,1:T(8,128)(2,1)} %get-tuple-element.156, s32[]{:T(128)S(6)} %select_n.18, s32[]{:T(128)S(6)} %add.72), kind=kOutput, calls=%fused_computation.4.clone.1 | convolution fusion | flops 96430080 | bytes 806920 | tf_op jit(solution)/shard_map/while/body/eval_jaxpr/nbt,jmt->nbjm/dot_general | solution.py:57
  285.6 3.9 %fusion.45 = bf16[12,8,9,32,256]{4,3,2,1,0:T(8,128)(2,1)} fusion(bf16[12,8,9,32,256]{4,3,2,1,0:T(8,128)(2,1)} %get-tuple-element.141, s32[]{:T(128)} %get-tuple-element.140, f32[8,9,32,256]{3,2,1,0:T(8,128)} %fusion.41, f32[8,9,32,256]{3,2,1,0:T(8,128)S(1)} %fusion.43, bf16[8,9,32,160]{3,0,2,1:T(8,128)(2,1)} %fusion.44, ...), kind=kOutput, calls=%fused_computation.15.clone.1 | convolution fusion | flops 190513152 | bytes 7733764 | tf_op jit(solution)/shard_map/while/body/eval_jaxpr/nbjm,nmc->nbjc/dot_general | solution.py:63
  290.7 3.8 fusion.42
  299.2 2.9 fusion.41
  302.1 3.8 %fusion.44 = bf16[8,9,32,160]{3,0,2,1:T(8,128)(2,1)} fusion(s32[32,160]{1,0:T(8,128)} %get-tuple-element.158, bf16[96,9,3,129]{3,0,2,1:T(8,128)(2,1)} %get-tuple-element.156, s32[]{:T(128)S(6)} %select_n.18, s32[]{:T(128)S(6)} %add.72), kind=kOutput, calls=%fused_computation.4.clone.1 | convolution fusion | flops 96430080 | bytes 806920 | tf_op jit(solution)/shard_map/while/body/eval_jaxpr/nbt,jmt->nbjm/dot_general | solution.py:57
  305.9 3.8 fusion.45
  311.0 3.8 fusion.42
  319.5 2.9 fusion.41
  322.4 3.8 %fusion.44 = bf16[8,9,32,160]{3,0,2,1:T(8,128)(2,1)} fusion(s32[32,160]{1,0:T(8,128)} %get-tuple-element.158, bf16[96,9,3,129]{3,0,2,1:T(8,128)(2,1)} %get-tuple-element.156, s32[]{:T(128)S(6)} %select_n.18, s32[]{:T(128)S(6)} %add.72), kind=kOutput, calls=%fused_computation.4.clone.1 | convolution fusion | flops 96430080 | bytes 806920 | tf_op jit(solution)/shard_map/while/body/eval_jaxpr/nbt,jmt->nbjm/dot_general | solution.py:57
  326.2 3.8 fusion.45
  331.3 3.8 fusion.42
  339.8 2.9 fusion.41
  342.7 3.8 %fusion.44 = bf16[8,9,32,160]{3,0,2,1:T(8,128)(2,1)} fusion(s32[32,160]{1,0:T(8,128)} %get-tuple-element.158, bf16[96,9,3,129]{3,0,2,1:T(8,128)(2,1)} %get-tuple-element.156, s32[]{:T(128)S(6)} %select_n.18, s32[]{:T(128)S(6)} %add.72), kind=kOutput, calls=%fused_computation.4.clone.1 | convolution fusion | flops 96430080 | bytes 806920 | tf_op jit(solution)/shard_map/while/body/eval_jaxpr/nbt,jmt->nbjm/dot_general | solution.py:57
  346.5 3.8 %fusion.45 = bf16[12,8,9,32,256]{4,3,2,1,0:T(8,128)(2,1)} fusion(bf16[12,8,9,32,256]{4,3,2,1,0:T(8,128)(2,1)} %get-tuple-element.141, s32[]{:T(128)} %get-tuple-element.140, f32[8,9,32,256]{3,2,1,0:T(8,128)} %fusion.41, f32[8,9,32,256]{3,2,1,0:T(8,128)S(1)} %fusion.43, bf16[8,9,32,160]{3,0,2,1:T(8,128)(2,1)} %fusion.44, ...), kind=kOutput, calls=%fused_computation.15.clone.1 | convolution fusion | flops 190513152 | bytes 7733764 | tf_op jit(solution)/shard_map/while/body/eval_jaxpr/nbjm,nmc->nbjc/dot_general | solution.py:63
  351.6 3.8 fusion.42
  360.1 2.9 fusion.41
  363.0 3.8 %fusion.44 = bf16[8,9,32,160]{3,0,2,1:T(8,128)(2,1)} fusion(s32[32,160]{1,0:T(8,128)} %get-tuple-element.158, bf16[96,9,3,129]{3,0,2,1:T(8,128)(2,1)} %get-tuple-element.156, s32[]{:T(128)S(6)} %select_n.18, s32[]{:T(128)S(6)} %add.72), kind=kOutput, calls=%fused_computation.4.clone.1 | convolution fusion | flops 96430080 | bytes 806920 | tf_op jit(solution)/shard_map/while/body/eval_jaxpr/nbt,jmt->nbjm/dot_general | solution.py:57
  366.8 3.8 fusion.45
  370.6 10.4 %fusion.23 = bf16[96,32,256]{2,1,0:T(8,128)(2,1)} fusion(bf16[96,32,256]{2,1,0:T(8,128)(2,1)} %param.7, bf16[96,9,32,256]{3,2,1,0:T(8,128)(2,1)} %bitcast.75, bf16[9,256,256]{2,1,0:T(8,128)(2,1)S(1)} %copy-done), kind=kOutput, calls=%fused_computation.31 | convolution fusion | flops 3626237952 | bytes 18481152 | tf_op jit(solution)/shard_map/nbjc,bcd->njd/dot_general | solution.py:95
  (64 shorter events, 60.0 us)
Async XLA Ops:
  0.0 370.6 %copy-start = (bf16[9,256,256]{2,1,0:T(8,128)(2,1)S(1)}, bf16[9,256,256]{2,1,0:T(8,128)(2,1)}, u32[]{:S(2)}) copy-start(bf16[9,256,256]{2,1,0:T(8,128)(2,1)} %param.11) | copy-start | bytes 3538948
  0.0 24.0 %copy-start.3 = (s32[96,3,129]{0,2,1:T(8,128)S(1)}, s32[96,3,129]{0,2,1:T(8,128)}, u32[]{:S(2)}) copy-start(s32[96,3,129]{0,2,1:T(8,128)} %param.9) | copy-start | bytes 445828
  0.0 25.3 %copy-start.4 = (s32[96]{0:T(128)S(1)}, s32[96]{0:T(128)}, u32[]{:S(2)}) copy-start(s32[96]{0:T(128)} %param.10) | copy-start | bytes 1156
  0.9 8.0 %collective-permute-start = (bf16[1,32,256]{2,1,0:T(8,128)(2,1)S(1)}, bf16[1,32,256]{2,1,0:T(8,128)(2,1)S(1)}, u32[]{:S(2)}, u32[]{:S(2)}) collective-permute-start(bf16[1,32,256]{2,1,0:T(8,128)(2,1)S(1)} %get-tuple-element.89), channel_id=1, source_target_pairs={{0,32},{32,64},{64,96},{96,128},{128,160},{160,192},{192,224},{1,3... | collective-permute-start | bytes 49160 | tf_op jit(solution)/shard_map/ppermute | solution.py:22
  4.3 7.8 %collective-permute-start.1 = (bf16[1,32,256]{2,1,0:T(8,128)(2,1)S(1)}, bf16[1,32,256]{2,1,0:T(8,128)(2,1)S(1)}, u32[]{:S(2)}, u32[]{:S(2)}) collective-permute-start(bf16[1,32,256]{2,1,0:T(8,128)(2,1)S(1)} %get-tuple-element.88), channel_id=1, source_target_pairs={{32,0},{64,32},{96,64},{128,96},{160,128},{192,160},{224,192},{33,... | collective-permute-start | bytes 49160 | tf_op jit(solution)/shard_map/ppermute | solution.py:23
  12.7 89.6 %collective-permute-start.2 = (bf16[98,32,256]{2,1,0:T(8,128)(2,1)}, bf16[98,32,256]{2,1,0:T(8,128)(2,1)}, u32[]{:S(2)}, u32[]{:S(2)}) collective-permute-start(bf16[98,32,256]{2,1,0:T(8,128)(2,1)} %constant_dynamic-update-slice_fusion), channel_id=1, source_target_pairs={{30,0},{31,1},{0,2},{1,3},{2,4},{3,5},{4,6},{5,7},{6,8},{7,9},{8,1... | collective-permute-start | bytes 4816904 | tf_op jit(solution)/shard_map/ppermute | solution.py:12
  14.8 89.0 %collective-permute-start.3 = (bf16[98,32,256]{2,1,0:T(8,128)(2,1)}, bf16[98,32,256]{2,1,0:T(8,128)(2,1)}, u32[]{:S(2)}, u32[]{:S(2)}) collective-permute-start(bf16[98,32,256]{2,1,0:T(8,128)(2,1)} %constant_dynamic-update-slice_fusion), channel_id=1, source_target_pairs={{31,0},{0,1},{1,2},{2,3},{3,4},{4,5},{5,6},{6,7},{7,8},{8,9},{9,10... | collective-permute-start | bytes 4816904 | tf_op jit(solution)/shard_map/ppermute | solution.py:12
  14.8 91.1 %collective-permute-start.4 = (bf16[98,32,256]{2,1,0:T(8,128)(2,1)}, bf16[98,32,256]{2,1,0:T(8,128)(2,1)}, u32[]{:S(2)}, u32[]{:S(2)}) collective-permute-start(bf16[98,32,256]{2,1,0:T(8,128)(2,1)} %constant_dynamic-update-slice_fusion), channel_id=1, source_target_pairs={{1,0},{2,1},{3,2},{4,3},{5,4},{6,5},{7,6},{8,7},{9,8},{10,9},{11,1... | collective-permute-start | bytes 4816904 | tf_op jit(solution)/shard_map/ppermute | solution.py:12
  20.8 102.9 %collective-permute-start.5 = (bf16[98,32,256]{2,1,0:T(8,128)(2,1)}, bf16[98,32,256]{2,1,0:T(8,128)(2,1)S(1)}, u32[]{:S(2)}, u32[]{:S(2)}) collective-permute-start(bf16[98,32,256]{2,1,0:T(8,128)(2,1)} %constant_dynamic-update-slice_fusion), channel_id=1, source_target_pairs={{2,0},{3,1},{4,2},{5,3},{6,4},{7,5},{8,6},{9,7},{10,8},{11,9},{12,... | collective-permute-start | bytes 4816904 | tf_op jit(solution)/shard_map/ppermute | solution.py:12
  103.9 1.9 copy-start.2
  123.8 3.2 copy-start.1
where the time goes:
time: 388 us; the launch traced here: 381 us
  matrix products  239 us (62%)
  waiting for transfers between devices  91.4 us (24%)
  local copies, waits for them, and re-layouts  21.9 us (6%)
  starting transfers between devices  18.6 us (5%)
  loops' own time  7.76 us (2%)
    dot_general x36, matrix products, one_block(): jnp.einsum('nbt,jmt->nbjm', block_values[:, :, offset_row], table, prefer...  124 us
    dot_general x36, matrix products, one_block(): jnp.einsum('nbjm,nmc->nbjc', kernel, rows[offset_row:offset_row + span_ro...  104 us
    ppermute x4, waiting for transfers between devices, shifted(): return lax.ppermute(block, axis, route)  91.4 us
    unnamed x20, local copies, waits for them, and re-layouts  12.7 us
    ppermute x4, starting transfers between devices, shifted(): return lax.ppermute(block, axis, route)  10.7 us
    dot_general x1, matrix products, body(): jnp.einsum('nbjc,bcd->njd', conv, mix_weight, preferred_element_type=jnp....  10.4 us
    another operation x1, loops' own time, band_rows(): result = lax.map(one_block, jnp.arange(blocks))  7.76 us
  transfers between devices with their start and end apart: 6, of which 2 were waited for; matrix products, arithmetic and copies ran while one was open for 3% of the time, Pallas kernels for 0%

commit v1 on v0

v1 whole, which is shorter than its diff:
```python
import jax
import jax.numpy as jnp
from jax import lax
from jax.sharding import PartitionSpec as P

POLAR = 8
NEAR = 16


def shifted(block, axis, distance):
    devices = range(lax.axis_size(axis))
    route = [((i - distance) % len(devices), i) for i in devices]
    return lax.ppermute(block, axis, route)


def lat_extended(value):
    count, length = lax.axis_size("lat"), value.shape[0]
    up = [(i, i + 1) for i in range(count - 1)]
    down = [(j, i) for i, j in up]
    before = lax.ppermute(value[length - 1 :], "lat", up)
    after = lax.ppermute(value[:1], "lat", down)
    return jnp.concatenate([before, value, after], axis=0)


def basis_table(quad_weights, cycle_index, widths, count):
    offsets = jnp.arange(quad_weights.shape[2]) - quad_weights.shape[2] // 2
    inside = jnp.abs(offsets)[None, None, :] <= widths[:, None, None]
    member = cycle_index[:, None, :, :] == jnp.arange(count)[None, :, None, None]
    scale_row = 1.0 / jnp.sqrt(3.0 * (2.0 * widths.astype(jnp.float32) + 1.0))
    values = jnp.where(
        member & inside[:, None, :, :], quad_weights[:, None, :, :], jnp.float32(0.0)
    )
    return (values * scale_row[:, None, None, None]).astype(jnp.bfloat16)


def shift_table(taps, columns):
    out_pos = jnp.arange(columns)[:, None, None]
    in_pos = jnp.arange(taps - 1 + columns)[None, :, None]
    offset = jnp.arange(taps)[None, None, :]
    return (in_pos - out_pos == offset).astype(jnp.bfloat16)


def conv_rows(extended, values):
    rows, taps = values.shape[0], values.shape[-1]
    columns = extended.shape[1] - (taps - 1)
    kernel = jnp.einsum(
        "nbrk,jmk->njbrm", values, shift_table(taps, columns),
        preferred_element_type=jnp.float32,
    ).astype(jnp.bfloat16)
    stacked = jnp.stack([extended[r : r + rows] for r in range(3)], axis=1)
    return jnp.einsum(
        "njbrm,nrmc->njbc", kernel, stacked, preferred_element_type=jnp.float32
    )


def body(features, quad_weights, cycle_index, widths, mix_weight):
    count = mix_weight.shape[0]
    lat_rows, columns = features.shape[0], features.shape[1]
    reach = quad_weights.shape[2] // 2
    basis_values = basis_table(quad_weights, cycle_index, widths, count)
    padded = lat_extended(features)

    near = jnp.concatenate(
        [shifted(padded[:, columns - NEAR :], "lon", 1), padded,
         shifted(padded[:, :NEAR], "lon", -1)], axis=1)
    conv = conv_rows(near, basis_values[:, :, :, reach - NEAR : reach + NEAR + 1])

    last_band = lax.axis_index("lat") == lax.axis_size("lat") - 1
    start = jnp.where(last_band, lat_rows - POLAR, 0)
    window = lax.dynamic_slice_in_dim(padded, start, POLAR + 2, 0)
    hops = reach // columns
    western = [shifted(window, "lon", hop) for hop in range(hops, 0, -1)]
    eastern = [shifted(window, "lon", -hop) for hop in range(1, hops + 1)]
    wide = jnp.concatenate(western + [window] + eastern, axis=1)
    wide = wide[:, hops * columns - reach : hops * columns + columns + reach]
    polar_values = lax.dynamic_slice_in_dim(basis_values, start, POLAR, 0)
    polar_conv = conv_rows(wide, polar_values)
    conv = lax.dynamic_update_slice_in_dim(conv, polar_conv, start, 0)

    conv = conv.astype(jnp.bfloat16).reshape(lat_rows * columns, -1)
    mixing = jnp.dot(conv, mix_weight.reshape(-1, mix_weight.shape[-1]),
                     preferred_element_type=jnp.float32)
    mixing = mixing.reshape(features.shape)
    return (features.astype(jnp.float32) + mixing).astype(jnp.bfloat16)


def solution(mesh):
    in_specs = (P("lat", "lon", None), P("lat", None, None), P("lat", None, None), P("lat"), P())
    out_specs = P("lat", "lon", None)
    return jax.shard_map(body, mesh=mesh, in_specs=in_specs, out_specs=out_specs, check_vma=False)
```

time: 388 us -> 131 us (0.34)
  the two profiles are of different devices: /device:TPU:2 before, /device:TPU:3 now
where the time goes in v1:
time: 131 us; the launch traced here: 130 us
  matrix products  43.8 us (33%)
  local copies, waits for them, and re-layouts  41.4 us (32%)
  starting transfers between devices  21.2 us (16%)
  waiting for transfers between devices  20.6 us (16%)
  other arithmetic  3.26 us (2%)
    convert_element_type x1, local copies, waits for them, and re-layouts, conv_rows(): kernel = jnp.einsum('nbrk,jmk->njbrm', values, shift_table(taps, columns)...  34.3 us
    dot_general x2, matrix products, conv_rows(): jnp.einsum('njbrm,nrmc->njbc', kernel, stacked, preferred_element_type=jn...  22.3 us
    ppermute x6, waiting for transfers between devices, shifted(): return lax.ppermute(block, axis, route)  20.6 us
    ppermute x6, starting transfers between devices, shifted(): return lax.ppermute(block, axis, route)  13.8 us
    dot_general x2, matrix products, conv_rows(): jnp.einsum('nbrk,jmk->njbrm', values, shift_table(taps, columns), preferr...  11.5 us
    dot_general x1, matrix products, body(): jnp.dot(conv, mix_weight.reshape(-1, mix_weight.shape[-1]), preferred_ele...  10 us
    another operation x2, local copies, waits for them, and re-layouts, conv_rows(): stacked = jnp.stack([extended[r:r + rows] for r in range(3)], axis=1)  4.68 us
    ppermute x1, starting transfers between devices, lat_extended(): after = lax.ppermute(value[:1], 'lat', down)  4.19 us
  transfers between devices with their start and end apart: 8, of which 3 were waited for; matrix products, arithmetic and copies ran while one was open for 39% of the time, Pallas kernels for 0%

profile of v1, /device:TPU:3, one launch (start us, length us, event | category | flops | bytes accessed | tf_op | source)
XLA Modules:
  0.0 130.4 jit_solution(15450954182336452834)
XLA Ops:
  0.0 0.0 copy-start
  0.0 0.8 fusion.30
  0.8 3.2 %collective-permute-start = (bf16[1,32,256]{2,1,0:T(8,128)(2,1)S(1)}, bf16[1,32,256]{2,1,0:T(8,128)(2,1)S(1)}, u32[]{:S(2)}, u32[]{:S(2)}) collective-permute-start(bf16[1,32,256]{2,1,0:T(8,128)(2,1)S(1)} %get-tuple-element.11), channel_id=1, source_target_pairs={{0,32},{32,64},{64,96},{96,128},{128,160},{160,192},{192,224},{1,3... | collective-permute-start | bytes 49160 | tf_op jit(solution)/shard_map/ppermute | solution.py:20
  4.0 4.2 %collective-permute-start.1 = (bf16[1,32,256]{2,1,0:T(8,128)(2,1)S(1)}, bf16[1,32,256]{2,1,0:T(8,128)(2,1)S(1)}, u32[]{:S(2)}, u32[]{:S(2)}) collective-permute-start(bf16[1,32,256]{2,1,0:T(8,128)(2,1)S(1)} %get-tuple-element.10), channel_id=1, source_target_pairs={{32,0},{64,32},{96,64},{128,96},{160,128},{192,160},{224,192},{33,... | collective-permute-start | bytes 49160 | tf_op jit(solution)/shard_map/ppermute | solution.py:21
  8.3 0.7 multiply_rsqrt_fusion
  8.9 0.7 broadcast_compare_fusion
  9.7 1.5 %multiply_convert_fusion = bf16[96,9,3,129]{0,3,2,1:T(8,128)(2,1)S(1)} fusion(f32[96]{0:T(128)S(1)} %multiply_rsqrt_fusion, f32[96,3,129]{0,2,1:T(8,128)} %param.6, s32[96,3,129]{0,2,1:T(8,128)} %param.7, pred[96,129]{0,1:T(8,128)(4,1)S(1)} %broadcast_compare_fusion), kind=kLoop, calls=%fused_computation.25 | loop fusion | flops 1671840 | bytes 978720 | tf_op jit(solution)/shard_map/convert_element_type | solution.py:33
  11.2 7.1 %convert_bitcast_fusion = bf16[96,32,9,3,64]{0,4,3,2,1:T(8,128)(2,1)} fusion(s32[32,64]{1,0:T(8,128)S(1)} %iota_subtract_fusion.1, bf16[96,9,3,129]{0,3,2,1:T(8,128)(2,1)S(1)} %multiply_convert_fusion), kind=kOutput, calls=%fused_computation.2 | convolution fusion | flops 355731456 | bytes 10909696 | tf_op jit(solution)/shard_map/nbrk,jmk->njbrm/dot_general | solution.py:46
  18.2 0.3 constant_dynamic-slice_fusion.1
  18.5 0.9 copy.13
  19.5 4.4 %convert_bitcast_fusion.1 = bf16[8,32,9,3,160]{4,2,3,0,1:T(8,128)(2,1)} fusion(s32[32,160]{1,0:T(8,128)S(1)} %iota_subtract_fusion, bf16[8,9,3,129]{3,1,2,0:T(8,128)(2,1)S(1)} %copy.13), kind=kOutput, calls=%fused_computation.9 | convolution fusion | flops 287093760 | bytes 2288048 | tf_op jit(solution)/shard_map/nbrk,jmk->njbrm/dot_general | solution.py:46
  23.9 0.0 copy-start.1
  23.9 34.3 %copy.12 = bf16[96,32,9,3,64]{4,1,3,2,0:T(8,128)(2,1)} copy(bf16[96,32,9,3,64]{0,4,3,2,1:T(8,128)(2,1)} %convert_bitcast_fusion) | data formatting | bytes 21233664 | tf_op jit(solution)/shard_map/convert_element_type | solution.py:49
  58.2 0.0 collective-permute-done
  58.2 0.0 copy-done.1
  58.2 0.1 constant_dynamic-update-slice_fusion.1
  58.3 0.0 collective-permute-done.1
  58.4 1.9 %collective-permute-start.4 = (bf16[10,32,256]{2,1,0:T(8,128)(2,1)S(1)}, bf16[10,32,256]{2,1,0:T(8,128)(2,1)S(1)}, u32[]{:S(2)}, u32[]{:S(2)}) collective-permute-start(bf16[10,32,256]{2,1,0:T(8,128)(2,1)S(1)} %constant_dynamic-slice_fusion), channel_id=1, source_target_pairs={{30,0},{31,1},{0,2},{1,3},{2,4},{3,5},{4,6},{5,7},{6,8},{7,9},{8,1... | collective-permute-start | bytes 491528 | tf_op jit(solution)/shard_map/ppermute | solution.py:13
  60.3 3.9 %collective-permute-start.5 = (bf16[10,32,256]{2,1,0:T(8,128)(2,1)S(1)}, bf16[10,32,256]{2,1,0:T(8,128)(2,1)S(1)}, u32[]{:S(2)}, u32[]{:S(2)}) collective-permute-start(bf16[10,32,256]{2,1,0:T(8,128)(2,1)S(1)} %constant_dynamic-slice_fusion), channel_id=1, source_target_pairs={{31,0},{0,1},{1,2},{2,3},{3,4},{4,5},{5,6},{6,7},{7,8},{8,9},{9,10... | collective-permute-start | bytes 491528 | tf_op jit(solution)/shard_map/ppermute | solution.py:13
  64.2 0.1 fusion.29
  64.3 0.1 collective-permute-start.6
  64.4 2.7 %collective-permute-start.7 = (bf16[10,32,256]{2,1,0:T(8,128)(2,1)S(1)}, bf16[10,32,256]{2,1,0:T(8,128)(2,1)S(1)}, u32[]{:S(2)}, u32[]{:S(2)}) collective-permute-start(bf16[10,32,256]{2,1,0:T(8,128)(2,1)S(1)} %constant_dynamic-slice_fusion), channel_id=1, source_target_pairs={{2,0},{3,1},{4,2},{5,3},{6,4},{7,5},{8,6},{9,7},{10,8},{11,9},{12,... | collective-permute-start | bytes 491528 | tf_op jit(solution)/shard_map/ppermute | solution.py:13
  67.2 3.4 %collective-permute-start.2 = (bf16[98,16,256]{2,1,0:T(8,128)(2,1)S(1)}, bf16[98,16,256]{2,1,0:T(8,128)(2,1)S(1)}, u32[]{:S(2)}, u32[]{:S(2)}) collective-permute-start(bf16[98,16,256]{2,1,0:T(8,128)(2,1)S(1)} %get-tuple-element.8), channel_id=1, source_target_pairs={{31,0},{0,1},{1,2},{2,3},{3,4},{4,5},{5,6},{6,7},{7,8},{8,9},{9,10... | collective-permute-start | bytes 2408456 | tf_op jit(solution)/shard_map/ppermute | solution.py:13
  70.5 0.0 collective-permute-done.4
  70.5 1.8 %collective-permute-start.3 = (bf16[98,16,256]{2,1,0:T(8,128)(2,1)S(1)}, bf16[98,16,256]{2,1,0:T(8,128)(2,1)S(1)}, u32[]{:S(2)}, u32[]{:S(2)}) collective-permute-start(bf16[98,16,256]{2,1,0:T(8,128)(2,1)S(1)} %get-tuple-element.9), channel_id=1, source_target_pairs={{1,0},{2,1},{3,2},{4,3},{5,4},{6,5},{7,6},{8,7},{9,8},{10,9},{11,1... | collective-permute-start | bytes 2408456 | tf_op jit(solution)/shard_map/ppermute | solution.py:13
  72.3 0.0 collective-permute-done.5
  72.4 2.9 %collective-permute-done.6 = bf16[10,32,256]{2,1,0:T(8,128)(2,1)S(1)} collective-permute-done((bf16[10,32,256]{2,1,0:T(8,128)(2,1)S(1)}, bf16[10,32,256]{2,1,0:T(8,128)(2,1)S(1)}, u32[]{:S(2)}, u32[]{:S(2)}) %collective-permute-start.6) | collective-permute-done | bytes 163872 | tf_op jit(solution)/shard_map/ppermute | solution.py:13
  75.4 0.0 collective-permute-done.7
  75.4 1.3 slice_bitcast_fusion.5
  76.7 13.6 %collective-permute-done.2 = bf16[98,16,256]{2,1,0:T(8,128)(2,1)S(1)} collective-permute-done((bf16[98,16,256]{2,1,0:T(8,128)(2,1)S(1)}, bf16[98,16,256]{2,1,0:T(8,128)(2,1)S(1)}, u32[]{:S(2)}, u32[]{:S(2)}) %collective-permute-start.2) | collective-permute-done | bytes 802848 | tf_op jit(solution)/shard_map/ppermute | solution.py:13
  90.2 4.1 %collective-permute-done.3 = bf16[98,16,256]{2,1,0:T(8,128)(2,1)S(1)} collective-permute-done((bf16[98,16,256]{2,1,0:T(8,128)(2,1)S(1)}, bf16[98,16,256]{2,1,0:T(8,128)(2,1)S(1)}, u32[]{:S(2)}, u32[]{:S(2)}) %collective-permute-start.3) | collective-permute-done | bytes 802848 | tf_op jit(solution)/shard_map/ppermute | solution.py:13
  94.3 0.4 pad_maximum_fusion
  94.7 0.0 slice-start
  94.7 3.4 %slice_bitcast_fusion.2 = (bf16[96,1,64,256]{3,2,1,0:T(8,128)(2,1)S(1)}, bf16[96,1,64,256]{3,2,1,0:T(8,128)(2,1)}, bf16[96,1,64,256]{3,2,1,0:T(8,128)(2,1)}) fusion(bf16[98,64,256]{2,1,0:T(8,128)(2,1)S(1)} %pad_maximum_fusion), kind=kLoop, calls=%fused_computation.18 | loop fusion | bytes 18874368 | tf_op jit(solution)/shard_map/stack | solution.py:50
  98.1 0.0 slice-start.1
  98.1 16.1 %convolution_bitcast_fusion = bf16[96,32,9,256]{3,1,2,0:T(8,128)(2,1)} fusion(bf16[96,32,9,3,64]{4,1,3,2,0:T(8,128)(2,1)} %copy.12, bf16[96,1,64,256]{3,2,1,0:T(8,128)(2,1)} %get-tuple-element.6, bf16[96,1,64,256]{3,2,1,0:T(8,128)(2,1)} %get-tuple-element.7, bf16[96,1,64,256]{3,2,1,0:T(8,128)(2,1)S(1)} %get-tuple-element.5), kind=kOutput, calls=%fused_computation.3 | convolution fusion | flops 2727346176 | bytes 34209792 | tf_op jit(solution)/shard_map/njbrm,nrmc->njbc/dot_general | solution.py:51
  114.2 0.0 slice-done
  114.2 0.0 slice-done.1
  114.2 6.2 %bitcast_dynamic-update-slice_fusion = bf16[96,32,9,256]{3,1,2,0:T(8,128)(2,1)} fusion(bf16[96,32,9,256]{3,1,2,0:T(8,128)(2,1)} %convolution_bitcast_fusion, s32[]{:T(128)S(6)} %select_n.12, bf16[8,32,9,3,160]{4,2,3,0,1:T(8,128)(2,1)S(1)} %bitcast.64, bf16[8,1,160,256]{3,2,0,1:T(8,128)(2,1)} %get-tuple-element.13, ...), kind=kOutput, calls=%fused_computation.21 | convolution fusion | flops 568197120 | bytes 6537220 | tf_op jit(solution)/shard_map/njbrm,nrmc->njbc/dot_general | solution.py:51
  120.4 0.0 copy-done
  120.4 10.0 %fusion.13 = bf16[96,32,256]{2,1,0:T(8,128)(2,1)} fusion(bf16[96,32,256]{2,1,0:T(8,128)(2,1)S(1)} %copy-done.1, bf16[96,32,9,256]{3,1,2,0:T(8,128)(2,1)} %bitcast_dynamic-update-slice_fusion, bf16[9,256,256]{2,1,0:T(8,128)(2,1)S(1)} %copy-done), kind=kOutput, calls=%fused_computation.20 | convolution fusion | flops 3626237952 | bytes 18481152 | tf_op jit(solution)/shard_map/dot_general | solution.py:81
  (12 shorter events, 0.1 us)
Async XLA Ops:
  0.0 120.4 %copy-start = (bf16[9,256,256]{2,1,0:T(8,128)(2,1)S(1)}, bf16[9,256,256]{2,1,0:T(8,128)(2,1)}, u32[]{:S(2)}) copy-start(bf16[9,256,256]{2,1,0:T(8,128)(2,1)} %param.9) | copy-start | bytes 3538948
  0.8 57.4 %collective-permute-start = (bf16[1,32,256]{2,1,0:T(8,128)(2,1)S(1)}, bf16[1,32,256]{2,1,0:T(8,128)(2,1)S(1)}, u32[]{:S(2)}, u32[]{:S(2)}) collective-permute-start(bf16[1,32,256]{2,1,0:T(8,128)(2,1)S(1)} %get-tuple-element.11), channel_id=1, source_target_pairs={{0,32},{32,64},{64,96},{96,128},{128,160},{160,192},{192,224},{1,3... | collective-permute-start | bytes 49160 | tf_op jit(solution)/shard_map/ppermute | solution.py:20
  4.0 54.3 %collective-permute-start.1 = (bf16[1,32,256]{2,1,0:T(8,128)(2,1)S(1)}, bf16[1,32,256]{2,1,0:T(8,128)(2,1)S(1)}, u32[]{:S(2)}, u32[]{:S(2)}) collective-permute-start(bf16[1,32,256]{2,1,0:T(8,128)(2,1)S(1)} %get-tuple-element.10), channel_id=1, source_target_pairs={{32,0},{64,32},{96,64},{128,96},{160,128},{192,160},{224,192},{33,... | collective-permute-start | bytes 49160 | tf_op jit(solution)/shard_map/ppermute | solution.py:21
  23.9 34.3 %copy-start.1 = (bf16[96,32,256]{2,1,0:T(8,128)(2,1)S(1)}, bf16[96,32,256]{2,1,0:T(8,128)(2,1)}, u32[]{:S(2)}) copy-start(bf16[96,32,256]{2,1,0:T(8,128)(2,1)} %param.5) | copy-start | bytes 4718596
  58.4 12.1 %collective-permute-start.4 = (bf16[10,32,256]{2,1,0:T(8,128)(2,1)S(1)}, bf16[10,32,256]{2,1,0:T(8,128)(2,1)S(1)}, u32[]{:S(2)}, u32[]{:S(2)}) collective-permute-start(bf16[10,32,256]{2,1,0:T(8,128)(2,1)S(1)} %constant_dynamic-slice_fusion), channel_id=1, source_target_pairs={{30,0},{31,1},{0,2},{1,3},{2,4},{3,5},{4,6},{5,7},{6,8},{7,9},{8,1... | collective-permute-start | bytes 491528 | tf_op jit(solution)/shard_map/ppermute | solution.py:13
  60.3 12.0 %collective-permute-start.5 = (bf16[10,32,256]{2,1,0:T(8,128)(2,1)S(1)}, bf16[10,32,256]{2,1,0:T(8,128)(2,1)S(1)}, u32[]{:S(2)}, u32[]{:S(2)}) collective-permute-start(bf16[10,32,256]{2,1,0:T(8,128)(2,1)S(1)} %constant_dynamic-slice_fusion), channel_id=1, source_target_pairs={{31,0},{0,1},{1,2},{2,3},{3,4},{4,5},{5,6},{6,7},{7,8},{8,9},{9,10... | collective-permute-start | bytes 491528 | tf_op jit(solution)/shard_map/ppermute | solution.py:13
  64.3 11.0 %collective-permute-start.6 = (bf16[10,32,256]{2,1,0:T(8,128)(2,1)S(1)}, bf16[10,32,256]{2,1,0:T(8,128)(2,1)S(1)}, u32[]{:S(2)}, u32[]{:S(2)}) collective-permute-start(bf16[10,32,256]{2,1,0:T(8,128)(2,1)S(1)} %constant_dynamic-slice_fusion), channel_id=1, source_target_pairs={{1,0},{2,1},{3,2},{4,3},{5,4},{6,5},{7,6},{8,7},{9,8},{10,9},{11,1... | collective-permute-start | bytes 491528 | tf_op jit(solution)/shard_map/ppermute | solution.py:13
  64.4 10.9 %collective-permute-start.7 = (bf16[10,32,256]{2,1,0:T(8,128)(2,1)S(1)}, bf16[10,32,256]{2,1,0:T(8,128)(2,1)S(1)}, u32[]{:S(2)}, u32[]{:S(2)}) collective-permute-start(bf16[10,32,256]{2,1,0:T(8,128)(2,1)S(1)} %constant_dynamic-slice_fusion), channel_id=1, source_target_pairs={{2,0},{3,1},{4,2},{5,3},{6,4},{7,5},{8,6},{9,7},{10,8},{11,9},{12,... | collective-permute-start | bytes 491528 | tf_op jit(solution)/shard_map/ppermute | solution.py:13
  67.2 23.1 %collective-permute-start.2 = (bf16[98,16,256]{2,1,0:T(8,128)(2,1)S(1)}, bf16[98,16,256]{2,1,0:T(8,128)(2,1)S(1)}, u32[]{:S(2)}, u32[]{:S(2)}) collective-permute-start(bf16[98,16,256]{2,1,0:T(8,128)(2,1)S(1)} %get-tuple-element.8), channel_id=1, source_target_pairs={{31,0},{0,1},{1,2},{2,3},{3,4},{4,5},{5,6},{6,7},{7,8},{8,9},{9,10... | collective-permute-start | bytes 2408456 | tf_op jit(solution)/shard_map/ppermute | solution.py:13
  70.5 23.8 %collective-permute-start.3 = (bf16[98,16,256]{2,1,0:T(8,128)(2,1)S(1)}, bf16[98,16,256]{2,1,0:T(8,128)(2,1)S(1)}, u32[]{:S(2)}, u32[]{:S(2)}) collective-permute-start(bf16[98,16,256]{2,1,0:T(8,128)(2,1)S(1)} %get-tuple-element.9), channel_id=1, source_target_pairs={{1,0},{2,1},{3,2},{4,3},{5,4},{6,5},{7,6},{8,7},{9,8},{10,9},{11,1... | collective-permute-start | bytes 2408456 | tf_op jit(solution)/shard_map/ppermute | solution.py:13
  94.7 19.5 %slice-start = ((s8[6291456]{0:T(1024)(128)(4,1)}), s8[4194304]{0:T(1024)(128)(4,1)S(1)}, s32[]{:S(2)}) async-start(s8[6291456]{0:T(1024)(128)(4,1)} %bitcast.63), calls=%async_computation | async-start | bytes 8388608
  98.1 16.1 %slice-start.1 = ((s8[6291456]{0:T(1024)(128)(4,1)}), s8[2097152]{0:T(1024)(128)(4,1)S(1)}, s32[]{:S(2)}) async-start(s8[6291456]{0:T(1024)(128)(4,1)} %bitcast.63), calls=%async_computation.1 | async-start | bytes 4194304

commit v2 on v1

v2 whole, which is shorter than its diff:
```python
import functools

import jax
import jax.numpy as jnp
from jax import lax
from jax.experimental import pallas as pl
from jax.experimental.pallas import tpu as pltpu
from jax.sharding import PartitionSpec as P

POLAR = 8
NEAR = 16
BLOCK = 8


def shifted(block, axis, distance):
    devices = range(lax.axis_size(axis))
    route = [((i - distance) % len(devices), i) for i in devices]
    return lax.ppermute(block, axis, route)


def lat_extended(value):
    count, length = lax.axis_size("lat"), value.shape[0]
    up = [(i, i + 1) for i in range(count - 1)]
    down = [(j, i) for i, j in up]
    before = lax.ppermute(value[length - 1 :], "lat", up)
    after = lax.ppermute(value[:1], "lat", down)
    return jnp.concatenate([before, value, after], axis=0)


def basis_table(quad_weights, cycle_index, widths, count):
    offsets = jnp.arange(quad_weights.shape[2]) - quad_weights.shape[2] // 2
    inside = jnp.abs(offsets)[None, None, :] <= widths[:, None, None]
    member = cycle_index[:, None, :, :] == jnp.arange(count)[None, :, None, None]
    scale_row = 1.0 / jnp.sqrt(3.0 * (2.0 * widths.astype(jnp.float32) + 1.0))
    values = jnp.where(
        member & inside[:, None, :, :], quad_weights[:, None, :, :], jnp.float32(0.0)
    )
    return (values * scale_row[:, None, None, None]).astype(jnp.bfloat16)


def toeplitz_stacked(values, columns):
    rows, count, offsets, taps = values.shape
    span = columns + taps - 1
    out_pos = jnp.arange(columns)[:, None, None, None, None]
    in_row = jnp.arange(offsets)[None, :, None, None, None]
    in_pos = jnp.arange(span)[None, None, :, None, None]
    tap_row = jnp.arange(offsets)[None, None, None, :, None]
    tap = jnp.arange(taps)[None, None, None, None, :]
    table = ((in_row == tap_row) & (in_pos - out_pos == tap)).astype(jnp.bfloat16)
    table = table.reshape(columns, offsets * span, offsets * taps)
    kernel = jnp.einsum(
        "nbs,jps->nbjp", values.reshape(rows, count, offsets * taps), table,
        preferred_element_type=jnp.float32,
    ).astype(jnp.bfloat16)
    return kernel.reshape(rows, count * columns, offsets * span)


def toeplitz_split(values, columns):
    rows, count, offsets, taps = values.shape
    span = columns + taps - 1
    out_pos = jnp.arange(columns)[:, None, None]
    in_pos = jnp.arange(span)[None, :, None]
    tap = jnp.arange(taps)[None, None, :]
    table = (in_pos - out_pos == tap).astype(jnp.bfloat16)
    kernel = jnp.einsum(
        "nbrk,jmk->nbjrm", values, table, preferred_element_type=jnp.float32
    ).astype(jnp.bfloat16)
    return kernel.reshape(rows, count * columns, offsets * span)


def conv_mix_kernel(start_ref, ext_ref, k_ref, f_ref, w_ref, *rest):
    o_ref, conv_scr = rest[-2], rest[-1]
    rows, columns, channels = f_ref.shape
    count = w_ref.shape[0]
    span = ext_ref.shape[1]
    base = pl.program_id(0) * rows
    for q in range(rows):
        window = ext_ref[pl.ds(base + q, 3)].reshape(3 * span, channels)
        conv = jnp.dot(k_ref[q], window, preferred_element_type=jnp.float32)
        conv = conv.astype(jnp.bfloat16)
        for b in range(count):
            conv_scr[b, q * columns : (q + 1) * columns, :] = conv[b * columns : (b + 1) * columns]
    acc = f_ref[...].reshape(rows * columns, channels).astype(jnp.float32)
    for b in range(count):
        acc = acc + jnp.dot(conv_scr[b], w_ref[b], preferred_element_type=jnp.float32)
    o_ref[...] = acc.reshape(rows, columns, channels).astype(o_ref.dtype)


def conv_mix(start, extended, kernel, features, mix_weight, previous=None):
    lat_rows, columns, channels = features.shape
    count = mix_weight.shape[0]
    rows = kernel.shape[0]
    blocks = rows // BLOCK
    if previous is None:
        row_map = lambda i, s: (i, 0, 0)
    else:
        row_map = lambda i, s: (s[0] // BLOCK + i, 0, 0)
    in_specs = [
        pl.BlockSpec(extended.shape, lambda i, s: (0, 0, 0)),
        pl.BlockSpec((BLOCK,) + kernel.shape[1:], lambda i, s: (i, 0, 0)),
        pl.BlockSpec((BLOCK, columns, channels), row_map),
        pl.BlockSpec(mix_weight.shape, lambda i, s: (0, 0, 0)),
    ]
    operands = [start, extended, kernel, features, mix_weight]
    aliases = {}
    if previous is not None:
        in_specs.append(pl.BlockSpec(memory_space=pl.ANY))
        operands.append(previous)
        aliases = {len(operands) - 1: 0}
    grid_spec = pltpu.PrefetchScalarGridSpec(
        num_scalar_prefetch=1,
        grid=(blocks,),
        in_specs=in_specs,
        out_specs=pl.BlockSpec((BLOCK, columns, channels), row_map),
        scratch_shapes=[pltpu.VMEM((count, BLOCK * columns, channels), jnp.bfloat16)],
    )
    return pl.pallas_call(
        conv_mix_kernel,
        grid_spec=grid_spec,
        out_shape=jax.ShapeDtypeStruct(features.shape, features.dtype),
        input_output_aliases=aliases,
    )(*operands)


def body(features, quad_weights, cycle_index, widths, mix_weight):
    count = mix_weight.shape[0]
    lat_rows, columns = features.shape[0], features.shape[1]
    reach = quad_weights.shape[2] // 2
    basis_values = basis_table(quad_weights, cycle_index, widths, count)
    padded = lat_extended(features)

    last_band = lax.axis_index("lat") == lax.axis_size("lat") - 1
    start = jnp.where(last_band, lat_rows - POLAR, 0).astype(jnp.int32)
    start_arr = start.reshape(1)

    near = jnp.concatenate(
        [shifted(padded[:, columns - NEAR :], "lon", 1), padded,
         shifted(padded[:, :NEAR], "lon", -1)], axis=1)
    near_kernel = toeplitz_stacked(basis_values[:, :, :, reach - NEAR : reach + NEAR + 1], columns)
    out = conv_mix(start_arr, near, near_kernel, features, mix_weight)

    window = lax.dynamic_slice_in_dim(padded, start, POLAR + 2, 0)
    hops = reach // columns
    western = [shifted(window, "lon", hop) for hop in range(hops, 0, -1)]
    eastern = [shifted(window, "lon", -hop) for hop in range(1, hops + 1)]
    wide = jnp.concatenate(western + [window] + eastern, axis=1)
    wide = wide[:, hops * columns - reach : hops * columns + columns + reach]
    polar_values = lax.dynamic_slice_in_dim(basis_values, start, POLAR, 0)
    wide_kernel = toeplitz_split(polar_values, columns)
    return conv_mix(start_arr, wide, wide_kernel, features, mix_weight, previous=out)


def solution(mesh):
    in_specs = (P("lat", "lon", None), P("lat", None, None), P("lat", None, None), P("lat"), P())
    out_specs = P("lat", "lon", None)
    return jax.shard_map(body, mesh=mesh, in_specs=in_specs, out_specs=out_specs, check_vma=False)
```

time: 131 us -> 115 us (0.88)
  the two profiles are of different devices: /device:TPU:3 before, /device:TPU:125 now
where the time goes in v2:
time: 115 us; the launch traced here: 114 us
  local copies, waits for them, and re-layouts  44.5 us (39%)
  Pallas kernels  24.3 us (21%)
  starting transfers between devices  16.6 us (14%)
  matrix products  11.7 us (10%)
  waiting for transfers between devices  8.48 us (7%)
  other arithmetic  8.3 us (7%)
    pallas_call x2, Pallas kernels, conv_mix(): pl.pallas_call(conv_mix_kernel, grid_spec=grid_spec, out_shape=jax.ShapeD...  24.3 us
    convert_element_type x1, local copies, waits for them, and re-layouts, toeplitz_stacked(): kernel = jnp.einsum('nbs,jps->nbjp', values.reshape(rows, count, offsets...  17.4 us
    reshape x1, local copies, waits for them, and re-layouts, toeplitz_split(): return kernel.reshape(rows, count * columns, offsets * span)  9.52 us
    ppermute x6, starting transfers between devices, shifted(): return lax.ppermute(block, axis, route)  9.26 us
    dot_general x1, matrix products, toeplitz_stacked(): jnp.einsum('nbs,jps->nbjp', values.reshape(rows, count, offsets * taps),...  8.93 us
    ppermute x6, waiting for transfers between devices, shifted(): return lax.ppermute(block, axis, route)  8.48 us
    ppermute x1, starting transfers between devices, lat_extended(): before = lax.ppermute(value[length - 1:], 'lat', up)  5.02 us
    unnamed x16, local copies, waits for them, and re-layouts  4.82 us
  transfers between devices with their start and end apart: 8, of which 1 were waited for; matrix products, arithmetic and copies ran while one was open for 52% of the time, Pallas kernels for 0%

profile of v2, /device:TPU:125, one launch (start us, length us, event | category | flops | bytes accessed | tf_op | source)
XLA Modules:
  0.0 114.3 jit_solution(1579965722710047468)
XLA Ops:
  0.0 0.7 fusion.13
  0.7 2.4 %collective-permute-start.1 = (bf16[1,32,256]{2,1,0:T(8,128)(2,1)S(1)}, bf16[1,32,256]{2,1,0:T(8,128)(2,1)S(1)}, u32[]{:S(2)}, u32[]{:S(2)}) collective-permute-start(bf16[1,32,256]{2,1,0:T(8,128)(2,1)S(1)} %get-tuple-element.7), channel_id=1, source_target_pairs={{32,0},{64,32},{96,64},{128,96},{160,128},{192,160},{224,192},{33,... | collective-permute-start | bytes 49160 | tf_op jit(solution)/shard_map/ppermute | solution.py:26
  3.1 5.0 %collective-permute-start = (bf16[1,32,256]{2,1,0:T(8,128)(2,1)S(1)}, bf16[1,32,256]{2,1,0:T(8,128)(2,1)S(1)}, u32[]{:S(2)}, u32[]{:S(2)}) collective-permute-start(bf16[1,32,256]{2,1,0:T(8,128)(2,1)S(1)} %get-tuple-element.8), channel_id=1, source_target_pairs={{0,32},{32,64},{64,96},{96,128},{128,160},{160,192},{192,224},{1,3... | collective-permute-start | bytes 49160 | tf_op jit(solution)/shard_map/ppermute | solution.py:25
  8.2 0.7 multiply_rsqrt_fusion
  8.8 0.7 broadcast_compare_fusion
  9.6 0.1 iota_compare_fusion.2
  9.7 1.1 %copy.12 = f32[96,3,129]{2,1,0:T(4,128)S(1)} copy(f32[96,3,129]{0,2,1:T(8,128)} %param.6) | data formatting | bytes 297216 | tf_op args[1]
  10.8 1.1 %copy.11 = s32[96,3,129]{2,1,0:T(4,128)S(1)} copy(s32[96,3,129]{0,2,1:T(8,128)} %param.7) | data formatting | bytes 297216 | tf_op args[2]
  12.0 2.0 %broadcast_and_fusion = pred[32,3,64,3,33]{2,1,0,4,3:T(4,128)(4,1)S(1)} fusion(pred[32,64,33]{1,0,2:T(8,128)(4,1)S(1)} %iota_compare_fusion.2, pred[3,3]{0,1:T(4,128)(4,1)S(1)} %iota_compare_fusion.3), kind=kLoop, calls=%fused_computation.8 | loop fusion | flops 608256 | bytes 675849 | tf_op jit(solution)/shard_map/and | solution.py:49
  13.9 2.3 %and.37 = pred[32,192,99]{1,0,2:T(32,128)(4,1)S(1)} reshape(pred[32,3,64,3,33]{2,1,0,4,3:T(4,128)(4,1)S(1)} %broadcast_and_fusion) | data formatting | bytes 1216512 | tf_op jit(solution)/shard_map/and | solution.py:49
  16.3 2.4 %copy.16 = pred[32,192,99]{2,1,0:T(32,128)(4,1)S(1)} copy(pred[32,192,99]{1,0,2:T(32,128)(4,1)S(1)} %and.37) | data formatting | bytes 1216512 | tf_op jit(solution)/shard_map/and | solution.py:49
  18.7 1.1 multiply_convert_fusion
  19.8 0.0 copy-start.1
  19.8 1.4 %copy-done.1 = bf16[96,9,3,129]{3,1,2,0:T(8,128)(2,1)} copy-done((bf16[96,9,3,129]{3,1,2,0:T(8,128)(2,1)}, bf16[96,9,3,129]{3,1,2,0:T(8,128)(2,1)S(1)}, u32[]{:S(2)}) %copy-start.1) | copy-done | bytes 668760
  21.3 0.4 slice.22
  21.6 0.8 copy.14
  22.4 0.1 reshape.120
  22.6 0.0 copy-start
  22.6 8.9 %convolution_convert_fusion = bf16[96,9,32,192]{3,0,2,1:T(8,128)(2,1)} fusion(pred[32,192,99]{2,1,0:T(32,128)(4,1)S(1)} %copy.16, bf16[96,9,99]{0,2,1:T(8,128)(2,1)S(1)} %reshape.120), kind=kOutput, calls=%fused_computation | convolution fusion | flops 1056374784 | bytes 11396160 | tf_op jit(solution)/shard_map/nbs,jps->nbjp/dot_general | solution.py:51
  31.5 0.6 iota_subtract_fusion
  32.1 0.0 collective-permute-done
  32.1 0.0 copy-done
  32.1 0.1 constant_dynamic-update-slice_fusion.1
  32.2 0.0 copy-start.3
  32.2 0.0 collective-permute-done.1
  32.3 4.2 %collective-permute-start.3 = (bf16[10,32,256]{2,1,0:T(8,128)(2,1)S(1)}, bf16[10,32,256]{2,1,0:T(8,128)(2,1)S(1)}, u32[]{:S(2)}, u32[]{:S(2)}) collective-permute-start(bf16[10,32,256]{2,1,0:T(8,128)(2,1)S(1)} %constant_dynamic-slice_fusion), channel_id=1, source_target_pairs={{31,0},{0,1},{1,2},{2,3},{3,4},{4,5},{5,6},{6,7},{7,8},{8,9},{9,10... | collective-permute-start | bytes 491528 | tf_op jit(solution)/shard_map/ppermute | solution.py:18
  36.5 2.7 %collective-permute-start.2 = (bf16[10,32,256]{2,1,0:T(8,128)(2,1)S(1)}, bf16[10,32,256]{2,1,0:T(8,128)(2,1)}, u32[]{:S(2)}, u32[]{:S(2)}) collective-permute-start(bf16[10,32,256]{2,1,0:T(8,128)(2,1)S(1)} %constant_dynamic-slice_fusion), channel_id=1, source_target_pairs={{30,0},{31,1},{0,2},{1,3},{2,4},{3,5},{4,6},{5,7},{6,8},{7,9},{8,1... | collective-permute-start | bytes 491528 | tf_op jit(solution)/shard_map/ppermute | solution.py:18
  39.2 1.3 %fusion.12 = (bf16[98,16,256]{2,1,0:T(8,128)(2,1)}, bf16[98,16,256]{2,1,0:T(8,128)(2,1)}) fusion(bf16[98,32,256]{2,1,0:T(8,128)(2,1)S(1)} %constant_dynamic-update-slice_fusion), kind=kLoop, calls=%fused_computation.32 | loop fusion | bytes 3211264 | tf_op jit(solution)/shard_map/slice | solution.py:137
  40.5 0.4 collective-permute-start.6
  40.9 0.1 collective-permute-start.7
  41.0 0.0 copy-done.3
  41.0 2.8 %convert_bitcast_fusion = bf16[8,9,32,3,160]{4,1,3,0,2:T(8,128)(2,1)S(1)} fusion(s32[32,160]{1,0:T(8,128)S(1)} %copy-done.3, bf16[96,9,3,129]{3,1,2,0:T(8,128)(2,1)} %copy-done.1, s32[]{:T(128)} %select_n.10), kind=kOutput, calls=%fused_computation.1 | convolution fusion | flops 287093760 | bytes 2429440 | tf_op jit(solution)/shard_map/nbrk,jmk->nbjrm/dot_general | solution.py:65
  43.8 4.7 %copy.13 = bf16[8,9,32,3,160]{4,3,2,1,0:T(4,128)(2,1)} copy(bf16[8,9,32,3,160]{4,1,3,0,2:T(8,128)(2,1)S(1)} %convert_bitcast_fusion) | data formatting | bytes 4423680 | tf_op jit(solution)/shard_map/convert_element_type | solution.py:67
  48.5 9.5 %reshape.119.k_ref = bf16[8,288,480]{2,1,0:T(8,128)(2,1)} reshape(bf16[8,9,32,3,160]{4,3,2,1,0:T(4,128)(2,1)} %copy.13) | data formatting | bytes 4423680 | tf_op jit(solution)/shard_map/reshape | solution.py:68
  58.0 17.4 %copy.17 = bf16[96,9,32,192]{3,2,1,0:T(8,128)(2,1)} copy(bf16[96,9,32,192]{3,0,2,1:T(8,128)(2,1)} %convolution_convert_fusion) | data formatting | bytes 21233664 | tf_op jit(solution)/shard_map/convert_element_type | solution.py:54
  75.4 0.2 collective-permute-start.5
  75.7 0.0 collective-permute-done.2
  75.7 1.6 %collective-permute-start.4 = (bf16[10,32,256]{2,1,0:T(8,128)(2,1)S(1)}, bf16[10,32,256]{2,1,0:T(8,128)(2,1)S(1)}, u32[]{:S(2)}, u32[]{:S(2)}) collective-permute-start(bf16[10,32,256]{2,1,0:T(8,128)(2,1)S(1)} %constant_dynamic-slice_fusion), channel_id=1, source_target_pairs={{1,0},{2,1},{3,2},{4,3},{5,4},{6,5},{7,6},{8,7},{9,8},{10,9},{11,1... | collective-permute-start | bytes 491528 | tf_op jit(solution)/shard_map/ppermute | solution.py:18
  77.3 0.9 constant_dynamic-update-slice_fusion.7
  78.2 0.0 collective-permute-done.3
  78.3 8.5 %collective-permute-done.4 = bf16[10,32,256]{2,1,0:T(8,128)(2,1)S(1)} collective-permute-done((bf16[10,32,256]{2,1,0:T(8,128)(2,1)S(1)}, bf16[10,32,256]{2,1,0:T(8,128)(2,1)S(1)}, u32[]{:S(2)}, u32[]{:S(2)}) %collective-permute-start.4) | collective-permute-done | bytes 163872 | tf_op jit(solution)/shard_map/ppermute | solution.py:18
  86.7 0.0 collective-permute-done.5
  86.8 0.0 copy-start.2
  86.8 0.0 collective-permute-done.6
  86.8 0.0 collective-permute-done.7
  86.8 3.1 %pad_maximum_fusion.ext_ref = bf16[98,64,256]{2,1,0:T(8,128)(2,1)} fusion(bf16[98,16,256]{2,1,0:T(8,128)(2,1)} %collective-permute-done.7, bf16[98,32,256]{2,1,0:T(8,128)(2,1)S(1)} %constant_dynamic-update-slice_fusion, bf16[98,16,256]{2,1,0:T(8,128)(2,1)S(1)} %collective-permute-done.6), kind=kLoop, calls=%fused_computation.9 | loop fusion | flops 9633792 | bytes 6422528 | tf_op jit(solution)/shard_map/concatenate | solution.py:136
  89.9 0.0 copy-done.2
  89.9 19.8 %shard_map.55.rest_0_ = bf16[96,32,256]{2,1,0:T(8,128)(2,1)} custom-call(s32[1]{0:T(128)} %bitcast.start_ref, bf16[98,64,256]{2,1,0:T(8,128)(2,1)} %pad_maximum_fusion.ext_ref, bf16[96,288,192]{2,1,0:T(8,128)(2,1)} %bitcast.26, bf16[96,32,256]{2,1,0:T(8,128)(2,1)} %f_ref.3, bf16[9,256,256]{2,1,0:T(8,128)(2,1)} %w_ref.3), custom_call_target="tpu_custom_call" | custom-call | tf_op jit(solution)/shard_map/pallas_call | solution.py:117
  109.7 4.6 %shard_map.56 = bf16[96,32,256]{2,1,0:T(8,128)(2,1)} custom-call(s32[1]{0:T(128)} %bitcast.start_ref, bf16[10,160,256]{2,1,0:T(8,128)(2,1)} %copy-done.2, bf16[8,288,480]{2,1,0:T(8,128)(2,1)} %reshape.119.k_ref, bf16[96,32,256]{2,1,0:T(8,128)(2,1)} %f_ref.3, bf16[9,256,256]{2,1,0:T(8,128)(2,1)} %w_ref.3, ...), custom_call_target="tpu_custom_call", output_to_operand_aliasing={{}: (5, {})} | custom-call | tf_op jit(solution)/shard_map/pallas_call | solution.py:117
  (10 shorter events, 0.1 us)
Async XLA Ops:
  0.7 31.5 %collective-permute-start.1 = (bf16[1,32,256]{2,1,0:T(8,128)(2,1)S(1)}, bf16[1,32,256]{2,1,0:T(8,128)(2,1)S(1)}, u32[]{:S(2)}, u32[]{:S(2)}) collective-permute-start(bf16[1,32,256]{2,1,0:T(8,128)(2,1)S(1)} %get-tuple-element.7), channel_id=1, source_target_pairs={{32,0},{64,32},{96,64},{128,96},{160,128},{192,160},{224,192},{33,... | collective-permute-start | bytes 49160 | tf_op jit(solution)/shard_map/ppermute | solution.py:26
  3.1 29.0 %collective-permute-start = (bf16[1,32,256]{2,1,0:T(8,128)(2,1)S(1)}, bf16[1,32,256]{2,1,0:T(8,128)(2,1)S(1)}, u32[]{:S(2)}, u32[]{:S(2)}) collective-permute-start(bf16[1,32,256]{2,1,0:T(8,128)(2,1)S(1)} %get-tuple-element.8), channel_id=1, source_target_pairs={{0,32},{32,64},{64,96},{96,128},{128,160},{160,192},{192,224},{1,3... | collective-permute-start | bytes 49160 | tf_op jit(solution)/shard_map/ppermute | solution.py:25
  19.8 1.4 %copy-start.1 = (bf16[96,9,3,129]{3,1,2,0:T(8,128)(2,1)}, bf16[96,9,3,129]{3,1,2,0:T(8,128)(2,1)S(1)}, u32[]{:S(2)}) copy-start(bf16[96,9,3,129]{3,1,2,0:T(8,128)(2,1)S(1)} %multiply_convert_fusion) | copy-start | bytes 2006212
  22.6 9.6 %copy-start = (bf16[96,32,256]{2,1,0:T(8,128)(2,1)S(1)}, bf16[96,32,256]{2,1,0:T(8,128)(2,1)}, u32[]{:S(2)}) copy-start(bf16[96,32,256]{2,1,0:T(8,128)(2,1)} %f_ref.3) | copy-start | bytes 4718596
  32.2 8.8 %copy-start.3 = (s32[32,160]{1,0:T(8,128)S(1)}, s32[32,160]{1,0:T(8,128)}, u32[]{:S(2)}) copy-start(s32[32,160]{1,0:T(8,128)} %iota_subtract_fusion) | copy-start | bytes 61444
  32.3 45.9 %collective-permute-start.3 = (bf16[10,32,256]{2,1,0:T(8,128)(2,1)S(1)}, bf16[10,32,256]{2,1,0:T(8,128)(2,1)S(1)}, u32[]{:S(2)}, u32[]{:S(2)}) collective-permute-start(bf16[10,32,256]{2,1,0:T(8,128)(2,1)S(1)} %constant_dynamic-slice_fusion), channel_id=1, source_target_pairs={{31,0},{0,1},{1,2},{2,3},{3,4},{4,5},{5,6},{6,7},{7,8},{8,9},{9,10... | collective-permute-start | bytes 491528 | tf_op jit(solution)/shard_map/ppermute | solution.py:18
  36.5 39.2 %collective-permute-start.2 = (bf16[10,32,256]{2,1,0:T(8,128)(2,1)S(1)}, bf16[10,32,256]{2,1,0:T(8,128)(2,1)}, u32[]{:S(2)}, u32[]{:S(2)}) collective-permute-start(bf16[10,32,256]{2,1,0:T(8,128)(2,1)S(1)} %constant_dynamic-slice_fusion), channel_id=1, source_target_pairs={{30,0},{31,1},{0,2},{1,3},{2,4},{3,5},{4,6},{5,7},{6,8},{7,9},{8,1... | collective-permute-start | bytes 491528 | tf_op jit(solution)/shard_map/ppermute | solution.py:18
  40.5 46.3 %collective-permute-start.6 = (bf16[98,16,256]{2,1,0:T(8,128)(2,1)}, bf16[98,16,256]{2,1,0:T(8,128)(2,1)S(1)}, u32[]{:S(2)}, u32[]{:S(2)}) collective-permute-start(bf16[98,16,256]{2,1,0:T(8,128)(2,1)} %get-tuple-element.5), channel_id=1, source_target_pairs={{31,0},{0,1},{1,2},{2,3},{3,4},{4,5},{5,6},{6,7},{7,8},{8,9},{9,10... | collective-permute-start | bytes 2408456 | tf_op jit(solution)/shard_map/ppermute | solution.py:18
  40.9 45.9 %collective-permute-start.7 = (bf16[98,16,256]{2,1,0:T(8,128)(2,1)}, bf16[98,16,256]{2,1,0:T(8,128)(2,1)}, u32[]{:S(2)}, u32[]{:S(2)}) collective-permute-start(bf16[98,16,256]{2,1,0:T(8,128)(2,1)} %get-tuple-element.6), channel_id=1, source_target_pairs={{1,0},{2,1},{3,2},{4,3},{5,4},{6,5},{7,6},{8,7},{9,8},{10,9},{11,1... | collective-permute-start | bytes 2408456 | tf_op jit(solution)/shard_map/ppermute | solution.py:18
  75.4 11.3 %collective-permute-start.5 = (bf16[10,32,256]{2,1,0:T(8,128)(2,1)S(1)}, bf16[10,32,256]{2,1,0:T(8,128)(2,1)S(1)}, u32[]{:S(2)}, u32[]{:S(2)}) collective-permute-start(bf16[10,32,256]{2,1,0:T(8,128)(2,1)S(1)} %constant_dynamic-slice_fusion), channel_id=1, source_target_pairs={{2,0},{3,1},{4,2},{5,3},{6,4},{7,5},{8,6},{9,7},{10,8},{11,9},{12,... | collective-permute-start | bytes 491528 | tf_op jit(solution)/shard_map/ppermute | solution.py:18
  75.7 11.1 %collective-permute-start.4 = (bf16[10,32,256]{2,1,0:T(8,128)(2,1)S(1)}, bf16[10,32,256]{2,1,0:T(8,128)(2,1)S(1)}, u32[]{:S(2)}, u32[]{:S(2)}) collective-permute-start(bf16[10,32,256]{2,1,0:T(8,128)(2,1)S(1)} %constant_dynamic-slice_fusion), channel_id=1, source_target_pairs={{1,0},{2,1},{3,2},{4,3},{5,4},{6,5},{7,6},{8,7},{9,8},{10,9},{11,1... | collective-permute-start | bytes 491528 | tf_op jit(solution)/shard_map/ppermute | solution.py:18
  86.8 3.1 %copy-start.2 = (bf16[10,160,256]{2,1,0:T(8,128)(2,1)}, bf16[10,160,256]{2,1,0:T(8,128)(2,1)S(1)}, u32[]{:S(2)}) copy-start(bf16[10,160,256]{2,1,0:T(8,128)(2,1)S(1)} %constant_dynamic-update-slice_fusion.3.ext_ref) | copy-start | bytes 2457604

commit v3 on v2

--- a/solution.py
+++ b/solution.py
@@ -38,45 +38,29 @@
     return (values * scale_row[:, None, None, None]).astype(jnp.bfloat16)
 
 
-def toeplitz_stacked(values, columns):
+def rolled_sources(values, span, lanes):
     rows, count, offsets, taps = values.shape
-    span = columns + taps - 1
-    out_pos = jnp.arange(columns)[:, None, None, None, None]
-    in_row = jnp.arange(offsets)[None, :, None, None, None]
-    in_pos = jnp.arange(span)[None, None, :, None, None]
-    tap_row = jnp.arange(offsets)[None, None, None, :, None]
-    tap = jnp.arange(taps)[None, None, None, None, :]
-    table = ((in_row == tap_row) & (in_pos - out_pos == tap)).astype(jnp.bfloat16)
-    table = table.reshape(columns, offsets * span, offsets * taps)
-    kernel = jnp.einsum(
-        "nbs,jps->nbjp", values.reshape(rows, count, offsets * taps), table,
-        preferred_element_type=jnp.float32,
-    ).astype(jnp.bfloat16)
-    return kernel.reshape(rows, count * columns, offsets * span)
+    columns = span - (taps - 1)
+    flat = jnp.pad(values, ((0, 0), (0, 0), (0, 0), (0, span - taps)))
+    flat = flat.reshape(rows, count, offsets * span)
+    flat = jnp.pad(flat, ((0, 0), (0, 0), (0, lanes - offsets * span))).astype(jnp.float32)
+    index = (jnp.arange(lanes)[None, :] + columns * jnp.arange(count)[:, None]) % lanes
+    return jnp.take_along_axis(flat, jnp.broadcast_to(index[None], flat.shape), axis=2)
 
 
-def toeplitz_split(values, columns):
-    rows, count, offsets, taps = values.shape
-    span = columns + taps - 1
-    out_pos = jnp.arange(columns)[:, None, None]
-    in_pos = jnp.arange(span)[None, :, None]
-    tap = jnp.arange(taps)[None, None, :]
-    table = (in_pos - out_pos == tap).astype(jnp.bfloat16)
-    kernel = jnp.einsum(
-        "nbrk,jmk->nbjrm", values, table, preferred_element_type=jnp.float32
-    ).astype(jnp.bfloat16)
-    return kernel.reshape(rows, count * columns, offsets * span)
-
-
-def conv_mix_kernel(start_ref, ext_ref, k_ref, f_ref, w_ref, *rest):
+def conv_mix_kernel(start_ref, ext_ref, src_ref, f_ref, w_ref, *rest):
     o_ref, conv_scr = rest[-2], rest[-1]
     rows, columns, channels = f_ref.shape
-    count = w_ref.shape[0]
+    count, lanes = src_ref.shape[1], src_ref.shape[2]
     span = ext_ref.shape[1]
     base = pl.program_id(0) * rows
     for q in range(rows):
-        window = ext_ref[pl.ds(base + q, 3)].reshape(3 * span, channels)
-        conv = jnp.dot(k_ref[q], window, preferred_element_type=jnp.float32)
+        source = src_ref[q]
+        spread = jnp.broadcast_to(source[:, None, :], (count, columns, lanes))
+        spread = spread.reshape(count * columns, lanes)
+        kernel = pltpu.roll(spread, 0, 1, stride=1, stride_axis=0).astype(jnp.bfloat16)
+        window = ext_ref[pl.ds(base + q, 4)].reshape(4 * span, channels)[:lanes]
+        conv = jnp.dot(kernel, window, preferred_element_type=jnp.float32)
         conv = conv.astype(jnp.bfloat16)
         for b in range(count):
             conv_scr[b, q * columns : (q + 1) * columns, :] = conv[b * columns : (b + 1) * columns]
@@ -86,10 +70,10 @@
     o_ref[...] = acc.reshape(rows, columns, channels).astype(o_ref.dtype)
 
 
-def conv_mix(start, extended, kernel, features, mix_weight, previous=None):
+def conv_mix(start, extended, sources, features, mix_weight, previous=None):
     lat_rows, columns, channels = features.shape
     count = mix_weight.shape[0]
-    rows = kernel.shape[0]
+    rows = sources.shape[0]
     blocks = rows // BLOCK
     if previous is None:
         row_map = lambda i, s: (i, 0, 0)
@@ -97,11 +81,11 @@
         row_map = lambda i, s: (s[0] // BLOCK + i, 0, 0)
     in_specs = [
         pl.BlockSpec(extended.shape, lambda i, s: (0, 0, 0)),
-        pl.BlockSpec((BLOCK,) + kernel.shape[1:], lambda i, s: (i, 0, 0)),
+        pl.BlockSpec((BLOCK,) + sources.shape[1:], lambda i, s: (i, 0, 0)),
         pl.BlockSpec((BLOCK, columns, channels), row_map),
         pl.BlockSpec(mix_weight.shape, lambda i, s: (0, 0, 0)),
     ]
-    operands = [start, extended, kernel, features, mix_weight]
+    operands = [start, extended, sources, features, mix_weight]
     aliases = {}
     if previous is not None:
         in_specs.append(pl.BlockSpec(memory_space=pl.ANY))
@@ -136,8 +120,10 @@
     near = jnp.concatenate(
         [shifted(padded[:, columns - NEAR :], "lon", 1), padded,
          shifted(padded[:, :NEAR], "lon", -1)], axis=1)
-    near_kernel = toeplitz_stacked(basis_values[:, :, :, reach - NEAR : reach + NEAR + 1], columns)
-    out = conv_mix(start_arr, near, near_kernel, features, mix_weight)
+    near = jnp.pad(near, ((0, 1), (0, 0), (0, 0)))
+    near_sources = rolled_sources(
+        basis_values[:, :, :, reach - NEAR : reach + NEAR + 1], columns + 2 * NEAR, 256)
+    out = conv_mix(start_arr, near, near_sources, features, mix_weight)
 
     window = lax.dynamic_slice_in_dim(padded, start, POLAR + 2, 0)
     hops = reach // columns
@@ -146,8 +132,9 @@
     wide = jnp.concatenate(western + [window] + eastern, axis=1)
     wide = wide[:, hops * columns - reach : hops * columns + columns + reach]
     polar_values = lax.dynamic_slice_in_dim(basis_values, start, POLAR, 0)
-    wide_kernel = toeplitz_split(polar_values, columns)
-    return conv_mix(start_arr, wide, wide_kernel, features, mix_weight, previous=out)
+    wide = jnp.pad(wide, ((0, 1), (0, 0), (0, 0)))
+    wide_sources = rolled_sources(polar_values, columns + 2 * reach, 512)
+    return conv_mix(start_arr, wide, wide_sources, features, mix_weight, previous=out)
 
 
 def solution(mesh):

time: 115 us -> 2620 us (22.78)
  the two profiles are of different devices: /device:TPU:125 before, /device:TPU:3 now
where the time goes in v3:
time: 2620 us
  local copies, waits for them, and re-layouts  2550 us (97%)
    gather x6, local copies, waits for them, and re-layouts, rolled_sources(): jnp.take_along_axis(flat, jnp.broadcast_to(index[None], flat.shape), axis=2)  2540 us
  transfers between devices with their start and end apart: 8, of which 2 were waited for; matrix products, arithmetic and copies ran while one was open for 97% of the time, Pallas kernels for 0%

profile of v3, /device:TPU:3, one launch (start us, length us, event | category | flops | bytes accessed | tf_op | source)
XLA Modules:
  0.0 2620.7 jit_solution(12750885408915208693)
XLA Ops:
  0.0 1.4 fusion.19
  1.4 3.2 collective-permute-start
  4.6 4.2 collective-permute-start.1
  8.8 0.7 broadcast_add_fusion
  9.5 0.7 broadcast_compare_fusion.1
  10.2 0.1 broadcast_add_fusion.1
  10.3 0.0 copy-start.4
  10.3 0.0 copy-start.6
  10.3 0.1 broadcast_compare_fusion.2
  10.4 0.0 copy-start.9
  10.4 0.7 multiply_rsqrt_fusion
  11.0 0.7 broadcast_compare_fusion
  11.8 1.5 multiply_convert_fusion
  13.3 0.3 constant_dynamic-slice_fusion
  13.6 0.2 pad.25
  13.9 1.3 copy.10
  15.1 0.1 pad.28
  15.2 1.0 copy.11
  16.3 0.2 pad_convert_fusion
  16.5 0.0 copy-done.4
  16.5 0.0 copy-done.6
  16.5 0.0 copy-done.9
  16.5 1.3 shift-left_or_fusion
  17.9 1.5 reshape.133
  19.4 2174.2 %gather_fusion.1 = f32[221184]{0:T(1024)S(1)} fusion(f32[96,9,256]{2,1,0:T(8,128)S(1)} %pad_convert_fusion, s32[221184]{0:T(1024)S(1)} %reshape.133), kind=kCustom, calls=%fused_computation.1 | custom fusion | bytes 4423680 | tf_op jit(solution)/shard_map/jit(take_along_axis)/gather | solution.py:48
  2193.6 0.0 copy-start.5
  2193.6 0.0 copy-start.7
  2193.6 0.0 copy-start.10
  2193.6 0.2 reshape.136
  2193.9 0.5 copy-done.5
  2194.3 0.0 copy-done.7
  2194.3 0.0 copy-done.10
  2194.3 0.0 copy-start.1
  2194.3 1.4 fusion.7.src_ref
  2195.7 0.0 copy-done.2
  2195.7 0.0 copy-done.3
  2195.7 0.0 copy-done.8
  2195.8 0.0 copy-done.1
  2195.8 0.0 copy-start
  2195.9 361.6 %gather_fusion = f32[36864]{0:T(1024)S(1)} fusion(f32[8,9,512]{2,1,0:T(8,128)S(1)} %pad_convert_fusion.1, s32[36864]{0:T(1024)S(1)} %reshape.127), kind=kCustom, calls=%fused_computation | custom fusion | bytes 737280 | tf_op jit(solution)/shard_map/jit(take_along_axis)/gather | solution.py:48
  2557.5 0.0 collective-permute-done
  2557.5 0.7 constant_dynamic-update-slice_fusion.2
  2558.2 0.0 copy-done
  2558.2 0.1 constant_dynamic-update-slice_fusion.1
  2558.3 0.0 collective-permute-done.1
  2558.4 0.7 constant_dynamic-update-slice_fusion
  2559.1 1.9 collective-permute-start.2
  2561.0 3.9 collective-permute-start.3
  2564.9 0.1 fusion.18
  2565.0 0.1 collective-permute-start.7
  2565.1 3.2 collective-permute-start.6
  2568.4 0.7 fusion.9.src_ref
  2569.1 0.0 collective-permute-start.4
  2569.1 0.5 collective-permute-done.2
  2569.6 4.2 collective-permute-start.5
  2573.8 0.0 collective-permute-done.3
  2573.9 19.3 collective-permute-done.4
  2593.3 0.0 collective-permute-done.5
  2593.3 1.0 pad.24.ext_ref
  2594.3 0.0 collective-permute-done.7
  2594.3 0.0 collective-permute-done.6
  2594.3 2.1 fusion.4.ext_ref
  2596.4 20.3 shard_map.55.rest_0_
  2616.7 4.0 shard_map.56
  (16 shorter events, 0.2 us)
Async XLA Ops:
  1.4 2556.1 %collective-permute-start = (bf16[1,32,256]{2,1,0:T(8,128)(2,1)}, bf16[1,32,256]{2,1,0:T(8,128)(2,1)}, u32[]{:S(2)}, u32[]{:S(2)}) collective-permute-start(bf16[1,32,256]{2,1,0:T(8,128)(2,1)} %get-tuple-element.8), channel_id=1, source_target_pairs={{0,32},{32,64},{64,96},{96,128},{128,160},{160,192},{192,224},{1,3... | collective-permute-start | bytes 49160 | tf_op jit(solution)/shard_map/ppermute | solution.py:25
  4.6 2553.8 %collective-permute-start.1 = (bf16[1,32,256]{2,1,0:T(8,128)(2,1)}, bf16[1,32,256]{2,1,0:T(8,128)(2,1)}, u32[]{:S(2)}, u32[]{:S(2)}) collective-permute-start(bf16[1,32,256]{2,1,0:T(8,128)(2,1)} %get-tuple-element.7), channel_id=1, source_target_pairs={{32,0},{64,32},{96,64},{128,96},{160,128},{192,160},{224,192},{33,... | collective-permute-start | bytes 49160 | tf_op jit(solution)/shard_map/ppermute | solution.py:26
  10.3 6.2 copy-start.4
  10.3 6.2 copy-start.6
  10.4 6.2 copy-start.9
  2193.6 0.7 copy-start.5
  2193.6 0.7 copy-start.7
  2193.6 0.7 copy-start.10
  2194.3 1.4 copy-start.2
  2194.3 1.4 copy-start.3
  2194.3 1.4 copy-start.8
  2194.3 1.4 copy-start.1
  2195.8 362.4 %copy-start = (bf16[96,32,256]{2,1,0:T(8,128)(2,1)S(1)}, bf16[96,32,256]{2,1,0:T(8,128)(2,1)}, u32[]{:S(2)}) copy-start(bf16[96,32,256]{2,1,0:T(8,128)(2,1)} %f_ref.3) | copy-start | bytes 4718596
  2559.1 10.5 collective-permute-start.2
  2561.0 12.8 collective-permute-start.3
  2565.0 29.3 %collective-permute-start.7 = (bf16[98,16,256]{2,1,0:T(8,128)(2,1)S(1)}, bf16[98,16,256]{2,1,0:T(8,128)(2,1)S(1)}, u32[]{:S(2)}, u32[]{:S(2)}) collective-permute-start(bf16[98,16,256]{2,1,0:T(8,128)(2,1)S(1)} %get-tuple-element.6), channel_id=1, source_target_pairs={{1,0},{2,1},{3,2},{4,3},{5,4},{6,5},{7,6},{8,7},{9,8},{10,9},{11,1... | collective-permute-start | bytes 2408456 | tf_op jit(solution)/shard_map/ppermute | solution.py:18
  2565.1 29.2 %collective-permute-start.6 = (bf16[98,16,256]{2,1,0:T(8,128)(2,1)S(1)}, bf16[98,16,256]{2,1,0:T(8,128)(2,1)S(1)}, u32[]{:S(2)}, u32[]{:S(2)}) collective-permute-start(bf16[98,16,256]{2,1,0:T(8,128)(2,1)S(1)} %get-tuple-element.5), channel_id=1, source_target_pairs={{31,0},{0,1},{1,2},{2,3},{3,4},{4,5},{5,6},{6,7},{7,8},{8,9},{9,10... | collective-permute-start | bytes 2408456 | tf_op jit(solution)/shard_map/ppermute | solution.py:18
  2569.1 24.2 collective-permute-start.4
  2569.6 23.7 collective-permute-start.5

commit v4 on v3

--- a/solution.py
+++ b/solution.py
@@ -44,8 +44,8 @@
     flat = jnp.pad(values, ((0, 0), (0, 0), (0, 0), (0, span - taps)))
     flat = flat.reshape(rows, count, offsets * span)
     flat = jnp.pad(flat, ((0, 0), (0, 0), (0, lanes - offsets * span))).astype(jnp.float32)
-    index = (jnp.arange(lanes)[None, :] + columns * jnp.arange(count)[:, None]) % lanes
-    return jnp.take_along_axis(flat, jnp.broadcast_to(index[None], flat.shape), axis=2)
+    return jnp.stack(
+        [jnp.roll(flat[:, b], -columns * b, axis=-1) for b in range(count)], axis=1)
 
 
 def conv_mix_kernel(start_ref, ext_ref, src_ref, f_ref, w_ref, *rest):

time: 2620 us -> 81.3 us (0.03)
  the two profiles are of different devices: /device:TPU:3 before, /device:TPU:2 now
where the time goes in v4:
time: 81.3 us; the launch traced here: 80.7 us
  Pallas kernels  24.3 us (30%)
  starting transfers between devices  21.8 us (27%)
  local copies, waits for them, and re-layouts  17.6 us (22%)
  waiting for transfers between devices  9.02 us (11%)
  other arithmetic  7.51 us (9%)
    pallas_call x2, Pallas kernels, conv_mix(): pl.pallas_call(conv_mix_kernel, grid_spec=grid_spec, out_shape=jax.ShapeD...  24.3 us
    ppermute x6, starting transfers between devices, shifted(): return lax.ppermute(block, axis, route)  13.8 us
    another operation x17, local copies, waits for them, and re-layouts, rolled_sources(): jnp.stack([jnp.roll(flat[:, b], -columns * b, axis=-1) for b in range(cou...  9.39 us
    ppermute x6, waiting for transfers between devices, shifted(): return lax.ppermute(block, axis, route)  9.01 us
    ppermute x1, starting transfers between devices, lat_extended(): after = lax.ppermute(value[:1], 'lat', down)  4.47 us
    ppermute x1, starting transfers between devices, lat_extended(): before = lax.ppermute(value[length - 1:], 'lat', up)  3.47 us
    concatenate x1, other arithmetic, body(): jnp.concatenate([shifted(padded[:, columns - NEAR:], 'lon', 1), padded, s...  3.01 us
    unnamed x12, local copies, waits for them, and re-layouts  2.07 us
  transfers between devices with their start and end apart: 8, of which 2 were waited for; matrix products, arithmetic and copies ran while one was open for 25% of the time, Pallas kernels for 0%

profile of v4, /device:TPU:2, one launch (start us, length us, event | category | flops | bytes accessed | tf_op | source)
XLA Modules:
  0.0 80.7 jit_solution(12449279884576081280)
XLA Ops:
  0.0 0.7 fusion.7
  0.7 3.5 %collective-permute-start = (bf16[1,32,256]{2,1,0:T(8,128)(2,1)S(1)}, bf16[1,32,256]{2,1,0:T(8,128)(2,1)S(1)}, u32[]{:S(2)}, u32[]{:S(2)}) collective-permute-start(bf16[1,32,256]{2,1,0:T(8,128)(2,1)S(1)} %get-tuple-element.8), channel_id=1, source_target_pairs={{0,32},{32,64},{64,96},{96,128},{128,160},{160,192},{192,224},{1,3... | collective-permute-start | bytes 49160 | tf_op jit(solution)/shard_map/ppermute | solution.py:25
  4.2 4.5 %collective-permute-start.1 = (bf16[1,32,256]{2,1,0:T(8,128)(2,1)S(1)}, bf16[1,32,256]{2,1,0:T(8,128)(2,1)S(1)}, u32[]{:S(2)}, u32[]{:S(2)}) collective-permute-start(bf16[1,32,256]{2,1,0:T(8,128)(2,1)S(1)} %get-tuple-element.7), channel_id=1, source_target_pairs={{32,0},{64,32},{96,64},{128,96},{160,128},{192,160},{224,192},{33,... | collective-permute-start | bytes 49160 | tf_op jit(solution)/shard_map/ppermute | solution.py:26
  8.7 0.7 multiply_rsqrt_fusion
  9.4 0.7 broadcast_compare_fusion
  10.1 1.5 %multiply_convert_fusion = bf16[96,9,3,129]{0,3,2,1:T(8,128)(2,1)S(1)} fusion(f32[96]{0:T(128)S(1)} %multiply_rsqrt_fusion, f32[96,3,129]{0,2,1:T(8,128)} %param.6, s32[96,3,129]{0,2,1:T(8,128)} %param.7, pred[96,129]{0,1:T(8,128)(4,1)S(1)} %broadcast_compare_fusion), kind=kLoop, calls=%fused_computation.6 | loop fusion | flops 1671840 | bytes 978720 | tf_op jit(solution)/shard_map/convert_element_type | solution.py:38
  11.6 0.3 constant_dynamic-slice_fusion
  11.9 0.2 pad.25
  12.2 0.4 copy.42
  12.6 0.1 slice.244
  12.6 0.1 slice.247
  12.7 0.1 slice.250
  12.8 0.1 slice.256
  12.9 0.1 slice.259
  13.0 0.1 pad.28
  13.1 1.0 %copy.34 = bf16[96,9,192]{2,1,0:T(8,128)(2,1)S(1)} copy(bf16[96,9,192]{0,2,1:T(8,128)(2,1)S(1)} %bitcast.66) | data formatting | bytes 663552 | tf_op jit(solution)/shard_map/reshape | solution.py:45
  14.1 0.6 pad_convert_fusion
  14.8 0.1 slice.270
  14.9 0.0 copy-start
  14.9 0.1 slice.272
  15.0 0.1 slice.274
  15.2 0.1 slice.278
  15.3 0.1 slice.280
  15.3 0.1 slice.282
  15.4 0.1 maximum_bitcast_fusion.7
  15.5 0.1 maximum_bitcast_fusion.8
  15.6 0.1 maximum_bitcast_fusion.9
  15.6 0.1 maximum_bitcast_fusion.11
  15.7 0.1 maximum_bitcast_fusion
  15.8 0.1 maximum_bitcast_fusion.1
  15.9 0.1 maximum_bitcast_fusion.2
  16.0 0.1 maximum_bitcast_fusion.4
  16.1 0.1 maximum_bitcast_fusion.5
  16.2 0.1 maximum_bitcast_fusion.6
  16.3 0.1 maximum_bitcast_fusion.12
  16.4 0.1 slice.262
  16.4 0.1 constant_dynamic-update-slice_fusion.1
  16.6 1.3 %fusion.6 = (bf16[98,16,256]{2,1,0:T(8,128)(2,1)}, bf16[98,16,256]{2,1,0:T(8,128)(2,1)}) fusion(bf16[98,32,256]{2,1,0:T(8,128)(2,1)S(1)} %constant_dynamic-update-slice_fusion), kind=kLoop, calls=%fused_computation.62 | loop fusion | bytes 3211264 | tf_op jit(solution)/shard_map/slice | solution.py:121
  17.9 2.1 %collective-permute-start.2 = (bf16[10,32,256]{2,1,0:T(8,128)(2,1)S(1)}, bf16[10,32,256]{2,1,0:T(8,128)(2,1)}, u32[]{:S(2)}, u32[]{:S(2)}) collective-permute-start(bf16[10,32,256]{2,1,0:T(8,128)(2,1)S(1)} %constant_dynamic-slice_fusion.1), channel_id=1, source_target_pairs={{30,0},{31,1},{0,2},{1,3},{2,4},{3,5},{4,6},{5,7},{6,8},{7,9},{8,1... | collective-permute-start | bytes 491528 | tf_op jit(solution)/shard_map/ppermute | solution.py:18
  20.0 4.2 %collective-permute-start.7 = (bf16[98,16,256]{2,1,0:T(8,128)(2,1)}, bf16[98,16,256]{2,1,0:T(8,128)(2,1)S(1)}, u32[]{:S(2)}, u32[]{:S(2)}) collective-permute-start(bf16[98,16,256]{2,1,0:T(8,128)(2,1)} %get-tuple-element.6), channel_id=1, source_target_pairs={{1,0},{2,1},{3,2},{4,3},{5,4},{6,5},{7,6},{8,7},{9,8},{10,9},{11,1... | collective-permute-start | bytes 2408456 | tf_op jit(solution)/shard_map/ppermute | solution.py:18
  24.2 0.1 maximum_bitcast_fusion.13
  24.3 0.0 collective-permute-start.3
  24.5 0.6 copy.32
  25.1 0.6 copy.33
  25.7 0.6 stack.61
  26.3 0.1 copy.35
  26.4 0.1 copy.36
  26.5 0.1 copy.37
  26.7 0.1 copy.38
  26.8 0.1 copy.39
  26.9 0.1 copy.40
  27.0 0.1 copy.41
  27.1 3.0 %stack.62.src_ref = f32[8,9,512]{2,1,0:T(8,128)} concatenate(f32[8,1,512]{2,1,0:T(1,128)S(1)} %copy.26, f32[8,1,512]{2,1,0:T(1,128)S(1)} %copy.27, f32[8,1,512]{2,1,0:T(1,128)S(1)} %copy.28, f32[8,1,512]{2,1,0:T(1,128)S(1)} %copy.29, f32[8,1,512]{2,1,0:T(1,128)S(1)} %copy.30, f32[8,1,512]{2,1,0:T(1,128)S(1)} %copy.31, f32[8,1,512]{2,1,0:T(1,128)} %copy.32, f32[8,1,512]{2,1,0:T(1,128)} %copy.33, ...), dimensions={1} | concatenate | bytes 294912 | tf_op jit(solution)/shard_map/stack | solution.py:47
  30.1 3.8 %stack.70.src_ref = f32[96,9,256]{2,1,0:T(8,128)} concatenate(f32[96,1,256]{2,1,0:T(1,128)S(1)} %get-tuple-element.17, f32[96,1,256]{2,1,0:T(1,128)S(1)} %copy.35, f32[96,1,256]{2,1,0:T(1,128)S(1)} %copy.36, f32[96,1,256]{2,1,0:T(1,128)S(1)} %copy.37, f32[96,1,256]{2,1,0:T(1,128)S(1)} %copy.38, f32[96,1,256]{2,1,0:T(1,128)S(1)} %copy.39, f32[96,1,256]{2,1,0:T(1,128)S(1)} %copy.40, ...), dimensions={1} | concatenate | bytes 1769472 | tf_op jit(solution)/shard_map/stack | solution.py:47
  33.8 5.4 %collective-permute-start.4 = (bf16[10,32,256]{2,1,0:T(8,128)(2,1)S(1)}, bf16[10,32,256]{2,1,0:T(8,128)(2,1)S(1)}, u32[]{:S(2)}, u32[]{:S(2)}) collective-permute-start(bf16[10,32,256]{2,1,0:T(8,128)(2,1)S(1)} %constant_dynamic-slice_fusion.1), channel_id=1, source_target_pairs={{1,0},{2,1},{3,2},{4,3},{5,4},{6,5},{7,6},{8,7},{9,8},{10,9},{11,1... | collective-permute-start | bytes 491528 | tf_op jit(solution)/shard_map/ppermute | solution.py:18
  39.2 2.2 %collective-permute-start.5 = (bf16[10,32,256]{2,1,0:T(8,128)(2,1)S(1)}, bf16[10,32,256]{2,1,0:T(8,128)(2,1)S(1)}, u32[]{:S(2)}, u32[]{:S(2)}) collective-permute-start(bf16[10,32,256]{2,1,0:T(8,128)(2,1)S(1)} %constant_dynamic-slice_fusion.1), channel_id=1, source_target_pairs={{2,0},{3,1},{4,2},{5,3},{6,4},{7,5},{8,6},{9,7},{10,8},{11,9},{12,... | collective-permute-start | bytes 491528 | tf_op jit(solution)/shard_map/ppermute | solution.py:18
  41.4 0.9 %constant_dynamic-update-slice_fusion.7 = bf16[10,160,256]{2,1,0:T(8,128)(2,1)S(1)} fusion(bf16[10,32,256]{2,1,0:T(8,128)(2,1)} %collective-permute-done.2), kind=kLoop, calls=%fused_computation.41 | loop fusion | bytes 327680
  42.3 0.9 %constant_dynamic-update-slice_fusion.6 = bf16[10,160,256]{2,1,0:T(8,128)(2,1)S(1)} fusion(bf16[10,160,256]{2,1,0:T(8,128)(2,1)S(1)} %constant_dynamic-update-slice_fusion.7, bf16[10,32,256]{2,1,0:T(8,128)(2,1)} %collective-permute-done.3), kind=kLoop, calls=%fused_computation.40 | loop fusion | bytes 327680
  43.3 0.5 collective-permute-done.4
  43.8 8.5 %collective-permute-done.5 = bf16[10,32,256]{2,1,0:T(8,128)(2,1)S(1)} collective-permute-done((bf16[10,32,256]{2,1,0:T(8,128)(2,1)S(1)}, bf16[10,32,256]{2,1,0:T(8,128)(2,1)S(1)}, u32[]{:S(2)}, u32[]{:S(2)}) %collective-permute-start.5) | collective-permute-done | bytes 163872 | tf_op jit(solution)/shard_map/ppermute | solution.py:18
  52.3 1.0 %pad.24.ext_ref = bf16[11,160,256]{2,1,0:T(8,128)(2,1)} pad(bf16[10,160,256]{2,1,0:T(8,128)(2,1)S(1)} %constant_dynamic-update-slice_fusion.3, bf16[]{:T(256)} %constant.9.clone.1), padding=0_1x0_0x0_0 | pad | bytes 1720322 | tf_op jit(solution)/shard_map/jit(_pad)/pad | solution.py:135
  53.3 3.0 %fusion.4.ext_ref = bf16[99,64,256]{2,1,0:T(8,128)(2,1)} fusion(bf16[98,16,256]{2,1,0:T(8,128)(2,1)S(1)} %collective-permute-done.7, bf16[98,32,256]{2,1,0:T(8,128)(2,1)S(1)} %constant_dynamic-update-slice_fusion, bf16[98,16,256]{2,1,0:T(8,128)(2,1)} %collective-permute-done.6), kind=kLoop, calls=%fused_computation.5 | loop fusion | flops 16220160 | bytes 6455296 | tf_op jit(solution)/shard_map/concatenate | solution.py:120
  56.3 20.3 %shard_map.55.rest_0_ = bf16[96,32,256]{2,1,0:T(8,128)(2,1)} custom-call(s32[1]{0:T(128)} %bitcast.start_ref, bf16[99,64,256]{2,1,0:T(8,128)(2,1)} %fusion.4.ext_ref, f32[96,9,256]{2,1,0:T(8,128)} %stack.70.src_ref, bf16[96,32,256]{2,1,0:T(8,128)(2,1)} %f_ref.3, bf16[9,256,256]{2,1,0:T(8,128)(2,1)} %w_ref.3), custom_call_target="tpu_custom_call" | custom-call | tf_op jit(solution)/shard_map/pallas_call | solution.py:101
  76.7 4.0 %shard_map.56 = bf16[96,32,256]{2,1,0:T(8,128)(2,1)} custom-call(s32[1]{0:T(128)} %bitcast.start_ref, bf16[11,160,256]{2,1,0:T(8,128)(2,1)} %pad.24.ext_ref, f32[8,9,512]{2,1,0:T(8,128)} %stack.62.src_ref, bf16[96,32,256]{2,1,0:T(8,128)(2,1)} %f_ref.3, bf16[9,256,256]{2,1,0:T(8,128)(2,1)} %w_ref.3, ...), custom_call_target="tpu_custom_call", output_to_operand_aliasing={{}: (5, {})} | custom-call | tf_op jit(solution)/shard_map/pallas_call | solution.py:101
  (44 shorter events, 0.4 us)
Async XLA Ops:
  0.7 15.7 %collective-permute-start = (bf16[1,32,256]{2,1,0:T(8,128)(2,1)S(1)}, bf16[1,32,256]{2,1,0:T(8,128)(2,1)S(1)}, u32[]{:S(2)}, u32[]{:S(2)}) collective-permute-start(bf16[1,32,256]{2,1,0:T(8,128)(2,1)S(1)} %get-tuple-element.8), channel_id=1, source_target_pairs={{0,32},{32,64},{64,96},{96,128},{128,160},{160,192},{192,224},{1,3... | collective-permute-start | bytes 49160 | tf_op jit(solution)/shard_map/ppermute | solution.py:25
  4.2 12.4 %collective-permute-start.1 = (bf16[1,32,256]{2,1,0:T(8,128)(2,1)S(1)}, bf16[1,32,256]{2,1,0:T(8,128)(2,1)S(1)}, u32[]{:S(2)}, u32[]{:S(2)}) collective-permute-start(bf16[1,32,256]{2,1,0:T(8,128)(2,1)S(1)} %get-tuple-element.7), channel_id=1, source_target_pairs={{32,0},{64,32},{96,64},{128,96},{160,128},{192,160},{224,192},{33,... | collective-permute-start | bytes 49160 | tf_op jit(solution)/shard_map/ppermute | solution.py:26
  14.9 1.5 %copy-start = (bf16[96,32,256]{2,1,0:T(8,128)(2,1)S(1)}, bf16[96,32,256]{2,1,0:T(8,128)(2,1)}, u32[]{:S(2)}) copy-start(bf16[96,32,256]{2,1,0:T(8,128)(2,1)} %f_ref.3) | copy-start | bytes 4718596
  17.9 21.3 %collective-permute-start.2 = (bf16[10,32,256]{2,1,0:T(8,128)(2,1)S(1)}, bf16[10,32,256]{2,1,0:T(8,128)(2,1)}, u32[]{:S(2)}, u32[]{:S(2)}) collective-permute-start(bf16[10,32,256]{2,1,0:T(8,128)(2,1)S(1)} %constant_dynamic-slice_fusion.1), channel_id=1, source_target_pairs={{30,0},{31,1},{0,2},{1,3},{2,4},{3,5},{4,6},{5,7},{6,8},{7,9},{8,1... | collective-permute-start | bytes 491528 | tf_op jit(solution)/shard_map/ppermute | solution.py:18
  20.0 33.3 %collective-permute-start.7 = (bf16[98,16,256]{2,1,0:T(8,128)(2,1)}, bf16[98,16,256]{2,1,0:T(8,128)(2,1)S(1)}, u32[]{:S(2)}, u32[]{:S(2)}) collective-permute-start(bf16[98,16,256]{2,1,0:T(8,128)(2,1)} %get-tuple-element.6), channel_id=1, source_target_pairs={{1,0},{2,1},{3,2},{4,3},{5,4},{6,5},{7,6},{8,7},{9,8},{10,9},{11,1... | collective-permute-start | bytes 2408456 | tf_op jit(solution)/shard_map/ppermute | solution.py:18
  24.2 29.1 %collective-permute-start.6 = (bf16[98,16,256]{2,1,0:T(8,128)(2,1)}, bf16[98,16,256]{2,1,0:T(8,128)(2,1)}, u32[]{:S(2)}, u32[]{:S(2)}) collective-permute-start(bf16[98,16,256]{2,1,0:T(8,128)(2,1)} %get-tuple-element.5), channel_id=1, source_target_pairs={{31,0},{0,1},{1,2},{2,3},{3,4},{4,5},{5,6},{6,7},{7,8},{8,9},{9,10... | collective-permute-start | bytes 2408456 | tf_op jit(solution)/shard_map/ppermute | solution.py:18
  24.3 18.0 %collective-permute-start.3 = (bf16[10,32,256]{2,1,0:T(8,128)(2,1)S(1)}, bf16[10,32,256]{2,1,0:T(8,128)(2,1)}, u32[]{:S(2)}, u32[]{:S(2)}) collective-permute-start(bf16[10,32,256]{2,1,0:T(8,128)(2,1)S(1)} %constant_dynamic-slice_fusion.1), channel_id=1, source_target_pairs={{31,0},{0,1},{1,2},{2,3},{3,4},{4,5},{5,6},{6,7},{7,8},{8,9},{9,10... | collective-permute-start | bytes 491528 | tf_op jit(solution)/shard_map/ppermute | solution.py:18
  33.8 9.9 %collective-permute-start.4 = (bf16[10,32,256]{2,1,0:T(8,128)(2,1)S(1)}, bf16[10,32,256]{2,1,0:T(8,128)(2,1)S(1)}, u32[]{:S(2)}, u32[]{:S(2)}) collective-permute-start(bf16[10,32,256]{2,1,0:T(8,128)(2,1)S(1)} %constant_dynamic-slice_fusion.1), channel_id=1, source_target_pairs={{1,0},{2,1},{3,2},{4,3},{5,4},{6,5},{7,6},{8,7},{9,8},{10,9},{11,1... | collective-permute-start | bytes 491528 | tf_op jit(solution)/shard_map/ppermute | solution.py:18
  39.2 13.1 %collective-permute-start.5 = (bf16[10,32,256]{2,1,0:T(8,128)(2,1)S(1)}, bf16[10,32,256]{2,1,0:T(8,128)(2,1)S(1)}, u32[]{:S(2)}, u32[]{:S(2)}) collective-permute-start(bf16[10,32,256]{2,1,0:T(8,128)(2,1)S(1)} %constant_dynamic-slice_fusion.1), channel_id=1, source_target_pairs={{2,0},{3,1},{4,2},{5,3},{6,4},{7,5},{8,6},{9,7},{10,8},{11,9},{12,... | collective-permute-start | bytes 491528 | tf_op jit(solution)/shard_map/ppermute | solution.py:18

commit v5 on v4

--- a/solution.py
+++ b/solution.py
@@ -54,20 +54,32 @@
     count, lanes = src_ref.shape[1], src_ref.shape[2]
     span = ext_ref.shape[1]
     base = pl.program_id(0) * rows
-    for q in range(rows):
-        source = src_ref[q]
-        spread = jnp.broadcast_to(source[:, None, :], (count, columns, lanes))
-        spread = spread.reshape(count * columns, lanes)
-        kernel = pltpu.roll(spread, 0, 1, stride=1, stride_axis=0).astype(jnp.bfloat16)
-        window = ext_ref[pl.ds(base + q, 4)].reshape(4 * span, channels)[:lanes]
-        conv = jnp.dot(kernel, window, preferred_element_type=jnp.float32)
-        conv = conv.astype(jnp.bfloat16)
+
+    def compute():
+        for q in range(rows):
+            source = src_ref[q]
+            spread = jnp.broadcast_to(source[:, None, :], (count, columns, lanes))
+            spread = spread.reshape(count * columns, lanes)
+            kernel = pltpu.roll(spread, 0, 1, stride=1, stride_axis=0).astype(jnp.bfloat16)
+            window = ext_ref[pl.ds(base + q, 4)].reshape(4 * span, channels)[:lanes]
+            conv = jnp.dot(kernel, window, preferred_element_type=jnp.float32)
+            conv = conv.astype(jnp.bfloat16)
+            for b in range(count):
+                conv_scr[b, q * columns : (q + 1) * columns, :] = conv[b * columns : (b + 1) * columns]
+        acc = f_ref[...].reshape(rows * columns, channels).astype(jnp.float32)
         for b in range(count):
-            conv_scr[b, q * columns : (q + 1) * columns, :] = conv[b * columns : (b + 1) * columns]
-    acc = f_ref[...].reshape(rows * columns, channels).astype(jnp.float32)
-    for b in range(count):
-        acc = acc + jnp.dot(conv_scr[b], w_ref[b], preferred_element_type=jnp.float32)
-    o_ref[...] = acc.reshape(rows, columns, channels).astype(o_ref.dtype)
+            acc = acc + jnp.dot(conv_scr[b], w_ref[b], preferred_element_type=jnp.float32)
+        o_ref[...] = acc.reshape(rows, columns, channels).astype(o_ref.dtype)
+
+    if len(rest) == 2:
+        compute()
+    else:
+        previous_ref = rest[0]
+        pl.when(start_ref[1] != 0)(compute)
+
+        @pl.when(start_ref[1] == 0)
+        def _():
+            o_ref[...] = previous_ref[...]
 
 
 def conv_mix(start, extended, sources, features, mix_weight, previous=None):
@@ -88,7 +100,7 @@
     operands = [start, extended, sources, features, mix_weight]
     aliases = {}
     if previous is not None:
-        in_specs.append(pl.BlockSpec(memory_space=pl.ANY))
+        in_specs.append(pl.BlockSpec((BLOCK, columns, channels), row_map))
         operands.append(previous)
         aliases = {len(operands) - 1: 0}
     grid_spec = pltpu.PrefetchScalarGridSpec(
@@ -108,33 +120,47 @@
 
 def body(features, quad_weights, cycle_index, widths, mix_weight):
     count = mix_weight.shape[0]
-    lat_rows, columns = features.shape[0], features.shape[1]
+    lat_rows, columns, channels = features.shape
     reach = quad_weights.shape[2] // 2
+    hops = reach // columns
+
+    lat_index, lat_count = lax.axis_index("lat"), lax.axis_size("lat")
+    last_band = lat_index == lat_count - 1
+    polar = (lat_index == 0) | last_band
+    start = jnp.where(last_band, lat_rows - POLAR, 0).astype(jnp.int32)
+    scalars = jnp.stack([start, polar.astype(jnp.int32)])
+
+    zero_row = jnp.zeros((1, columns, channels), features.dtype)
+    window = lax.dynamic_slice_in_dim(
+        jnp.concatenate([zero_row, features, zero_row], axis=0), start, POLAR + 2, 0)
+    flat_window = window.reshape(-1, channels)
+    near_count = lat_rows * NEAR
+    from_west = shifted(jnp.concatenate(
+        [features[:, columns - NEAR :].reshape(-1, channels), flat_window]), "lon", 1)
+    from_east = shifted(jnp.concatenate(
+        [features[:, :NEAR].reshape(-1, channels), flat_window]), "lon", -1)
+    west_far = [shifted(window, "lon", hop) for hop in range(hops, 1, -1)]
+    east_far = [shifted(window, "lon", -hop) for hop in range(2, hops + 1)]
+
     basis_values = basis_table(quad_weights, cycle_index, widths, count)
-    padded = lat_extended(features)
-
-    last_band = lax.axis_index("lat") == lax.axis_size("lat") - 1
-    start = jnp.where(last_band, lat_rows - POLAR, 0).astype(jnp.int32)
-    start_arr = start.reshape(1)
-
-    near = jnp.concatenate(
-        [shifted(padded[:, columns - NEAR :], "lon", 1), padded,
-         shifted(padded[:, :NEAR], "lon", -1)], axis=1)
-    near = jnp.pad(near, ((0, 1), (0, 0), (0, 0)))
     near_sources = rolled_sources(
         basis_values[:, :, :, reach - NEAR : reach + NEAR + 1], columns + 2 * NEAR, 256)
-    out = conv_mix(start_arr, near, near_sources, features, mix_weight)
+    polar_values = lax.dynamic_slice_in_dim(basis_values, start, POLAR, 0)
+    wide_sources = rolled_sources(polar_values, columns + 2 * reach, 512)
 
-    window = lax.dynamic_slice_in_dim(padded, start, POLAR + 2, 0)
-    hops = reach // columns
-    western = [shifted(window, "lon", hop) for hop in range(hops, 0, -1)]
-    eastern = [shifted(window, "lon", -hop) for hop in range(1, hops + 1)]
-    wide = jnp.concatenate(western + [window] + eastern, axis=1)
+    west_near = from_west[:near_count].reshape(lat_rows, NEAR, channels)
+    east_near = from_east[:near_count].reshape(lat_rows, NEAR, channels)
+    near = jnp.concatenate([west_near, features, east_near], axis=1)
+    near = lat_extended(near)
+    near = jnp.pad(near, ((0, 1), (0, 0), (0, 0)))
+    out = conv_mix(scalars, near, near_sources, features, mix_weight)
+
+    west_one = from_west[near_count:].reshape(window.shape)
+    east_one = from_east[near_count:].reshape(window.shape)
+    wide = jnp.concatenate(west_far + [west_one, window, east_one] + east_far, axis=1)
     wide = wide[:, hops * columns - reach : hops * columns + columns + reach]
-    polar_values = lax.dynamic_slice_in_dim(basis_values, start, POLAR, 0)
     wide = jnp.pad(wide, ((0, 1), (0, 0), (0, 0)))
-    wide_sources = rolled_sources(polar_values, columns + 2 * reach, 512)
-    return conv_mix(start_arr, wide, wide_sources, features, mix_weight, previous=out)
+    return conv_mix(scalars, wide, wide_sources, features, mix_weight, previous=out)
 
 
 def solution(mesh):

time: 81.3 us -> 77 us (0.947)
  the two profiles are of different devices: /device:TPU:2 before, /device:TPU:102 now
where the time goes in v5:
time: 77 us; the launch traced here: 76.6 us
  Pallas kernels  24 us (31%)
  local copies, waits for them, and re-layouts  16.8 us (22%)
  waiting for transfers between devices  14.4 us (19%)
  starting transfers between devices  13.5 us (18%)
  other arithmetic  7.42 us (10%)
    pallas_call x2, Pallas kernels, conv_mix(): pl.pallas_call(conv_mix_kernel, grid_spec=grid_spec, out_shape=jax.ShapeD...  24 us
    ppermute x4, waiting for transfers between devices, shifted(): return lax.ppermute(block, axis, route)  10.4 us
    ppermute x4, starting transfers between devices, shifted(): return lax.ppermute(block, axis, route)  7.3 us
    another operation x17, local copies, waits for them, and re-layouts, rolled_sources(): jnp.stack([jnp.roll(flat[:, b], -columns * b, axis=-1) for b in range(cou...  6.08 us
    ppermute x1, starting transfers between devices, lat_extended(): after = lax.ppermute(value[:1], 'lat', down)  4.29 us
    ppermute x1, waiting for transfers between devices, lat_extended(): before = lax.ppermute(value[length - 1:], 'lat', up)  4.01 us
    reshape x2, local copies, waits for them, and re-layouts, rolled_sources(): flat = flat.reshape(rows, count, offsets * span)  2.61 us
    concatenate x1, other arithmetic, lat_extended(): return jnp.concatenate([before, value, after], axis=0)  2.14 us
  transfers between devices with their start and end apart: 6, of which 2 were waited for; matrix products, arithmetic and copies ran while one was open for 27% of the time, Pallas kernels for 0%

profile of v5, /device:TPU:102, one launch (start us, length us, event | category | flops | bytes accessed | tf_op | source)
XLA Modules:
  0.0 76.6 jit_solution(12829724039317775290)
XLA Ops:
  0.0 1.1 %fusion.11 = bf16[10,32,256]{2,1,0:T(8,128)(2,1)S(1)} fusion(s32[]{:T(128)} %select_n.10, bf16[1,32,256]{2,1,0:T(8,128)(2,1)S(1)} %broadcast_in_dim.10, bf16[96,32,256]{2,1,0:T(8,128)(2,1)} %f_ref.3), kind=kLoop, calls=%fused_computation.19 | loop fusion | flops 163840 | bytes 1753092 | tf_op jit(solution)/shard_map/concatenate | solution.py:135
  1.1 4.0 %collective-permute-start = (bf16[10,32,256]{2,1,0:T(8,128)(2,1)S(1)}, bf16[10,32,256]{2,1,0:T(8,128)(2,1)S(1)}, u32[]{:S(2)}, u32[]{:S(2)}) collective-permute-start(bf16[10,32,256]{2,1,0:T(8,128)(2,1)S(1)} %fusion.11), channel_id=1, source_target_pairs={{30,0},{31,1},{0,2},{1,3},{2,4},{3,5},{4,6},{5,7},{6,8},{7,9},{8,1... | collective-permute-start | bytes 491528 | tf_op jit(solution)/shard_map/ppermute | solution.py:18
  5.2 0.1 fusion.12
  5.3 0.0 copy-start.3
  5.3 0.0 copy-start.1
  5.3 0.0 copy-start.2
  5.3 1.4 %pad_maximum_fusion = (bf16[1856,256]{1,0:T(8,128)(2,1)}, bf16[1856,256]{1,0:T(8,128)(2,1)}) fusion(bf16[320,256]{1,0:T(8,128)(2,1)S(1)} %bitcast.81, bf16[1536,256]{1,0:T(8,128)(2,1)S(1)} %bitcast.78, bf16[1536,256]{1,0:T(8,128)(2,1)S(1)} %bitcast.79), kind=kLoop, calls=%fused_computation.16 | loop fusion | flops 3325952 | bytes 3637248 | tf_op jit(solution)/shard_map/concatenate | solution.py:140
  6.7 0.0 collective-permute-start.1
  6.7 3.2 %collective-permute-start.2 = (bf16[1856,256]{1,0:T(8,128)(2,1)}, bf16[1856,256]{1,0:T(8,128)(2,1)}, u32[]{:S(2)}, u32[]{:S(2)}) collective-permute-start(bf16[1856,256]{1,0:T(8,128)(2,1)} %get-tuple-element.18), channel_id=1, source_target_pairs={{1,0},{2,1},{3,2},{4,3},{5,4},{6,5},{7,6},{8,7},{9,8},{10,9},{11,1... | collective-permute-start | bytes 2850824 | tf_op jit(solution)/shard_map/ppermute | solution.py:18
  10.0 0.1 broadcast_compare_fusion
  10.1 0.4 multiply_convert_fusion
  10.5 0.3 constant_dynamic-slice_fusion
  10.8 1.2 %pad.25 = bf16[8,9,3,160]{0,3,2,1:T(8,128)(2,1)} pad(bf16[8,9,3,129]{0,3,2,1:T(8,128)(2,1)S(1)} %constant_dynamic-slice_fusion, bf16[]{:T(256)} %constant.8.clone.1), padding=0_0x0_0x0_0x0_31 | pad | bytes 124850 | tf_op jit(solution)/shard_map/jit(_pad)/pad | solution.py:44
  12.0 1.6 %copy.42 = bf16[8,9,480]{2,0,1:T(8,128)(2,1)S(1)} copy(bf16[8,9,480]{0,2,1:T(8,128)(2,1)} %bitcast.77) | data formatting | bytes 138240 | tf_op jit(solution)/shard_map/reshape | solution.py:45
  13.7 0.1 slice.262
  13.8 0.1 slice.265
  13.8 0.1 slice.268
  13.9 0.1 slice.274
  14.0 0.1 slice.277
  14.1 0.1 pad.28
  14.2 1.0 %copy.34 = bf16[96,9,192]{2,1,0:T(8,128)(2,1)S(1)} copy(bf16[96,9,192]{0,2,1:T(8,128)(2,1)S(1)} %bitcast.80) | data formatting | bytes 663552 | tf_op jit(solution)/shard_map/reshape | solution.py:45
  15.3 0.6 pad_convert_fusion
  15.9 0.1 slice.288
  16.0 0.1 slice.290
  16.1 0.1 slice.292
  16.2 0.1 slice.296
  16.3 0.1 maximum_bitcast_fusion.7
  16.4 0.1 maximum_bitcast_fusion.8
  16.5 0.1 maximum_bitcast_fusion.9
  16.6 0.1 maximum_bitcast_fusion.11
  16.6 0.1 maximum_bitcast_fusion
  16.7 0.1 maximum_bitcast_fusion.1
  16.8 0.1 maximum_bitcast_fusion.2
  16.9 0.1 maximum_bitcast_fusion.4
  17.0 0.1 maximum_bitcast_fusion.12
  17.1 0.1 slice.280
  17.2 0.1 slice.298
  17.2 0.1 maximum_bitcast_fusion.5
  17.4 0.1 maximum_bitcast_fusion.13
  17.4 0.1 slice.300
  17.5 0.1 maximum_bitcast_fusion.6
  17.9 0.1 copy.35
  18.0 0.1 copy.36
  18.1 0.1 copy.37
  18.2 0.1 copy.38
  18.3 0.1 copy.39
  18.4 0.1 copy.40
  18.5 0.1 copy.41
  18.6 1.6 %stack.78.src_ref = f32[8,9,512]{2,1,0:T(8,128)} concatenate(f32[8,1,512]{2,1,0:T(1,128)S(1)} %copy.26, f32[8,1,512]{2,1,0:T(1,128)S(1)} %copy.27, f32[8,1,512]{2,1,0:T(1,128)S(1)} %copy.28, f32[8,1,512]{2,1,0:T(1,128)S(1)} %copy.29, f32[8,1,512]{2,1,0:T(1,128)S(1)} %copy.30, f32[8,1,512]{2,1,0:T(1,128)S(1)} %copy.31, f32[8,1,512]{2,1,0:T(1,128)S(1)} %copy.32, ...), dimensions={1} | concatenate | bytes 294912 | tf_op jit(solution)/shard_map/stack | solution.py:47
  20.2 3.7 %stack.86.src_ref = f32[96,9,256]{2,1,0:T(8,128)} concatenate(f32[96,1,256]{2,1,0:T(1,128)S(1)} %get-tuple-element.17, f32[96,1,256]{2,1,0:T(1,128)S(1)} %copy.35, f32[96,1,256]{2,1,0:T(1,128)S(1)} %copy.36, f32[96,1,256]{2,1,0:T(1,128)S(1)} %copy.37, f32[96,1,256]{2,1,0:T(1,128)S(1)} %copy.38, f32[96,1,256]{2,1,0:T(1,128)S(1)} %copy.39, f32[96,1,256]{2,1,0:T(1,128)S(1)} %copy.40, ...), dimensions={1} | concatenate | bytes 1769472 | tf_op jit(solution)/shard_map/stack | solution.py:47
  23.9 0.6 pad_add_fusion.start_ref
  24.5 10.4 %collective-permute-done.1 = bf16[1856,256]{1,0:T(8,128)(2,1)} collective-permute-done((bf16[1856,256]{1,0:T(8,128)(2,1)}, bf16[1856,256]{1,0:T(8,128)(2,1)}, u32[]{:S(2)}, u32[]{:S(2)}) %collective-permute-start.1) | collective-permute-done | bytes 950304 | tf_op jit(solution)/shard_map/ppermute | solution.py:18
  34.9 0.9 %slice.258 = bf16[320,256]{1,0:T(8,128)(2,1)S(1)} slice(bf16[1856,256]{1,0:T(8,128)(2,1)} %collective-permute-done.1), slice={[1536:1856], [0:256]} | slice | bytes 327680 | tf_op jit(solution)/shard_map/slice | solution.py:158
  35.8 1.2 %slice.285 = bf16[1536,256]{1,0:T(8,128)(2,1)S(1)} slice(bf16[1856,256]{1,0:T(8,128)(2,1)} %collective-permute-done.1), slice={[0:1536], [0:256]} | slice | bytes 1572864 | tf_op jit(solution)/shard_map/slice | solution.py:151
  37.0 0.1 constant_dynamic-update-slice_fusion.2
  37.1 1.2 %slice.286 = bf16[1536,256]{1,0:T(8,128)(2,1)S(1)} slice(bf16[1856,256]{1,0:T(8,128)(2,1)} %collective-permute-done.2), slice={[0:1536], [0:256]} | slice | bytes 1572864 | tf_op jit(solution)/shard_map/slice | solution.py:152
  38.3 4.3 %collective-permute-start.5 = (bf16[1,64,256]{2,1,0:T(8,128)(2,1)S(1)}, bf16[1,64,256]{2,1,0:T(8,128)(2,1)S(1)}, u32[]{:S(2)}, u32[]{:S(2)}) collective-permute-start(bf16[1,64,256]{2,1,0:T(8,128)(2,1)S(1)} %get-tuple-element.6), channel_id=1, source_target_pairs={{32,0},{64,32},{96,64},{128,96},{160,128},{192,160},{224,192},{33,... | collective-permute-start | bytes 98312 | tf_op jit(solution)/shard_map/ppermute | solution.py:26
  42.6 1.9 %collective-permute-start.4 = (bf16[1,64,256]{2,1,0:T(8,128)(2,1)S(1)}, bf16[1,64,256]{2,1,0:T(8,128)(2,1)S(1)}, u32[]{:S(2)}, u32[]{:S(2)}) collective-permute-start(bf16[1,64,256]{2,1,0:T(8,128)(2,1)S(1)} %get-tuple-element.5), channel_id=1, source_target_pairs={{0,32},{32,64},{64,96},{96,128},{128,160},{160,192},{192,224},{1,3... | collective-permute-start | bytes 98312 | tf_op jit(solution)/shard_map/ppermute | solution.py:25
  44.5 0.9 %slice.259 = bf16[320,256]{1,0:T(8,128)(2,1)S(1)} slice(bf16[1856,256]{1,0:T(8,128)(2,1)} %collective-permute-done.2), slice={[1536:1856], [0:256]} | slice | bytes 327680 | tf_op jit(solution)/shard_map/slice | solution.py:159
  45.5 1.0 %pad.24.ext_ref = bf16[11,160,256]{2,1,0:T(8,128)(2,1)} pad(bf16[10,160,256]{2,1,0:T(8,128)(2,1)S(1)} %constant_dynamic-update-slice_fusion, bf16[]{:T(256)} %constant.8.clone.1), padding=0_1x0_0x0_0 | pad | bytes 1720322 | tf_op jit(solution)/shard_map/jit(_pad)/pad | solution.py:162
  46.5 4.0 %collective-permute-done.4 = bf16[1,64,256]{2,1,0:T(8,128)(2,1)S(1)} collective-permute-done((bf16[1,64,256]{2,1,0:T(8,128)(2,1)S(1)}, bf16[1,64,256]{2,1,0:T(8,128)(2,1)S(1)}, u32[]{:S(2)}, u32[]{:S(2)}) %collective-permute-start.4) | collective-permute-done | bytes 32800 | tf_op jit(solution)/shard_map/ppermute | solution.py:25
  50.5 2.1 %fusion.6.ext_ref = bf16[99,64,256]{2,1,0:T(8,128)(2,1)} fusion(bf16[1,64,256]{2,1,0:T(8,128)(2,1)S(1)} %collective-permute-done.5, bf16[1,64,256]{2,1,0:T(8,128)(2,1)S(1)} %collective-permute-done.4, bf16[96,16,256]{2,1,0:T(8,128)(2,1)S(1)} %bitcast.76, bf16[96,32,256]{2,1,0:T(8,128)(2,1)S(1)} %copy-done, bf16[96,16,256]{2,1,0:T(8,128)(2,1)S(1)} %bitcast.74), kind=kLoop, calls=%fused_computation.7 | loop fusion | flops 25952256 | bytes 6455296 | tf_op jit(solution)/shard_map/concatenate | solution.py:27
  52.7 21.0 %shard_map.55.rest_0_ = bf16[96,32,256]{2,1,0:T(8,128)(2,1)} custom-call(s32[2]{0:T(128)} %pad_add_fusion.start_ref, bf16[99,64,256]{2,1,0:T(8,128)(2,1)} %fusion.6.ext_ref, f32[96,9,256]{2,1,0:T(8,128)} %stack.86.src_ref, bf16[96,32,256]{2,1,0:T(8,128)(2,1)} %f_ref.3, bf16[9,256,256]{2,1,0:T(8,128)(2,1)} %w_ref.3), custom_call_target="tpu_custom_call" | custom-call | tf_op jit(solution)/shard_map/pallas_call | solution.py:113
  73.7 3.0 %shard_map.56 = bf16[96,32,256]{2,1,0:T(8,128)(2,1)} custom-call(s32[2]{0:T(128)} %pad_add_fusion.start_ref, bf16[11,160,256]{2,1,0:T(8,128)(2,1)} %pad.24.ext_ref, f32[8,9,512]{2,1,0:T(8,128)} %stack.78.src_ref, bf16[96,32,256]{2,1,0:T(8,128)(2,1)} %f_ref.3, bf16[9,256,256]{2,1,0:T(8,128)(2,1)} %w_ref.3, ...), custom_call_target="tpu_custom_call", output_to_operand_aliasing={{}: (5, {})} | custom-call | tf_op jit(solution)/shard_map/pallas_call | solution.py:113
  (50 shorter events, 0.4 us)
Async XLA Ops:
  0.0 5.1 %copy-start = (bf16[96,32,256]{2,1,0:T(8,128)(2,1)S(1)}, bf16[96,32,256]{2,1,0:T(8,128)(2,1)}, u32[]{:S(2)}) copy-start(bf16[96,32,256]{2,1,0:T(8,128)(2,1)} %f_ref.3) | copy-start | bytes 4718596
  1.1 23.4 %collective-permute-start = (bf16[10,32,256]{2,1,0:T(8,128)(2,1)S(1)}, bf16[10,32,256]{2,1,0:T(8,128)(2,1)S(1)}, u32[]{:S(2)}, u32[]{:S(2)}) collective-permute-start(bf16[10,32,256]{2,1,0:T(8,128)(2,1)S(1)} %fusion.11), channel_id=1, source_target_pairs={{30,0},{31,1},{0,2},{1,3},{2,4},{3,5},{4,6},{5,7},{6,8},{7,9},{8,1... | collective-permute-start | bytes 491528 | tf_op jit(solution)/shard_map/ppermute | solution.py:18
  5.1 40.4 %collective-permute-start.3 = (bf16[10,32,256]{2,1,0:T(8,128)(2,1)S(1)}, bf16[10,32,256]{2,1,0:T(8,128)(2,1)S(1)}, u32[]{:S(2)}, u32[]{:S(2)}) collective-permute-start(bf16[10,32,256]{2,1,0:T(8,128)(2,1)S(1)} %fusion.11), channel_id=1, source_target_pairs={{2,0},{3,1},{4,2},{5,3},{6,4},{7,5},{8,6},{9,7},{10,8},{11,9},{12,... | collective-permute-start | bytes 491528 | tf_op jit(solution)/shard_map/ppermute | solution.py:18
  5.3 4.7 %copy-start.3 = (s32[96]{0:T(128)S(1)}, s32[96]{0:T(128)}, u32[]{:S(2)}) copy-start(s32[96]{0:T(128)} %param.8) | copy-start | bytes 1156
  5.3 4.8 %copy-start.1 = (f32[96,3,129]{0,2,1:T(8,128)S(1)}, f32[96,3,129]{0,2,1:T(8,128)}, u32[]{:S(2)}) copy-start(f32[96,3,129]{0,2,1:T(8,128)} %param.6) | copy-start | bytes 445828
  5.3 4.8 %copy-start.2 = (s32[96,3,129]{0,2,1:T(8,128)S(1)}, s32[96,3,129]{0,2,1:T(8,128)}, u32[]{:S(2)}) copy-start(s32[96,3,129]{0,2,1:T(8,128)} %param.7) | copy-start | bytes 445828
  6.7 28.2 %collective-permute-start.1 = (bf16[1856,256]{1,0:T(8,128)(2,1)}, bf16[1856,256]{1,0:T(8,128)(2,1)}, u32[]{:S(2)}, u32[]{:S(2)}) collective-permute-start(bf16[1856,256]{1,0:T(8,128)(2,1)} %get-tuple-element.19), channel_id=1, source_target_pairs={{31,0},{0,1},{1,2},{2,3},{3,4},{4,5},{5,6},{6,7},{7,8},{8,9},{9,10... | collective-permute-start | bytes 2850824 | tf_op jit(solution)/shard_map/ppermute | solution.py:18
  6.7 30.4 %collective-permute-start.2 = (bf16[1856,256]{1,0:T(8,128)(2,1)}, bf16[1856,256]{1,0:T(8,128)(2,1)}, u32[]{:S(2)}, u32[]{:S(2)}) collective-permute-start(bf16[1856,256]{1,0:T(8,128)(2,1)} %get-tuple-element.18), channel_id=1, source_target_pairs={{1,0},{2,1},{3,2},{4,3},{5,4},{6,5},{7,6},{8,7},{9,8},{10,9},{11,1... | collective-permute-start | bytes 2850824 | tf_op jit(solution)/shard_map/ppermute | solution.py:18
  38.3 8.2 %collective-permute-start.5 = (bf16[1,64,256]{2,1,0:T(8,128)(2,1)S(1)}, bf16[1,64,256]{2,1,0:T(8,128)(2,1)S(1)}, u32[]{:S(2)}, u32[]{:S(2)}) collective-permute-start(bf16[1,64,256]{2,1,0:T(8,128)(2,1)S(1)} %get-tuple-element.6), channel_id=1, source_target_pairs={{32,0},{64,32},{96,64},{128,96},{160,128},{192,160},{224,192},{33,... | collective-permute-start | bytes 98312 | tf_op jit(solution)/shard_map/ppermute | solution.py:26
  42.6 7.9 %collective-permute-start.4 = (bf16[1,64,256]{2,1,0:T(8,128)(2,1)S(1)}, bf16[1,64,256]{2,1,0:T(8,128)(2,1)S(1)}, u32[]{:S(2)}, u32[]{:S(2)}) collective-permute-start(bf16[1,64,256]{2,1,0:T(8,128)(2,1)S(1)} %get-tuple-element.5), channel_id=1, source_target_pairs={{0,32},{32,64},{64,96},{96,128},{128,160},{160,192},{192,224},{1,3... | collective-permute-start | bytes 98312 | tf_op jit(solution)/shard_map/ppermute | solution.py:25

commit v6 on v5

v6 whole, which is shorter than its diff:
```python
import functools

import jax
import jax.numpy as jnp
from jax import lax
from jax.experimental import pallas as pl
from jax.experimental.pallas import tpu as pltpu
from jax.sharding import PartitionSpec as P

POLAR = 8
NEAR = 16
BLOCK = 8


def shifted(block, axis, distance):
    devices = range(lax.axis_size(axis))
    route = [((i - distance) % len(devices), i) for i in devices]
    return lax.ppermute(block, axis, route)


def lat_extended(value):
    count, length = lax.axis_size("lat"), value.shape[0]
    up = [(i, i + 1) for i in range(count - 1)]
    down = [(j, i) for i, j in up]
    before = lax.ppermute(value[length - 1 :], "lat", up)
    after = lax.ppermute(value[:1], "lat", down)
    return jnp.concatenate([before, value, after], axis=0)


def basis_table(quad_weights, cycle_index, widths, count):
    offsets = jnp.arange(quad_weights.shape[2]) - quad_weights.shape[2] // 2
    inside = jnp.abs(offsets)[None, None, :] <= widths[:, None, None]
    member = cycle_index[:, None, :, :] == jnp.arange(count)[None, :, None, None]
    scale_row = 1.0 / jnp.sqrt(3.0 * (2.0 * widths.astype(jnp.float32) + 1.0))
    values = jnp.where(
        member & inside[:, None, :, :], quad_weights[:, None, :, :], jnp.float32(0.0)
    )
    return (values * scale_row[:, None, None, None]).astype(jnp.bfloat16)


def flat_sources(values, span, lanes):
    rows, count, offsets, taps = values.shape
    flat = jnp.pad(values, ((0, 0), (0, 0), (0, 0), (0, span - taps)))
    flat = flat.reshape(rows, count, offsets * span)
    return jnp.pad(flat, ((0, 0), (0, 0), (0, lanes - offsets * span)))


def conv_block(ext_ref, src_ref, f_ref, w_ref, o_ref, conv_scr, base):
    rows, columns, channels = f_ref.shape
    count, lanes = src_ref.shape[1], src_ref.shape[2]
    span = ext_ref.shape[1]
    for q in range(rows):
        source = src_ref[q].astype(jnp.float32)
        pieces = []
        for b in range(count):
            spread = jnp.broadcast_to(source[b : b + 1], (columns, lanes))
            pieces.append(pltpu.roll(spread, 0, 1, stride=1, stride_axis=0))
        kernel = jnp.concatenate(pieces, axis=0).astype(jnp.bfloat16)
        window = ext_ref[pl.ds(base + q, 4)].reshape(4 * span, channels)[:lanes]
        conv = jnp.dot(kernel, window, preferred_element_type=jnp.float32)
        conv = conv.astype(jnp.bfloat16)
        for b in range(count):
            conv_scr[b, q * columns : (q + 1) * columns, :] = conv[b * columns : (b + 1) * columns]
    acc = f_ref[...].reshape(rows * columns, channels).astype(jnp.float32)
    for b in range(count):
        acc = acc + jnp.dot(conv_scr[b], w_ref[b], preferred_element_type=jnp.float32)
    o_ref[...] = acc.reshape(rows, columns, channels).astype(o_ref.dtype)


def near_kernel(scalar_ref, src_ref, f_ref, all_ref, west_ref, east_ref, north_ref,
                south_ref, w_ref, o_ref, ext_scr, conv_scr):
    rows, columns, channels = f_ref.shape
    lat_rows = all_ref.shape[0]
    halo = (ext_scr.shape[1] - columns) // 2
    step = pl.program_id(0)
    base = step * rows

    def put(k, row):
        ext_scr[k, :halo] = west_ref[pl.ds(pl.multiple_of(row * halo, halo), halo)]
        ext_scr[k, halo : halo + columns] = all_ref[row]
        ext_scr[k, halo + columns :] = east_ref[pl.ds(pl.multiple_of(row * halo, halo), halo)]

    for k in range(1, rows + 1):
        put(k, base + k - 1)

    @pl.when(step == 0)
    def _():
        ext_scr[0] = north_ref[0]

    @pl.when(step > 0)
    def _():
        put(0, base - 1)

    @pl.when(step == pl.num_programs(0) - 1)
    def _():
        ext_scr[rows + 1] = south_ref[0]

    @pl.when(step < pl.num_programs(0) - 1)
    def _():
        put(rows + 1, jnp.minimum(base + rows, lat_rows - 1))

    ext_scr[rows + 2] = jnp.zeros(ext_scr.shape[1:], ext_scr.dtype)
    conv_block(ext_scr, src_ref, f_ref, w_ref, o_ref, conv_scr, 0)


def wide_kernel(scalar_ref, ext_ref, src_ref, f_ref, w_ref, prev_ref, o_ref, conv_scr):
    @pl.when(scalar_ref[1] != 0)
    def _():
        conv_block(ext_ref, src_ref, f_ref, w_ref, o_ref, conv_scr, 0)

    @pl.when(scalar_ref[1] == 0)
    def _():
        o_ref[...] = prev_ref[...]


def full_spec(shape):
    return pl.BlockSpec(shape, lambda i, s: (0,) * len(shape))


def near_call(scalars, sources, features, west, east, north, south, mix_weight):
    lat_rows, columns, channels = features.shape
    count = mix_weight.shape[0]
    halo = (north.shape[1] - columns) // 2
    row_map = lambda i, s: (i, 0, 0)
    grid_spec = pltpu.PrefetchScalarGridSpec(
        num_scalar_prefetch=1,
        grid=(lat_rows // BLOCK,),
        in_specs=[
            pl.BlockSpec((BLOCK,) + sources.shape[1:], row_map),
            pl.BlockSpec((BLOCK, columns, channels), row_map),
            full_spec(features.shape), full_spec(west.shape), full_spec(east.shape),
            full_spec(north.shape), full_spec(south.shape), full_spec(mix_weight.shape),
        ],
        out_specs=pl.BlockSpec((BLOCK, columns, channels), row_map),
        scratch_shapes=[
            pltpu.VMEM((BLOCK + 3, columns + 2 * halo, channels), features.dtype),
            pltpu.VMEM((count, BLOCK * columns, channels), jnp.bfloat16),
        ],
    )
    return pl.pallas_call(
        near_kernel, grid_spec=grid_spec,
        out_shape=jax.ShapeDtypeStruct(features.shape, features.dtype),
    )(scalars, sources, features, features, west, east, north, south, mix_weight)


def wide_call(scalars, extended, sources, features, mix_weight, previous):
    lat_rows, columns, channels = features.shape
    count = mix_weight.shape[0]
    row_map = lambda i, s: (s[0] // BLOCK + i, 0, 0)
    grid_spec = pltpu.PrefetchScalarGridSpec(
        num_scalar_prefetch=1,
        grid=(sources.shape[0] // BLOCK,),
        in_specs=[
            full_spec(extended.shape),
            pl.BlockSpec((BLOCK,) + sources.shape[1:], lambda i, s: (i, 0, 0)),
            pl.BlockSpec((BLOCK, columns, channels), row_map),
            full_spec(mix_weight.shape),
            pl.BlockSpec((BLOCK, columns, channels), row_map),
        ],
        out_specs=pl.BlockSpec((BLOCK, columns, channels), row_map),
        scratch_shapes=[pltpu.VMEM((count, BLOCK * columns, channels), jnp.bfloat16)],
    )
    return pl.pallas_call(
        wide_kernel, grid_spec=grid_spec,
        out_shape=jax.ShapeDtypeStruct(features.shape, features.dtype),
        input_output_aliases={5: 0},
    )(scalars, extended, sources, features, mix_weight, previous)


def body(features, quad_weights, cycle_index, widths, mix_weight):
    count = mix_weight.shape[0]
    lat_rows, columns, channels = features.shape
    reach = quad_weights.shape[2] // 2
    hops = reach // columns

    lat_index, lat_count = lax.axis_index("lat"), lax.axis_size("lat")
    last_band = lat_index == lat_count - 1
    polar = (lat_index == 0) | last_band
    start = jnp.where(last_band, lat_rows - POLAR, 0).astype(jnp.int32)
    scalars = jnp.stack([start, polar.astype(jnp.int32)])

    zero_row = jnp.zeros((1, columns, channels), features.dtype)
    window = lax.dynamic_slice_in_dim(
        jnp.concatenate([zero_row, features, zero_row], axis=0), start, POLAR + 2, 0)
    flat_window = window.reshape(-1, channels)
    near_count = lat_rows * NEAR
    from_west = shifted(jnp.concatenate(
        [features[:, columns - NEAR :].reshape(-1, channels), flat_window]), "lon", 1)
    from_east = shifted(jnp.concatenate(
        [features[:, :NEAR].reshape(-1, channels), flat_window]), "lon", -1)
    west_far = [shifted(window, "lon", hop) for hop in range(hops, 1, -1)]
    east_far = [shifted(window, "lon", -hop) for hop in range(2, hops + 1)]

    basis_values = basis_table(quad_weights, cycle_index, widths, count)
    near_sources = flat_sources(
        basis_values[:, :, :, reach - NEAR : reach + NEAR + 1], columns + 2 * NEAR, 256)
    polar_values = lax.dynamic_slice_in_dim(basis_values, start, POLAR, 0)
    wide_sources = flat_sources(polar_values, columns + 2 * reach, 512)

    def edge(row):
        return jnp.concatenate(
            [from_west[row * NEAR : (row + 1) * NEAR][None], features[row : row + 1],
             from_east[row * NEAR : (row + 1) * NEAR][None]], axis=1)

    count_lat = lax.axis_size("lat")
    up = [(i, i + 1) for i in range(count_lat - 1)]
    down = [(j, i) for i, j in up]
    north = lax.ppermute(edge(lat_rows - 1), "lat", up)
    south = lax.ppermute(edge(0), "lat", down)
    out = near_call(scalars, near_sources, features, from_west, from_east, north, south,
                    mix_weight)

    west_one = from_west[near_count:].reshape(window.shape)
    east_one = from_east[near_count:].reshape(window.shape)
    wide = jnp.concatenate(west_far + [west_one, window, east_one] + east_far, axis=1)
    wide = wide[:, hops * columns - reach : hops * columns + columns + reach]
    wide = jnp.pad(wide, ((0, 1), (0, 0), (0, 0)))
    return wide_call(scalars, wide, wide_sources, features, mix_weight, out)


def solution(mesh):
    in_specs = (P("lat", "lon", None), P("lat", None, None), P("lat", None, None), P("lat"), P())
    out_specs = P("lat", "lon", None)
    return jax.shard_map(body, mesh=mesh, in_specs=in_specs, out_specs=out_specs, check_vma=False)
```

time: 77 us -> 73.3 us (0.952)
  the two profiles are of different devices: /device:TPU:102 before, /device:TPU:3 now
where the time goes in v6:
time: 73.3 us; the launch traced here: 72.3 us
  Pallas kernels  24.4 us (33%)
  starting transfers between devices  16 us (22%)
  waiting for transfers between devices  15.2 us (21%)
  local copies, waits for them, and re-layouts  12.8 us (17%)
  other arithmetic  3.7 us (5%)
    pallas_call x1, Pallas kernels, near_call(): pl.pallas_call(near_kernel, grid_spec=grid_spec, out_shape=jax.ShapeDtype...  21.4 us
    ppermute x4, waiting for transfers between devices, shifted(): return lax.ppermute(block, axis, route)  15.2 us
    ppermute x4, starting transfers between devices, shifted(): return lax.ppermute(block, axis, route)  8.26 us
    ppermute x1, starting transfers between devices, body(): south = lax.ppermute(edge(0), 'lat', down)  4.58 us
    ppermute x1, starting transfers between devices, body(): north = lax.ppermute(edge(lat_rows - 1), 'lat', up)  3.19 us
    pallas_call x1, Pallas kernels, wide_call(): pl.pallas_call(wide_kernel, grid_spec=grid_spec, out_shape=jax.ShapeDtype...  2.97 us
    unnamed x15, local copies, waits for them, and re-layouts  2.17 us
    pad x2, local copies, waits for them, and re-layouts, flat_sources(): return jnp.pad(flat, ((0, 0), (0, 0), (0, lanes - offsets * span)))  1.75 us
  transfers between devices with their start and end apart: 6, of which 2 were waited for; matrix products, arithmetic and copies ran while one was open for 20% of the time, Pallas kernels for 0%

profile of v6, /device:TPU:3, one launch (start us, length us, event | category | flops | bytes accessed | tf_op | source)
XLA Modules:
  0.0 72.3 jit_solution(3386191551131433374)
XLA Ops:
  0.0 0.0 copy-start
  0.0 1.1 %fusion.2 = bf16[10,32,256]{2,1,0:T(8,128)(2,1)S(1)} fusion(s32[]{:T(128)} %select_n.10, bf16[1,32,256]{2,1,0:T(8,128)(2,1)S(1)} %broadcast_in_dim.34, bf16[96,32,256]{2,1,0:T(8,128)(2,1)} %f_ref.3), kind=kLoop, calls=%fused_computation.9 | loop fusion | flops 163840 | bytes 1753092 | tf_op jit(solution)/shard_map/concatenate | solution.py:184
  1.1 1.9 %collective-permute-start = (bf16[10,32,256]{2,1,0:T(8,128)(2,1)S(1)}, bf16[10,32,256]{2,1,0:T(8,128)(2,1)}, u32[]{:S(2)}, u32[]{:S(2)}) collective-permute-start(bf16[10,32,256]{2,1,0:T(8,128)(2,1)S(1)} %fusion.2), channel_id=1, source_target_pairs={{30,0},{31,1},{0,2},{1,3},{2,4},{3,5},{4,6},{5,7},{6,8},{7,9},{8,1... | collective-permute-start | bytes 491528 | tf_op jit(solution)/shard_map/ppermute | solution.py:18
  3.0 5.4 %collective-permute-start.3 = (bf16[10,32,256]{2,1,0:T(8,128)(2,1)S(1)}, bf16[10,32,256]{2,1,0:T(8,128)(2,1)S(1)}, u32[]{:S(2)}, u32[]{:S(2)}) collective-permute-start(bf16[10,32,256]{2,1,0:T(8,128)(2,1)S(1)} %fusion.2), channel_id=1, source_target_pairs={{2,0},{3,1},{4,2},{5,3},{6,4},{7,5},{8,6},{9,7},{10,8},{11,9},{12,... | collective-permute-start | bytes 491528 | tf_op jit(solution)/shard_map/ppermute | solution.py:18
  8.4 0.0 copy-done
  8.4 0.1 fusion.4
  8.5 0.0 copy-start.5
  8.5 0.0 copy-start.1
  8.6 0.0 copy-start.2
  8.6 1.4 %pad_maximum_fusion = (bf16[1856,256]{1,0:T(8,128)(2,1)}, bf16[1856,256]{1,0:T(8,128)(2,1)}) fusion(bf16[320,256]{1,0:T(8,128)(2,1)S(1)} %bitcast.21, bf16[1536,256]{1,0:T(8,128)(2,1)S(1)} %bitcast.18, bf16[1536,256]{1,0:T(8,128)(2,1)S(1)} %bitcast.19), kind=kLoop, calls=%fused_computation.6 | loop fusion | flops 3325952 | bytes 3637248 | tf_op jit(solution)/shard_map/concatenate | solution.py:189
  10.0 0.0 collective-permute-start.1
  10.0 1.0 %collective-permute-start.2 = (bf16[1856,256]{1,0:T(8,128)(2,1)}, bf16[1856,256]{1,0:T(8,128)(2,1)}, u32[]{:S(2)}, u32[]{:S(2)}) collective-permute-start(bf16[1856,256]{1,0:T(8,128)(2,1)} %get-tuple-element.13), channel_id=1, source_target_pairs={{1,0},{2,1},{3,2},{4,3},{5,4},{6,5},{7,6},{8,7},{9,8},{10,9},{11,1... | collective-permute-start | bytes 2850824 | tf_op jit(solution)/shard_map/ppermute | solution.py:18
  10.9 0.0 copy-done.5
  10.9 0.1 broadcast_compare_fusion
  11.0 0.0 copy-done.1
  11.0 0.0 copy-done.2
  11.1 0.4 multiply_convert_fusion
  11.5 1.3 %constant_dynamic-slice_fusion = bf16[8,9,3,129]{0,3,2,1:T(8,128)(2,1)} fusion(bf16[96,9,3,129]{0,3,2,1:T(8,128)(2,1)S(1)} %multiply_convert_fusion, s32[]{:T(128)} %select_n.10), kind=kLoop, calls=%fused_computation.23 | loop fusion | bytes 111460 | tf_op jit(solution)/shard_map/dynamic_slice | solution.py:197
  12.8 0.1 pad.23
  12.9 1.0 %copy.11 = bf16[96,9,192]{2,1,0:T(8,128)(2,1)S(1)} copy(bf16[96,9,192]{0,2,1:T(8,128)(2,1)S(1)} %bitcast.20) | data formatting | bytes 663552 | tf_op jit(solution)/shard_map/reshape | solution.py:44
  14.0 1.1 %pad.24.src_ref = bf16[96,9,256]{2,1,0:T(8,128)(2,1)} pad(bf16[96,9,192]{2,1,0:T(8,128)(2,1)S(1)} %copy.11, bf16[]{:T(256)} %constant.8.clone.1), padding=0_0x0_0x0_64 | pad | bytes 774146 | tf_op jit(solution)/shard_map/jit(_pad)/pad | solution.py:45
  15.0 1.4 %pad.21 = bf16[8,9,3,160]{0,3,2,1:T(8,128)(2,1)S(1)} pad(bf16[8,9,3,129]{0,3,2,1:T(8,128)(2,1)} %constant_dynamic-slice_fusion, bf16[]{:T(256)} %constant.8.clone.1), padding=0_0x0_0x0_0x0_31 | pad | bytes 124850 | tf_op jit(solution)/shard_map/jit(_pad)/pad | solution.py:43
  16.4 0.6 copy.10
  17.0 0.7 pad.22.src_ref
  17.7 0.6 pad_add_fusion.scalar_ref
  18.3 0.0 collective-permute-done
  18.3 0.9 %constant_dynamic-update-slice_fusion.4 = bf16[10,160,256]{2,1,0:T(8,128)(2,1)S(1)} fusion(bf16[10,32,256]{2,1,0:T(8,128)(2,1)} %collective-permute-done), kind=kLoop, calls=%fused_computation.17 | loop fusion | bytes 327680
  19.3 11.9 %collective-permute-done.1.west_ref = bf16[1856,256]{1,0:T(8,128)(2,1)} collective-permute-done((bf16[1856,256]{1,0:T(8,128)(2,1)}, bf16[1856,256]{1,0:T(8,128)(2,1)}, u32[]{:S(2)}, u32[]{:S(2)}) %collective-permute-start.1) | collective-permute-done | bytes 950304 | tf_op jit(solution)/shard_map/ppermute | solution.py:18
  31.1 0.7 slice_bitcast_fusion.1
  31.9 3.3 %collective-permute-done.2.east_ref = bf16[1856,256]{1,0:T(8,128)(2,1)} collective-permute-done((bf16[1856,256]{1,0:T(8,128)(2,1)}, bf16[1856,256]{1,0:T(8,128)(2,1)}, u32[]{:S(2)}, u32[]{:S(2)}) %collective-permute-start.2) | collective-permute-done | bytes 950304 | tf_op jit(solution)/shard_map/ppermute | solution.py:18
  35.1 0.7 slice_bitcast_fusion
  35.9 3.2 %collective-permute-start.4 = (bf16[1,64,256]{2,1,0:T(8,128)(2,1)S(1)}, bf16[1,64,256]{2,1,0:T(8,128)(2,1)S(1)}, u32[]{:S(2)}, u32[]{:S(2)}) collective-permute-start(bf16[1,64,256]{2,1,0:T(8,128)(2,1)S(1)} %pad_maximum_fusion.2), channel_id=1, source_target_pairs={{0,32},{32,64},{64,96},{96,128},{128,160},{160,192},{192,224},{1,3... | collective-permute-start | bytes 98312 | tf_op jit(solution)/shard_map/ppermute | solution.py:208
  39.1 4.6 %collective-permute-start.5 = (bf16[1,64,256]{2,1,0:T(8,128)(2,1)S(1)}, bf16[1,64,256]{2,1,0:T(8,128)(2,1)S(1)}, u32[]{:S(2)}, u32[]{:S(2)}) collective-permute-start(bf16[1,64,256]{2,1,0:T(8,128)(2,1)S(1)} %pad_maximum_fusion.3), channel_id=1, source_target_pairs={{32,0},{64,32},{96,64},{128,96},{160,128},{192,160},{224,192},{33,... | collective-permute-start | bytes 98312 | tf_op jit(solution)/shard_map/ppermute | solution.py:209
  43.7 0.9 %slice.44 = bf16[320,256]{1,0:T(8,128)(2,1)S(1)} slice(bf16[1856,256]{1,0:T(8,128)(2,1)} %collective-permute-done.1.west_ref), slice={[1536:1856], [0:256]} | slice | bytes 327680 | tf_op jit(solution)/shard_map/slice | solution.py:213
  44.6 0.1 constant_dynamic-update-slice_fusion.2
  44.7 0.9 %slice.45 = bf16[320,256]{1,0:T(8,128)(2,1)S(1)} slice(bf16[1856,256]{1,0:T(8,128)(2,1)} %collective-permute-done.2.east_ref), slice={[1536:1856], [0:256]} | slice | bytes 327680 | tf_op jit(solution)/shard_map/slice | solution.py:214
  45.6 0.0 collective-permute-done.3
  45.7 1.0 %pad.20.ext_ref = bf16[11,160,256]{2,1,0:T(8,128)(2,1)} pad(bf16[10,160,256]{2,1,0:T(8,128)(2,1)S(1)} %constant_dynamic-update-slice_fusion, bf16[]{:T(256)} %constant.8.clone.1), padding=0_1x0_0x0_0 | pad | bytes 1720322 | tf_op jit(solution)/shard_map/jit(_pad)/pad | solution.py:217
  46.7 0.0 collective-permute-done.4.north_ref
  46.7 0.0 copy-start.3
  46.7 0.0 collective-permute-done.5.south_ref
  46.7 0.6 copy-done.3
  47.3 0.0 copy-start.4
  47.3 0.6 copy-done.4
  47.9 21.4 %shard_map.55.prev_ref = bf16[96,32,256]{2,1,0:T(8,128)(2,1)} custom-call(s32[2]{0:T(128)} %pad_add_fusion.scalar_ref, bf16[96,9,256]{2,1,0:T(8,128)(2,1)} %pad.24.src_ref, bf16[96,32,256]{2,1,0:T(8,128)(2,1)} %f_ref.3, bf16[96,32,256]{2,1,0:T(8,128)(2,1)} %f_ref.3, bf16[1856,256]{1,0:T(8,128)(2,1)} %collective-permute-done.1.west_ref, ...), custom_call_target="tpu_custom_call" | custom-call | tf_op jit(solution)/shard_map/pallas_call | solution.py:140
  69.3 3.0 %shard_map.56 = bf16[96,32,256]{2,1,0:T(8,128)(2,1)} custom-call(s32[2]{0:T(128)} %pad_add_fusion.scalar_ref, bf16[11,160,256]{2,1,0:T(8,128)(2,1)} %pad.20.ext_ref, bf16[8,9,512]{2,1,0:T(8,128)(2,1)} %pad.22.src_ref, bf16[96,32,256]{2,1,0:T(8,128)(2,1)} %f_ref.3, bf16[9,256,256]{2,1,0:T(8,128)(2,1)} %w_ref.3, ...), custom_call_target="tpu_custom_call", output_to_operand_aliasing={{}: (5, {})} | custom-call | tf_op jit(solution)/shard_map/pallas_call | solution.py:163
  (10 shorter events, 0.1 us)
Async XLA Ops:
  0.0 8.4 %copy-start = (bf16[96,32,256]{2,1,0:T(8,128)(2,1)S(1)}, bf16[96,32,256]{2,1,0:T(8,128)(2,1)}, u32[]{:S(2)}) copy-start(bf16[96,32,256]{2,1,0:T(8,128)(2,1)} %f_ref.3) | copy-start | bytes 4718596
  1.1 17.2 %collective-permute-start = (bf16[10,32,256]{2,1,0:T(8,128)(2,1)S(1)}, bf16[10,32,256]{2,1,0:T(8,128)(2,1)}, u32[]{:S(2)}, u32[]{:S(2)}) collective-permute-start(bf16[10,32,256]{2,1,0:T(8,128)(2,1)S(1)} %fusion.2), channel_id=1, source_target_pairs={{30,0},{31,1},{0,2},{1,3},{2,4},{3,5},{4,6},{5,7},{6,8},{7,9},{8,1... | collective-permute-start | bytes 491528 | tf_op jit(solution)/shard_map/ppermute | solution.py:18
  3.0 42.6 %collective-permute-start.3 = (bf16[10,32,256]{2,1,0:T(8,128)(2,1)S(1)}, bf16[10,32,256]{2,1,0:T(8,128)(2,1)S(1)}, u32[]{:S(2)}, u32[]{:S(2)}) collective-permute-start(bf16[10,32,256]{2,1,0:T(8,128)(2,1)S(1)} %fusion.2), channel_id=1, source_target_pairs={{2,0},{3,1},{4,2},{5,3},{6,4},{7,5},{8,6},{9,7},{10,8},{11,9},{12,... | collective-permute-start | bytes 491528 | tf_op jit(solution)/shard_map/ppermute | solution.py:18
  8.5 2.4 %copy-start.5 = (s32[96]{0:T(128)S(1)}, s32[96]{0:T(128)}, u32[]{:S(2)}) copy-start(s32[96]{0:T(128)} %param.8) | copy-start | bytes 1156
  8.5 2.5 %copy-start.1 = (f32[96,3,129]{0,2,1:T(8,128)S(1)}, f32[96,3,129]{0,2,1:T(8,128)}, u32[]{:S(2)}) copy-start(f32[96,3,129]{0,2,1:T(8,128)} %param.6) | copy-start | bytes 445828
  8.6 2.5 %copy-start.2 = (s32[96,3,129]{0,2,1:T(8,128)S(1)}, s32[96,3,129]{0,2,1:T(8,128)}, u32[]{:S(2)}) copy-start(s32[96,3,129]{0,2,1:T(8,128)} %param.7) | copy-start | bytes 445828
  10.0 21.2 %collective-permute-start.1 = (bf16[1856,256]{1,0:T(8,128)(2,1)}, bf16[1856,256]{1,0:T(8,128)(2,1)}, u32[]{:S(2)}, u32[]{:S(2)}) collective-permute-start(bf16[1856,256]{1,0:T(8,128)(2,1)} %get-tuple-element.14), channel_id=1, source_target_pairs={{31,0},{0,1},{1,2},{2,3},{3,4},{4,5},{5,6},{6,7},{7,8},{8,9},{9,10... | collective-permute-start | bytes 2850824 | tf_op jit(solution)/shard_map/ppermute | solution.py:18
  10.0 25.2 %collective-permute-start.2 = (bf16[1856,256]{1,0:T(8,128)(2,1)}, bf16[1856,256]{1,0:T(8,128)(2,1)}, u32[]{:S(2)}, u32[]{:S(2)}) collective-permute-start(bf16[1856,256]{1,0:T(8,128)(2,1)} %get-tuple-element.13), channel_id=1, source_target_pairs={{1,0},{2,1},{3,2},{4,3},{5,4},{6,5},{7,6},{8,7},{9,8},{10,9},{11,1... | collective-permute-start | bytes 2850824 | tf_op jit(solution)/shard_map/ppermute | solution.py:18
  35.9 10.8 %collective-permute-start.4 = (bf16[1,64,256]{2,1,0:T(8,128)(2,1)S(1)}, bf16[1,64,256]{2,1,0:T(8,128)(2,1)S(1)}, u32[]{:S(2)}, u32[]{:S(2)}) collective-permute-start(bf16[1,64,256]{2,1,0:T(8,128)(2,1)S(1)} %pad_maximum_fusion.2), channel_id=1, source_target_pairs={{0,32},{32,64},{64,96},{96,128},{128,160},{160,192},{192,224},{1,3... | collective-permute-start | bytes 98312 | tf_op jit(solution)/shard_map/ppermute | solution.py:208
  39.1 7.6 %collective-permute-start.5 = (bf16[1,64,256]{2,1,0:T(8,128)(2,1)S(1)}, bf16[1,64,256]{2,1,0:T(8,128)(2,1)S(1)}, u32[]{:S(2)}, u32[]{:S(2)}) collective-permute-start(bf16[1,64,256]{2,1,0:T(8,128)(2,1)S(1)} %pad_maximum_fusion.3), channel_id=1, source_target_pairs={{32,0},{64,32},{96,64},{128,96},{160,128},{192,160},{224,192},{33,... | collective-permute-start | bytes 98312 | tf_op jit(solution)/shard_map/ppermute | solution.py:209
  46.7 0.6 copy-start.3
  47.3 0.6 copy-start.4

commit v7 on v6

--- a/solution.py
+++ b/solution.py
@@ -75,29 +75,31 @@
     step = pl.program_id(0)
     base = step * rows
 
-    def put(k, row):
-        ext_scr[k, :halo] = west_ref[pl.ds(pl.multiple_of(row * halo, halo), halo)]
-        ext_scr[k, halo : halo + columns] = all_ref[row]
-        ext_scr[k, halo + columns :] = east_ref[pl.ds(pl.multiple_of(row * halo, halo), halo)]
-
+    def sides(k, row):
+        start = pl.multiple_of((row + 1) * halo, halo)
+        ext_scr[k, :halo] = west_ref[pl.ds(start, halo)]
+        ext_scr[k, halo + columns :] = east_ref[pl.ds(start, halo)]
+
+    for k in range(rows + 2):
+        sides(k, base + k - 1)
     for k in range(1, rows + 1):
-        put(k, base + k - 1)
+        ext_scr[k, halo : halo + columns] = all_ref[base + k - 1]
 
     @pl.when(step == 0)
     def _():
-        ext_scr[0] = north_ref[0]
+        ext_scr[0, halo : halo + columns] = north_ref[0]
 
     @pl.when(step > 0)
     def _():
-        put(0, base - 1)
+        ext_scr[0, halo : halo + columns] = all_ref[jnp.maximum(base - 1, 0)]
 
     @pl.when(step == pl.num_programs(0) - 1)
     def _():
-        ext_scr[rows + 1] = south_ref[0]
+        ext_scr[rows + 1, halo : halo + columns] = south_ref[0]
 
     @pl.when(step < pl.num_programs(0) - 1)
     def _():
-        put(rows + 1, jnp.minimum(base + rows, lat_rows - 1))
+        ext_scr[rows + 1, halo : halo + columns] = all_ref[jnp.minimum(base + rows, lat_rows - 1)]
 
     ext_scr[rows + 2] = jnp.zeros(ext_scr.shape[1:], ext_scr.dtype)
     conv_block(ext_scr, src_ref, f_ref, w_ref, o_ref, conv_scr, 0)
@@ -120,7 +122,7 @@
 def near_call(scalars, sources, features, west, east, north, south, mix_weight):
     lat_rows, columns, channels = features.shape
     count = mix_weight.shape[0]
-    halo = (north.shape[1] - columns) // 2
+    halo = NEAR
     row_map = lambda i, s: (i, 0, 0)
     grid_spec = pltpu.PrefetchScalarGridSpec(
         num_scalar_prefetch=1,
@@ -183,11 +185,17 @@
     window = lax.dynamic_slice_in_dim(
         jnp.concatenate([zero_row, features, zero_row], axis=0), start, POLAR + 2, 0)
     flat_window = window.reshape(-1, channels)
-    near_count = lat_rows * NEAR
+    count_lat = lax.axis_size("lat")
+    up = [(i, i + 1) for i in range(count_lat - 1)]
+    down = [(j, i) for i, j in up]
+    north = lax.ppermute(features[lat_rows - 1 :], "lat", up)
+    south = lax.ppermute(features[:1], "lat", down)
+    padded = jnp.concatenate([north, features, south], axis=0)
+    near_count = (lat_rows + 2) * NEAR
     from_west = shifted(jnp.concatenate(
-        [features[:, columns - NEAR :].reshape(-1, channels), flat_window]), "lon", 1)
+        [padded[:, columns - NEAR :].reshape(-1, channels), flat_window]), "lon", 1)
     from_east = shifted(jnp.concatenate(
-        [features[:, :NEAR].reshape(-1, channels), flat_window]), "lon", -1)
+        [padded[:, :NEAR].reshape(-1, channels), flat_window]), "lon", -1)
     west_far = [shifted(window, "lon", hop) for hop in range(hops, 1, -1)]
     east_far = [shifted(window, "lon", -hop) for hop in range(2, hops + 1)]
 
@@ -197,16 +205,6 @@
     polar_values = lax.dynamic_slice_in_dim(basis_values, start, POLAR, 0)
     wide_sources = flat_sources(polar_values, columns + 2 * reach, 512)
 
-    def edge(row):
-        return jnp.concatenate(
-            [from_west[row * NEAR : (row + 1) * NEAR][None], features[row : row + 1],
-             from_east[row * NEAR : (row + 1) * NEAR][None]], axis=1)
-
-    count_lat = lax.axis_size("lat")
-    up = [(i, i + 1) for i in range(count_lat - 1)]
-    down = [(j, i) for i, j in up]
-    north = lax.ppermute(edge(lat_rows - 1), "lat", up)
-    south = lax.ppermute(edge(0), "lat", down)
     out = near_call(scalars, near_sources, features, from_west, from_east, north, south,
                     mix_weight)
 

time: 73.3 us -> 77.5 us (1.057)
  waiting for transfers between devices: 15.2 us -> 18.5 us
  other arithmetic: 3.7 us -> 5.29 us
  local copies, waits for them, and re-layouts: 12.8 us -> 11.7 us
  starting transfers between devices: 16 us -> 17 us
    ppermute x2, waiting for transfers between devices: 0.01 us -> 4.66 us  [the longest x1 4.65 us: body(): north = lax.ppermute(features[lat_rows - 1:], 'lat', up)]
    broadcast_in_dim x2 -> x0, local copies, waits for them, and re-layouts: 1.43 us -> none  [the longest x1 0.72 us: edge(): from_east[row * NEAR:(row + 1) * NEAR][None]]
    ppermute x4, waiting for transfers between devices: 15.2 us -> 13.8 us  [shifted(): return lax.ppermute(block, axis, route)]
    ppermute x4, starting transfers between devices: 8.26 us -> 9.6 us  [shifted(): return lax.ppermute(block, axis, route)]
    reshape x2, local copies, waits for them, and re-layouts: 1.65 us -> 2.92 us  [flat_sources(): flat = flat.reshape(rows, count, offsets * span)]
    dynamic_slice x1, local copies, waits for them, and re-layouts: 1.27 us -> 0.33 us  [body(): polar_values = lax.dynamic_slice_in_dim(basis_values, start, POLAR, 0)]
    concatenate x3 -> x1, other arithmetic: 1.4 us -> 2.34 us  [body(): jnp.concatenate([padded[:, :NEAR].reshape(-1, channels), flat_window])]
    concatenate x1, local copies, waits for them, and re-layouts: 0.01 us -> 0.93 us  [body(): jnp.concatenate(west_far + [west_one, window, east_one] + east_far, axis=1)]
  transfers between devices with their start and end apart: 6 -> 6, of which waited for: 2 -> 3; matrix products, arithmetic and copies ran while one was open for 20% -> 17% of each run, Pallas kernels for 0% -> 0%
where the time goes in v7:
time: 77.5 us; the launch traced here: 77.2 us
  Pallas kernels  24.4 us (31%)
  waiting for transfers between devices  18.5 us (24%)
  starting transfers between devices  17 us (22%)
  local copies, waits for them, and re-layouts  11.7 us (15%)
  other arithmetic  5.29 us (7%)
    pallas_call x1, Pallas kernels, near_call(): pl.pallas_call(near_kernel, grid_spec=grid_spec, out_shape=jax.ShapeDtype...  21.5 us
    ppermute x4, waiting for transfers between devices, shifted(): return lax.ppermute(block, axis, route)  13.8 us
    ppermute x4, starting transfers between devices, shifted(): return lax.ppermute(block, axis, route)  9.6 us
    ppermute x1, starting transfers between devices, body(): south = lax.ppermute(features[:1], 'lat', down)  5.5 us
    ppermute x1, waiting for transfers between devices, body(): north = lax.ppermute(features[lat_rows - 1:], 'lat', up)  4.65 us
    pallas_call x1, Pallas kernels, wide_call(): pl.pallas_call(wide_kernel, grid_spec=grid_spec, out_shape=jax.ShapeDtype...  2.97 us
    reshape x2, local copies, waits for them, and re-layouts, flat_sources(): flat = flat.reshape(rows, count, offsets * span)  2.92 us
    concatenate x1, other arithmetic, body(): jnp.concatenate([padded[:, :NEAR].reshape(-1, channels), flat_window])  2.34 us
  transfers between devices with their start and end apart: 6, of which 3 were waited for; matrix products, arithmetic and copies ran while one was open for 17% of the time, Pallas kernels for 0%

profile of v7, /device:TPU:3, one launch (start us, length us, event | category | flops | bytes accessed | tf_op | source)
XLA Modules:
  0.0 77.2 jit_solution(12591267300177784075)
XLA Ops:
  0.0 0.0 copy-start
  0.0 1.7 %fusion.2 = bf16[10,32,256]{2,1,0:T(8,128)(2,1)} fusion(s32[]{:T(128)} %select_n.10, bf16[1,32,256]{2,1,0:T(8,128)(2,1)S(1)} %broadcast_in_dim.10, bf16[96,32,256]{2,1,0:T(8,128)(2,1)} %f_ref.3), kind=kLoop, calls=%fused_computation.9 | loop fusion | flops 163840 | bytes 1753092 | tf_op jit(solution)/shard_map/concatenate | solution.py:186
  1.7 1.8 %collective-permute-start = (bf16[10,32,256]{2,1,0:T(8,128)(2,1)}, bf16[10,32,256]{2,1,0:T(8,128)(2,1)}, u32[]{:S(2)}, u32[]{:S(2)}) collective-permute-start(bf16[10,32,256]{2,1,0:T(8,128)(2,1)} %fusion.2), channel_id=1, source_target_pairs={{30,0},{31,1},{0,2},{1,3},{2,4},{3,5},{4,6},{5,7},{6,8},{7,9},{8,1... | collective-permute-start | bytes 491528 | tf_op jit(solution)/shard_map/ppermute | solution.py:18
  3.6 5.3 %collective-permute-start.5 = (bf16[10,32,256]{2,1,0:T(8,128)(2,1)}, bf16[10,32,256]{2,1,0:T(8,128)(2,1)}, u32[]{:S(2)}, u32[]{:S(2)}) collective-permute-start(bf16[10,32,256]{2,1,0:T(8,128)(2,1)} %fusion.2), channel_id=1, source_target_pairs={{2,0},{3,1},{4,2},{5,3},{6,4},{7,5},{8,6},{9,7},{10,8},{11,9},{12,... | collective-permute-start | bytes 491528 | tf_op jit(solution)/shard_map/ppermute | solution.py:18
  8.9 0.0 copy-done
  8.9 5.5 %collective-permute-start.2 = (bf16[1,32,256]{2,1,0:T(8,128)(2,1)S(1)}, bf16[1,32,256]{2,1,0:T(8,128)(2,1)S(1)}, u32[]{:S(2)}, u32[]{:S(2)}) collective-permute-start(bf16[1,32,256]{2,1,0:T(8,128)(2,1)S(1)} %get-tuple-element.7), channel_id=1, source_target_pairs={{32,0},{64,32},{96,64},{128,96},{160,128},{192,160},{224,192},{33,... | collective-permute-start | bytes 49160 | tf_op jit(solution)/shard_map/ppermute | solution.py:192
  14.4 1.9 %collective-permute-start.1 = (bf16[1,32,256]{2,1,0:T(8,128)(2,1)S(1)}, bf16[1,32,256]{2,1,0:T(8,128)(2,1)S(1)}, u32[]{:S(2)}, u32[]{:S(2)}) collective-permute-start(bf16[1,32,256]{2,1,0:T(8,128)(2,1)S(1)} %get-tuple-element.8), channel_id=1, source_target_pairs={{0,32},{32,64},{64,96},{96,128},{128,160},{160,192},{192,224},{1,3... | collective-permute-start | bytes 49160 | tf_op jit(solution)/shard_map/ppermute | solution.py:191
  16.3 4.7 %collective-permute-done.1.north_ref = bf16[1,32,256]{2,1,0:T(8,128)(2,1)S(1)} collective-permute-done((bf16[1,32,256]{2,1,0:T(8,128)(2,1)S(1)}, bf16[1,32,256]{2,1,0:T(8,128)(2,1)S(1)}, u32[]{:S(2)}, u32[]{:S(2)}) %collective-permute-start.1) | collective-permute-done | bytes 16416 | tf_op jit(solution)/shard_map/ppermute | solution.py:191
  21.0 0.0 copy-start.5
  21.0 0.1 constant_dynamic-update-slice_fusion.1
  21.1 0.0 collective-permute-done.2.south_ref
  21.1 0.0 copy-start.4
  21.2 0.4 copy-done.5
  21.6 0.1 fusion.3
  21.7 0.0 copy-done.4
  21.7 0.0 copy-start.6
  21.7 0.0 copy-start.2
  21.8 0.0 copy-start.3
  21.8 2.3 %pad_maximum_fusion = (bf16[1888,256]{1,0:T(8,128)(2,1)}, bf16[1888,256]{1,0:T(8,128)(2,1)}) fusion(bf16[320,256]{1,0:T(8,128)(2,1)} %bitcast.3, bf16[1568,256]{1,0:T(8,128)(2,1)S(1)} %bitcast.10, bf16[1568,256]{1,0:T(8,128)(2,1)S(1)} %bitcast.11), kind=kLoop, calls=%fused_computation.6 | loop fusion | flops 3383296 | bytes 3702784 | tf_op jit(solution)/shard_map/concatenate | solution.py:197
  24.1 0.0 collective-permute-start.3
  24.1 0.0 copy-done.6
  24.1 0.1 broadcast_compare_fusion
  24.2 2.5 %collective-permute-start.4 = (bf16[1888,256]{1,0:T(8,128)(2,1)}, bf16[1888,256]{1,0:T(8,128)(2,1)}, u32[]{:S(2)}, u32[]{:S(2)}) collective-permute-start(bf16[1888,256]{1,0:T(8,128)(2,1)} %get-tuple-element.9), channel_id=1, source_target_pairs={{1,0},{2,1},{3,2},{4,3},{5,4},{6,5},{7,6},{8,7},{9,8},{10,9},{11,1... | collective-permute-start | bytes 2899976 | tf_op jit(solution)/shard_map/ppermute | solution.py:18
  26.7 0.0 copy-done.2
  26.7 0.0 copy-done.3
  26.7 0.4 multiply_convert_fusion
  27.1 0.0 copy-start.1
  27.1 0.3 constant_dynamic-slice_fusion
  27.5 1.2 %pad.21 = bf16[8,9,3,160]{0,3,2,1:T(8,128)(2,1)} pad(bf16[8,9,3,129]{0,3,2,1:T(8,128)(2,1)S(1)} %constant_dynamic-slice_fusion, bf16[]{:T(256)} %constant.8.clone.1), padding=0_0x0_0x0_0x0_31 | pad | bytes 124850 | tf_op jit(solution)/shard_map/jit(_pad)/pad | solution.py:43
  28.7 0.0 copy-done.1
  28.7 0.0 slice-start
  28.7 1.9 %copy.10 = bf16[8,9,480]{2,1,0:T(8,128)(2,1)S(1)} copy(bf16[8,9,480]{0,2,1:T(8,128)(2,1)} %bitcast.9) | data formatting | bytes 138240 | tf_op jit(solution)/shard_map/reshape | solution.py:44
  30.6 0.7 pad.22.src_ref
  31.3 0.0 slice-done
  31.3 0.1 pad.23
  31.4 1.0 %copy.11 = bf16[96,9,192]{2,1,0:T(8,128)(2,1)S(1)} copy(bf16[96,9,192]{0,2,1:T(8,128)(2,1)S(1)} %bitcast.12) | data formatting | bytes 663552 | tf_op jit(solution)/shard_map/reshape | solution.py:44
  32.4 1.0 %pad.24.src_ref = bf16[96,9,256]{2,1,0:T(8,128)(2,1)} pad(bf16[96,9,192]{2,1,0:T(8,128)(2,1)S(1)} %copy.11, bf16[]{:T(256)} %constant.8.clone.1), padding=0_0x0_0x0_64 | pad | bytes 774146 | tf_op jit(solution)/shard_map/jit(_pad)/pad | solution.py:45
  33.4 0.6 pad_add_fusion.scalar_ref
  34.1 0.0 collective-permute-done
  34.1 0.9 %constant_dynamic-update-slice_fusion.7 = bf16[10,160,256]{2,1,0:T(8,128)(2,1)S(1)} fusion(bf16[10,32,256]{2,1,0:T(8,128)(2,1)} %collective-permute-done), kind=kLoop, calls=%fused_computation.18 | loop fusion | bytes 327680
  35.0 10.7 %collective-permute-done.3.west_ref = bf16[1888,256]{1,0:T(8,128)(2,1)} collective-permute-done((bf16[1888,256]{1,0:T(8,128)(2,1)}, bf16[1888,256]{1,0:T(8,128)(2,1)}, u32[]{:S(2)}, u32[]{:S(2)}) %collective-permute-start.3) | collective-permute-done | bytes 966688 | tf_op jit(solution)/shard_map/ppermute | solution.py:18
  45.7 0.9 %slice.29 = bf16[320,256]{1,0:T(8,128)(2,1)S(1)} slice(bf16[1888,256]{1,0:T(8,128)(2,1)} %collective-permute-done.3.west_ref), slice={[1568:1888], [0:256]} | slice | bytes 327680 | tf_op jit(solution)/shard_map/slice | solution.py:211
  46.6 0.1 constant_dynamic-update-slice_fusion.5
  46.7 3.1 %collective-permute-done.4.east_ref = bf16[1888,256]{1,0:T(8,128)(2,1)} collective-permute-done((bf16[1888,256]{1,0:T(8,128)(2,1)}, bf16[1888,256]{1,0:T(8,128)(2,1)}, u32[]{:S(2)}, u32[]{:S(2)}) %collective-permute-start.4) | collective-permute-done | bytes 966688 | tf_op jit(solution)/shard_map/ppermute | solution.py:18
  49.8 0.9 %slice.31 = bf16[320,256]{1,0:T(8,128)(2,1)S(1)} slice(bf16[1888,256]{1,0:T(8,128)(2,1)} %collective-permute-done.4.east_ref), slice={[1568:1888], [0:256]} | slice | bytes 327680 | tf_op jit(solution)/shard_map/slice | solution.py:212
  50.8 0.0 collective-permute-done.5
  50.8 0.9 %constant_dynamic-update-slice_fusion.3 = bf16[10,160,256]{2,1,0:T(8,128)(2,1)S(1)} fusion(bf16[10,160,256]{2,1,0:T(8,128)(2,1)S(1)} %constant_dynamic-update-slice_fusion.4, bf16[10,32,256]{2,1,0:T(8,128)(2,1)} %collective-permute-done.5), kind=kLoop, calls=%fused_computation.14 | loop fusion | bytes 327680 | tf_op jit(solution)/shard_map/concatenate | solution.py:213
  51.7 1.0 %pad.20.ext_ref = bf16[11,160,256]{2,1,0:T(8,128)(2,1)} pad(bf16[10,160,256]{2,1,0:T(8,128)(2,1)S(1)} %constant_dynamic-update-slice_fusion.3, bf16[]{:T(256)} %constant.8.clone.1), padding=0_1x0_0x0_0 | pad | bytes 1720322 | tf_op jit(solution)/shard_map/jit(_pad)/pad | solution.py:215
  52.7 21.5 %shard_map.55.prev_ref = bf16[96,32,256]{2,1,0:T(8,128)(2,1)} custom-call(s32[2]{0:T(128)} %pad_add_fusion.scalar_ref, bf16[96,9,256]{2,1,0:T(8,128)(2,1)} %pad.24.src_ref, bf16[96,32,256]{2,1,0:T(8,128)(2,1)} %f_ref.3, bf16[96,32,256]{2,1,0:T(8,128)(2,1)} %f_ref.3, bf16[1888,256]{1,0:T(8,128)(2,1)} %collective-permute-done.3.west_ref, ...), custom_call_target="tpu_custom_call" | custom-call | tf_op jit(solution)/shard_map/pallas_call | solution.py:142
  74.2 3.0 %shard_map.56 = bf16[96,32,256]{2,1,0:T(8,128)(2,1)} custom-call(s32[2]{0:T(128)} %pad_add_fusion.scalar_ref, bf16[11,160,256]{2,1,0:T(8,128)(2,1)} %pad.20.ext_ref, bf16[8,9,512]{2,1,0:T(8,128)(2,1)} %pad.22.src_ref, bf16[96,32,256]{2,1,0:T(8,128)(2,1)} %f_ref.3, bf16[9,256,256]{2,1,0:T(8,128)(2,1)} %w_ref.3, ...), custom_call_target="tpu_custom_call", output_to_operand_aliasing={{}: (5, {})} | custom-call | tf_op jit(solution)/shard_map/pallas_call | solution.py:165
  (8 shorter events, 0.1 us)
Async XLA Ops:
  0.0 8.9 %copy-start = (bf16[96,32,256]{2,1,0:T(8,128)(2,1)S(1)}, bf16[96,32,256]{2,1,0:T(8,128)(2,1)}, u32[]{:S(2)}) copy-start(bf16[96,32,256]{2,1,0:T(8,128)(2,1)} %f_ref.3) | copy-start | bytes 4718596
  1.7 32.3 %collective-permute-start = (bf16[10,32,256]{2,1,0:T(8,128)(2,1)}, bf16[10,32,256]{2,1,0:T(8,128)(2,1)}, u32[]{:S(2)}, u32[]{:S(2)}) collective-permute-start(bf16[10,32,256]{2,1,0:T(8,128)(2,1)} %fusion.2), channel_id=1, source_target_pairs={{30,0},{31,1},{0,2},{1,3},{2,4},{3,5},{4,6},{5,7},{6,8},{7,9},{8,1... | collective-permute-start | bytes 491528 | tf_op jit(solution)/shard_map/ppermute | solution.py:18
  3.6 47.2 %collective-permute-start.5 = (bf16[10,32,256]{2,1,0:T(8,128)(2,1)}, bf16[10,32,256]{2,1,0:T(8,128)(2,1)}, u32[]{:S(2)}, u32[]{:S(2)}) collective-permute-start(bf16[10,32,256]{2,1,0:T(8,128)(2,1)} %fusion.2), channel_id=1, source_target_pairs={{2,0},{3,1},{4,2},{5,3},{6,4},{7,5},{8,6},{9,7},{10,8},{11,9},{12,... | collective-permute-start | bytes 491528 | tf_op jit(solution)/shard_map/ppermute | solution.py:18
  8.9 12.2 %collective-permute-start.2 = (bf16[1,32,256]{2,1,0:T(8,128)(2,1)S(1)}, bf16[1,32,256]{2,1,0:T(8,128)(2,1)S(1)}, u32[]{:S(2)}, u32[]{:S(2)}) collective-permute-start(bf16[1,32,256]{2,1,0:T(8,128)(2,1)S(1)} %get-tuple-element.7), channel_id=1, source_target_pairs={{32,0},{64,32},{96,64},{128,96},{160,128},{192,160},{224,192},{33,... | collective-permute-start | bytes 49160 | tf_op jit(solution)/shard_map/ppermute | solution.py:192
  14.4 6.6 %collective-permute-start.1 = (bf16[1,32,256]{2,1,0:T(8,128)(2,1)S(1)}, bf16[1,32,256]{2,1,0:T(8,128)(2,1)S(1)}, u32[]{:S(2)}, u32[]{:S(2)}) collective-permute-start(bf16[1,32,256]{2,1,0:T(8,128)(2,1)S(1)} %get-tuple-element.8), channel_id=1, source_target_pairs={{0,32},{32,64},{64,96},{96,128},{128,160},{160,192},{192,224},{1,3... | collective-permute-start | bytes 49160 | tf_op jit(solution)/shard_map/ppermute | solution.py:191
  21.0 0.6 copy-start.5
  21.1 0.6 copy-start.4
  21.7 2.4 %copy-start.6 = (s32[96]{0:T(128)S(1)}, s32[96]{0:T(128)}, u32[]{:S(2)}) copy-start(s32[96]{0:T(128)} %param.8) | copy-start | bytes 1156
  21.7 4.9 %copy-start.2 = (f32[96,3,129]{0,2,1:T(8,128)S(1)}, f32[96,3,129]{0,2,1:T(8,128)}, u32[]{:S(2)}) copy-start(f32[96,3,129]{0,2,1:T(8,128)} %param.6) | copy-start | bytes 445828
  21.8 4.9 %copy-start.3 = (s32[96,3,129]{0,2,1:T(8,128)S(1)}, s32[96,3,129]{0,2,1:T(8,128)}, u32[]{:S(2)}) copy-start(s32[96,3,129]{0,2,1:T(8,128)} %param.7) | copy-start | bytes 445828
  24.1 21.5 %collective-permute-start.3 = (bf16[1888,256]{1,0:T(8,128)(2,1)}, bf16[1888,256]{1,0:T(8,128)(2,1)}, u32[]{:S(2)}, u32[]{:S(2)}) collective-permute-start(bf16[1888,256]{1,0:T(8,128)(2,1)} %get-tuple-element.10), channel_id=1, source_target_pairs={{31,0},{0,1},{1,2},{2,3},{3,4},{4,5},{5,6},{6,7},{7,8},{8,9},{9,10... | collective-permute-start | bytes 2899976 | tf_op jit(solution)/shard_map/ppermute | solution.py:18
  24.2 25.6 %collective-permute-start.4 = (bf16[1888,256]{1,0:T(8,128)(2,1)}, bf16[1888,256]{1,0:T(8,128)(2,1)}, u32[]{:S(2)}, u32[]{:S(2)}) collective-permute-start(bf16[1888,256]{1,0:T(8,128)(2,1)} %get-tuple-element.9), channel_id=1, source_target_pairs={{1,0},{2,1},{3,2},{4,3},{5,4},{6,5},{7,6},{8,7},{9,8},{10,9},{11,1... | collective-permute-start | bytes 2899976 | tf_op jit(solution)/shard_map/ppermute | solution.py:18
  27.1 1.6 %copy-start.1 = (bf16[96,9,3,129]{0,3,2,1:T(8,128)(2,1)}, bf16[96,9,3,129]{0,3,2,1:T(8,128)(2,1)S(1)}, u32[]{:S(2)}) copy-start(bf16[96,9,3,129]{0,3,2,1:T(8,128)(2,1)S(1)} %multiply_convert_fusion) | copy-start | bytes 2006212
  28.7 2.6 %slice-start = ((bf16[96,9,3,129]{0,3,2,1:T(8,128)(2,1)}), bf16[96,9,3,33]{0,3,2,1:T(8,128)(2,1)S(1)}, s32[]{:S(2)}) async-start(bf16[96,9,3,129]{0,3,2,1:T(8,128)(2,1)} %copy-done.1), calls=%async_computation | async-start | bytes 552960 | tf_op jit(solution)/shard_map/slice | solution.py:204

commit v8 on v6

--- a/solution.py
+++ b/solution.py
@@ -10,6 +10,7 @@
 POLAR = 8
 NEAR = 16
 BLOCK = 8
+NEAR_BLOCK = 16
 
 
 def shifted(block, axis, distance):
@@ -124,17 +125,17 @@
     row_map = lambda i, s: (i, 0, 0)
     grid_spec = pltpu.PrefetchScalarGridSpec(
         num_scalar_prefetch=1,
-        grid=(lat_rows // BLOCK,),
+        grid=(lat_rows // NEAR_BLOCK,),
         in_specs=[
-            pl.BlockSpec((BLOCK,) + sources.shape[1:], row_map),
-            pl.BlockSpec((BLOCK, columns, channels), row_map),
+            pl.BlockSpec((NEAR_BLOCK,) + sources.shape[1:], row_map),
+            pl.BlockSpec((NEAR_BLOCK, columns, channels), row_map),
             full_spec(features.shape), full_spec(west.shape), full_spec(east.shape),
             full_spec(north.shape), full_spec(south.shape), full_spec(mix_weight.shape),
         ],
-        out_specs=pl.BlockSpec((BLOCK, columns, channels), row_map),
+        out_specs=pl.BlockSpec((NEAR_BLOCK, columns, channels), row_map),
         scratch_shapes=[
-            pltpu.VMEM((BLOCK + 3, columns + 2 * halo, channels), features.dtype),
-            pltpu.VMEM((count, BLOCK * columns, channels), jnp.bfloat16),
+            pltpu.VMEM((NEAR_BLOCK + 3, columns + 2 * halo, channels), features.dtype),
+            pltpu.VMEM((count, NEAR_BLOCK * columns, channels), jnp.bfloat16),
         ],
     )
     return pl.pallas_call(

time: 73.3 us -> 65 us (0.89)
  Pallas kernels: 24.4 us -> 16 us
    pallas_call x1, Pallas kernels: 21.4 us -> 13.1 us  [near_call(): pl.pallas_call(near_kernel, grid_spec=grid_spec, out_shape=jax.ShapeDtype...]
  transfers between devices with their start and end apart: 6 -> 6, of which waited for: 2 -> 2; matrix products, arithmetic and copies ran while one was open for 20% -> 22% of each run, Pallas kernels for 0% -> 0%
where the time goes in v8:
time: 65 us; the launch traced here: 63.9 us
  starting transfers between devices  16 us (25%)
  Pallas kernels  16 us (25%)
  waiting for transfers between devices  15.2 us (23%)
  local copies, waits for them, and re-layouts  12.8 us (20%)
  other arithmetic  3.7 us (6%)
    ppermute x4, waiting for transfers between devices, shifted(): return lax.ppermute(block, axis, route)  15.2 us
    pallas_call x1, Pallas kernels, near_call(): pl.pallas_call(near_kernel, grid_spec=grid_spec, out_shape=jax.ShapeDtype...  13.1 us
    ppermute x4, starting transfers between devices, shifted(): return lax.ppermute(block, axis, route)  8.26 us
    ppermute x1, starting transfers between devices, body(): south = lax.ppermute(edge(0), 'lat', down)  4.58 us
    ppermute x1, starting transfers between devices, body(): north = lax.ppermute(edge(lat_rows - 1), 'lat', up)  3.19 us
    pallas_call x1, Pallas kernels, wide_call(): pl.pallas_call(wide_kernel, grid_spec=grid_spec, out_shape=jax.ShapeDtype...  2.97 us
    unnamed x15, local copies, waits for them, and re-layouts  2.17 us
    pad x2, local copies, waits for them, and re-layouts, flat_sources(): return jnp.pad(flat, ((0, 0), (0, 0), (0, lanes - offsets * span)))  1.75 us
  transfers between devices with their start and end apart: 6, of which 2 were waited for; matrix products, arithmetic and copies ran while one was open for 22% of the time, Pallas kernels for 0%

profile of v8, /device:TPU:3, one launch (start us, length us, event | category | flops | bytes accessed | tf_op | source)
XLA Modules:
  0.0 63.9 jit_solution(15916129984522913931)
XLA Ops:
  0.0 0.0 copy-start
  0.0 1.1 %fusion.2 = bf16[10,32,256]{2,1,0:T(8,128)(2,1)S(1)} fusion(s32[]{:T(128)} %select_n.10, bf16[1,32,256]{2,1,0:T(8,128)(2,1)S(1)} %broadcast_in_dim.34, bf16[96,32,256]{2,1,0:T(8,128)(2,1)} %f_ref.3), kind=kLoop, calls=%fused_computation.9 | loop fusion | flops 163840 | bytes 1753092 | tf_op jit(solution)/shard_map/concatenate | solution.py:185
  1.1 1.9 %collective-permute-start = (bf16[10,32,256]{2,1,0:T(8,128)(2,1)S(1)}, bf16[10,32,256]{2,1,0:T(8,128)(2,1)}, u32[]{:S(2)}, u32[]{:S(2)}) collective-permute-start(bf16[10,32,256]{2,1,0:T(8,128)(2,1)S(1)} %fusion.2), channel_id=1, source_target_pairs={{30,0},{31,1},{0,2},{1,3},{2,4},{3,5},{4,6},{5,7},{6,8},{7,9},{8,1... | collective-permute-start | bytes 491528 | tf_op jit(solution)/shard_map/ppermute | solution.py:19
  3.0 5.4 %collective-permute-start.3 = (bf16[10,32,256]{2,1,0:T(8,128)(2,1)S(1)}, bf16[10,32,256]{2,1,0:T(8,128)(2,1)S(1)}, u32[]{:S(2)}, u32[]{:S(2)}) collective-permute-start(bf16[10,32,256]{2,1,0:T(8,128)(2,1)S(1)} %fusion.2), channel_id=1, source_target_pairs={{2,0},{3,1},{4,2},{5,3},{6,4},{7,5},{8,6},{9,7},{10,8},{11,9},{12,... | collective-permute-start | bytes 491528 | tf_op jit(solution)/shard_map/ppermute | solution.py:19
  8.4 0.0 copy-done
  8.4 0.1 fusion.4
  8.5 0.0 copy-start.5
  8.5 0.0 copy-start.1
  8.6 0.0 copy-start.2
  8.6 1.4 %pad_maximum_fusion = (bf16[1856,256]{1,0:T(8,128)(2,1)}, bf16[1856,256]{1,0:T(8,128)(2,1)}) fusion(bf16[320,256]{1,0:T(8,128)(2,1)S(1)} %bitcast.21, bf16[1536,256]{1,0:T(8,128)(2,1)S(1)} %bitcast.18, bf16[1536,256]{1,0:T(8,128)(2,1)S(1)} %bitcast.19), kind=kLoop, calls=%fused_computation.6 | loop fusion | flops 3325952 | bytes 3637248 | tf_op jit(solution)/shard_map/concatenate | solution.py:190
  10.0 0.0 collective-permute-start.1
  10.0 1.0 %collective-permute-start.2 = (bf16[1856,256]{1,0:T(8,128)(2,1)}, bf16[1856,256]{1,0:T(8,128)(2,1)}, u32[]{:S(2)}, u32[]{:S(2)}) collective-permute-start(bf16[1856,256]{1,0:T(8,128)(2,1)} %get-tuple-element.13), channel_id=1, source_target_pairs={{1,0},{2,1},{3,2},{4,3},{5,4},{6,5},{7,6},{8,7},{9,8},{10,9},{11,1... | collective-permute-start | bytes 2850824 | tf_op jit(solution)/shard_map/ppermute | solution.py:19
  10.9 0.0 copy-done.5
  10.9 0.1 broadcast_compare_fusion
  11.0 0.0 copy-done.1
  11.0 0.0 copy-done.2
  11.1 0.4 multiply_convert_fusion
  11.5 1.3 %constant_dynamic-slice_fusion = bf16[8,9,3,129]{0,3,2,1:T(8,128)(2,1)} fusion(bf16[96,9,3,129]{0,3,2,1:T(8,128)(2,1)S(1)} %multiply_convert_fusion, s32[]{:T(128)} %select_n.10), kind=kLoop, calls=%fused_computation.23 | loop fusion | bytes 111460 | tf_op jit(solution)/shard_map/dynamic_slice | solution.py:198
  12.8 0.1 pad.23
  12.9 1.0 %copy.11 = bf16[96,9,192]{2,1,0:T(8,128)(2,1)S(1)} copy(bf16[96,9,192]{0,2,1:T(8,128)(2,1)S(1)} %bitcast.20) | data formatting | bytes 663552 | tf_op jit(solution)/shard_map/reshape | solution.py:45
  14.0 1.1 %pad.24.src_ref = bf16[96,9,256]{2,1,0:T(8,128)(2,1)} pad(bf16[96,9,192]{2,1,0:T(8,128)(2,1)S(1)} %copy.11, bf16[]{:T(256)} %constant.8.clone.1), padding=0_0x0_0x0_64 | pad | bytes 774146 | tf_op jit(solution)/shard_map/jit(_pad)/pad | solution.py:46
  15.0 1.4 %pad.21 = bf16[8,9,3,160]{0,3,2,1:T(8,128)(2,1)S(1)} pad(bf16[8,9,3,129]{0,3,2,1:T(8,128)(2,1)} %constant_dynamic-slice_fusion, bf16[]{:T(256)} %constant.8.clone.1), padding=0_0x0_0x0_0x0_31 | pad | bytes 124850 | tf_op jit(solution)/shard_map/jit(_pad)/pad | solution.py:44
  16.4 0.6 copy.10
  17.0 0.7 %pad.22.src_ref = bf16[8,9,512]{2,1,0:T(8,128)(2,1)} pad(bf16[8,9,480]{2,1,0:T(8,128)(2,1)S(1)} %copy.10, bf16[]{:T(256)} %constant.8.clone.1), padding=0_0x0_0x0_32 | pad | bytes 142850 | tf_op jit(solution)/shard_map/jit(_pad)/pad | solution.py:46
  17.7 0.6 pad_add_fusion.scalar_ref
  18.3 0.0 collective-permute-done
  18.3 0.9 %constant_dynamic-update-slice_fusion.4 = bf16[10,160,256]{2,1,0:T(8,128)(2,1)S(1)} fusion(bf16[10,32,256]{2,1,0:T(8,128)(2,1)} %collective-permute-done), kind=kLoop, calls=%fused_computation.17 | loop fusion | bytes 327680
  19.3 11.9 %collective-permute-done.1.west_ref = bf16[1856,256]{1,0:T(8,128)(2,1)} collective-permute-done((bf16[1856,256]{1,0:T(8,128)(2,1)}, bf16[1856,256]{1,0:T(8,128)(2,1)}, u32[]{:S(2)}, u32[]{:S(2)}) %collective-permute-start.1) | collective-permute-done | bytes 950304 | tf_op jit(solution)/shard_map/ppermute | solution.py:19
  31.1 0.7 %slice_bitcast_fusion.1 = (bf16[1,16,256]{2,1,0:T(8,128)(2,1)S(1)}, bf16[1,16,256]{2,1,0:T(8,128)(2,1)S(1)}) fusion(bf16[1856,256]{1,0:T(8,128)(2,1)} %collective-permute-done.1.west_ref), kind=kLoop, calls=%fused_computation.19 | loop fusion | bytes 32768 | tf_op jit(solution)/shard_map/broadcast_in_dim | solution.py:203
  31.9 3.3 %collective-permute-done.2.east_ref = bf16[1856,256]{1,0:T(8,128)(2,1)} collective-permute-done((bf16[1856,256]{1,0:T(8,128)(2,1)}, bf16[1856,256]{1,0:T(8,128)(2,1)}, u32[]{:S(2)}, u32[]{:S(2)}) %collective-permute-start.2) | collective-permute-done | bytes 950304 | tf_op jit(solution)/shard_map/ppermute | solution.py:19
  35.1 0.7 %slice_bitcast_fusion = (bf16[1,16,256]{2,1,0:T(8,128)(2,1)S(1)}, bf16[1,16,256]{2,1,0:T(8,128)(2,1)S(1)}) fusion(bf16[1856,256]{1,0:T(8,128)(2,1)} %collective-permute-done.2.east_ref), kind=kLoop, calls=%fused_computation.18 | loop fusion | bytes 32768 | tf_op jit(solution)/shard_map/broadcast_in_dim | solution.py:204
  35.9 3.2 %collective-permute-start.4 = (bf16[1,64,256]{2,1,0:T(8,128)(2,1)S(1)}, bf16[1,64,256]{2,1,0:T(8,128)(2,1)S(1)}, u32[]{:S(2)}, u32[]{:S(2)}) collective-permute-start(bf16[1,64,256]{2,1,0:T(8,128)(2,1)S(1)} %pad_maximum_fusion.2), channel_id=1, source_target_pairs={{0,32},{32,64},{64,96},{96,128},{128,160},{160,192},{192,224},{1,3... | collective-permute-start | bytes 98312 | tf_op jit(solution)/shard_map/ppermute | solution.py:209
  39.1 4.6 %collective-permute-start.5 = (bf16[1,64,256]{2,1,0:T(8,128)(2,1)S(1)}, bf16[1,64,256]{2,1,0:T(8,128)(2,1)S(1)}, u32[]{:S(2)}, u32[]{:S(2)}) collective-permute-start(bf16[1,64,256]{2,1,0:T(8,128)(2,1)S(1)} %pad_maximum_fusion.3), channel_id=1, source_target_pairs={{32,0},{64,32},{96,64},{128,96},{160,128},{192,160},{224,192},{33,... | collective-permute-start | bytes 98312 | tf_op jit(solution)/shard_map/ppermute | solution.py:210
  43.7 0.9 %slice.44 = bf16[320,256]{1,0:T(8,128)(2,1)S(1)} slice(bf16[1856,256]{1,0:T(8,128)(2,1)} %collective-permute-done.1.west_ref), slice={[1536:1856], [0:256]} | slice | bytes 327680 | tf_op jit(solution)/shard_map/slice | solution.py:214
  44.6 0.1 constant_dynamic-update-slice_fusion.2
  44.7 0.9 %slice.45 = bf16[320,256]{1,0:T(8,128)(2,1)S(1)} slice(bf16[1856,256]{1,0:T(8,128)(2,1)} %collective-permute-done.2.east_ref), slice={[1536:1856], [0:256]} | slice | bytes 327680 | tf_op jit(solution)/shard_map/slice | solution.py:215
  45.6 0.0 collective-permute-done.3
  45.7 1.0 %pad.20.ext_ref = bf16[11,160,256]{2,1,0:T(8,128)(2,1)} pad(bf16[10,160,256]{2,1,0:T(8,128)(2,1)S(1)} %constant_dynamic-update-slice_fusion, bf16[]{:T(256)} %constant.8.clone.1), padding=0_1x0_0x0_0 | pad | bytes 1720322 | tf_op jit(solution)/shard_map/jit(_pad)/pad | solution.py:218
  46.7 0.0 collective-permute-done.4.north_ref
  46.7 0.0 copy-start.3
  46.7 0.0 collective-permute-done.5.south_ref
  46.7 0.6 copy-done.3
  47.3 0.0 copy-start.4
  47.3 0.6 copy-done.4
  47.9 13.1 %shard_map.55.prev_ref = bf16[96,32,256]{2,1,0:T(8,128)(2,1)} custom-call(s32[2]{0:T(128)} %pad_add_fusion.scalar_ref, bf16[96,9,256]{2,1,0:T(8,128)(2,1)} %pad.24.src_ref, bf16[96,32,256]{2,1,0:T(8,128)(2,1)} %f_ref.3, bf16[96,32,256]{2,1,0:T(8,128)(2,1)} %f_ref.3, bf16[1856,256]{1,0:T(8,128)(2,1)} %collective-permute-done.1.west_ref, ...), custom_call_target="tpu_custom_call" | custom-call | tf_op jit(solution)/shard_map/pallas_call | solution.py:141
  61.0 3.0 %shard_map.56 = bf16[96,32,256]{2,1,0:T(8,128)(2,1)} custom-call(s32[2]{0:T(128)} %pad_add_fusion.scalar_ref, bf16[11,160,256]{2,1,0:T(8,128)(2,1)} %pad.20.ext_ref, bf16[8,9,512]{2,1,0:T(8,128)(2,1)} %pad.22.src_ref, bf16[96,32,256]{2,1,0:T(8,128)(2,1)} %f_ref.3, bf16[9,256,256]{2,1,0:T(8,128)(2,1)} %w_ref.3, ...), custom_call_target="tpu_custom_call", output_to_operand_aliasing={{}: (5, {})} | custom-call | tf_op jit(solution)/shard_map/pallas_call | solution.py:164
  (10 shorter events, 0.1 us)
Async XLA Ops:
  0.0 8.4 %copy-start = (bf16[96,32,256]{2,1,0:T(8,128)(2,1)S(1)}, bf16[96,32,256]{2,1,0:T(8,128)(2,1)}, u32[]{:S(2)}) copy-start(bf16[96,32,256]{2,1,0:T(8,128)(2,1)} %f_ref.3) | copy-start | bytes 4718596
  1.1 17.2 %collective-permute-start = (bf16[10,32,256]{2,1,0:T(8,128)(2,1)S(1)}, bf16[10,32,256]{2,1,0:T(8,128)(2,1)}, u32[]{:S(2)}, u32[]{:S(2)}) collective-permute-start(bf16[10,32,256]{2,1,0:T(8,128)(2,1)S(1)} %fusion.2), channel_id=1, source_target_pairs={{30,0},{31,1},{0,2},{1,3},{2,4},{3,5},{4,6},{5,7},{6,8},{7,9},{8,1... | collective-permute-start | bytes 491528 | tf_op jit(solution)/shard_map/ppermute | solution.py:19
  3.0 42.6 %collective-permute-start.3 = (bf16[10,32,256]{2,1,0:T(8,128)(2,1)S(1)}, bf16[10,32,256]{2,1,0:T(8,128)(2,1)S(1)}, u32[]{:S(2)}, u32[]{:S(2)}) collective-permute-start(bf16[10,32,256]{2,1,0:T(8,128)(2,1)S(1)} %fusion.2), channel_id=1, source_target_pairs={{2,0},{3,1},{4,2},{5,3},{6,4},{7,5},{8,6},{9,7},{10,8},{11,9},{12,... | collective-permute-start | bytes 491528 | tf_op jit(solution)/shard_map/ppermute | solution.py:19
  8.5 2.4 %copy-start.5 = (s32[96]{0:T(128)S(1)}, s32[96]{0:T(128)}, u32[]{:S(2)}) copy-start(s32[96]{0:T(128)} %param.8) | copy-start | bytes 1156
  8.5 2.5 %copy-start.1 = (f32[96,3,129]{0,2,1:T(8,128)S(1)}, f32[96,3,129]{0,2,1:T(8,128)}, u32[]{:S(2)}) copy-start(f32[96,3,129]{0,2,1:T(8,128)} %param.6) | copy-start | bytes 445828
  8.6 2.5 %copy-start.2 = (s32[96,3,129]{0,2,1:T(8,128)S(1)}, s32[96,3,129]{0,2,1:T(8,128)}, u32[]{:S(2)}) copy-start(s32[96,3,129]{0,2,1:T(8,128)} %param.7) | copy-start | bytes 445828
  10.0 21.2 %collective-permute-start.1 = (bf16[1856,256]{1,0:T(8,128)(2,1)}, bf16[1856,256]{1,0:T(8,128)(2,1)}, u32[]{:S(2)}, u32[]{:S(2)}) collective-permute-start(bf16[1856,256]{1,0:T(8,128)(2,1)} %get-tuple-element.14), channel_id=1, source_target_pairs={{31,0},{0,1},{1,2},{2,3},{3,4},{4,5},{5,6},{6,7},{7,8},{8,9},{9,10... | collective-permute-start | bytes 2850824 | tf_op jit(solution)/shard_map/ppermute | solution.py:19
  10.0 25.2 %collective-permute-start.2 = (bf16[1856,256]{1,0:T(8,128)(2,1)}, bf16[1856,256]{1,0:T(8,128)(2,1)}, u32[]{:S(2)}, u32[]{:S(2)}) collective-permute-start(bf16[1856,256]{1,0:T(8,128)(2,1)} %get-tuple-element.13), channel_id=1, source_target_pairs={{1,0},{2,1},{3,2},{4,3},{5,4},{6,5},{7,6},{8,7},{9,8},{10,9},{11,1... | collective-permute-start | bytes 2850824 | tf_op jit(solution)/shard_map/ppermute | solution.py:19
  35.9 10.8 %collective-permute-start.4 = (bf16[1,64,256]{2,1,0:T(8,128)(2,1)S(1)}, bf16[1,64,256]{2,1,0:T(8,128)(2,1)S(1)}, u32[]{:S(2)}, u32[]{:S(2)}) collective-permute-start(bf16[1,64,256]{2,1,0:T(8,128)(2,1)S(1)} %pad_maximum_fusion.2), channel_id=1, source_target_pairs={{0,32},{32,64},{64,96},{96,128},{128,160},{160,192},{192,224},{1,3... | collective-permute-start | bytes 98312 | tf_op jit(solution)/shard_map/ppermute | solution.py:209
  39.1 7.6 %collective-permute-start.5 = (bf16[1,64,256]{2,1,0:T(8,128)(2,1)S(1)}, bf16[1,64,256]{2,1,0:T(8,128)(2,1)S(1)}, u32[]{:S(2)}, u32[]{:S(2)}) collective-permute-start(bf16[1,64,256]{2,1,0:T(8,128)(2,1)S(1)} %pad_maximum_fusion.3), channel_id=1, source_target_pairs={{32,0},{64,32},{96,64},{128,96},{160,128},{192,160},{224,192},{33,... | collective-permute-start | bytes 98312 | tf_op jit(solution)/shard_map/ppermute | solution.py:210
  46.7 0.6 copy-start.3
  47.3 0.6 copy-start.4

commit v9 on v8

--- a/solution.py
+++ b/solution.py
@@ -10,7 +10,7 @@
 POLAR = 8
 NEAR = 16
 BLOCK = 8
-NEAR_BLOCK = 16
+NEAR_BLOCK = 32
 
 
 def shifted(block, axis, distance):

time: 65 us -> 64.3 us (0.989)
  no operation moved by 1% of the time
where the time goes in v9:
time: 64.3 us; the launch traced here: 63.3 us
  starting transfers between devices  16 us (25%)
  Pallas kernels  15.4 us (24%)
  waiting for transfers between devices  15.2 us (24%)
  local copies, waits for them, and re-layouts  12.8 us (20%)
  other arithmetic  3.7 us (6%)
    ppermute x4, waiting for transfers between devices, shifted(): return lax.ppermute(block, axis, route)  15.2 us
    pallas_call x1, Pallas kernels, near_call(): pl.pallas_call(near_kernel, grid_spec=grid_spec, out_shape=jax.ShapeDtype...  12.4 us
    ppermute x4, starting transfers between devices, shifted(): return lax.ppermute(block, axis, route)  8.26 us
    ppermute x1, starting transfers between devices, body(): south = lax.ppermute(edge(0), 'lat', down)  4.58 us
    ppermute x1, starting transfers between devices, body(): north = lax.ppermute(edge(lat_rows - 1), 'lat', up)  3.19 us
    pallas_call x1, Pallas kernels, wide_call(): pl.pallas_call(wide_kernel, grid_spec=grid_spec, out_shape=jax.ShapeDtype...  2.97 us
    unnamed x15, local copies, waits for them, and re-layouts  2.17 us
    pad x2, local copies, waits for them, and re-layouts, flat_sources(): return jnp.pad(flat, ((0, 0), (0, 0), (0, lanes - offsets * span)))  1.75 us
  transfers between devices with their start and end apart: 6, of which 2 were waited for; matrix products, arithmetic and copies ran while one was open for 22% of the time, Pallas kernels for 0%

profile of v9, /device:TPU:3, one launch (start us, length us, event | category | flops | bytes accessed | tf_op | source)
XLA Modules:
  0.0 63.3 jit_solution(4948692889537251937)
XLA Ops:
  0.0 0.0 copy-start
  0.0 1.1 %fusion.2 = bf16[10,32,256]{2,1,0:T(8,128)(2,1)S(1)} fusion(s32[]{:T(128)} %select_n.10, bf16[1,32,256]{2,1,0:T(8,128)(2,1)S(1)} %broadcast_in_dim.34, bf16[96,32,256]{2,1,0:T(8,128)(2,1)} %f_ref.3), kind=kLoop, calls=%fused_computation.9 | loop fusion | flops 163840 | bytes 1753092 | tf_op jit(solution)/shard_map/concatenate | solution.py:185
  1.1 1.9 %collective-permute-start = (bf16[10,32,256]{2,1,0:T(8,128)(2,1)S(1)}, bf16[10,32,256]{2,1,0:T(8,128)(2,1)}, u32[]{:S(2)}, u32[]{:S(2)}) collective-permute-start(bf16[10,32,256]{2,1,0:T(8,128)(2,1)S(1)} %fusion.2), channel_id=1, source_target_pairs={{30,0},{31,1},{0,2},{1,3},{2,4},{3,5},{4,6},{5,7},{6,8},{7,9},{8,1... | collective-permute-start | bytes 491528 | tf_op jit(solution)/shard_map/ppermute | solution.py:19
  3.0 5.4 %collective-permute-start.3 = (bf16[10,32,256]{2,1,0:T(8,128)(2,1)S(1)}, bf16[10,32,256]{2,1,0:T(8,128)(2,1)S(1)}, u32[]{:S(2)}, u32[]{:S(2)}) collective-permute-start(bf16[10,32,256]{2,1,0:T(8,128)(2,1)S(1)} %fusion.2), channel_id=1, source_target_pairs={{2,0},{3,1},{4,2},{5,3},{6,4},{7,5},{8,6},{9,7},{10,8},{11,9},{12,... | collective-permute-start | bytes 491528 | tf_op jit(solution)/shard_map/ppermute | solution.py:19
  8.4 0.0 copy-done
  8.4 0.1 fusion.4
  8.5 0.0 copy-start.5
  8.5 0.0 copy-start.1
  8.6 0.0 copy-start.2
  8.6 1.4 %pad_maximum_fusion = (bf16[1856,256]{1,0:T(8,128)(2,1)}, bf16[1856,256]{1,0:T(8,128)(2,1)}) fusion(bf16[320,256]{1,0:T(8,128)(2,1)S(1)} %bitcast.21, bf16[1536,256]{1,0:T(8,128)(2,1)S(1)} %bitcast.18, bf16[1536,256]{1,0:T(8,128)(2,1)S(1)} %bitcast.19), kind=kLoop, calls=%fused_computation.6 | loop fusion | flops 3325952 | bytes 3637248 | tf_op jit(solution)/shard_map/concatenate | solution.py:190
  10.0 0.0 collective-permute-start.1
  10.0 1.0 %collective-permute-start.2 = (bf16[1856,256]{1,0:T(8,128)(2,1)}, bf16[1856,256]{1,0:T(8,128)(2,1)}, u32[]{:S(2)}, u32[]{:S(2)}) collective-permute-start(bf16[1856,256]{1,0:T(8,128)(2,1)} %get-tuple-element.13), channel_id=1, source_target_pairs={{1,0},{2,1},{3,2},{4,3},{5,4},{6,5},{7,6},{8,7},{9,8},{10,9},{11,1... | collective-permute-start | bytes 2850824 | tf_op jit(solution)/shard_map/ppermute | solution.py:19
  10.9 0.0 copy-done.5
  10.9 0.1 broadcast_compare_fusion
  11.0 0.0 copy-done.1
  11.0 0.0 copy-done.2
  11.1 0.4 multiply_convert_fusion
  11.5 1.3 %constant_dynamic-slice_fusion = bf16[8,9,3,129]{0,3,2,1:T(8,128)(2,1)} fusion(bf16[96,9,3,129]{0,3,2,1:T(8,128)(2,1)S(1)} %multiply_convert_fusion, s32[]{:T(128)} %select_n.10), kind=kLoop, calls=%fused_computation.23 | loop fusion | bytes 111460 | tf_op jit(solution)/shard_map/dynamic_slice | solution.py:198
  12.8 0.1 pad.23
  12.9 1.0 %copy.11 = bf16[96,9,192]{2,1,0:T(8,128)(2,1)S(1)} copy(bf16[96,9,192]{0,2,1:T(8,128)(2,1)S(1)} %bitcast.20) | data formatting | bytes 663552 | tf_op jit(solution)/shard_map/reshape | solution.py:45
  14.0 1.1 %pad.24.src_ref = bf16[96,9,256]{2,1,0:T(8,128)(2,1)} pad(bf16[96,9,192]{2,1,0:T(8,128)(2,1)S(1)} %copy.11, bf16[]{:T(256)} %constant.8.clone.1), padding=0_0x0_0x0_64 | pad | bytes 774146 | tf_op jit(solution)/shard_map/jit(_pad)/pad | solution.py:46
  15.0 1.4 %pad.21 = bf16[8,9,3,160]{0,3,2,1:T(8,128)(2,1)S(1)} pad(bf16[8,9,3,129]{0,3,2,1:T(8,128)(2,1)} %constant_dynamic-slice_fusion, bf16[]{:T(256)} %constant.8.clone.1), padding=0_0x0_0x0_0x0_31 | pad | bytes 124850 | tf_op jit(solution)/shard_map/jit(_pad)/pad | solution.py:44
  16.4 0.6 copy.10
  17.0 0.7 %pad.22.src_ref = bf16[8,9,512]{2,1,0:T(8,128)(2,1)} pad(bf16[8,9,480]{2,1,0:T(8,128)(2,1)S(1)} %copy.10, bf16[]{:T(256)} %constant.8.clone.1), padding=0_0x0_0x0_32 | pad | bytes 142850 | tf_op jit(solution)/shard_map/jit(_pad)/pad | solution.py:46
  17.7 0.6 pad_add_fusion.scalar_ref
  18.3 0.0 collective-permute-done
  18.3 0.9 %constant_dynamic-update-slice_fusion.4 = bf16[10,160,256]{2,1,0:T(8,128)(2,1)S(1)} fusion(bf16[10,32,256]{2,1,0:T(8,128)(2,1)} %collective-permute-done), kind=kLoop, calls=%fused_computation.17 | loop fusion | bytes 327680
  19.3 11.9 %collective-permute-done.1.west_ref = bf16[1856,256]{1,0:T(8,128)(2,1)} collective-permute-done((bf16[1856,256]{1,0:T(8,128)(2,1)}, bf16[1856,256]{1,0:T(8,128)(2,1)}, u32[]{:S(2)}, u32[]{:S(2)}) %collective-permute-start.1) | collective-permute-done | bytes 950304 | tf_op jit(solution)/shard_map/ppermute | solution.py:19
  31.1 0.7 %slice_bitcast_fusion.1 = (bf16[1,16,256]{2,1,0:T(8,128)(2,1)S(1)}, bf16[1,16,256]{2,1,0:T(8,128)(2,1)S(1)}) fusion(bf16[1856,256]{1,0:T(8,128)(2,1)} %collective-permute-done.1.west_ref), kind=kLoop, calls=%fused_computation.19 | loop fusion | bytes 32768 | tf_op jit(solution)/shard_map/broadcast_in_dim | solution.py:203
  31.9 3.3 %collective-permute-done.2.east_ref = bf16[1856,256]{1,0:T(8,128)(2,1)} collective-permute-done((bf16[1856,256]{1,0:T(8,128)(2,1)}, bf16[1856,256]{1,0:T(8,128)(2,1)}, u32[]{:S(2)}, u32[]{:S(2)}) %collective-permute-start.2) | collective-permute-done | bytes 950304 | tf_op jit(solution)/shard_map/ppermute | solution.py:19
  35.1 0.7 %slice_bitcast_fusion = (bf16[1,16,256]{2,1,0:T(8,128)(2,1)S(1)}, bf16[1,16,256]{2,1,0:T(8,128)(2,1)S(1)}) fusion(bf16[1856,256]{1,0:T(8,128)(2,1)} %collective-permute-done.2.east_ref), kind=kLoop, calls=%fused_computation.18 | loop fusion | bytes 32768 | tf_op jit(solution)/shard_map/broadcast_in_dim | solution.py:204
  35.9 3.2 %collective-permute-start.4 = (bf16[1,64,256]{2,1,0:T(8,128)(2,1)S(1)}, bf16[1,64,256]{2,1,0:T(8,128)(2,1)S(1)}, u32[]{:S(2)}, u32[]{:S(2)}) collective-permute-start(bf16[1,64,256]{2,1,0:T(8,128)(2,1)S(1)} %pad_maximum_fusion.2), channel_id=1, source_target_pairs={{0,32},{32,64},{64,96},{96,128},{128,160},{160,192},{192,224},{1,3... | collective-permute-start | bytes 98312 | tf_op jit(solution)/shard_map/ppermute | solution.py:209
  39.1 4.6 %collective-permute-start.5 = (bf16[1,64,256]{2,1,0:T(8,128)(2,1)S(1)}, bf16[1,64,256]{2,1,0:T(8,128)(2,1)S(1)}, u32[]{:S(2)}, u32[]{:S(2)}) collective-permute-start(bf16[1,64,256]{2,1,0:T(8,128)(2,1)S(1)} %pad_maximum_fusion.3), channel_id=1, source_target_pairs={{32,0},{64,32},{96,64},{128,96},{160,128},{192,160},{224,192},{33,... | collective-permute-start | bytes 98312 | tf_op jit(solution)/shard_map/ppermute | solution.py:210
  43.7 0.9 %slice.44 = bf16[320,256]{1,0:T(8,128)(2,1)S(1)} slice(bf16[1856,256]{1,0:T(8,128)(2,1)} %collective-permute-done.1.west_ref), slice={[1536:1856], [0:256]} | slice | bytes 327680 | tf_op jit(solution)/shard_map/slice | solution.py:214
  44.6 0.1 constant_dynamic-update-slice_fusion.2
  44.7 0.9 %slice.45 = bf16[320,256]{1,0:T(8,128)(2,1)S(1)} slice(bf16[1856,256]{1,0:T(8,128)(2,1)} %collective-permute-done.2.east_ref), slice={[1536:1856], [0:256]} | slice | bytes 327680 | tf_op jit(solution)/shard_map/slice | solution.py:215
  45.6 0.0 collective-permute-done.3
  45.7 1.0 %pad.20.ext_ref = bf16[11,160,256]{2,1,0:T(8,128)(2,1)} pad(bf16[10,160,256]{2,1,0:T(8,128)(2,1)S(1)} %constant_dynamic-update-slice_fusion, bf16[]{:T(256)} %constant.8.clone.1), padding=0_1x0_0x0_0 | pad | bytes 1720322 | tf_op jit(solution)/shard_map/jit(_pad)/pad | solution.py:218
  46.7 0.0 collective-permute-done.4.north_ref
  46.7 0.0 copy-start.3
  46.7 0.0 collective-permute-done.5.south_ref
  46.7 0.6 copy-done.3
  47.3 0.0 copy-start.4
  47.3 0.6 copy-done.4
  47.9 12.4 %shard_map.55.prev_ref = bf16[96,32,256]{2,1,0:T(8,128)(2,1)} custom-call(s32[2]{0:T(128)} %pad_add_fusion.scalar_ref, bf16[96,9,256]{2,1,0:T(8,128)(2,1)} %pad.24.src_ref, bf16[96,32,256]{2,1,0:T(8,128)(2,1)} %f_ref.3, bf16[96,32,256]{2,1,0:T(8,128)(2,1)} %f_ref.3, bf16[1856,256]{1,0:T(8,128)(2,1)} %collective-permute-done.1.west_ref, ...), custom_call_target="tpu_custom_call" | custom-call | tf_op jit(solution)/shard_map/pallas_call | solution.py:141
  60.3 3.0 %shard_map.56 = bf16[96,32,256]{2,1,0:T(8,128)(2,1)} custom-call(s32[2]{0:T(128)} %pad_add_fusion.scalar_ref, bf16[11,160,256]{2,1,0:T(8,128)(2,1)} %pad.20.ext_ref, bf16[8,9,512]{2,1,0:T(8,128)(2,1)} %pad.22.src_ref, bf16[96,32,256]{2,1,0:T(8,128)(2,1)} %f_ref.3, bf16[9,256,256]{2,1,0:T(8,128)(2,1)} %w_ref.3, ...), custom_call_target="tpu_custom_call", output_to_operand_aliasing={{}: (5, {})} | custom-call | tf_op jit(solution)/shard_map/pallas_call | solution.py:164
  (10 shorter events, 0.1 us)
Async XLA Ops:
  0.0 8.4 %copy-start = (bf16[96,32,256]{2,1,0:T(8,128)(2,1)S(1)}, bf16[96,32,256]{2,1,0:T(8,128)(2,1)}, u32[]{:S(2)}) copy-start(bf16[96,32,256]{2,1,0:T(8,128)(2,1)} %f_ref.3) | copy-start | bytes 4718596
  1.1 17.2 %collective-permute-start = (bf16[10,32,256]{2,1,0:T(8,128)(2,1)S(1)}, bf16[10,32,256]{2,1,0:T(8,128)(2,1)}, u32[]{:S(2)}, u32[]{:S(2)}) collective-permute-start(bf16[10,32,256]{2,1,0:T(8,128)(2,1)S(1)} %fusion.2), channel_id=1, source_target_pairs={{30,0},{31,1},{0,2},{1,3},{2,4},{3,5},{4,6},{5,7},{6,8},{7,9},{8,1... | collective-permute-start | bytes 491528 | tf_op jit(solution)/shard_map/ppermute | solution.py:19
  3.0 42.6 %collective-permute-start.3 = (bf16[10,32,256]{2,1,0:T(8,128)(2,1)S(1)}, bf16[10,32,256]{2,1,0:T(8,128)(2,1)S(1)}, u32[]{:S(2)}, u32[]{:S(2)}) collective-permute-start(bf16[10,32,256]{2,1,0:T(8,128)(2,1)S(1)} %fusion.2), channel_id=1, source_target_pairs={{2,0},{3,1},{4,2},{5,3},{6,4},{7,5},{8,6},{9,7},{10,8},{11,9},{12,... | collective-permute-start | bytes 491528 | tf_op jit(solution)/shard_map/ppermute | solution.py:19
  8.5 2.4 %copy-start.5 = (s32[96]{0:T(128)S(1)}, s32[96]{0:T(128)}, u32[]{:S(2)}) copy-start(s32[96]{0:T(128)} %param.8) | copy-start | bytes 1156
  8.5 2.5 %copy-start.1 = (f32[96,3,129]{0,2,1:T(8,128)S(1)}, f32[96,3,129]{0,2,1:T(8,128)}, u32[]{:S(2)}) copy-start(f32[96,3,129]{0,2,1:T(8,128)} %param.6) | copy-start | bytes 445828
  8.6 2.5 %copy-start.2 = (s32[96,3,129]{0,2,1:T(8,128)S(1)}, s32[96,3,129]{0,2,1:T(8,128)}, u32[]{:S(2)}) copy-start(s32[96,3,129]{0,2,1:T(8,128)} %param.7) | copy-start | bytes 445828
  10.0 21.2 %collective-permute-start.1 = (bf16[1856,256]{1,0:T(8,128)(2,1)}, bf16[1856,256]{1,0:T(8,128)(2,1)}, u32[]{:S(2)}, u32[]{:S(2)}) collective-permute-start(bf16[1856,256]{1,0:T(8,128)(2,1)} %get-tuple-element.14), channel_id=1, source_target_pairs={{31,0},{0,1},{1,2},{2,3},{3,4},{4,5},{5,6},{6,7},{7,8},{8,9},{9,10... | collective-permute-start | bytes 2850824 | tf_op jit(solution)/shard_map/ppermute | solution.py:19
  10.0 25.2 %collective-permute-start.2 = (bf16[1856,256]{1,0:T(8,128)(2,1)}, bf16[1856,256]{1,0:T(8,128)(2,1)}, u32[]{:S(2)}, u32[]{:S(2)}) collective-permute-start(bf16[1856,256]{1,0:T(8,128)(2,1)} %get-tuple-element.13), channel_id=1, source_target_pairs={{1,0},{2,1},{3,2},{4,3},{5,4},{6,5},{7,6},{8,7},{9,8},{10,9},{11,1... | collective-permute-start | bytes 2850824 | tf_op jit(solution)/shard_map/ppermute | solution.py:19
  35.9 10.8 %collective-permute-start.4 = (bf16[1,64,256]{2,1,0:T(8,128)(2,1)S(1)}, bf16[1,64,256]{2,1,0:T(8,128)(2,1)S(1)}, u32[]{:S(2)}, u32[]{:S(2)}) collective-permute-start(bf16[1,64,256]{2,1,0:T(8,128)(2,1)S(1)} %pad_maximum_fusion.2), channel_id=1, source_target_pairs={{0,32},{32,64},{64,96},{96,128},{128,160},{160,192},{192,224},{1,3... | collective-permute-start | bytes 98312 | tf_op jit(solution)/shard_map/ppermute | solution.py:209
  39.1 7.6 %collective-permute-start.5 = (bf16[1,64,256]{2,1,0:T(8,128)(2,1)S(1)}, bf16[1,64,256]{2,1,0:T(8,128)(2,1)S(1)}, u32[]{:S(2)}, u32[]{:S(2)}) collective-permute-start(bf16[1,64,256]{2,1,0:T(8,128)(2,1)S(1)} %pad_maximum_fusion.3), channel_id=1, source_target_pairs={{32,0},{64,32},{96,64},{128,96},{160,128},{192,160},{224,192},{33,... | collective-permute-start | bytes 98312 | tf_op jit(solution)/shard_map/ppermute | solution.py:210
  46.7 0.6 copy-start.3
  47.3 0.6 copy-start.4

commit v10 on v9

--- a/solution.py
+++ b/solution.py
@@ -189,8 +189,9 @@
         [features[:, columns - NEAR :].reshape(-1, channels), flat_window]), "lon", 1)
     from_east = shifted(jnp.concatenate(
         [features[:, :NEAR].reshape(-1, channels), flat_window]), "lon", -1)
-    west_far = [shifted(window, "lon", hop) for hop in range(hops, 1, -1)]
-    east_far = [shifted(window, "lon", -hop) for hop in range(2, hops + 1)]
+    late_window, from_west, from_east = lax.optimization_barrier((window, from_west, from_east))
+    west_far = [shifted(late_window, "lon", hop) for hop in range(hops, 1, -1)]
+    east_far = [shifted(late_window, "lon", -hop) for hop in range(2, hops + 1)]
 
     basis_values = basis_table(quad_weights, cycle_index, widths, count)
     near_sources = flat_sources(

time: 64.3 us -> 72.3 us (1.12)
  the two profiles are of different devices: /device:TPU:3 before, /device:TPU:2 now
where the time goes in v10:
time: 72.3 us; the launch traced here: 72 us
  starting transfers between devices  24.3 us (34%)
  Pallas kernels  15.6 us (22%)
  waiting for transfers between devices  15.3 us (21%)
  local copies, waits for them, and re-layouts  10.8 us (15%)
  other arithmetic  5.89 us (8%)
    ppermute x4, starting transfers between devices, shifted(): return lax.ppermute(block, axis, route)  15.8 us
    ppermute x4, waiting for transfers between devices, shifted(): return lax.ppermute(block, axis, route)  15.3 us
    pallas_call x1, Pallas kernels, near_call(): pl.pallas_call(near_kernel, grid_spec=grid_spec, out_shape=jax.ShapeDtype...  12.6 us
    ppermute x1, starting transfers between devices, body(): south = lax.ppermute(edge(0), 'lat', down)  5.06 us
    ppermute x1, starting transfers between devices, body(): north = lax.ppermute(edge(lat_rows - 1), 'lat', up)  3.47 us
    pallas_call x1, Pallas kernels, wide_call(): pl.pallas_call(wide_kernel, grid_spec=grid_spec, out_shape=jax.ShapeDtype...  2.97 us
    unnamed x17, local copies, waits for them, and re-layouts  2.48 us
    concatenate x1, other arithmetic, body(): jnp.concatenate([features[:, :NEAR].reshape(-1, channels), flat_window])  2.33 us
  transfers between devices with their start and end apart: 6, of which 2 were waited for; matrix products, arithmetic and copies ran while one was open for 12% of the time, Pallas kernels for 17%

profile of v10, /device:TPU:2, one launch (start us, length us, event | category | flops | bytes accessed | tf_op | source)
XLA Modules:
  0.0 72.0 jit_solution(10492736388286468500)
XLA Ops:
  0.0 0.0 copy-start
  0.0 1.6 %fusion.4 = (bf16[96,16,256]{2,1,0:T(8,128)(2,1)S(1)}, bf16[96,16,256]{2,1,0:T(8,128)(2,1)S(1)}) fusion(bf16[96,32,256]{2,1,0:T(8,128)(2,1)} %f_ref.3), kind=kLoop, calls=%fused_computation.27 | loop fusion | bytes 3145728 | tf_op jit(solution)/shard_map/slice | solution.py:191
  1.6 0.3 copy-done
  1.9 0.7 fusion.2
  2.6 0.0 copy-start.6
  2.6 2.3 %pad_maximum_fusion = (bf16[1856,256]{1,0:T(8,128)(2,1)}, bf16[1856,256]{1,0:T(8,128)(2,1)}) fusion(bf16[320,256]{1,0:T(8,128)(2,1)} %bitcast.3, bf16[1536,256]{1,0:T(8,128)(2,1)S(1)} %bitcast.18, bf16[1536,256]{1,0:T(8,128)(2,1)S(1)} %bitcast.19), kind=kLoop, calls=%fused_computation.6 | loop fusion | flops 3325952 | bytes 3637248 | tf_op jit(solution)/shard_map/concatenate | solution.py:190
  4.9 6.9 %collective-permute-start.1 = (bf16[1856,256]{1,0:T(8,128)(2,1)}, bf16[1856,256]{1,0:T(8,128)(2,1)S(1)}, u32[]{:S(2)}, u32[]{:S(2)}) collective-permute-start(bf16[1856,256]{1,0:T(8,128)(2,1)} %get-tuple-element.19), channel_id=1, source_target_pairs={{1,0},{2,1},{3,2},{4,3},{5,4},{6,5},{7,6},{8,7},{9,8},{10,9},{11,1... | collective-permute-start | bytes 2850824 | tf_op jit(solution)/shard_map/ppermute | solution.py:19
  11.8 0.0 collective-permute-start
  11.8 0.0 copy-done.6
  11.8 0.1 broadcast_compare_fusion
  11.9 1.5 %multiply_convert_fusion = bf16[96,9,3,129]{0,3,2,1:T(8,128)(2,1)S(1)} fusion(f32[96]{0:T(128)S(1)} %multiply_rsqrt_fusion, f32[96,3,129]{0,2,1:T(8,128)} %param.6, s32[96,3,129]{0,2,1:T(8,128)} %param.7, pred[96,129]{0,1:T(8,128)(4,1)S(1)} %broadcast_compare_fusion), kind=kLoop, calls=%fused_computation | loop fusion | flops 1671840 | bytes 978720 | tf_op jit(solution)/shard_map/convert_element_type | solution.py:39
  13.4 0.0 copy-start.2
  13.4 0.3 constant_dynamic-slice_fusion
  13.7 9.7 %collective-permute-done.1.east_ref = bf16[1856,256]{1,0:T(8,128)(2,1)S(1)} collective-permute-done((bf16[1856,256]{1,0:T(8,128)(2,1)}, bf16[1856,256]{1,0:T(8,128)(2,1)S(1)}, u32[]{:S(2)}, u32[]{:S(2)}) %collective-permute-start.1) | collective-permute-done | bytes 950304 | tf_op jit(solution)/shard_map/ppermute | solution.py:19
  23.4 0.0 copy-start.3
  23.4 5.6 %collective-permute-done.west_ref = bf16[1856,256]{1,0:T(8,128)(2,1)} collective-permute-done((bf16[1856,256]{1,0:T(8,128)(2,1)}, bf16[1856,256]{1,0:T(8,128)(2,1)}, u32[]{:S(2)}, u32[]{:S(2)}) %collective-permute-start) | collective-permute-done | bytes 950304 | tf_op jit(solution)/shard_map/ppermute | solution.py:19
  29.0 0.7 slice_bitcast_fusion
  29.7 3.5 %collective-permute-start.4 = (bf16[1,64,256]{2,1,0:T(8,128)(2,1)S(1)}, bf16[1,64,256]{2,1,0:T(8,128)(2,1)S(1)}, u32[]{:S(2)}, u32[]{:S(2)}) collective-permute-start(bf16[1,64,256]{2,1,0:T(8,128)(2,1)S(1)} %pad_maximum_fusion.2), channel_id=1, source_target_pairs={{0,32},{32,64},{64,96},{96,128},{128,160},{160,192},{192,224},{1,3... | collective-permute-start | bytes 98312 | tf_op jit(solution)/shard_map/ppermute | solution.py:210
  33.2 4.2 %collective-permute-start.2 = (bf16[10,32,256]{2,1,0:T(8,128)(2,1)}, bf16[10,32,256]{2,1,0:T(8,128)(2,1)}, u32[]{:S(2)}, u32[]{:S(2)}) collective-permute-start(bf16[10,32,256]{2,1,0:T(8,128)(2,1)} %fusion.2), channel_id=1, source_target_pairs={{30,0},{31,1},{0,2},{1,3},{2,4},{3,5},{4,6},{5,7},{6,8},{7,9},{8,1... | collective-permute-start | bytes 491528 | tf_op jit(solution)/shard_map/ppermute | solution.py:19
  37.4 0.6 pad_maximum_fusion.3
  38.0 5.1 %collective-permute-start.5 = (bf16[1,64,256]{2,1,0:T(8,128)(2,1)}, bf16[1,64,256]{2,1,0:T(8,128)(2,1)S(1)}, u32[]{:S(2)}, u32[]{:S(2)}) collective-permute-start(bf16[1,64,256]{2,1,0:T(8,128)(2,1)} %pad_maximum_fusion.3), channel_id=1, source_target_pairs={{32,0},{64,32},{96,64},{128,96},{160,128},{192,160},{224,192},{33,... | collective-permute-start | bytes 98312 | tf_op jit(solution)/shard_map/ppermute | solution.py:211
  43.0 0.6 pad_add_fusion.scalar_ref
  43.6 0.2 pad.21
  43.8 0.0 copy-done.2
  43.9 0.0 slice-start
  43.9 0.6 copy.10
  44.5 0.7 pad.22.src_ref
  45.2 0.0 slice-done
  45.2 0.1 pad.23
  45.3 1.0 %copy.11 = bf16[96,9,192]{2,1,0:T(8,128)(2,1)S(1)} copy(bf16[96,9,192]{0,2,1:T(8,128)(2,1)S(1)} %bitcast.20) | data formatting | bytes 663552 | tf_op jit(solution)/shard_map/reshape | solution.py:45
  46.3 1.0 %pad.24.src_ref = bf16[96,9,256]{2,1,0:T(8,128)(2,1)} pad(bf16[96,9,192]{2,1,0:T(8,128)(2,1)S(1)} %copy.11, bf16[]{:T(256)} %constant.8.clone.1), padding=0_0x0_0x0_64 | pad | bytes 774146 | tf_op jit(solution)/shard_map/jit(_pad)/pad | solution.py:46
  47.4 0.9 %slice.35 = bf16[320,256]{1,0:T(8,128)(2,1)S(1)} slice(bf16[1856,256]{1,0:T(8,128)(2,1)} %collective-permute-done.west_ref), slice={[1536:1856], [0:256]} | slice | bytes 327680 | tf_op jit(solution)/shard_map/slice | solution.py:215
  48.3 0.0 copy-done.3
  48.3 4.8 %collective-permute-start.3 = (bf16[10,32,256]{2,1,0:T(8,128)(2,1)}, bf16[10,32,256]{2,1,0:T(8,128)(2,1)S(1)}, u32[]{:S(2)}, u32[]{:S(2)}) collective-permute-start(bf16[10,32,256]{2,1,0:T(8,128)(2,1)} %fusion.2), channel_id=1, source_target_pairs={{2,0},{3,1},{4,2},{5,3},{6,4},{7,5},{8,6},{9,7},{10,8},{11,9},{12,... | collective-permute-start | bytes 491528 | tf_op jit(solution)/shard_map/ppermute | solution.py:19
  53.1 0.0 collective-permute-done.4.north_ref
  53.1 0.0 copy-start.4
  53.1 0.0 collective-permute-done.5.south_ref
  53.1 0.6 copy-done.4
  53.7 0.0 copy-start.5
  53.7 0.6 copy-done.5
  54.3 0.0 copy-start.1
  54.3 12.6 %shard_map.55.prev_ref = bf16[96,32,256]{2,1,0:T(8,128)(2,1)} custom-call(s32[2]{0:T(128)} %pad_add_fusion.scalar_ref, bf16[96,9,256]{2,1,0:T(8,128)(2,1)} %pad.24.src_ref, bf16[96,32,256]{2,1,0:T(8,128)(2,1)} %f_ref.3, bf16[96,32,256]{2,1,0:T(8,128)(2,1)} %f_ref.3, bf16[1856,256]{1,0:T(8,128)(2,1)} %collective-permute-done.west_ref, ...), custom_call_target="tpu_custom_call" | custom-call | tf_op jit(solution)/shard_map/pallas_call | solution.py:141
  66.9 0.0 slice-start.1
  66.9 0.0 collective-permute-done.2
  66.9 1.0 %constant_dynamic-update-slice_fusion.4 = bf16[10,160,256]{2,1,0:T(8,128)(2,1)S(1)} fusion(bf16[10,32,256]{2,1,0:T(8,128)(2,1)} %collective-permute-done.2), kind=kLoop, calls=%fused_computation.17 | loop fusion | bytes 327680
  67.9 0.0 copy-done.1
  67.9 0.1 constant_dynamic-update-slice_fusion.2
  68.0 0.0 slice-done.1
  68.0 0.0 collective-permute-done.3
  68.1 1.0 %pad.20.ext_ref = bf16[11,160,256]{2,1,0:T(8,128)(2,1)} pad(bf16[10,160,256]{2,1,0:T(8,128)(2,1)S(1)} %constant_dynamic-update-slice_fusion, bf16[]{:T(256)} %constant.8.clone.1), padding=0_1x0_0x0_0 | pad | bytes 1720322 | tf_op jit(solution)/shard_map/jit(_pad)/pad | solution.py:219
  69.0 3.0 %shard_map.56 = bf16[96,32,256]{2,1,0:T(8,128)(2,1)} custom-call(s32[2]{0:T(128)} %pad_add_fusion.scalar_ref, bf16[11,160,256]{2,1,0:T(8,128)(2,1)} %pad.20.ext_ref, bf16[8,9,512]{2,1,0:T(8,128)(2,1)} %pad.22.src_ref, bf16[96,32,256]{2,1,0:T(8,128)(2,1)} %f_ref.3, bf16[9,256,256]{2,1,0:T(8,128)(2,1)} %w_ref.3, ...), custom_call_target="tpu_custom_call", output_to_operand_aliasing={{}: (5, {})} | custom-call | tf_op jit(solution)/shard_map/pallas_call | solution.py:164
  (8 shorter events, 0.1 us)
Async XLA Ops:
  0.0 1.9 %copy-start = (bf16[96,32,256]{2,1,0:T(8,128)(2,1)S(1)}, bf16[96,32,256]{2,1,0:T(8,128)(2,1)}, u32[]{:S(2)}) copy-start(bf16[96,32,256]{2,1,0:T(8,128)(2,1)} %f_ref.3) | copy-start | bytes 4718596
  2.6 9.2 %copy-start.6 = (s32[96]{0:T(128)S(1)}, s32[96]{0:T(128)}, u32[]{:S(2)}) copy-start(s32[96]{0:T(128)} %param.8) | copy-start | bytes 1156
  4.9 18.5 %collective-permute-start.1 = (bf16[1856,256]{1,0:T(8,128)(2,1)}, bf16[1856,256]{1,0:T(8,128)(2,1)S(1)}, u32[]{:S(2)}, u32[]{:S(2)}) collective-permute-start(bf16[1856,256]{1,0:T(8,128)(2,1)} %get-tuple-element.19), channel_id=1, source_target_pairs={{1,0},{2,1},{3,2},{4,3},{5,4},{6,5},{7,6},{8,7},{9,8},{10,9},{11,1... | collective-permute-start | bytes 2850824 | tf_op jit(solution)/shard_map/ppermute | solution.py:19
  11.8 17.2 %collective-permute-start = (bf16[1856,256]{1,0:T(8,128)(2,1)}, bf16[1856,256]{1,0:T(8,128)(2,1)}, u32[]{:S(2)}, u32[]{:S(2)}) collective-permute-start(bf16[1856,256]{1,0:T(8,128)(2,1)} %get-tuple-element.20), channel_id=1, source_target_pairs={{31,0},{0,1},{1,2},{2,3},{3,4},{4,5},{5,6},{6,7},{7,8},{8,9},{9,10... | collective-permute-start | bytes 2850824 | tf_op jit(solution)/shard_map/ppermute | solution.py:19
  13.4 30.5 %copy-start.2 = (bf16[96,9,3,129]{0,3,2,1:T(8,128)(2,1)}, bf16[96,9,3,129]{0,3,2,1:T(8,128)(2,1)S(1)}, u32[]{:S(2)}) copy-start(bf16[96,9,3,129]{0,3,2,1:T(8,128)(2,1)S(1)} %multiply_convert_fusion) | copy-start | bytes 2006212
  23.4 24.9 %copy-start.3 = (bf16[1856,256]{1,0:T(8,128)(2,1)}, bf16[1856,256]{1,0:T(8,128)(2,1)S(1)}, u32[]{:S(2)}) copy-start(bf16[1856,256]{1,0:T(8,128)(2,1)S(1)} %collective-permute-done.1.east_ref) | copy-start | bytes 2850820
  29.7 23.4 %collective-permute-start.4 = (bf16[1,64,256]{2,1,0:T(8,128)(2,1)S(1)}, bf16[1,64,256]{2,1,0:T(8,128)(2,1)S(1)}, u32[]{:S(2)}, u32[]{:S(2)}) collective-permute-start(bf16[1,64,256]{2,1,0:T(8,128)(2,1)S(1)} %pad_maximum_fusion.2), channel_id=1, source_target_pairs={{0,32},{32,64},{64,96},{96,128},{128,160},{160,192},{192,224},{1,3... | collective-permute-start | bytes 98312 | tf_op jit(solution)/shard_map/ppermute | solution.py:210
  33.2 33.7 %collective-permute-start.2 = (bf16[10,32,256]{2,1,0:T(8,128)(2,1)}, bf16[10,32,256]{2,1,0:T(8,128)(2,1)}, u32[]{:S(2)}, u32[]{:S(2)}) collective-permute-start(bf16[10,32,256]{2,1,0:T(8,128)(2,1)} %fusion.2), channel_id=1, source_target_pairs={{30,0},{31,1},{0,2},{1,3},{2,4},{3,5},{4,6},{5,7},{6,8},{7,9},{8,1... | collective-permute-start | bytes 491528 | tf_op jit(solution)/shard_map/ppermute | solution.py:19
  38.0 15.1 %collective-permute-start.5 = (bf16[1,64,256]{2,1,0:T(8,128)(2,1)}, bf16[1,64,256]{2,1,0:T(8,128)(2,1)S(1)}, u32[]{:S(2)}, u32[]{:S(2)}) collective-permute-start(bf16[1,64,256]{2,1,0:T(8,128)(2,1)} %pad_maximum_fusion.3), channel_id=1, source_target_pairs={{32,0},{64,32},{96,64},{128,96},{160,128},{192,160},{224,192},{33,... | collective-permute-start | bytes 98312 | tf_op jit(solution)/shard_map/ppermute | solution.py:211
  43.9 1.3 %slice-start = ((bf16[96,9,3,129]{0,3,2,1:T(8,128)(2,1)}), bf16[96,9,3,33]{0,3,2,1:T(8,128)(2,1)S(1)}, s32[]{:S(2)}) async-start(bf16[96,9,3,129]{0,3,2,1:T(8,128)(2,1)} %copy-done.2), calls=%async_computation | async-start | bytes 552960 | tf_op jit(solution)/shard_map/slice | solution.py:198
  48.3 19.7 %collective-permute-start.3 = (bf16[10,32,256]{2,1,0:T(8,128)(2,1)}, bf16[10,32,256]{2,1,0:T(8,128)(2,1)S(1)}, u32[]{:S(2)}, u32[]{:S(2)}) collective-permute-start(bf16[10,32,256]{2,1,0:T(8,128)(2,1)} %fusion.2), channel_id=1, source_target_pairs={{2,0},{3,1},{4,2},{5,3},{6,4},{7,5},{8,6},{9,7},{10,8},{11,9},{12,... | collective-permute-start | bytes 491528 | tf_op jit(solution)/shard_map/ppermute | solution.py:19
  53.1 0.6 copy-start.4
  53.7 0.6 copy-start.5
  54.3 13.6 %copy-start.1 = (bf16[96,32,256]{2,1,0:T(8,128)(2,1)S(1)}, bf16[96,32,256]{2,1,0:T(8,128)(2,1)}, u32[]{:S(2)}) copy-start(bf16[96,32,256]{2,1,0:T(8,128)(2,1)} %f_ref.3) | copy-start | bytes 4718596
  66.9 1.1 %slice-start.1 = ((bf16[1856,256]{1,0:T(8,128)(2,1)}), bf16[320,256]{1,0:T(8,128)(2,1)S(1)}, s32[]{:S(2)}) async-start(bf16[1856,256]{1,0:T(8,128)(2,1)} %copy-done.3), calls=%async_computation.1 | async-start | bytes 327680 | tf_op jit(solution)/shard_map/slice | solution.py:216

commit v11 on v9

--- a/solution.py
+++ b/solution.py
@@ -198,16 +198,25 @@
     polar_values = lax.dynamic_slice_in_dim(basis_values, start, POLAR, 0)
     wide_sources = flat_sources(polar_values, columns + 2 * reach, 512)
 
-    def edge(row):
-        return jnp.concatenate(
-            [from_west[row * NEAR : (row + 1) * NEAR][None], features[row : row + 1],
-             from_east[row * NEAR : (row + 1) * NEAR][None]], axis=1)
+    lon_count = lax.axis_size("lon")
+
+    def from_band(block, lat_step, lon_step):
+        pairs = []
+        for a in range(count_lat):
+            if 0 <= a - lat_step < count_lat:
+                for b in range(lon_count):
+                    source = (a - lat_step) * lon_count + (b - lon_step) % lon_count
+                    pairs.append((source, a * lon_count + b))
+        return lax.ppermute(block, ("lat", "lon"), pairs)
 
     count_lat = lax.axis_size("lat")
-    up = [(i, i + 1) for i in range(count_lat - 1)]
-    down = [(j, i) for i, j in up]
-    north = lax.ppermute(edge(lat_rows - 1), "lat", up)
-    south = lax.ppermute(edge(0), "lat", down)
+    last, first = features[lat_rows - 1 :], features[:1]
+    north = jnp.concatenate(
+        [from_band(last[:, columns - NEAR :], 1, 1), from_band(last, 1, 0),
+         from_band(last[:, :NEAR], 1, -1)], axis=1)
+    south = jnp.concatenate(
+        [from_band(first[:, columns - NEAR :], -1, 1), from_band(first, -1, 0),
+         from_band(first[:, :NEAR], -1, -1)], axis=1)
     out = near_call(scalars, near_sources, features, from_west, from_east, north, south,
                     mix_weight)
 

time: 64.3 us -> 78.2 us (1.22)
  the two profiles are of different devices: /device:TPU:3 before, /device:TPU:103 now
where the time goes in v11:
time: 78.2 us; the launch traced here: 77.8 us
  starting transfers between devices  31.1 us (40%)
  waiting for transfers between devices  16.2 us (21%)
  Pallas kernels  15.4 us (20%)
  local copies, waits for them, and re-layouts  11 us (14%)
  other arithmetic  3.81 us (5%)
    ppermute x6, starting transfers between devices, from_band(): return lax.ppermute(block, ('lat', 'lon'), pairs)  20.8 us
    pallas_call x1, Pallas kernels, near_call(): pl.pallas_call(near_kernel, grid_spec=grid_spec, out_shape=jax.ShapeDtype...  12.4 us
    ppermute x6, waiting for transfers between devices, from_band(): return lax.ppermute(block, ('lat', 'lon'), pairs)  11.1 us
    ppermute x4, starting transfers between devices, shifted(): return lax.ppermute(block, axis, route)  10.3 us
    ppermute x4, waiting for transfers between devices, shifted(): return lax.ppermute(block, axis, route)  5.15 us
    pallas_call x1, Pallas kernels, wide_call(): pl.pallas_call(wide_kernel, grid_spec=grid_spec, out_shape=jax.ShapeDtype...  2.97 us
    pad x2, local copies, waits for them, and re-layouts, flat_sources(): return jnp.pad(flat, ((0, 0), (0, 0), (0, lanes - offsets * span)))  1.72 us
    reshape x2, local copies, waits for them, and re-layouts, flat_sources(): flat = flat.reshape(rows, count, offsets * span)  1.65 us
  transfers between devices with their start and end apart: 10, of which 3 were waited for; matrix products, arithmetic and copies ran while one was open for 13% of the time, Pallas kernels for 0%

profile of v11, /device:TPU:103, one launch (start us, length us, event | category | flops | bytes accessed | tf_op | source)
XLA Modules:
  0.0 77.8 jit_solution(6249275485942468259)
XLA Ops:
  0.0 0.0 copy-start
  0.0 1.6 %fusion.5 = (bf16[96,16,256]{2,1,0:T(8,128)(2,1)S(1)}, bf16[96,16,256]{2,1,0:T(8,128)(2,1)S(1)}) fusion(bf16[96,32,256]{2,1,0:T(8,128)(2,1)} %f_ref.3), kind=kLoop, calls=%fused_computation.24 | loop fusion | bytes 3145728 | tf_op jit(solution)/shard_map/slice | solution.py:191
  1.6 0.3 copy-done
  1.9 0.0 copy-start.3
  2.0 0.0 copy-start.1
  2.0 0.0 copy-start.2
  2.0 1.4 %pad_maximum_fusion = (bf16[1856,256]{1,0:T(8,128)(2,1)}, bf16[1856,256]{1,0:T(8,128)(2,1)}) fusion(bf16[320,256]{1,0:T(8,128)(2,1)S(1)} %bitcast.13, bf16[1536,256]{1,0:T(8,128)(2,1)S(1)} %bitcast.10, bf16[1536,256]{1,0:T(8,128)(2,1)S(1)} %bitcast.11), kind=kLoop, calls=%fused_computation.6 | loop fusion | flops 3325952 | bytes 3637248 | tf_op jit(solution)/shard_map/concatenate | solution.py:190
  3.4 4.3 %collective-permute-start.1 = (bf16[1856,256]{1,0:T(8,128)(2,1)}, bf16[1856,256]{1,0:T(8,128)(2,1)}, u32[]{:S(2)}, u32[]{:S(2)}) collective-permute-start(bf16[1856,256]{1,0:T(8,128)(2,1)} %get-tuple-element.14), channel_id=1, source_target_pairs={{31,0},{0,1},{1,2},{2,3},{3,4},{4,5},{5,6},{6,7},{7,8},{8,9},{9,10... | collective-permute-start | bytes 2850824 | tf_op jit(solution)/shard_map/ppermute | solution.py:19
  7.6 0.0 collective-permute-start.2
  7.6 8.3 %collective-permute-start.4 = (bf16[1,16,256]{2,1,0:T(8,128)(2,1)S(1)}, bf16[1,16,256]{2,1,0:T(8,128)(2,1)S(1)}, u32[]{:S(2)}, u32[]{:S(2)}) collective-permute-start(bf16[1,16,256]{2,1,0:T(8,128)(2,1)S(1)} %get-tuple-element.8), channel_id=1, source_target_pairs={{31,32},{0,33},{1,34},{2,35},{3,36},{4,37},{5,38},{6,39},{7,40},{8... | collective-permute-start | bytes 24584 | tf_op jit(solution)/shard_map/ppermute | solution.py:210
  15.9 1.9 %collective-permute-start.6 = (bf16[1,16,256]{2,1,0:T(8,128)(2,1)S(1)}, bf16[1,16,256]{2,1,0:T(8,128)(2,1)S(1)}, u32[]{:S(2)}, u32[]{:S(2)}) collective-permute-start(bf16[1,16,256]{2,1,0:T(8,128)(2,1)S(1)} %get-tuple-element.7), channel_id=1, source_target_pairs={{1,32},{2,33},{3,34},{4,35},{5,36},{6,37},{7,38},{8,39},{9,40},{10... | collective-permute-start | bytes 24584 | tf_op jit(solution)/shard_map/ppermute | solution.py:210
  17.8 3.2 %collective-permute-start.5 = (bf16[1,32,256]{2,1,0:T(8,128)(2,1)S(1)}, bf16[1,32,256]{2,1,0:T(8,128)(2,1)S(1)}, u32[]{:S(2)}, u32[]{:S(2)}) collective-permute-start(bf16[1,32,256]{2,1,0:T(8,128)(2,1)S(1)} %get-tuple-element.10), channel_id=1, source_target_pairs={{0,32},{1,33},{2,34},{3,35},{4,36},{5,37},{6,38},{7,39},{8,40},{9,... | collective-permute-start | bytes 49160 | tf_op jit(solution)/shard_map/ppermute | solution.py:210
  21.1 0.0 copy-done.3
  21.1 0.1 broadcast_compare_fusion
  21.2 0.0 copy-done.1
  21.2 0.0 copy-done.2
  21.2 0.4 multiply_convert_fusion
  21.6 1.3 %constant_dynamic-slice_fusion = bf16[8,9,3,129]{0,3,2,1:T(8,128)(2,1)} fusion(bf16[96,9,3,129]{0,3,2,1:T(8,128)(2,1)S(1)} %multiply_convert_fusion, s32[]{:T(128)} %select_n.10), kind=kLoop, calls=%fused_computation.19 | loop fusion | bytes 111460 | tf_op jit(solution)/shard_map/dynamic_slice | solution.py:198
  22.9 7.1 %collective-permute-done.4 = bf16[1,16,256]{2,1,0:T(8,128)(2,1)S(1)} collective-permute-done((bf16[1,16,256]{2,1,0:T(8,128)(2,1)S(1)}, bf16[1,16,256]{2,1,0:T(8,128)(2,1)S(1)}, u32[]{:S(2)}, u32[]{:S(2)}) %collective-permute-start.4) | collective-permute-done | bytes 8224 | tf_op jit(solution)/shard_map/ppermute | solution.py:210
  30.0 2.5 %collective-permute-start.7 = (bf16[1,16,256]{2,1,0:T(8,128)(2,1)S(1)}, bf16[1,16,256]{2,1,0:T(8,128)(2,1)S(1)}, u32[]{:S(2)}, u32[]{:S(2)}) collective-permute-start(bf16[1,16,256]{2,1,0:T(8,128)(2,1)S(1)} %get-tuple-element.5), channel_id=1, source_target_pairs={{63,0},{32,1},{33,2},{34,3},{35,4},{36,5},{37,6},{38,7},{39,8},{40... | collective-permute-start | bytes 24584 | tf_op jit(solution)/shard_map/ppermute | solution.py:210
  32.6 0.6 pad_add_fusion.scalar_ref
  33.1 0.1 pad.23
  33.3 1.0 %copy.11 = bf16[96,9,192]{2,1,0:T(8,128)(2,1)S(1)} copy(bf16[96,9,192]{0,2,1:T(8,128)(2,1)S(1)} %bitcast.12) | data formatting | bytes 663552 | tf_op jit(solution)/shard_map/reshape | solution.py:45
  34.3 1.1 %pad.24.src_ref = bf16[96,9,256]{2,1,0:T(8,128)(2,1)} pad(bf16[96,9,192]{2,1,0:T(8,128)(2,1)S(1)} %copy.11, bf16[]{:T(256)} %constant.8.clone.1), padding=0_0x0_0x0_64 | pad | bytes 774146 | tf_op jit(solution)/shard_map/jit(_pad)/pad | solution.py:46
  35.4 1.4 %pad.21 = bf16[8,9,3,160]{0,3,2,1:T(8,128)(2,1)S(1)} pad(bf16[8,9,3,129]{0,3,2,1:T(8,128)(2,1)} %constant_dynamic-slice_fusion, bf16[]{:T(256)} %constant.8.clone.1), padding=0_0x0_0x0_0x0_31 | pad | bytes 124850 | tf_op jit(solution)/shard_map/jit(_pad)/pad | solution.py:44
  36.8 0.6 copy.10
  37.4 0.7 pad.22.src_ref
  38.0 0.0 collective-permute-done.6
  38.0 6.1 %collective-permute-start = (bf16[10,32,256]{2,1,0:T(8,128)(2,1)S(1)}, bf16[10,32,256]{2,1,0:T(8,128)(2,1)S(1)}, u32[]{:S(2)}, u32[]{:S(2)}) collective-permute-start(bf16[10,32,256]{2,1,0:T(8,128)(2,1)S(1)} %fusion.2), channel_id=1, source_target_pairs={{30,0},{31,1},{0,2},{1,3},{2,4},{3,5},{4,6},{5,7},{6,8},{7,9},{8,1... | collective-permute-start | bytes 491528 | tf_op jit(solution)/shard_map/ppermute | solution.py:19
  44.1 0.0 collective-permute-done.7
  44.1 1.9 %collective-permute-start.9 = (bf16[1,16,256]{2,1,0:T(8,128)(2,1)S(1)}, bf16[1,16,256]{2,1,0:T(8,128)(2,1)S(1)}, u32[]{:S(2)}, u32[]{:S(2)}) collective-permute-start(bf16[1,16,256]{2,1,0:T(8,128)(2,1)S(1)} %get-tuple-element.6), channel_id=1, source_target_pairs={{33,0},{34,1},{35,2},{36,3},{37,4},{38,5},{39,6},{40,7},{41,8},{42... | collective-permute-start | bytes 24584 | tf_op jit(solution)/shard_map/ppermute | solution.py:210
  46.0 0.0 collective-permute-done.5
  46.0 3.0 %collective-permute-start.8 = (bf16[1,32,256]{2,1,0:T(8,128)(2,1)S(1)}, bf16[1,32,256]{2,1,0:T(8,128)(2,1)S(1)}, u32[]{:S(2)}, u32[]{:S(2)}) collective-permute-start(bf16[1,32,256]{2,1,0:T(8,128)(2,1)S(1)} %get-tuple-element.9), channel_id=1, source_target_pairs={{32,0},{33,1},{34,2},{35,3},{36,4},{37,5},{38,6},{39,7},{40,8},{41... | collective-permute-start | bytes 49160 | tf_op jit(solution)/shard_map/ppermute | solution.py:210
  49.0 0.6 pad_maximum_fusion.2.north_ref
  49.6 4.0 %collective-permute-done.9 = bf16[1,16,256]{2,1,0:T(8,128)(2,1)S(1)} collective-permute-done((bf16[1,16,256]{2,1,0:T(8,128)(2,1)S(1)}, bf16[1,16,256]{2,1,0:T(8,128)(2,1)S(1)}, u32[]{:S(2)}, u32[]{:S(2)}) %collective-permute-start.9) | collective-permute-done | bytes 8224 | tf_op jit(solution)/shard_map/ppermute | solution.py:210
  53.6 0.0 collective-permute-start.3
  53.6 0.0 collective-permute-done.8
  53.6 0.6 pad_maximum_fusion.3.south_ref
  54.2 0.0 collective-permute-done
  54.2 0.0 collective-permute-done.1.west_ref
  54.2 0.9 %slice.48 = bf16[320,256]{1,0:T(8,128)(2,1)S(1)} slice(bf16[1856,256]{1,0:T(8,128)(2,1)} %collective-permute-done.1.west_ref), slice={[1536:1856], [0:256]} | slice | bytes 327680 | tf_op jit(solution)/shard_map/slice | solution.py:223
  55.2 0.1 constant_dynamic-update-slice_fusion.2
  55.3 0.0 collective-permute-done.2.east_ref
  55.3 0.9 %slice.49 = bf16[320,256]{1,0:T(8,128)(2,1)S(1)} slice(bf16[1856,256]{1,0:T(8,128)(2,1)} %collective-permute-done.2.east_ref), slice={[1536:1856], [0:256]} | slice | bytes 327680 | tf_op jit(solution)/shard_map/slice | solution.py:224
  56.2 5.1 %collective-permute-done.3 = bf16[10,32,256]{2,1,0:T(8,128)(2,1)S(1)} collective-permute-done((bf16[10,32,256]{2,1,0:T(8,128)(2,1)S(1)}, bf16[10,32,256]{2,1,0:T(8,128)(2,1)S(1)}, u32[]{:S(2)}, u32[]{:S(2)}) %collective-permute-start.3) | collective-permute-done | bytes 163872 | tf_op jit(solution)/shard_map/ppermute | solution.py:19
  61.4 1.0 %pad.20.ext_ref = bf16[11,160,256]{2,1,0:T(8,128)(2,1)} pad(bf16[10,160,256]{2,1,0:T(8,128)(2,1)S(1)} %constant_dynamic-update-slice_fusion, bf16[]{:T(256)} %constant.8.clone.1), padding=0_1x0_0x0_0 | pad | bytes 1720322 | tf_op jit(solution)/shard_map/jit(_pad)/pad | solution.py:227
  62.4 12.4 %shard_map.55.prev_ref = bf16[96,32,256]{2,1,0:T(8,128)(2,1)} custom-call(s32[2]{0:T(128)} %pad_add_fusion.scalar_ref, bf16[96,9,256]{2,1,0:T(8,128)(2,1)} %pad.24.src_ref, bf16[96,32,256]{2,1,0:T(8,128)(2,1)} %f_ref.3, bf16[96,32,256]{2,1,0:T(8,128)(2,1)} %f_ref.3, bf16[1856,256]{1,0:T(8,128)(2,1)} %collective-permute-done.1.west_ref, ...), custom_call_target="tpu_custom_call" | custom-call | tf_op jit(solution)/shard_map/pallas_call | solution.py:141
  74.8 3.0 %shard_map.56 = bf16[96,32,256]{2,1,0:T(8,128)(2,1)} custom-call(s32[2]{0:T(128)} %pad_add_fusion.scalar_ref, bf16[11,160,256]{2,1,0:T(8,128)(2,1)} %pad.20.ext_ref, bf16[8,9,512]{2,1,0:T(8,128)(2,1)} %pad.22.src_ref, bf16[96,32,256]{2,1,0:T(8,128)(2,1)} %f_ref.3, bf16[9,256,256]{2,1,0:T(8,128)(2,1)} %w_ref.3, ...), custom_call_target="tpu_custom_call", output_to_operand_aliasing={{}: (5, {})} | custom-call | tf_op jit(solution)/shard_map/pallas_call | solution.py:164
  (11 shorter events, 0.1 us)
Async XLA Ops:
  0.0 1.9 %copy-start = (bf16[96,32,256]{2,1,0:T(8,128)(2,1)S(1)}, bf16[96,32,256]{2,1,0:T(8,128)(2,1)}, u32[]{:S(2)}) copy-start(bf16[96,32,256]{2,1,0:T(8,128)(2,1)} %f_ref.3) | copy-start | bytes 4718596
  1.9 19.1 %copy-start.3 = (s32[96]{0:T(128)S(1)}, s32[96]{0:T(128)}, u32[]{:S(2)}) copy-start(s32[96]{0:T(128)} %param.8) | copy-start | bytes 1156
  2.0 19.2 %copy-start.1 = (f32[96,3,129]{0,2,1:T(8,128)S(1)}, f32[96,3,129]{0,2,1:T(8,128)}, u32[]{:S(2)}) copy-start(f32[96,3,129]{0,2,1:T(8,128)} %param.6) | copy-start | bytes 445828
  2.0 19.2 %copy-start.2 = (s32[96,3,129]{0,2,1:T(8,128)S(1)}, s32[96,3,129]{0,2,1:T(8,128)}, u32[]{:S(2)}) copy-start(s32[96,3,129]{0,2,1:T(8,128)} %param.7) | copy-start | bytes 445828
  3.4 50.8 %collective-permute-start.1 = (bf16[1856,256]{1,0:T(8,128)(2,1)}, bf16[1856,256]{1,0:T(8,128)(2,1)}, u32[]{:S(2)}, u32[]{:S(2)}) collective-permute-start(bf16[1856,256]{1,0:T(8,128)(2,1)} %get-tuple-element.14), channel_id=1, source_target_pairs={{31,0},{0,1},{1,2},{2,3},{3,4},{4,5},{5,6},{6,7},{7,8},{8,9},{9,10... | collective-permute-start | bytes 2850824 | tf_op jit(solution)/shard_map/ppermute | solution.py:19
  7.6 47.6 %collective-permute-start.2 = (bf16[1856,256]{1,0:T(8,128)(2,1)}, bf16[1856,256]{1,0:T(8,128)(2,1)}, u32[]{:S(2)}, u32[]{:S(2)}) collective-permute-start(bf16[1856,256]{1,0:T(8,128)(2,1)} %get-tuple-element.13), channel_id=1, source_target_pairs={{1,0},{2,1},{3,2},{4,3},{5,4},{6,5},{7,6},{8,7},{9,8},{10,9},{11,1... | collective-permute-start | bytes 2850824 | tf_op jit(solution)/shard_map/ppermute | solution.py:19
  7.6 22.4 %collective-permute-start.4 = (bf16[1,16,256]{2,1,0:T(8,128)(2,1)S(1)}, bf16[1,16,256]{2,1,0:T(8,128)(2,1)S(1)}, u32[]{:S(2)}, u32[]{:S(2)}) collective-permute-start(bf16[1,16,256]{2,1,0:T(8,128)(2,1)S(1)} %get-tuple-element.8), channel_id=1, source_target_pairs={{31,32},{0,33},{1,34},{2,35},{3,36},{4,37},{5,38},{6,39},{7,40},{8... | collective-permute-start | bytes 24584 | tf_op jit(solution)/shard_map/ppermute | solution.py:210
  15.9 22.1 %collective-permute-start.6 = (bf16[1,16,256]{2,1,0:T(8,128)(2,1)S(1)}, bf16[1,16,256]{2,1,0:T(8,128)(2,1)S(1)}, u32[]{:S(2)}, u32[]{:S(2)}) collective-permute-start(bf16[1,16,256]{2,1,0:T(8,128)(2,1)S(1)} %get-tuple-element.7), channel_id=1, source_target_pairs={{1,32},{2,33},{3,34},{4,35},{5,36},{6,37},{7,38},{8,39},{9,40},{10... | collective-permute-start | bytes 24584 | tf_op jit(solution)/shard_map/ppermute | solution.py:210
  17.8 28.2 %collective-permute-start.5 = (bf16[1,32,256]{2,1,0:T(8,128)(2,1)S(1)}, bf16[1,32,256]{2,1,0:T(8,128)(2,1)S(1)}, u32[]{:S(2)}, u32[]{:S(2)}) collective-permute-start(bf16[1,32,256]{2,1,0:T(8,128)(2,1)S(1)} %get-tuple-element.10), channel_id=1, source_target_pairs={{0,32},{1,33},{2,34},{3,35},{4,36},{5,37},{6,38},{7,39},{8,40},{9,... | collective-permute-start | bytes 49160 | tf_op jit(solution)/shard_map/ppermute | solution.py:210
  30.0 14.1 %collective-permute-start.7 = (bf16[1,16,256]{2,1,0:T(8,128)(2,1)S(1)}, bf16[1,16,256]{2,1,0:T(8,128)(2,1)S(1)}, u32[]{:S(2)}, u32[]{:S(2)}) collective-permute-start(bf16[1,16,256]{2,1,0:T(8,128)(2,1)S(1)} %get-tuple-element.5), channel_id=1, source_target_pairs={{63,0},{32,1},{33,2},{34,3},{35,4},{36,5},{37,6},{38,7},{39,8},{40... | collective-permute-start | bytes 24584 | tf_op jit(solution)/shard_map/ppermute | solution.py:210
  38.0 16.1 %collective-permute-start = (bf16[10,32,256]{2,1,0:T(8,128)(2,1)S(1)}, bf16[10,32,256]{2,1,0:T(8,128)(2,1)S(1)}, u32[]{:S(2)}, u32[]{:S(2)}) collective-permute-start(bf16[10,32,256]{2,1,0:T(8,128)(2,1)S(1)} %fusion.2), channel_id=1, source_target_pairs={{30,0},{31,1},{0,2},{1,3},{2,4},{3,5},{4,6},{5,7},{6,8},{7,9},{8,1... | collective-permute-start | bytes 491528 | tf_op jit(solution)/shard_map/ppermute | solution.py:19
  44.1 9.5 %collective-permute-start.9 = (bf16[1,16,256]{2,1,0:T(8,128)(2,1)S(1)}, bf16[1,16,256]{2,1,0:T(8,128)(2,1)S(1)}, u32[]{:S(2)}, u32[]{:S(2)}) collective-permute-start(bf16[1,16,256]{2,1,0:T(8,128)(2,1)S(1)} %get-tuple-element.6), channel_id=1, source_target_pairs={{33,0},{34,1},{35,2},{36,3},{37,4},{38,5},{39,6},{40,7},{41,8},{42... | collective-permute-start | bytes 24584 | tf_op jit(solution)/shard_map/ppermute | solution.py:210
  46.0 7.5 %collective-permute-start.8 = (bf16[1,32,256]{2,1,0:T(8,128)(2,1)S(1)}, bf16[1,32,256]{2,1,0:T(8,128)(2,1)S(1)}, u32[]{:S(2)}, u32[]{:S(2)}) collective-permute-start(bf16[1,32,256]{2,1,0:T(8,128)(2,1)S(1)} %get-tuple-element.9), channel_id=1, source_target_pairs={{32,0},{33,1},{34,2},{35,3},{36,4},{37,5},{38,6},{39,7},{40,8},{41... | collective-permute-start | bytes 49160 | tf_op jit(solution)/shard_map/ppermute | solution.py:210
  53.6 7.8 %collective-permute-start.3 = (bf16[10,32,256]{2,1,0:T(8,128)(2,1)S(1)}, bf16[10,32,256]{2,1,0:T(8,128)(2,1)S(1)}, u32[]{:S(2)}, u32[]{:S(2)}) collective-permute-start(bf16[10,32,256]{2,1,0:T(8,128)(2,1)S(1)} %fusion.2), channel_id=1, source_target_pairs={{2,0},{3,1},{4,2},{5,3},{6,4},{7,5},{8,6},{9,7},{10,8},{11,9},{12,... | collective-permute-start | bytes 491528 | tf_op jit(solution)/shard_map/ppermute | solution.py:19

commit v12 on v7

--- a/solution.py
+++ b/solution.py
@@ -10,6 +10,7 @@
 POLAR = 8
 NEAR = 16
 BLOCK = 8
+NEAR_BLOCK = 16
 
 
 def shifted(block, axis, distance):
@@ -68,15 +69,16 @@
 
 
 def near_kernel(scalar_ref, src_ref, f_ref, all_ref, west_ref, east_ref, north_ref,
-                south_ref, w_ref, o_ref, ext_scr, conv_scr):
+                south_ref, w_ref, *rest, first, lowest):
+    o_ref, ext_scr, conv_scr = rest[-3], rest[-2], rest[-1]
     rows, columns, channels = f_ref.shape
     lat_rows = all_ref.shape[0]
     halo = (ext_scr.shape[1] - columns) // 2
     step = pl.program_id(0)
-    base = step * rows
+    base = first + step * rows
 
     def sides(k, row):
-        start = pl.multiple_of((row + 1) * halo, halo)
+        start = pl.multiple_of((row - lowest) * halo, halo)
         ext_scr[k, :halo] = west_ref[pl.ds(start, halo)]
         ext_scr[k, halo + columns :] = east_ref[pl.ds(start, halo)]
 
@@ -85,19 +87,19 @@
     for k in range(1, rows + 1):
         ext_scr[k, halo : halo + columns] = all_ref[base + k - 1]
 
-    @pl.when(step == 0)
+    @pl.when(base == 0)
     def _():
         ext_scr[0, halo : halo + columns] = north_ref[0]
 
-    @pl.when(step > 0)
+    @pl.when(base > 0)
     def _():
         ext_scr[0, halo : halo + columns] = all_ref[jnp.maximum(base - 1, 0)]
 
-    @pl.when(step == pl.num_programs(0) - 1)
+    @pl.when(base + rows == lat_rows)
     def _():
         ext_scr[rows + 1, halo : halo + columns] = south_ref[0]
 
-    @pl.when(step < pl.num_programs(0) - 1)
+    @pl.when(base + rows < lat_rows)
     def _():
         ext_scr[rows + 1, halo : halo + columns] = all_ref[jnp.minimum(base + rows, lat_rows - 1)]
 
@@ -119,30 +121,40 @@
     return pl.BlockSpec(shape, lambda i, s: (0,) * len(shape))
 
 
-def near_call(scalars, sources, features, west, east, north, south, mix_weight):
+def near_call(scalars, sources, features, west, east, north, south, mix_weight,
+              first, count_rows, lowest, previous=None):
     lat_rows, columns, channels = features.shape
     count = mix_weight.shape[0]
     halo = NEAR
-    row_map = lambda i, s: (i, 0, 0)
+    offset = first // NEAR_BLOCK
+    row_map = lambda i, s: (i + offset, 0, 0)
+    in_specs = [
+        pl.BlockSpec((NEAR_BLOCK,) + sources.shape[1:], row_map),
+        pl.BlockSpec((NEAR_BLOCK, columns, channels), row_map),
+        full_spec(features.shape), full_spec(west.shape), full_spec(east.shape),
+        full_spec(north.shape), full_spec(south.shape), full_spec(mix_weight.shape),
+    ]
+    operands = [scalars, sources, features, features, west, east, north, south, mix_weight]
+    aliases = {}
+    if previous is not None:
+        in_specs.append(pl.BlockSpec(memory_space=pl.ANY))
+        operands.append(previous)
+        aliases = {len(operands) - 1: 0}
     grid_spec = pltpu.PrefetchScalarGridSpec(
         num_scalar_prefetch=1,
-        grid=(lat_rows // BLOCK,),
-        in_specs=[
-            pl.BlockSpec((BLOCK,) + sources.shape[1:], row_map),
-            pl.BlockSpec((BLOCK, columns, channels), row_map),
-            full_spec(features.shape), full_spec(west.shape), full_spec(east.shape),
-            full_spec(north.shape), full_spec(south.shape), full_spec(mix_weight.shape),
-        ],
-        out_specs=pl.BlockSpec((BLOCK, columns, channels), row_map),
+        grid=(count_rows // NEAR_BLOCK,),
+        in_specs=in_specs,
+        out_specs=pl.BlockSpec((NEAR_BLOCK, columns, channels), row_map),
         scratch_shapes=[
-            pltpu.VMEM((BLOCK + 3, columns + 2 * halo, channels), features.dtype),
-            pltpu.VMEM((count, BLOCK * columns, channels), jnp.bfloat16),
+            pltpu.VMEM((NEAR_BLOCK + 3, columns + 2 * halo, channels), features.dtype),
+            pltpu.VMEM((count, NEAR_BLOCK * columns, channels), jnp.bfloat16),
         ],
     )
     return pl.pallas_call(
-        near_kernel, grid_spec=grid_spec,
+        functools.partial(near_kernel, first=first, lowest=lowest), grid_spec=grid_spec,
         out_shape=jax.ShapeDtypeStruct(features.shape, features.dtype),
-    )(scalars, sources, features, features, west, east, north, south, mix_weight)
+        input_output_aliases=aliases,
+    )(*operands)
 
 
 def wide_call(scalars, extended, sources, features, mix_weight, previous):
@@ -191,11 +203,16 @@
     north = lax.ppermute(features[lat_rows - 1 :], "lat", up)
     south = lax.ppermute(features[:1], "lat", down)
     padded = jnp.concatenate([north, features, south], axis=0)
-    near_count = (lat_rows + 2) * NEAR
+    half = lat_rows // 2
+    head = padded[: half + 2]
+    tail = padded[half:]
+    head_west = shifted(head[:, columns - NEAR :].reshape(-1, channels), "lon", 1)
+    head_east = shifted(head[:, :NEAR].reshape(-1, channels), "lon", -1)
     from_west = shifted(jnp.concatenate(
-        [padded[:, columns - NEAR :].reshape(-1, channels), flat_window]), "lon", 1)
+        [tail[:, columns - NEAR :].reshape(-1, channels), flat_window]), "lon", 1)
     from_east = shifted(jnp.concatenate(
-        [padded[:, :NEAR].reshape(-1, channels), flat_window]), "lon", -1)
+        [tail[:, :NEAR].reshape(-1, channels), flat_window]), "lon", -1)
+    near_count = tail.shape[0] * NEAR
     west_far = [shifted(window, "lon", hop) for hop in range(hops, 1, -1)]
     east_far = [shifted(window, "lon", -hop) for hop in range(2, hops + 1)]
 
@@ -205,8 +222,10 @@
     polar_values = lax.dynamic_slice_in_dim(basis_values, start, POLAR, 0)
     wide_sources = flat_sources(polar_values, columns + 2 * reach, 512)
 
+    out = near_call(scalars, near_sources, features, head_west, head_east, north, south,
+                    mix_weight, 0, half, -1)
     out = near_call(scalars, near_sources, features, from_west, from_east, north, south,
-                    mix_weight)
+                    mix_weight, half, lat_rows - half, half - 1, previous=out)
 
     west_one = from_west[near_count:].reshape(window.shape)
     east_one = from_east[near_count:].reshape(window.shape)

time: 77.5 us -> 60.2 us (0.78)
  waiting for transfers between devices: 18.5 us -> 5.62 us
  Pallas kernels: 24.4 us -> 19.5 us
  starting transfers between devices: 17 us -> 21.2 us
  local copies, waits for them, and re-layouts: 11.7 us -> 9.52 us
  other arithmetic: 5.29 us -> 3.29 us
    ppermute x4 -> x6, waiting for transfers between devices: 13.8 us -> 5.62 us  [shifted(): return lax.ppermute(block, axis, route)]
    pallas_call x1 -> x2, Pallas kernels: 21.5 us -> 16.5 us  [near_call(): pl.pallas_call(functools.partial(near_kernel, first=first, lowest=lowest)...]
    ppermute x1, waiting for transfers between devices: 4.65 us -> 0.01 us  [body(): north = lax.ppermute(features[lat_rows - 1:], 'lat', up)]
    ppermute x4 -> x6, starting transfers between devices: 9.6 us -> 13.8 us  [shifted(): return lax.ppermute(block, axis, route)]
    slice x2 -> x3, local copies, waits for them, and re-layouts: 0.12 us -> 1.88 us  [the longest x1 0.95 us: body(): head_east = shifted(head[:, :NEAR].reshape(-1, channels), 'lon', -1)]
    ppermute x1, starting transfers between devices: 5.5 us -> 4.19 us  [body(): south = lax.ppermute(features[:1], 'lat', down)]
    reshape x2, local copies, waits for them, and re-layouts: 2.92 us -> 1.65 us  [flat_sources(): flat = flat.reshape(rows, count, offsets * span)]
    ppermute x1, starting transfers between devices: 1.92 us -> 3.19 us  [body(): north = lax.ppermute(features[lat_rows - 1:], 'lat', up)]
  transfers between devices with their start and end apart: 6 -> 8, of which waited for: 3 -> 1; matrix products, arithmetic and copies ran while one was open for 17% -> 18% of each run, Pallas kernels for 0% -> 14%
where the time goes in v12:
time: 60.2 us; the launch traced here: 59.4 us
  starting transfers between devices  21.2 us (35%)
  Pallas kernels  19.5 us (32%)
  local copies, waits for them, and re-layouts  9.52 us (16%)
  waiting for transfers between devices  5.62 us (9%)
  other arithmetic  3.29 us (5%)
    pallas_call x2, Pallas kernels, near_call(): pl.pallas_call(functools.partial(near_kernel, first=first, lowest=lowest)...  16.5 us
    ppermute x6, starting transfers between devices, shifted(): return lax.ppermute(block, axis, route)  13.8 us
    ppermute x6, waiting for transfers between devices, shifted(): return lax.ppermute(block, axis, route)  5.62 us
    ppermute x1, starting transfers between devices, body(): south = lax.ppermute(features[:1], 'lat', down)  4.19 us
    ppermute x1, starting transfers between devices, body(): north = lax.ppermute(features[lat_rows - 1:], 'lat', up)  3.19 us
    pallas_call x1, Pallas kernels, wide_call(): pl.pallas_call(wide_kernel, grid_spec=grid_spec, out_shape=jax.ShapeDtype...  2.97 us
    pad x2, local copies, waits for them, and re-layouts, flat_sources(): return jnp.pad(flat, ((0, 0), (0, 0), (0, lanes - offsets * span)))  1.75 us
    reshape x2, local copies, waits for them, and re-layouts, flat_sources(): flat = flat.reshape(rows, count, offsets * span)  1.65 us
  transfers between devices with their start and end apart: 8, of which 1 were waited for; matrix products, arithmetic and copies ran while one was open for 18% of the time, Pallas kernels for 14%

profile of v12, /device:TPU:3, one launch (start us, length us, event | category | flops | bytes accessed | tf_op | source)
XLA Modules:
  0.0 59.4 jit_solution(8553865610690353245)
XLA Ops:
  0.0 0.0 copy-start
  0.0 0.0 copy-start.7
  0.0 0.9 %fusion.5 = (bf16[1,32,256]{2,1,0:T(8,128)(2,1)S(1)}, bf16[1,32,256]{2,1,0:T(8,128)(2,1)S(1)}) fusion(bf16[96,32,256]{2,1,0:T(8,128)(2,1)} %f_ref.5), kind=kLoop, calls=%fused_computation.26 | loop fusion | bytes 65536 | tf_op jit(solution)/shard_map/slice | solution.py:203
  0.9 3.2 %collective-permute-start.5 = (bf16[1,32,256]{2,1,0:T(8,128)(2,1)S(1)}, bf16[1,32,256]{2,1,0:T(8,128)(2,1)S(1)}, u32[]{:S(2)}, u32[]{:S(2)}) collective-permute-start(bf16[1,32,256]{2,1,0:T(8,128)(2,1)S(1)} %get-tuple-element.11), channel_id=1, source_target_pairs={{0,32},{32,64},{64,96},{96,128},{128,160},{160,192},{192,224},{1,3... | collective-permute-start | bytes 49160 | tf_op jit(solution)/shard_map/ppermute | solution.py:203
  4.1 4.2 %collective-permute-start.1 = (bf16[1,32,256]{2,1,0:T(8,128)(2,1)S(1)}, bf16[1,32,256]{2,1,0:T(8,128)(2,1)S(1)}, u32[]{:S(2)}, u32[]{:S(2)}) collective-permute-start(bf16[1,32,256]{2,1,0:T(8,128)(2,1)S(1)} %get-tuple-element.12), channel_id=1, source_target_pairs={{32,0},{64,32},{96,64},{128,96},{160,128},{192,160},{224,192},{33,... | collective-permute-start | bytes 49160 | tf_op jit(solution)/shard_map/ppermute | solution.py:204
  8.3 1.0 %fusion.2 = bf16[10,32,256]{2,1,0:T(8,128)(2,1)S(1)} fusion(s32[]{:T(128)} %select_n.10, bf16[1,32,256]{2,1,0:T(8,128)(2,1)S(1)} %broadcast_in_dim.10, bf16[96,32,256]{2,1,0:T(8,128)(2,1)} %f_ref.5), kind=kLoop, calls=%fused_computation.9 | loop fusion | flops 163840 | bytes 1753092 | tf_op jit(solution)/shard_map/concatenate | solution.py:198
  9.3 1.9 %collective-permute-start = (bf16[10,32,256]{2,1,0:T(8,128)(2,1)S(1)}, bf16[10,32,256]{2,1,0:T(8,128)(2,1)}, u32[]{:S(2)}, u32[]{:S(2)}) collective-permute-start(bf16[10,32,256]{2,1,0:T(8,128)(2,1)S(1)} %fusion.2), channel_id=1, source_target_pairs={{30,0},{31,1},{0,2},{1,3},{2,4},{3,5},{4,6},{5,7},{6,8},{7,9},{8,1... | collective-permute-start | bytes 491528 | tf_op jit(solution)/shard_map/ppermute | solution.py:19
  11.2 0.0 copy-done.7
  11.2 0.1 broadcast_compare_fusion
  11.3 0.0 collective-permute-done.5.north_ref
  11.3 0.0 copy-start.5
  11.3 0.0 copy-done
  11.3 0.2 constant_dynamic-update-slice_fusion.7
  11.6 0.3 copy-done.5
  11.9 1.0 %fusion.3 = (bf16[50,16,256]{2,1,0:T(8,128)(2,1)}, bf16[50,16,256]{2,1,0:T(8,128)(2,1)}) fusion(bf16[97,32,256]{2,1,0:T(8,128)(2,1)S(1)} %get-tuple-element.9), kind=kLoop, calls=%fused_computation.24 | loop fusion | bytes 1638400 | tf_op jit(solution)/shard_map/slice | solution.py:210
  12.9 3.9 %collective-permute-start.6 = (bf16[800,256]{1,0:T(8,128)(2,1)}, bf16[800,256]{1,0:T(8,128)(2,1)}, u32[]{:S(2)}, u32[]{:S(2)}) collective-permute-start(bf16[800,256]{1,0:T(8,128)(2,1)} %bitcast.9), channel_id=1, source_target_pairs={{31,0},{0,1},{1,2},{2,3},{3,4},{4,5},{5,6},{6,7},{7,8},{8,9},{9,10... | collective-permute-start | bytes 1228808 | tf_op jit(solution)/shard_map/ppermute | solution.py:19
  16.7 0.0 collective-permute-start.7
  16.7 0.0 collective-permute-done.1.south_ref
  16.8 0.0 copy-start.6
  16.8 0.0 copy-start.3
  16.8 0.0 copy-start.4
  16.8 0.1 fusion.4
  16.9 1.1 %pad_maximum_fusion = (bf16[1120,256]{1,0:T(8,128)(2,1)}, bf16[1120,256]{1,0:T(8,128)(2,1)}) fusion(bf16[320,256]{1,0:T(8,128)(2,1)S(1)} %bitcast.15, bf16[800,256]{1,0:T(8,128)(2,1)S(1)} %bitcast.13, bf16[800,256]{1,0:T(8,128)(2,1)S(1)} %bitcast.14), kind=kLoop, calls=%fused_computation.6 | loop fusion | flops 2007040 | bytes 2129920 | tf_op jit(solution)/shard_map/concatenate | solution.py:213
  17.9 0.0 copy-done.6
  17.9 3.2 %collective-permute-start.2 = (bf16[1120,256]{1,0:T(8,128)(2,1)}, bf16[1120,256]{1,0:T(8,128)(2,1)S(1)}, u32[]{:S(2)}, u32[]{:S(2)}) collective-permute-start(bf16[1120,256]{1,0:T(8,128)(2,1)} %get-tuple-element.14), channel_id=1, source_target_pairs={{31,0},{0,1},{1,2},{2,3},{3,4},{4,5},{5,6},{6,7},{7,8},{8,9},{9,10... | collective-permute-start | bytes 1720328 | tf_op jit(solution)/shard_map/ppermute | solution.py:19
  21.2 0.0 copy-done.3
  21.2 0.0 copy-done.4
  21.2 0.4 multiply_convert_fusion
  21.6 0.1 collective-permute-start.3
  21.7 0.3 constant_dynamic-slice_fusion
  22.1 0.1 pad.23
  22.2 1.0 %copy.12 = bf16[96,9,192]{2,1,0:T(8,128)(2,1)S(1)} copy(bf16[96,9,192]{0,2,1:T(8,128)(2,1)S(1)} %bitcast.12) | data formatting | bytes 663552 | tf_op jit(solution)/shard_map/reshape | solution.py:45
  23.2 1.1 %pad.24.src_ref = bf16[96,9,256]{2,1,0:T(8,128)(2,1)} pad(bf16[96,9,192]{2,1,0:T(8,128)(2,1)S(1)} %copy.12, bf16[]{:T(256)} %constant.8.clone.1), padding=0_0x0_0x0_64 | pad | bytes 774146 | tf_op jit(solution)/shard_map/jit(_pad)/pad | solution.py:46
  24.3 0.2 pad.21
  24.5 0.6 %copy.11 = bf16[8,9,480]{2,1,0:T(8,128)(2,1)S(1)} copy(bf16[8,9,480]{0,2,1:T(8,128)(2,1)S(1)} %bitcast.11) | data formatting | bytes 138240 | tf_op jit(solution)/shard_map/reshape | solution.py:45
  25.1 0.7 %pad.22.src_ref = bf16[8,9,512]{2,1,0:T(8,128)(2,1)} pad(bf16[8,9,480]{2,1,0:T(8,128)(2,1)S(1)} %copy.11, bf16[]{:T(256)} %constant.8.clone.1), padding=0_0x0_0x0_32 | pad | bytes 142850 | tf_op jit(solution)/shard_map/jit(_pad)/pad | solution.py:46
  25.8 0.6 %pad_add_fusion.scalar_ref = s32[2]{0:T(128)} fusion(s32[1]{0:T(128)} %bitcast.1, s32[1]{0:T(128)} %bitcast), kind=kLoop, calls=%fused_computation.22 | loop fusion | flops 2 | bytes 16 | tf_op jit(solution)/shard_map/stack | solution.py:194
  26.5 0.0 collective-permute-done
  26.5 4.7 %collective-permute-start.4 = (bf16[10,32,256]{2,1,0:T(8,128)(2,1)S(1)}, bf16[10,32,256]{2,1,0:T(8,128)(2,1)S(1)}, u32[]{:S(2)}, u32[]{:S(2)}) collective-permute-start(bf16[10,32,256]{2,1,0:T(8,128)(2,1)S(1)} %fusion.2), channel_id=1, source_target_pairs={{2,0},{3,1},{4,2},{5,3},{6,4},{7,5},{8,6},{9,7},{10,8},{11,9},{12,... | collective-permute-start | bytes 491528 | tf_op jit(solution)/shard_map/ppermute | solution.py:19
  31.2 0.9 %constant_dynamic-update-slice_fusion.6 = bf16[10,160,256]{2,1,0:T(8,128)(2,1)S(1)} fusion(bf16[10,32,256]{2,1,0:T(8,128)(2,1)} %collective-permute-done), kind=kLoop, calls=%fused_computation.17 | loop fusion | bytes 327680
  32.1 0.0 collective-permute-done.6.west_ref
  32.1 5.6 %collective-permute-done.7.east_ref = bf16[800,256]{1,0:T(8,128)(2,1)} collective-permute-done((bf16[800,256]{1,0:T(8,128)(2,1)}, bf16[800,256]{1,0:T(8,128)(2,1)}, u32[]{:S(2)}, u32[]{:S(2)}) %collective-permute-start.7) | collective-permute-done | bytes 409632 | tf_op jit(solution)/shard_map/ppermute | solution.py:19
  37.7 0.0 copy-start.1
  37.7 8.3 %shard_map.55.rest_0_ = bf16[96,32,256]{2,1,0:T(8,128)(2,1)} custom-call(s32[2]{0:T(128)} %pad_add_fusion.scalar_ref, bf16[96,9,256]{2,1,0:T(8,128)(2,1)} %pad.24.src_ref, bf16[96,32,256]{2,1,0:T(8,128)(2,1)} %f_ref.5, bf16[96,32,256]{2,1,0:T(8,128)(2,1)} %f_ref.5, bf16[800,256]{1,0:T(8,128)(2,1)} %collective-permute-done.6.west_ref, ...), custom_call_target="tpu_custom_call" | custom-call | tf_op jit(solution)/shard_map/pallas_call | solution.py:153
  46.0 0.0 collective-permute-done.2.west_ref
  46.0 0.0 copy-start.2
  46.1 0.0 copy-done.1
  46.1 0.1 constant_dynamic-update-slice_fusion.4
  46.1 0.0 collective-permute-done.3.east_ref
  46.2 1.0 %slice.47 = bf16[320,256]{1,0:T(8,128)(2,1)S(1)} slice(bf16[1120,256]{1,0:T(8,128)(2,1)} %collective-permute-done.3.east_ref), slice={[800:1120], [0:256]} | slice | bytes 327680 | tf_op jit(solution)/shard_map/slice | solution.py:231
  47.2 0.0 collective-permute-done.4
  47.2 0.0 copy-done.2
  47.2 1.0 %pad.20.ext_ref = bf16[11,160,256]{2,1,0:T(8,128)(2,1)} pad(bf16[10,160,256]{2,1,0:T(8,128)(2,1)S(1)} %constant_dynamic-update-slice_fusion.2, bf16[]{:T(256)} %constant.8.clone.1), padding=0_1x0_0x0_0 | pad | bytes 1720322 | tf_op jit(solution)/shard_map/jit(_pad)/pad | solution.py:234
  48.2 8.2 %shard_map.56.prev_ref = bf16[96,32,256]{2,1,0:T(8,128)(2,1)} custom-call(s32[2]{0:T(128)} %pad_add_fusion.scalar_ref, bf16[96,9,256]{2,1,0:T(8,128)(2,1)} %pad.24.src_ref, bf16[96,32,256]{2,1,0:T(8,128)(2,1)} %f_ref.5, bf16[96,32,256]{2,1,0:T(8,128)(2,1)} %f_ref.5, bf16[1120,256]{1,0:T(8,128)(2,1)} %copy-done.2, ...), custom_call_target="tpu_custom_call", output_to_operand_aliasing={{}: (9, {})} | custom-call | tf_op jit(solution)/shard_map/pallas_call | solution.py:153
  56.4 3.0 %shard_map.57 = bf16[96,32,256]{2,1,0:T(8,128)(2,1)} custom-call(s32[2]{0:T(128)} %pad_add_fusion.scalar_ref, bf16[11,160,256]{2,1,0:T(8,128)(2,1)} %pad.20.ext_ref, bf16[8,9,512]{2,1,0:T(8,128)(2,1)} %pad.22.src_ref, bf16[96,32,256]{2,1,0:T(8,128)(2,1)} %f_ref.5, bf16[9,256,256]{2,1,0:T(8,128)(2,1)} %w_ref.5, ...), custom_call_target="tpu_custom_call", output_to_operand_aliasing={{}: (5, {})} | custom-call | tf_op jit(solution)/shard_map/pallas_call | solution.py:177
  (10 shorter events, 0.1 us)
Async XLA Ops:
  0.0 11.3 %copy-start = (bf16[96,32,256]{2,1,0:T(8,128)(2,1)S(1)}, bf16[96,32,256]{2,1,0:T(8,128)(2,1)}, u32[]{:S(2)}) copy-start(bf16[96,32,256]{2,1,0:T(8,128)(2,1)} %f_ref.5) | copy-start | bytes 4718596
  0.0 11.2 %copy-start.7 = (s32[96]{0:T(128)S(1)}, s32[96]{0:T(128)}, u32[]{:S(2)}) copy-start(s32[96]{0:T(128)} %param.8) | copy-start | bytes 1156
  0.9 10.4 %collective-permute-start.5 = (bf16[1,32,256]{2,1,0:T(8,128)(2,1)S(1)}, bf16[1,32,256]{2,1,0:T(8,128)(2,1)S(1)}, u32[]{:S(2)}, u32[]{:S(2)}) collective-permute-start(bf16[1,32,256]{2,1,0:T(8,128)(2,1)S(1)} %get-tuple-element.11), channel_id=1, source_target_pairs={{0,32},{32,64},{64,96},{96,128},{128,160},{160,192},{192,224},{1,3... | collective-permute-start | bytes 49160 | tf_op jit(solution)/shard_map/ppermute | solution.py:203
  4.1 12.7 %collective-permute-start.1 = (bf16[1,32,256]{2,1,0:T(8,128)(2,1)S(1)}, bf16[1,32,256]{2,1,0:T(8,128)(2,1)S(1)}, u32[]{:S(2)}, u32[]{:S(2)}) collective-permute-start(bf16[1,32,256]{2,1,0:T(8,128)(2,1)S(1)} %get-tuple-element.12), channel_id=1, source_target_pairs={{32,0},{64,32},{96,64},{128,96},{160,128},{192,160},{224,192},{33,... | collective-permute-start | bytes 49160 | tf_op jit(solution)/shard_map/ppermute | solution.py:204
  9.3 17.2 %collective-permute-start = (bf16[10,32,256]{2,1,0:T(8,128)(2,1)S(1)}, bf16[10,32,256]{2,1,0:T(8,128)(2,1)}, u32[]{:S(2)}, u32[]{:S(2)}) collective-permute-start(bf16[10,32,256]{2,1,0:T(8,128)(2,1)S(1)} %fusion.2), channel_id=1, source_target_pairs={{30,0},{31,1},{0,2},{1,3},{2,4},{3,5},{4,6},{5,7},{6,8},{7,9},{8,1... | collective-permute-start | bytes 491528 | tf_op jit(solution)/shard_map/ppermute | solution.py:19
  11.3 0.6 %copy-start.5 = (bf16[1,32,256]{2,1,0:T(8,128)(2,1)}, bf16[1,32,256]{2,1,0:T(8,128)(2,1)S(1)}, u32[]{:S(2)}) copy-start(bf16[1,32,256]{2,1,0:T(8,128)(2,1)S(1)} %collective-permute-done.5.north_ref) | copy-start | bytes 49156
  12.9 19.3 %collective-permute-start.6 = (bf16[800,256]{1,0:T(8,128)(2,1)}, bf16[800,256]{1,0:T(8,128)(2,1)}, u32[]{:S(2)}, u32[]{:S(2)}) collective-permute-start(bf16[800,256]{1,0:T(8,128)(2,1)} %bitcast.9), channel_id=1, source_target_pairs={{31,0},{0,1},{1,2},{2,3},{3,4},{4,5},{5,6},{6,7},{7,8},{8,9},{9,10... | collective-permute-start | bytes 1228808 | tf_op jit(solution)/shard_map/ppermute | solution.py:19
  16.7 21.0 %collective-permute-start.7 = (bf16[800,256]{1,0:T(8,128)(2,1)}, bf16[800,256]{1,0:T(8,128)(2,1)}, u32[]{:S(2)}, u32[]{:S(2)}) collective-permute-start(bf16[800,256]{1,0:T(8,128)(2,1)} %bitcast.10), channel_id=1, source_target_pairs={{1,0},{2,1},{3,2},{4,3},{5,4},{6,5},{7,6},{8,7},{9,8},{10,9},{11,1... | collective-permute-start | bytes 1228808 | tf_op jit(solution)/shard_map/ppermute | solution.py:19
  16.8 1.2 %copy-start.6 = (bf16[1,32,256]{2,1,0:T(8,128)(2,1)}, bf16[1,32,256]{2,1,0:T(8,128)(2,1)S(1)}, u32[]{:S(2)}) copy-start(bf16[1,32,256]{2,1,0:T(8,128)(2,1)S(1)} %collective-permute-done.1.south_ref) | copy-start | bytes 49156
  16.8 4.4 %copy-start.3 = (f32[96,3,129]{0,2,1:T(8,128)S(1)}, f32[96,3,129]{0,2,1:T(8,128)}, u32[]{:S(2)}) copy-start(f32[96,3,129]{0,2,1:T(8,128)} %param.6) | copy-start | bytes 445828
  16.8 4.4 %copy-start.4 = (s32[96,3,129]{0,2,1:T(8,128)S(1)}, s32[96,3,129]{0,2,1:T(8,128)}, u32[]{:S(2)}) copy-start(s32[96,3,129]{0,2,1:T(8,128)} %param.7) | copy-start | bytes 445828
  17.9 28.1 %collective-permute-start.2 = (bf16[1120,256]{1,0:T(8,128)(2,1)}, bf16[1120,256]{1,0:T(8,128)(2,1)S(1)}, u32[]{:S(2)}, u32[]{:S(2)}) collective-permute-start(bf16[1120,256]{1,0:T(8,128)(2,1)} %get-tuple-element.14), channel_id=1, source_target_pairs={{31,0},{0,1},{1,2},{2,3},{3,4},{4,5},{5,6},{6,7},{7,8},{8,9},{9,10... | collective-permute-start | bytes 1720328 | tf_op jit(solution)/shard_map/ppermute | solution.py:19
  21.6 24.5 %collective-permute-start.3 = (bf16[1120,256]{1,0:T(8,128)(2,1)}, bf16[1120,256]{1,0:T(8,128)(2,1)}, u32[]{:S(2)}, u32[]{:S(2)}) collective-permute-start(bf16[1120,256]{1,0:T(8,128)(2,1)} %get-tuple-element.13), channel_id=1, source_target_pairs={{1,0},{2,1},{3,2},{4,3},{5,4},{6,5},{7,6},{8,7},{9,8},{10,9},{11,1... | collective-permute-start | bytes 1720328 | tf_op jit(solution)/shard_map/ppermute | solution.py:19
  26.5 20.7 %collective-permute-start.4 = (bf16[10,32,256]{2,1,0:T(8,128)(2,1)S(1)}, bf16[10,32,256]{2,1,0:T(8,128)(2,1)S(1)}, u32[]{:S(2)}, u32[]{:S(2)}) collective-permute-start(bf16[10,32,256]{2,1,0:T(8,128)(2,1)S(1)} %fusion.2), channel_id=1, source_target_pairs={{2,0},{3,1},{4,2},{5,3},{6,4},{7,5},{8,6},{9,7},{10,8},{11,9},{12,... | collective-permute-start | bytes 491528 | tf_op jit(solution)/shard_map/ppermute | solution.py:19
  37.7 8.3 %copy-start.1 = (bf16[96,32,256]{2,1,0:T(8,128)(2,1)S(1)}, bf16[96,32,256]{2,1,0:T(8,128)(2,1)}, u32[]{:S(2)}) copy-start(bf16[96,32,256]{2,1,0:T(8,128)(2,1)} %f_ref.5) | copy-start | bytes 4718596
  46.0 1.2 %copy-start.2 = (bf16[1120,256]{1,0:T(8,128)(2,1)}, bf16[1120,256]{1,0:T(8,128)(2,1)S(1)}, u32[]{:S(2)}) copy-start(bf16[1120,256]{1,0:T(8,128)(2,1)S(1)} %collective-permute-done.2.west_ref) | copy-start | bytes 1720324

commit v13 on v12

--- a/solution.py
+++ b/solution.py
@@ -10,7 +10,7 @@
 POLAR = 8
 NEAR = 16
 BLOCK = 8
-NEAR_BLOCK = 16
+NEAR_BLOCK = 24
 
 
 def shifted(block, axis, distance):

time: 60.2 us -> 60.1 us (level)
  no operation moved by 1% of the time
where the time goes in v13:
time: 60.1 us; the launch traced here: 59.3 us
  starting transfers between devices  21.2 us (35%)
  Pallas kernels  19.3 us (32%)
  local copies, waits for them, and re-layouts  9.52 us (16%)
  waiting for transfers between devices  5.62 us (9%)
  other arithmetic  3.29 us (5%)
    pallas_call x2, Pallas kernels, near_call(): pl.pallas_call(functools.partial(near_kernel, first=first, lowest=lowest)...  16.4 us
    ppermute x6, starting transfers between devices, shifted(): return lax.ppermute(block, axis, route)  13.8 us
    ppermute x6, waiting for transfers between devices, shifted(): return lax.ppermute(block, axis, route)  5.62 us
    ppermute x1, starting transfers between devices, body(): south = lax.ppermute(features[:1], 'lat', down)  4.19 us
    ppermute x1, starting transfers between devices, body(): north = lax.ppermute(features[lat_rows - 1:], 'lat', up)  3.19 us
    pallas_call x1, Pallas kernels, wide_call(): pl.pallas_call(wide_kernel, grid_spec=grid_spec, out_shape=jax.ShapeDtype...  2.97 us
    pad x2, local copies, waits for them, and re-layouts, flat_sources(): return jnp.pad(flat, ((0, 0), (0, 0), (0, lanes - offsets * span)))  1.75 us
    reshape x2, local copies, waits for them, and re-layouts, flat_sources(): flat = flat.reshape(rows, count, offsets * span)  1.65 us
  transfers between devices with their start and end apart: 8, of which 1 were waited for; matrix products, arithmetic and copies ran while one was open for 18% of the time, Pallas kernels for 14%

profile of v13, /device:TPU:3, one launch (start us, length us, event | category | flops | bytes accessed | tf_op | source)
XLA Modules:
  0.0 59.3 jit_solution(2637296612040066817)
XLA Ops:
  0.0 0.0 copy-start
  0.0 0.0 copy-start.7
  0.0 0.9 %fusion.5 = (bf16[1,32,256]{2,1,0:T(8,128)(2,1)S(1)}, bf16[1,32,256]{2,1,0:T(8,128)(2,1)S(1)}) fusion(bf16[96,32,256]{2,1,0:T(8,128)(2,1)} %f_ref.5), kind=kLoop, calls=%fused_computation.26 | loop fusion | bytes 65536 | tf_op jit(solution)/shard_map/slice | solution.py:203
  0.9 3.2 %collective-permute-start.5 = (bf16[1,32,256]{2,1,0:T(8,128)(2,1)S(1)}, bf16[1,32,256]{2,1,0:T(8,128)(2,1)S(1)}, u32[]{:S(2)}, u32[]{:S(2)}) collective-permute-start(bf16[1,32,256]{2,1,0:T(8,128)(2,1)S(1)} %get-tuple-element.11), channel_id=1, source_target_pairs={{0,32},{32,64},{64,96},{96,128},{128,160},{160,192},{192,224},{1,3... | collective-permute-start | bytes 49160 | tf_op jit(solution)/shard_map/ppermute | solution.py:203
  4.1 4.2 %collective-permute-start.1 = (bf16[1,32,256]{2,1,0:T(8,128)(2,1)S(1)}, bf16[1,32,256]{2,1,0:T(8,128)(2,1)S(1)}, u32[]{:S(2)}, u32[]{:S(2)}) collective-permute-start(bf16[1,32,256]{2,1,0:T(8,128)(2,1)S(1)} %get-tuple-element.12), channel_id=1, source_target_pairs={{32,0},{64,32},{96,64},{128,96},{160,128},{192,160},{224,192},{33,... | collective-permute-start | bytes 49160 | tf_op jit(solution)/shard_map/ppermute | solution.py:204
  8.3 1.0 %fusion.2 = bf16[10,32,256]{2,1,0:T(8,128)(2,1)S(1)} fusion(s32[]{:T(128)} %select_n.10, bf16[1,32,256]{2,1,0:T(8,128)(2,1)S(1)} %broadcast_in_dim.10, bf16[96,32,256]{2,1,0:T(8,128)(2,1)} %f_ref.5), kind=kLoop, calls=%fused_computation.9 | loop fusion | flops 163840 | bytes 1753092 | tf_op jit(solution)/shard_map/concatenate | solution.py:198
  9.3 1.9 %collective-permute-start = (bf16[10,32,256]{2,1,0:T(8,128)(2,1)S(1)}, bf16[10,32,256]{2,1,0:T(8,128)(2,1)}, u32[]{:S(2)}, u32[]{:S(2)}) collective-permute-start(bf16[10,32,256]{2,1,0:T(8,128)(2,1)S(1)} %fusion.2), channel_id=1, source_target_pairs={{30,0},{31,1},{0,2},{1,3},{2,4},{3,5},{4,6},{5,7},{6,8},{7,9},{8,1... | collective-permute-start | bytes 491528 | tf_op jit(solution)/shard_map/ppermute | solution.py:19
  11.2 0.0 copy-done.7
  11.2 0.1 broadcast_compare_fusion
  11.3 0.0 collective-permute-done.5.north_ref
  11.3 0.0 copy-start.5
  11.3 0.0 copy-done
  11.3 0.2 constant_dynamic-update-slice_fusion.7
  11.6 0.3 copy-done.5
  11.9 1.0 %fusion.3 = (bf16[50,16,256]{2,1,0:T(8,128)(2,1)}, bf16[50,16,256]{2,1,0:T(8,128)(2,1)}) fusion(bf16[97,32,256]{2,1,0:T(8,128)(2,1)S(1)} %get-tuple-element.9), kind=kLoop, calls=%fused_computation.24 | loop fusion | bytes 1638400 | tf_op jit(solution)/shard_map/slice | solution.py:210
  12.9 3.9 %collective-permute-start.6 = (bf16[800,256]{1,0:T(8,128)(2,1)}, bf16[800,256]{1,0:T(8,128)(2,1)}, u32[]{:S(2)}, u32[]{:S(2)}) collective-permute-start(bf16[800,256]{1,0:T(8,128)(2,1)} %bitcast.9), channel_id=1, source_target_pairs={{31,0},{0,1},{1,2},{2,3},{3,4},{4,5},{5,6},{6,7},{7,8},{8,9},{9,10... | collective-permute-start | bytes 1228808 | tf_op jit(solution)/shard_map/ppermute | solution.py:19
  16.7 0.0 collective-permute-start.7
  16.7 0.0 collective-permute-done.1.south_ref
  16.8 0.0 copy-start.6
  16.8 0.0 copy-start.3
  16.8 0.0 copy-start.4
  16.8 0.1 fusion.4
  16.9 1.1 %pad_maximum_fusion = (bf16[1120,256]{1,0:T(8,128)(2,1)}, bf16[1120,256]{1,0:T(8,128)(2,1)}) fusion(bf16[320,256]{1,0:T(8,128)(2,1)S(1)} %bitcast.15, bf16[800,256]{1,0:T(8,128)(2,1)S(1)} %bitcast.13, bf16[800,256]{1,0:T(8,128)(2,1)S(1)} %bitcast.14), kind=kLoop, calls=%fused_computation.6 | loop fusion | flops 2007040 | bytes 2129920 | tf_op jit(solution)/shard_map/concatenate | solution.py:213
  17.9 0.0 copy-done.6
  17.9 3.2 %collective-permute-start.2 = (bf16[1120,256]{1,0:T(8,128)(2,1)}, bf16[1120,256]{1,0:T(8,128)(2,1)S(1)}, u32[]{:S(2)}, u32[]{:S(2)}) collective-permute-start(bf16[1120,256]{1,0:T(8,128)(2,1)} %get-tuple-element.14), channel_id=1, source_target_pairs={{31,0},{0,1},{1,2},{2,3},{3,4},{4,5},{5,6},{6,7},{7,8},{8,9},{9,10... | collective-permute-start | bytes 1720328 | tf_op jit(solution)/shard_map/ppermute | solution.py:19
  21.2 0.0 copy-done.3
  21.2 0.0 copy-done.4
  21.2 0.4 multiply_convert_fusion
  21.6 0.1 collective-permute-start.3
  21.7 0.3 constant_dynamic-slice_fusion
  22.1 0.1 pad.23
  22.2 1.0 %copy.12 = bf16[96,9,192]{2,1,0:T(8,128)(2,1)S(1)} copy(bf16[96,9,192]{0,2,1:T(8,128)(2,1)S(1)} %bitcast.12) | data formatting | bytes 663552 | tf_op jit(solution)/shard_map/reshape | solution.py:45
  23.2 1.1 %pad.24.src_ref = bf16[96,9,256]{2,1,0:T(8,128)(2,1)} pad(bf16[96,9,192]{2,1,0:T(8,128)(2,1)S(1)} %copy.12, bf16[]{:T(256)} %constant.8.clone.1), padding=0_0x0_0x0_64 | pad | bytes 774146 | tf_op jit(solution)/shard_map/jit(_pad)/pad | solution.py:46
  24.3 0.2 pad.21
  24.5 0.6 %copy.11 = bf16[8,9,480]{2,1,0:T(8,128)(2,1)S(1)} copy(bf16[8,9,480]{0,2,1:T(8,128)(2,1)S(1)} %bitcast.11) | data formatting | bytes 138240 | tf_op jit(solution)/shard_map/reshape | solution.py:45
  25.1 0.7 %pad.22.src_ref = bf16[8,9,512]{2,1,0:T(8,128)(2,1)} pad(bf16[8,9,480]{2,1,0:T(8,128)(2,1)S(1)} %copy.11, bf16[]{:T(256)} %constant.8.clone.1), padding=0_0x0_0x0_32 | pad | bytes 142850 | tf_op jit(solution)/shard_map/jit(_pad)/pad | solution.py:46
  25.8 0.6 %pad_add_fusion.scalar_ref = s32[2]{0:T(128)} fusion(s32[1]{0:T(128)} %bitcast.1, s32[1]{0:T(128)} %bitcast), kind=kLoop, calls=%fused_computation.22 | loop fusion | flops 2 | bytes 16 | tf_op jit(solution)/shard_map/stack | solution.py:194
  26.5 0.0 collective-permute-done
  26.5 4.7 %collective-permute-start.4 = (bf16[10,32,256]{2,1,0:T(8,128)(2,1)S(1)}, bf16[10,32,256]{2,1,0:T(8,128)(2,1)S(1)}, u32[]{:S(2)}, u32[]{:S(2)}) collective-permute-start(bf16[10,32,256]{2,1,0:T(8,128)(2,1)S(1)} %fusion.2), channel_id=1, source_target_pairs={{2,0},{3,1},{4,2},{5,3},{6,4},{7,5},{8,6},{9,7},{10,8},{11,9},{12,... | collective-permute-start | bytes 491528 | tf_op jit(solution)/shard_map/ppermute | solution.py:19
  31.2 0.9 %constant_dynamic-update-slice_fusion.6 = bf16[10,160,256]{2,1,0:T(8,128)(2,1)S(1)} fusion(bf16[10,32,256]{2,1,0:T(8,128)(2,1)} %collective-permute-done), kind=kLoop, calls=%fused_computation.17 | loop fusion | bytes 327680
  32.1 0.0 collective-permute-done.6.west_ref
  32.1 5.6 %collective-permute-done.7.east_ref = bf16[800,256]{1,0:T(8,128)(2,1)} collective-permute-done((bf16[800,256]{1,0:T(8,128)(2,1)}, bf16[800,256]{1,0:T(8,128)(2,1)}, u32[]{:S(2)}, u32[]{:S(2)}) %collective-permute-start.7) | collective-permute-done | bytes 409632 | tf_op jit(solution)/shard_map/ppermute | solution.py:19
  37.7 0.0 copy-start.1
  37.7 8.3 %shard_map.55.rest_0_ = bf16[96,32,256]{2,1,0:T(8,128)(2,1)} custom-call(s32[2]{0:T(128)} %pad_add_fusion.scalar_ref, bf16[96,9,256]{2,1,0:T(8,128)(2,1)} %pad.24.src_ref, bf16[96,32,256]{2,1,0:T(8,128)(2,1)} %f_ref.5, bf16[96,32,256]{2,1,0:T(8,128)(2,1)} %f_ref.5, bf16[800,256]{1,0:T(8,128)(2,1)} %collective-permute-done.6.west_ref, ...), custom_call_target="tpu_custom_call" | custom-call | tf_op jit(solution)/shard_map/pallas_call | solution.py:153
  46.0 0.0 collective-permute-done.2.west_ref
  46.0 0.0 copy-start.2
  46.1 0.0 copy-done.1
  46.1 0.1 constant_dynamic-update-slice_fusion.4
  46.2 0.0 collective-permute-done.3.east_ref
  46.2 1.0 %slice.47 = bf16[320,256]{1,0:T(8,128)(2,1)S(1)} slice(bf16[1120,256]{1,0:T(8,128)(2,1)} %collective-permute-done.3.east_ref), slice={[800:1120], [0:256]} | slice | bytes 327680 | tf_op jit(solution)/shard_map/slice | solution.py:231
  47.2 0.0 collective-permute-done.4
  47.2 0.0 copy-done.2
  47.2 1.0 %pad.20.ext_ref = bf16[11,160,256]{2,1,0:T(8,128)(2,1)} pad(bf16[10,160,256]{2,1,0:T(8,128)(2,1)S(1)} %constant_dynamic-update-slice_fusion.2, bf16[]{:T(256)} %constant.8.clone.1), padding=0_1x0_0x0_0 | pad | bytes 1720322 | tf_op jit(solution)/shard_map/jit(_pad)/pad | solution.py:234
  48.2 8.1 %shard_map.56.prev_ref = bf16[96,32,256]{2,1,0:T(8,128)(2,1)} custom-call(s32[2]{0:T(128)} %pad_add_fusion.scalar_ref, bf16[96,9,256]{2,1,0:T(8,128)(2,1)} %pad.24.src_ref, bf16[96,32,256]{2,1,0:T(8,128)(2,1)} %f_ref.5, bf16[96,32,256]{2,1,0:T(8,128)(2,1)} %f_ref.5, bf16[1120,256]{1,0:T(8,128)(2,1)} %copy-done.2, ...), custom_call_target="tpu_custom_call", output_to_operand_aliasing={{}: (9, {})} | custom-call | tf_op jit(solution)/shard_map/pallas_call | solution.py:153
  56.3 3.0 %shard_map.57 = bf16[96,32,256]{2,1,0:T(8,128)(2,1)} custom-call(s32[2]{0:T(128)} %pad_add_fusion.scalar_ref, bf16[11,160,256]{2,1,0:T(8,128)(2,1)} %pad.20.ext_ref, bf16[8,9,512]{2,1,0:T(8,128)(2,1)} %pad.22.src_ref, bf16[96,32,256]{2,1,0:T(8,128)(2,1)} %f_ref.5, bf16[9,256,256]{2,1,0:T(8,128)(2,1)} %w_ref.5, ...), custom_call_target="tpu_custom_call", output_to_operand_aliasing={{}: (5, {})} | custom-call | tf_op jit(solution)/shard_map/pallas_call | solution.py:177
  (10 shorter events, 0.1 us)
Async XLA Ops:
  0.0 11.3 %copy-start = (bf16[96,32,256]{2,1,0:T(8,128)(2,1)S(1)}, bf16[96,32,256]{2,1,0:T(8,128)(2,1)}, u32[]{:S(2)}) copy-start(bf16[96,32,256]{2,1,0:T(8,128)(2,1)} %f_ref.5) | copy-start | bytes 4718596
  0.0 11.2 %copy-start.7 = (s32[96]{0:T(128)S(1)}, s32[96]{0:T(128)}, u32[]{:S(2)}) copy-start(s32[96]{0:T(128)} %param.8) | copy-start | bytes 1156
  0.9 10.4 %collective-permute-start.5 = (bf16[1,32,256]{2,1,0:T(8,128)(2,1)S(1)}, bf16[1,32,256]{2,1,0:T(8,128)(2,1)S(1)}, u32[]{:S(2)}, u32[]{:S(2)}) collective-permute-start(bf16[1,32,256]{2,1,0:T(8,128)(2,1)S(1)} %get-tuple-element.11), channel_id=1, source_target_pairs={{0,32},{32,64},{64,96},{96,128},{128,160},{160,192},{192,224},{1,3... | collective-permute-start | bytes 49160 | tf_op jit(solution)/shard_map/ppermute | solution.py:203
  4.1 12.7 %collective-permute-start.1 = (bf16[1,32,256]{2,1,0:T(8,128)(2,1)S(1)}, bf16[1,32,256]{2,1,0:T(8,128)(2,1)S(1)}, u32[]{:S(2)}, u32[]{:S(2)}) collective-permute-start(bf16[1,32,256]{2,1,0:T(8,128)(2,1)S(1)} %get-tuple-element.12), channel_id=1, source_target_pairs={{32,0},{64,32},{96,64},{128,96},{160,128},{192,160},{224,192},{33,... | collective-permute-start | bytes 49160 | tf_op jit(solution)/shard_map/ppermute | solution.py:204
  9.3 17.2 %collective-permute-start = (bf16[10,32,256]{2,1,0:T(8,128)(2,1)S(1)}, bf16[10,32,256]{2,1,0:T(8,128)(2,1)}, u32[]{:S(2)}, u32[]{:S(2)}) collective-permute-start(bf16[10,32,256]{2,1,0:T(8,128)(2,1)S(1)} %fusion.2), channel_id=1, source_target_pairs={{30,0},{31,1},{0,2},{1,3},{2,4},{3,5},{4,6},{5,7},{6,8},{7,9},{8,1... | collective-permute-start | bytes 491528 | tf_op jit(solution)/shard_map/ppermute | solution.py:19
  11.3 0.6 %copy-start.5 = (bf16[1,32,256]{2,1,0:T(8,128)(2,1)}, bf16[1,32,256]{2,1,0:T(8,128)(2,1)S(1)}, u32[]{:S(2)}) copy-start(bf16[1,32,256]{2,1,0:T(8,128)(2,1)S(1)} %collective-permute-done.5.north_ref) | copy-start | bytes 49156
  12.9 19.3 %collective-permute-start.6 = (bf16[800,256]{1,0:T(8,128)(2,1)}, bf16[800,256]{1,0:T(8,128)(2,1)}, u32[]{:S(2)}, u32[]{:S(2)}) collective-permute-start(bf16[800,256]{1,0:T(8,128)(2,1)} %bitcast.9), channel_id=1, source_target_pairs={{31,0},{0,1},{1,2},{2,3},{3,4},{4,5},{5,6},{6,7},{7,8},{8,9},{9,10... | collective-permute-start | bytes 1228808 | tf_op jit(solution)/shard_map/ppermute | solution.py:19
  16.7 21.0 %collective-permute-start.7 = (bf16[800,256]{1,0:T(8,128)(2,1)}, bf16[800,256]{1,0:T(8,128)(2,1)}, u32[]{:S(2)}, u32[]{:S(2)}) collective-permute-start(bf16[800,256]{1,0:T(8,128)(2,1)} %bitcast.10), channel_id=1, source_target_pairs={{1,0},{2,1},{3,2},{4,3},{5,4},{6,5},{7,6},{8,7},{9,8},{10,9},{11,1... | collective-permute-start | bytes 1228808 | tf_op jit(solution)/shard_map/ppermute | solution.py:19
  16.8 1.2 %copy-start.6 = (bf16[1,32,256]{2,1,0:T(8,128)(2,1)}, bf16[1,32,256]{2,1,0:T(8,128)(2,1)S(1)}, u32[]{:S(2)}) copy-start(bf16[1,32,256]{2,1,0:T(8,128)(2,1)S(1)} %collective-permute-done.1.south_ref) | copy-start | bytes 49156
  16.8 4.4 %copy-start.3 = (f32[96,3,129]{0,2,1:T(8,128)S(1)}, f32[96,3,129]{0,2,1:T(8,128)}, u32[]{:S(2)}) copy-start(f32[96,3,129]{0,2,1:T(8,128)} %param.6) | copy-start | bytes 445828
  16.8 4.4 %copy-start.4 = (s32[96,3,129]{0,2,1:T(8,128)S(1)}, s32[96,3,129]{0,2,1:T(8,128)}, u32[]{:S(2)}) copy-start(s32[96,3,129]{0,2,1:T(8,128)} %param.7) | copy-start | bytes 445828
  17.9 28.1 %collective-permute-start.2 = (bf16[1120,256]{1,0:T(8,128)(2,1)}, bf16[1120,256]{1,0:T(8,128)(2,1)S(1)}, u32[]{:S(2)}, u32[]{:S(2)}) collective-permute-start(bf16[1120,256]{1,0:T(8,128)(2,1)} %get-tuple-element.14), channel_id=1, source_target_pairs={{31,0},{0,1},{1,2},{2,3},{3,4},{4,5},{5,6},{6,7},{7,8},{8,9},{9,10... | collective-permute-start | bytes 1720328 | tf_op jit(solution)/shard_map/ppermute | solution.py:19
  21.6 24.6 %collective-permute-start.3 = (bf16[1120,256]{1,0:T(8,128)(2,1)}, bf16[1120,256]{1,0:T(8,128)(2,1)}, u32[]{:S(2)}, u32[]{:S(2)}) collective-permute-start(bf16[1120,256]{1,0:T(8,128)(2,1)} %get-tuple-element.13), channel_id=1, source_target_pairs={{1,0},{2,1},{3,2},{4,3},{5,4},{6,5},{7,6},{8,7},{9,8},{10,9},{11,1... | collective-permute-start | bytes 1720328 | tf_op jit(solution)/shard_map/ppermute | solution.py:19
  26.5 20.7 %collective-permute-start.4 = (bf16[10,32,256]{2,1,0:T(8,128)(2,1)S(1)}, bf16[10,32,256]{2,1,0:T(8,128)(2,1)S(1)}, u32[]{:S(2)}, u32[]{:S(2)}) collective-permute-start(bf16[10,32,256]{2,1,0:T(8,128)(2,1)S(1)} %fusion.2), channel_id=1, source_target_pairs={{2,0},{3,1},{4,2},{5,3},{6,4},{7,5},{8,6},{9,7},{10,8},{11,9},{12,... | collective-permute-start | bytes 491528 | tf_op jit(solution)/shard_map/ppermute | solution.py:19
  37.7 8.4 %copy-start.1 = (bf16[96,32,256]{2,1,0:T(8,128)(2,1)S(1)}, bf16[96,32,256]{2,1,0:T(8,128)(2,1)}, u32[]{:S(2)}) copy-start(bf16[96,32,256]{2,1,0:T(8,128)(2,1)} %f_ref.5) | copy-start | bytes 4718596
  46.0 1.2 %copy-start.2 = (bf16[1120,256]{1,0:T(8,128)(2,1)}, bf16[1120,256]{1,0:T(8,128)(2,1)S(1)}, u32[]{:S(2)}) copy-start(bf16[1120,256]{1,0:T(8,128)(2,1)S(1)} %collective-permute-done.2.west_ref) | copy-start | bytes 1720324

commit v14 on v13

--- a/solution.py
+++ b/solution.py
@@ -46,11 +46,26 @@
     return jnp.pad(flat, ((0, 0), (0, 0), (0, lanes - offsets * span)))
 
 
-def conv_block(ext_ref, src_ref, f_ref, w_ref, o_ref, conv_scr, base):
+def conv_block(ext_ref, src_ref, f_ref, w_ref, o_ref, conv_scr, base, needed=None):
     rows, columns, channels = f_ref.shape
     count, lanes = src_ref.shape[1], src_ref.shape[2]
     span = ext_ref.shape[1]
     for q in range(rows):
+        if needed is None:
+            conv_row(ext_ref, src_ref, conv_scr, base, q)
+        else:
+            pl.when(needed(q))(functools.partial(conv_row, ext_ref, src_ref, conv_scr, base, q))
+    acc = f_ref[...].reshape(rows * columns, channels).astype(jnp.float32)
+    for b in range(count):
+        acc = acc + jnp.dot(conv_scr[b], w_ref[b], preferred_element_type=jnp.float32)
+    o_ref[...] = acc.reshape(rows, columns, channels).astype(o_ref.dtype)
+
+
+def conv_row(ext_ref, src_ref, conv_scr, base, q):
+    count, lanes = src_ref.shape[1], src_ref.shape[2]
+    span, channels = ext_ref.shape[1], ext_ref.shape[2]
+    columns = conv_scr.shape[1] // src_ref.shape[0]
+    if True:
         source = src_ref[q].astype(jnp.float32)
         pieces = []
         for b in range(count):
@@ -62,10 +77,6 @@
         conv = conv.astype(jnp.bfloat16)
         for b in range(count):
             conv_scr[b, q * columns : (q + 1) * columns, :] = conv[b * columns : (b + 1) * columns]
-    acc = f_ref[...].reshape(rows * columns, channels).astype(jnp.float32)
-    for b in range(count):
-        acc = acc + jnp.dot(conv_scr[b], w_ref[b], preferred_element_type=jnp.float32)
-    o_ref[...] = acc.reshape(rows, columns, channels).astype(o_ref.dtype)
 
 
 def near_kernel(scalar_ref, src_ref, f_ref, all_ref, west_ref, east_ref, north_ref,
@@ -104,7 +115,11 @@
         ext_scr[rows + 1, halo : halo + columns] = all_ref[jnp.minimum(base + rows, lat_rows - 1)]
 
     ext_scr[rows + 2] = jnp.zeros(ext_scr.shape[1:], ext_scr.dtype)
-    conv_block(ext_scr, src_ref, f_ref, w_ref, o_ref, conv_scr, 0)
+    def needed(q):
+        inside = (base + q >= scalar_ref[0]) & (base + q < scalar_ref[0] + POLAR)
+        return jnp.logical_not(inside & (scalar_ref[1] != 0))
+
+    conv_block(ext_scr, src_ref, f_ref, w_ref, o_ref, conv_scr, 0, needed)
 
 
 def wide_kernel(scalar_ref, ext_ref, src_ref, f_ref, w_ref, prev_ref, o_ref, conv_scr):

time: 60.1 us -> 79.1 us (1.32)
  Pallas kernels: 19.3 us -> 38.9 us
    pallas_call x2, Pallas kernels: 16.4 us -> 36 us  [near_call(): pl.pallas_call(functools.partial(near_kernel, first=first, lowest=lowest)...]
  transfers between devices with their start and end apart: 8 -> 8, of which waited for: 1 -> 1; matrix products, arithmetic and copies ran while one was open for 18% -> 13% of each run, Pallas kernels for 14% -> 23%
where the time goes in v14:
time: 79.1 us; the launch traced here: 78.9 us
  Pallas kernels  38.9 us (49%)
  starting transfers between devices  21.2 us (27%)
  local copies, waits for them, and re-layouts  9.52 us (12%)
  waiting for transfers between devices  5.62 us (7%)
  other arithmetic  3.29 us (4%)
    pallas_call x2, Pallas kernels, near_call(): pl.pallas_call(functools.partial(near_kernel, first=first, lowest=lowest)...  36 us
    ppermute x6, starting transfers between devices, shifted(): return lax.ppermute(block, axis, route)  13.8 us
    ppermute x6, waiting for transfers between devices, shifted(): return lax.ppermute(block, axis, route)  5.62 us
    ppermute x1, starting transfers between devices, body(): south = lax.ppermute(features[:1], 'lat', down)  4.19 us
    ppermute x1, starting transfers between devices, body(): north = lax.ppermute(features[lat_rows - 1:], 'lat', up)  3.19 us
    pallas_call x1, Pallas kernels, wide_call(): pl.pallas_call(wide_kernel, grid_spec=grid_spec, out_shape=jax.ShapeDtype...  2.97 us
    pad x2, local copies, waits for them, and re-layouts, flat_sources(): return jnp.pad(flat, ((0, 0), (0, 0), (0, lanes - offsets * span)))  1.75 us
    reshape x2, local copies, waits for them, and re-layouts, flat_sources(): flat = flat.reshape(rows, count, offsets * span)  1.65 us
  transfers between devices with their start and end apart: 8, of which 1 were waited for; matrix products, arithmetic and copies ran while one was open for 13% of the time, Pallas kernels for 23%

profile of v14, /device:TPU:3, one launch (start us, length us, event | category | flops | bytes accessed | tf_op | source)
XLA Modules:
  0.0 78.9 jit_solution(12405494880299971771)
XLA Ops:
  0.0 0.0 copy-start
  0.0 0.0 copy-start.7
  0.0 0.9 %fusion.5 = (bf16[1,32,256]{2,1,0:T(8,128)(2,1)S(1)}, bf16[1,32,256]{2,1,0:T(8,128)(2,1)S(1)}) fusion(bf16[96,32,256]{2,1,0:T(8,128)(2,1)} %f_ref.5), kind=kLoop, calls=%fused_computation.26 | loop fusion | bytes 65536 | tf_op jit(solution)/shard_map/slice | solution.py:218
  0.9 3.2 %collective-permute-start.5 = (bf16[1,32,256]{2,1,0:T(8,128)(2,1)S(1)}, bf16[1,32,256]{2,1,0:T(8,128)(2,1)S(1)}, u32[]{:S(2)}, u32[]{:S(2)}) collective-permute-start(bf16[1,32,256]{2,1,0:T(8,128)(2,1)S(1)} %get-tuple-element.11), channel_id=1, source_target_pairs={{0,32},{32,64},{64,96},{96,128},{128,160},{160,192},{192,224},{1,3... | collective-permute-start | bytes 49160 | tf_op jit(solution)/shard_map/ppermute | solution.py:218
  4.1 4.2 %collective-permute-start.1 = (bf16[1,32,256]{2,1,0:T(8,128)(2,1)S(1)}, bf16[1,32,256]{2,1,0:T(8,128)(2,1)S(1)}, u32[]{:S(2)}, u32[]{:S(2)}) collective-permute-start(bf16[1,32,256]{2,1,0:T(8,128)(2,1)S(1)} %get-tuple-element.12), channel_id=1, source_target_pairs={{32,0},{64,32},{96,64},{128,96},{160,128},{192,160},{224,192},{33,... | collective-permute-start | bytes 49160 | tf_op jit(solution)/shard_map/ppermute | solution.py:219
  8.3 1.0 %fusion.2 = bf16[10,32,256]{2,1,0:T(8,128)(2,1)S(1)} fusion(s32[]{:T(128)} %select_n.10, bf16[1,32,256]{2,1,0:T(8,128)(2,1)S(1)} %broadcast_in_dim.10, bf16[96,32,256]{2,1,0:T(8,128)(2,1)} %f_ref.5), kind=kLoop, calls=%fused_computation.9 | loop fusion | flops 163840 | bytes 1753092 | tf_op jit(solution)/shard_map/concatenate | solution.py:213
  9.3 1.9 %collective-permute-start = (bf16[10,32,256]{2,1,0:T(8,128)(2,1)S(1)}, bf16[10,32,256]{2,1,0:T(8,128)(2,1)}, u32[]{:S(2)}, u32[]{:S(2)}) collective-permute-start(bf16[10,32,256]{2,1,0:T(8,128)(2,1)S(1)} %fusion.2), channel_id=1, source_target_pairs={{30,0},{31,1},{0,2},{1,3},{2,4},{3,5},{4,6},{5,7},{6,8},{7,9},{8,1... | collective-permute-start | bytes 491528 | tf_op jit(solution)/shard_map/ppermute | solution.py:19
  11.2 0.0 copy-done.7
  11.2 0.1 broadcast_compare_fusion
  11.3 0.0 collective-permute-done.5.north_ref
  11.3 0.0 copy-start.5
  11.3 0.0 copy-done
  11.3 0.2 constant_dynamic-update-slice_fusion.7
  11.6 0.3 copy-done.5
  11.9 1.0 %fusion.3 = (bf16[50,16,256]{2,1,0:T(8,128)(2,1)}, bf16[50,16,256]{2,1,0:T(8,128)(2,1)}) fusion(bf16[97,32,256]{2,1,0:T(8,128)(2,1)S(1)} %get-tuple-element.9), kind=kLoop, calls=%fused_computation.24 | loop fusion | bytes 1638400 | tf_op jit(solution)/shard_map/slice | solution.py:225
  12.9 3.9 %collective-permute-start.6 = (bf16[800,256]{1,0:T(8,128)(2,1)}, bf16[800,256]{1,0:T(8,128)(2,1)}, u32[]{:S(2)}, u32[]{:S(2)}) collective-permute-start(bf16[800,256]{1,0:T(8,128)(2,1)} %bitcast.9), channel_id=1, source_target_pairs={{31,0},{0,1},{1,2},{2,3},{3,4},{4,5},{5,6},{6,7},{7,8},{8,9},{9,10... | collective-permute-start | bytes 1228808 | tf_op jit(solution)/shard_map/ppermute | solution.py:19
  16.7 0.0 collective-permute-start.7
  16.7 0.0 collective-permute-done.1.south_ref
  16.8 0.0 copy-start.6
  16.8 0.0 copy-start.3
  16.8 0.0 copy-start.4
  16.8 0.1 fusion.4
  16.9 1.1 %pad_maximum_fusion = (bf16[1120,256]{1,0:T(8,128)(2,1)}, bf16[1120,256]{1,0:T(8,128)(2,1)}) fusion(bf16[320,256]{1,0:T(8,128)(2,1)S(1)} %bitcast.15, bf16[800,256]{1,0:T(8,128)(2,1)S(1)} %bitcast.13, bf16[800,256]{1,0:T(8,128)(2,1)S(1)} %bitcast.14), kind=kLoop, calls=%fused_computation.6 | loop fusion | flops 2007040 | bytes 2129920 | tf_op jit(solution)/shard_map/concatenate | solution.py:228
  17.9 0.0 copy-done.6
  17.9 3.2 %collective-permute-start.2 = (bf16[1120,256]{1,0:T(8,128)(2,1)}, bf16[1120,256]{1,0:T(8,128)(2,1)S(1)}, u32[]{:S(2)}, u32[]{:S(2)}) collective-permute-start(bf16[1120,256]{1,0:T(8,128)(2,1)} %get-tuple-element.14), channel_id=1, source_target_pairs={{31,0},{0,1},{1,2},{2,3},{3,4},{4,5},{5,6},{6,7},{7,8},{8,9},{9,10... | collective-permute-start | bytes 1720328 | tf_op jit(solution)/shard_map/ppermute | solution.py:19
  21.2 0.0 copy-done.3
  21.2 0.0 copy-done.4
  21.2 0.4 multiply_convert_fusion
  21.6 0.1 collective-permute-start.3
  21.7 0.3 constant_dynamic-slice_fusion
  22.1 0.1 pad.23
  22.2 1.0 %copy.12 = bf16[96,9,192]{2,1,0:T(8,128)(2,1)S(1)} copy(bf16[96,9,192]{0,2,1:T(8,128)(2,1)S(1)} %bitcast.12) | data formatting | bytes 663552 | tf_op jit(solution)/shard_map/reshape | solution.py:45
  23.2 1.1 %pad.24.src_ref = bf16[96,9,256]{2,1,0:T(8,128)(2,1)} pad(bf16[96,9,192]{2,1,0:T(8,128)(2,1)S(1)} %copy.12, bf16[]{:T(256)} %constant.8.clone.1), padding=0_0x0_0x0_64 | pad | bytes 774146 | tf_op jit(solution)/shard_map/jit(_pad)/pad | solution.py:46
  24.3 0.2 pad.21
  24.5 0.6 copy.11
  25.1 0.7 pad.22.src_ref
  25.8 0.6 pad_add_fusion.scalar_ref
  26.5 0.0 collective-permute-done
  26.5 4.7 %collective-permute-start.4 = (bf16[10,32,256]{2,1,0:T(8,128)(2,1)S(1)}, bf16[10,32,256]{2,1,0:T(8,128)(2,1)S(1)}, u32[]{:S(2)}, u32[]{:S(2)}) collective-permute-start(bf16[10,32,256]{2,1,0:T(8,128)(2,1)S(1)} %fusion.2), channel_id=1, source_target_pairs={{2,0},{3,1},{4,2},{5,3},{6,4},{7,5},{8,6},{9,7},{10,8},{11,9},{12,... | collective-permute-start | bytes 491528 | tf_op jit(solution)/shard_map/ppermute | solution.py:19
  31.2 0.9 %constant_dynamic-update-slice_fusion.6 = bf16[10,160,256]{2,1,0:T(8,128)(2,1)S(1)} fusion(bf16[10,32,256]{2,1,0:T(8,128)(2,1)} %collective-permute-done), kind=kLoop, calls=%fused_computation.17 | loop fusion | bytes 327680
  32.1 0.0 collective-permute-done.6.west_ref
  32.1 5.6 %collective-permute-done.7.east_ref = bf16[800,256]{1,0:T(8,128)(2,1)} collective-permute-done((bf16[800,256]{1,0:T(8,128)(2,1)}, bf16[800,256]{1,0:T(8,128)(2,1)}, u32[]{:S(2)}, u32[]{:S(2)}) %collective-permute-start.7) | collective-permute-done | bytes 409632 | tf_op jit(solution)/shard_map/ppermute | solution.py:19
  37.7 0.0 copy-start.1
  37.7 18.0 %shard_map.55.rest_0_ = bf16[96,32,256]{2,1,0:T(8,128)(2,1)} custom-call(s32[2]{0:T(128)} %pad_add_fusion.scalar_ref, bf16[96,9,256]{2,1,0:T(8,128)(2,1)} %pad.24.src_ref, bf16[96,32,256]{2,1,0:T(8,128)(2,1)} %f_ref.5, bf16[96,32,256]{2,1,0:T(8,128)(2,1)} %f_ref.5, bf16[800,256]{1,0:T(8,128)(2,1)} %collective-permute-done.6.west_ref, ...), custom_call_target="tpu_custom_call" | custom-call | tf_op jit(solution)/shard_map/pallas_call | solution.py:168
  55.7 0.0 collective-permute-done.2.west_ref
  55.7 0.0 copy-start.2
  55.8 0.0 copy-done.1
  55.8 0.1 constant_dynamic-update-slice_fusion.4
  55.9 0.0 collective-permute-done.3.east_ref
  55.9 1.0 %slice.47 = bf16[320,256]{1,0:T(8,128)(2,1)S(1)} slice(bf16[1120,256]{1,0:T(8,128)(2,1)} %collective-permute-done.3.east_ref), slice={[800:1120], [0:256]} | slice | bytes 327680 | tf_op jit(solution)/shard_map/slice | solution.py:246
  56.9 0.0 collective-permute-done.4
  56.9 0.0 copy-done.2
  56.9 1.0 %pad.20.ext_ref = bf16[11,160,256]{2,1,0:T(8,128)(2,1)} pad(bf16[10,160,256]{2,1,0:T(8,128)(2,1)S(1)} %constant_dynamic-update-slice_fusion.2, bf16[]{:T(256)} %constant.8.clone.1), padding=0_1x0_0x0_0 | pad | bytes 1720322 | tf_op jit(solution)/shard_map/jit(_pad)/pad | solution.py:249
  57.9 18.0 %shard_map.56.prev_ref = bf16[96,32,256]{2,1,0:T(8,128)(2,1)} custom-call(s32[2]{0:T(128)} %pad_add_fusion.scalar_ref, bf16[96,9,256]{2,1,0:T(8,128)(2,1)} %pad.24.src_ref, bf16[96,32,256]{2,1,0:T(8,128)(2,1)} %f_ref.5, bf16[96,32,256]{2,1,0:T(8,128)(2,1)} %f_ref.5, bf16[1120,256]{1,0:T(8,128)(2,1)} %copy-done.2, ...), custom_call_target="tpu_custom_call", output_to_operand_aliasing={{}: (9, {})} | custom-call | tf_op jit(solution)/shard_map/pallas_call | solution.py:168
  75.9 3.0 %shard_map.57 = bf16[96,32,256]{2,1,0:T(8,128)(2,1)} custom-call(s32[2]{0:T(128)} %pad_add_fusion.scalar_ref, bf16[11,160,256]{2,1,0:T(8,128)(2,1)} %pad.20.ext_ref, bf16[8,9,512]{2,1,0:T(8,128)(2,1)} %pad.22.src_ref, bf16[96,32,256]{2,1,0:T(8,128)(2,1)} %f_ref.5, bf16[9,256,256]{2,1,0:T(8,128)(2,1)} %w_ref.5, ...), custom_call_target="tpu_custom_call", output_to_operand_aliasing={{}: (5, {})} | custom-call | tf_op jit(solution)/shard_map/pallas_call | solution.py:192
  (10 shorter events, 0.1 us)
Async XLA Ops:
  0.0 11.3 %copy-start = (bf16[96,32,256]{2,1,0:T(8,128)(2,1)S(1)}, bf16[96,32,256]{2,1,0:T(8,128)(2,1)}, u32[]{:S(2)}) copy-start(bf16[96,32,256]{2,1,0:T(8,128)(2,1)} %f_ref.5) | copy-start | bytes 4718596
  0.0 11.2 %copy-start.7 = (s32[96]{0:T(128)S(1)}, s32[96]{0:T(128)}, u32[]{:S(2)}) copy-start(s32[96]{0:T(128)} %param.8) | copy-start | bytes 1156
  0.9 10.4 %collective-permute-start.5 = (bf16[1,32,256]{2,1,0:T(8,128)(2,1)S(1)}, bf16[1,32,256]{2,1,0:T(8,128)(2,1)S(1)}, u32[]{:S(2)}, u32[]{:S(2)}) collective-permute-start(bf16[1,32,256]{2,1,0:T(8,128)(2,1)S(1)} %get-tuple-element.11), channel_id=1, source_target_pairs={{0,32},{32,64},{64,96},{96,128},{128,160},{160,192},{192,224},{1,3... | collective-permute-start | bytes 49160 | tf_op jit(solution)/shard_map/ppermute | solution.py:218
  4.1 12.7 %collective-permute-start.1 = (bf16[1,32,256]{2,1,0:T(8,128)(2,1)S(1)}, bf16[1,32,256]{2,1,0:T(8,128)(2,1)S(1)}, u32[]{:S(2)}, u32[]{:S(2)}) collective-permute-start(bf16[1,32,256]{2,1,0:T(8,128)(2,1)S(1)} %get-tuple-element.12), channel_id=1, source_target_pairs={{32,0},{64,32},{96,64},{128,96},{160,128},{192,160},{224,192},{33,... | collective-permute-start | bytes 49160 | tf_op jit(solution)/shard_map/ppermute | solution.py:219
  9.3 17.2 %collective-permute-start = (bf16[10,32,256]{2,1,0:T(8,128)(2,1)S(1)}, bf16[10,32,256]{2,1,0:T(8,128)(2,1)}, u32[]{:S(2)}, u32[]{:S(2)}) collective-permute-start(bf16[10,32,256]{2,1,0:T(8,128)(2,1)S(1)} %fusion.2), channel_id=1, source_target_pairs={{30,0},{31,1},{0,2},{1,3},{2,4},{3,5},{4,6},{5,7},{6,8},{7,9},{8,1... | collective-permute-start | bytes 491528 | tf_op jit(solution)/shard_map/ppermute | solution.py:19
  11.3 0.6 copy-start.5
  12.9 19.3 %collective-permute-start.6 = (bf16[800,256]{1,0:T(8,128)(2,1)}, bf16[800,256]{1,0:T(8,128)(2,1)}, u32[]{:S(2)}, u32[]{:S(2)}) collective-permute-start(bf16[800,256]{1,0:T(8,128)(2,1)} %bitcast.9), channel_id=1, source_target_pairs={{31,0},{0,1},{1,2},{2,3},{3,4},{4,5},{5,6},{6,7},{7,8},{8,9},{9,10... | collective-permute-start | bytes 1228808 | tf_op jit(solution)/shard_map/ppermute | solution.py:19
  16.7 21.0 %collective-permute-start.7 = (bf16[800,256]{1,0:T(8,128)(2,1)}, bf16[800,256]{1,0:T(8,128)(2,1)}, u32[]{:S(2)}, u32[]{:S(2)}) collective-permute-start(bf16[800,256]{1,0:T(8,128)(2,1)} %bitcast.10), channel_id=1, source_target_pairs={{1,0},{2,1},{3,2},{4,3},{5,4},{6,5},{7,6},{8,7},{9,8},{10,9},{11,1... | collective-permute-start | bytes 1228808 | tf_op jit(solution)/shard_map/ppermute | solution.py:19
  16.8 1.2 %copy-start.6 = (bf16[1,32,256]{2,1,0:T(8,128)(2,1)}, bf16[1,32,256]{2,1,0:T(8,128)(2,1)S(1)}, u32[]{:S(2)}) copy-start(bf16[1,32,256]{2,1,0:T(8,128)(2,1)S(1)} %collective-permute-done.1.south_ref) | copy-start | bytes 49156
  16.8 4.4 %copy-start.3 = (f32[96,3,129]{0,2,1:T(8,128)S(1)}, f32[96,3,129]{0,2,1:T(8,128)}, u32[]{:S(2)}) copy-start(f32[96,3,129]{0,2,1:T(8,128)} %param.6) | copy-start | bytes 445828
  16.8 4.4 %copy-start.4 = (s32[96,3,129]{0,2,1:T(8,128)S(1)}, s32[96,3,129]{0,2,1:T(8,128)}, u32[]{:S(2)}) copy-start(s32[96,3,129]{0,2,1:T(8,128)} %param.7) | copy-start | bytes 445828
  17.9 37.8 %collective-permute-start.2 = (bf16[1120,256]{1,0:T(8,128)(2,1)}, bf16[1120,256]{1,0:T(8,128)(2,1)S(1)}, u32[]{:S(2)}, u32[]{:S(2)}) collective-permute-start(bf16[1120,256]{1,0:T(8,128)(2,1)} %get-tuple-element.14), channel_id=1, source_target_pairs={{31,0},{0,1},{1,2},{2,3},{3,4},{4,5},{5,6},{6,7},{7,8},{8,9},{9,10... | collective-permute-start | bytes 1720328 | tf_op jit(solution)/shard_map/ppermute | solution.py:19
  21.6 34.3 %collective-permute-start.3 = (bf16[1120,256]{1,0:T(8,128)(2,1)}, bf16[1120,256]{1,0:T(8,128)(2,1)}, u32[]{:S(2)}, u32[]{:S(2)}) collective-permute-start(bf16[1120,256]{1,0:T(8,128)(2,1)} %get-tuple-element.13), channel_id=1, source_target_pairs={{1,0},{2,1},{3,2},{4,3},{5,4},{6,5},{7,6},{8,7},{9,8},{10,9},{11,1... | collective-permute-start | bytes 1720328 | tf_op jit(solution)/shard_map/ppermute | solution.py:19
  26.5 30.4 %collective-permute-start.4 = (bf16[10,32,256]{2,1,0:T(8,128)(2,1)S(1)}, bf16[10,32,256]{2,1,0:T(8,128)(2,1)S(1)}, u32[]{:S(2)}, u32[]{:S(2)}) collective-permute-start(bf16[10,32,256]{2,1,0:T(8,128)(2,1)S(1)} %fusion.2), channel_id=1, source_target_pairs={{2,0},{3,1},{4,2},{5,3},{6,4},{7,5},{8,6},{9,7},{10,8},{11,9},{12,... | collective-permute-start | bytes 491528 | tf_op jit(solution)/shard_map/ppermute | solution.py:19
  37.7 18.1 %copy-start.1 = (bf16[96,32,256]{2,1,0:T(8,128)(2,1)S(1)}, bf16[96,32,256]{2,1,0:T(8,128)(2,1)}, u32[]{:S(2)}) copy-start(bf16[96,32,256]{2,1,0:T(8,128)(2,1)} %f_ref.5) | copy-start | bytes 4718596
  55.7 1.2 %copy-start.2 = (bf16[1120,256]{1,0:T(8,128)(2,1)}, bf16[1120,256]{1,0:T(8,128)(2,1)S(1)}, u32[]{:S(2)}) copy-start(bf16[1120,256]{1,0:T(8,128)(2,1)S(1)} %collective-permute-done.2.west_ref) | copy-start | bytes 1720324

commit v15 on v13

--- a/solution.py
+++ b/solution.py
@@ -46,7 +46,7 @@
     return jnp.pad(flat, ((0, 0), (0, 0), (0, lanes - offsets * span)))
 
 
-def conv_block(ext_ref, src_ref, f_ref, w_ref, o_ref, conv_scr, base):
+def conv_block(ext_ref, src_ref, f_ref, w_ref, o_ref, conv_scr, base, before_mix=None):
     rows, columns, channels = f_ref.shape
     count, lanes = src_ref.shape[1], src_ref.shape[2]
     span = ext_ref.shape[1]
@@ -62,20 +62,26 @@
         conv = conv.astype(jnp.bfloat16)
         for b in range(count):
             conv_scr[b, q * columns : (q + 1) * columns, :] = conv[b * columns : (b + 1) * columns]
+    if before_mix is not None:
+        before_mix()
     acc = f_ref[...].reshape(rows * columns, channels).astype(jnp.float32)
     for b in range(count):
         acc = acc + jnp.dot(conv_scr[b], w_ref[b], preferred_element_type=jnp.float32)
     o_ref[...] = acc.reshape(rows, columns, channels).astype(o_ref.dtype)
 
 
-def near_kernel(scalar_ref, src_ref, f_ref, all_ref, west_ref, east_ref, north_ref,
-                south_ref, w_ref, *rest, first, lowest):
-    o_ref, ext_scr, conv_scr = rest[-3], rest[-2], rest[-1]
+def near_kernel(scalar_ref, src_ref, f_ref, prev_ref, next_ref, west_ref, east_ref,
+                north_ref, south_ref, w_hbm, *rest, first, lowest, lat_rows):
+    o_ref, ext_scr, conv_scr, w_ref, w_sem = rest[-5:]
     rows, columns, channels = f_ref.shape
-    lat_rows = all_ref.shape[0]
     halo = (ext_scr.shape[1] - columns) // 2
     step = pl.program_id(0)
     base = first + step * rows
+    weights = pltpu.make_async_copy(w_hbm, w_ref, w_sem)
+
+    @pl.when(step == 0)
+    def _():
+        weights.start()
 
     def sides(k, row):
         start = pl.multiple_of((row - lowest) * halo, halo)
@@ -85,7 +91,7 @@
     for k in range(rows + 2):
         sides(k, base + k - 1)
     for k in range(1, rows + 1):
-        ext_scr[k, halo : halo + columns] = all_ref[base + k - 1]
+        ext_scr[k, halo : halo + columns] = f_ref[k - 1]
 
     @pl.when(base == 0)
     def _():
@@ -93,7 +99,7 @@
 
     @pl.when(base > 0)
     def _():
-        ext_scr[0, halo : halo + columns] = all_ref[jnp.maximum(base - 1, 0)]
+        ext_scr[0, halo : halo + columns] = prev_ref[0]
 
     @pl.when(base + rows == lat_rows)
     def _():
@@ -101,10 +107,16 @@
 
     @pl.when(base + rows < lat_rows)
     def _():
-        ext_scr[rows + 1, halo : halo + columns] = all_ref[jnp.minimum(base + rows, lat_rows - 1)]
+        ext_scr[rows + 1, halo : halo + columns] = next_ref[0]
 
     ext_scr[rows + 2] = jnp.zeros(ext_scr.shape[1:], ext_scr.dtype)
-    conv_block(ext_scr, src_ref, f_ref, w_ref, o_ref, conv_scr, 0)
+
+    def wait_weights():
+        @pl.when(step == 0)
+        def _():
+            weights.wait()
+
+    conv_block(ext_scr, src_ref, f_ref, w_ref, o_ref, conv_scr, 0, wait_weights)
 
 
 def wide_kernel(scalar_ref, ext_ref, src_ref, f_ref, w_ref, prev_ref, o_ref, conv_scr):
@@ -128,13 +140,18 @@
     halo = NEAR
     offset = first // NEAR_BLOCK
     row_map = lambda i, s: (i + offset, 0, 0)
+    prev_map = lambda i, s: (jnp.maximum(first + i * NEAR_BLOCK - 1, 0), 0, 0)
+    next_map = lambda i, s: (jnp.minimum(first + (i + 1) * NEAR_BLOCK, lat_rows - 1), 0, 0)
     in_specs = [
         pl.BlockSpec((NEAR_BLOCK,) + sources.shape[1:], row_map),
         pl.BlockSpec((NEAR_BLOCK, columns, channels), row_map),
-        full_spec(features.shape), full_spec(west.shape), full_spec(east.shape),
-        full_spec(north.shape), full_spec(south.shape), full_spec(mix_weight.shape),
+        pl.BlockSpec((1, columns, channels), prev_map),
+        pl.BlockSpec((1, columns, channels), next_map),
+        full_spec(west.shape), full_spec(east.shape),
+        full_spec(north.shape), full_spec(south.shape), pl.BlockSpec(memory_space=pl.ANY),
     ]
-    operands = [scalars, sources, features, features, west, east, north, south, mix_weight]
+    operands = [scalars, sources, features, features, features, west, east, north, south,
+                mix_weight]
     aliases = {}
     if previous is not None:
         in_specs.append(pl.BlockSpec(memory_space=pl.ANY))
@@ -148,10 +165,13 @@
         scratch_shapes=[
             pltpu.VMEM((NEAR_BLOCK + 3, columns + 2 * halo, channels), features.dtype),
             pltpu.VMEM((count, NEAR_BLOCK * columns, channels), jnp.bfloat16),
+            pltpu.VMEM(mix_weight.shape, mix_weight.dtype),
+            pltpu.SemaphoreType.DMA(()),
         ],
     )
     return pl.pallas_call(
-        functools.partial(near_kernel, first=first, lowest=lowest), grid_spec=grid_spec,
+        functools.partial(near_kernel, first=first, lowest=lowest, lat_rows=lat_rows),
+        grid_spec=grid_spec,
         out_shape=jax.ShapeDtypeStruct(features.shape, features.dtype),
         input_output_aliases=aliases,
     )(*operands)

time: 60.1 us -> 59.5 us (0.990)
  Pallas kernels: 19.3 us -> 18.6 us
    pallas_call x2, Pallas kernels: 16.4 us -> 15.6 us  [near_call(): pl.pallas_call(functools.partial(near_kernel, first=first, lowest=lowest,...]
  transfers between devices with their start and end apart: 8 -> 8, of which waited for: 1 -> 1; matrix products, arithmetic and copies ran while one was open for 18% -> 18% of each run, Pallas kernels for 14% -> 13%
where the time goes in v15:
time: 59.5 us; the launch traced here: 58.6 us
  starting transfers between devices  21.2 us (36%)
  Pallas kernels  18.6 us (31%)
  local copies, waits for them, and re-layouts  9.51 us (16%)
  waiting for transfers between devices  5.62 us (9%)
  other arithmetic  3.29 us (6%)
    pallas_call x2, Pallas kernels, near_call(): pl.pallas_call(functools.partial(near_kernel, first=first, lowest=lowest,...  15.6 us
    ppermute x6, starting transfers between devices, shifted(): return lax.ppermute(block, axis, route)  13.8 us
    ppermute x6, waiting for transfers between devices, shifted(): return lax.ppermute(block, axis, route)  5.62 us
    ppermute x1, starting transfers between devices, body(): south = lax.ppermute(features[:1], 'lat', down)  4.19 us
    ppermute x1, starting transfers between devices, body(): north = lax.ppermute(features[lat_rows - 1:], 'lat', up)  3.19 us
    pallas_call x1, Pallas kernels, wide_call(): pl.pallas_call(wide_kernel, grid_spec=grid_spec, out_shape=jax.ShapeDtype...  2.97 us
    pad x2, local copies, waits for them, and re-layouts, flat_sources(): return jnp.pad(flat, ((0, 0), (0, 0), (0, lanes - offsets * span)))  1.75 us
    reshape x2, local copies, waits for them, and re-layouts, flat_sources(): flat = flat.reshape(rows, count, offsets * span)  1.65 us
  transfers between devices with their start and end apart: 8, of which 1 were waited for; matrix products, arithmetic and copies ran while one was open for 18% of the time, Pallas kernels for 13%

profile of v15, /device:TPU:3, one launch (start us, length us, event | category | flops | bytes accessed | tf_op | source)
XLA Modules:
  0.0 58.6 jit_solution(17700805116516146701)
XLA Ops:
  0.0 0.0 copy-start
  0.0 0.0 copy-start.7
  0.0 0.9 %fusion.5 = (bf16[1,32,256]{2,1,0:T(8,128)(2,1)S(1)}, bf16[1,32,256]{2,1,0:T(8,128)(2,1)S(1)}) fusion(bf16[96,32,256]{2,1,0:T(8,128)(2,1)} %f_ref.5), kind=kLoop, calls=%fused_computation.26 | loop fusion | bytes 65536 | tf_op jit(solution)/shard_map/slice | solution.py:223
  0.9 3.2 %collective-permute-start.5 = (bf16[1,32,256]{2,1,0:T(8,128)(2,1)S(1)}, bf16[1,32,256]{2,1,0:T(8,128)(2,1)S(1)}, u32[]{:S(2)}, u32[]{:S(2)}) collective-permute-start(bf16[1,32,256]{2,1,0:T(8,128)(2,1)S(1)} %get-tuple-element.11), channel_id=1, source_target_pairs={{0,32},{32,64},{64,96},{96,128},{128,160},{160,192},{192,224},{1,3... | collective-permute-start | bytes 49160 | tf_op jit(solution)/shard_map/ppermute | solution.py:223
  4.1 4.2 %collective-permute-start.1 = (bf16[1,32,256]{2,1,0:T(8,128)(2,1)S(1)}, bf16[1,32,256]{2,1,0:T(8,128)(2,1)S(1)}, u32[]{:S(2)}, u32[]{:S(2)}) collective-permute-start(bf16[1,32,256]{2,1,0:T(8,128)(2,1)S(1)} %get-tuple-element.12), channel_id=1, source_target_pairs={{32,0},{64,32},{96,64},{128,96},{160,128},{192,160},{224,192},{33,... | collective-permute-start | bytes 49160 | tf_op jit(solution)/shard_map/ppermute | solution.py:224
  8.3 1.0 %fusion.2 = bf16[10,32,256]{2,1,0:T(8,128)(2,1)S(1)} fusion(s32[]{:T(128)} %select_n.10, bf16[1,32,256]{2,1,0:T(8,128)(2,1)S(1)} %broadcast_in_dim.10, bf16[96,32,256]{2,1,0:T(8,128)(2,1)} %f_ref.5), kind=kLoop, calls=%fused_computation.9 | loop fusion | flops 163840 | bytes 1753092 | tf_op jit(solution)/shard_map/concatenate | solution.py:218
  9.3 1.9 %collective-permute-start = (bf16[10,32,256]{2,1,0:T(8,128)(2,1)S(1)}, bf16[10,32,256]{2,1,0:T(8,128)(2,1)}, u32[]{:S(2)}, u32[]{:S(2)}) collective-permute-start(bf16[10,32,256]{2,1,0:T(8,128)(2,1)S(1)} %fusion.2), channel_id=1, source_target_pairs={{30,0},{31,1},{0,2},{1,3},{2,4},{3,5},{4,6},{5,7},{6,8},{7,9},{8,1... | collective-permute-start | bytes 491528 | tf_op jit(solution)/shard_map/ppermute | solution.py:19
  11.2 0.0 copy-done.7
  11.2 0.1 broadcast_compare_fusion
  11.3 0.0 collective-permute-done.5.north_ref
  11.3 0.0 copy-start.5
  11.3 0.0 copy-done
  11.3 0.2 constant_dynamic-update-slice_fusion.7
  11.6 0.3 copy-done.5
  11.9 1.0 %fusion.3 = (bf16[50,16,256]{2,1,0:T(8,128)(2,1)}, bf16[50,16,256]{2,1,0:T(8,128)(2,1)}) fusion(bf16[97,32,256]{2,1,0:T(8,128)(2,1)S(1)} %get-tuple-element.9), kind=kLoop, calls=%fused_computation.24 | loop fusion | bytes 1638400 | tf_op jit(solution)/shard_map/slice | solution.py:230
  12.9 3.9 %collective-permute-start.6 = (bf16[800,256]{1,0:T(8,128)(2,1)}, bf16[800,256]{1,0:T(8,128)(2,1)}, u32[]{:S(2)}, u32[]{:S(2)}) collective-permute-start(bf16[800,256]{1,0:T(8,128)(2,1)} %bitcast.9), channel_id=1, source_target_pairs={{31,0},{0,1},{1,2},{2,3},{3,4},{4,5},{5,6},{6,7},{7,8},{8,9},{9,10... | collective-permute-start | bytes 1228808 | tf_op jit(solution)/shard_map/ppermute | solution.py:19
  16.7 0.0 collective-permute-start.7
  16.7 0.0 collective-permute-done.1.south_ref
  16.8 0.0 copy-start.6
  16.8 0.0 copy-start.3
  16.8 0.0 copy-start.4
  16.8 0.1 fusion.4
  16.9 1.1 %pad_maximum_fusion = (bf16[1120,256]{1,0:T(8,128)(2,1)}, bf16[1120,256]{1,0:T(8,128)(2,1)}) fusion(bf16[320,256]{1,0:T(8,128)(2,1)S(1)} %bitcast.15, bf16[800,256]{1,0:T(8,128)(2,1)S(1)} %bitcast.13, bf16[800,256]{1,0:T(8,128)(2,1)S(1)} %bitcast.14), kind=kLoop, calls=%fused_computation.6 | loop fusion | flops 2007040 | bytes 2129920 | tf_op jit(solution)/shard_map/concatenate | solution.py:233
  17.9 0.0 copy-done.6
  17.9 3.2 %collective-permute-start.2 = (bf16[1120,256]{1,0:T(8,128)(2,1)}, bf16[1120,256]{1,0:T(8,128)(2,1)S(1)}, u32[]{:S(2)}, u32[]{:S(2)}) collective-permute-start(bf16[1120,256]{1,0:T(8,128)(2,1)} %get-tuple-element.14), channel_id=1, source_target_pairs={{31,0},{0,1},{1,2},{2,3},{3,4},{4,5},{5,6},{6,7},{7,8},{8,9},{9,10... | collective-permute-start | bytes 1720328 | tf_op jit(solution)/shard_map/ppermute | solution.py:19
  21.2 0.0 copy-done.3
  21.2 0.0 copy-done.4
  21.2 0.4 multiply_convert_fusion
  21.6 0.1 collective-permute-start.3
  21.7 0.3 constant_dynamic-slice_fusion
  22.1 0.1 pad.23
  22.2 1.0 %copy.12 = bf16[96,9,192]{2,1,0:T(8,128)(2,1)S(1)} copy(bf16[96,9,192]{0,2,1:T(8,128)(2,1)S(1)} %bitcast.12) | data formatting | bytes 663552 | tf_op jit(solution)/shard_map/reshape | solution.py:45
  23.2 1.1 %pad.24.src_ref = bf16[96,9,256]{2,1,0:T(8,128)(2,1)} pad(bf16[96,9,192]{2,1,0:T(8,128)(2,1)S(1)} %copy.12, bf16[]{:T(256)} %constant.8.clone.1), padding=0_0x0_0x0_64 | pad | bytes 774146 | tf_op jit(solution)/shard_map/jit(_pad)/pad | solution.py:46
  24.3 0.2 pad.21
  24.5 0.6 %copy.11 = bf16[8,9,480]{2,1,0:T(8,128)(2,1)S(1)} copy(bf16[8,9,480]{0,2,1:T(8,128)(2,1)S(1)} %bitcast.11) | data formatting | bytes 138240 | tf_op jit(solution)/shard_map/reshape | solution.py:45
  25.1 0.7 %pad.22.src_ref = bf16[8,9,512]{2,1,0:T(8,128)(2,1)} pad(bf16[8,9,480]{2,1,0:T(8,128)(2,1)S(1)} %copy.11, bf16[]{:T(256)} %constant.8.clone.1), padding=0_0x0_0x0_32 | pad | bytes 142850 | tf_op jit(solution)/shard_map/jit(_pad)/pad | solution.py:46
  25.8 0.6 %pad_add_fusion.scalar_ref = s32[2]{0:T(128)} fusion(s32[1]{0:T(128)} %bitcast.1, s32[1]{0:T(128)} %bitcast), kind=kLoop, calls=%fused_computation.22 | loop fusion | flops 2 | bytes 16 | tf_op jit(solution)/shard_map/stack | solution.py:214
  26.5 0.0 collective-permute-done
  26.5 4.7 %collective-permute-start.4 = (bf16[10,32,256]{2,1,0:T(8,128)(2,1)S(1)}, bf16[10,32,256]{2,1,0:T(8,128)(2,1)S(1)}, u32[]{:S(2)}, u32[]{:S(2)}) collective-permute-start(bf16[10,32,256]{2,1,0:T(8,128)(2,1)S(1)} %fusion.2), channel_id=1, source_target_pairs={{2,0},{3,1},{4,2},{5,3},{6,4},{7,5},{8,6},{9,7},{10,8},{11,9},{12,... | collective-permute-start | bytes 491528 | tf_op jit(solution)/shard_map/ppermute | solution.py:19
  31.2 0.9 %constant_dynamic-update-slice_fusion.6 = bf16[10,160,256]{2,1,0:T(8,128)(2,1)S(1)} fusion(bf16[10,32,256]{2,1,0:T(8,128)(2,1)} %collective-permute-done), kind=kLoop, calls=%fused_computation.17 | loop fusion | bytes 327680
  32.1 0.0 collective-permute-done.6.west_ref
  32.1 5.6 %collective-permute-done.7.east_ref = bf16[800,256]{1,0:T(8,128)(2,1)} collective-permute-done((bf16[800,256]{1,0:T(8,128)(2,1)}, bf16[800,256]{1,0:T(8,128)(2,1)}, u32[]{:S(2)}, u32[]{:S(2)}) %collective-permute-start.7) | collective-permute-done | bytes 409632 | tf_op jit(solution)/shard_map/ppermute | solution.py:19
  37.7 0.0 copy-start.1
  37.7 7.8 %shard_map.55.rest_0_ = bf16[96,32,256]{2,1,0:T(8,128)(2,1)} custom-call(s32[2]{0:T(128)} %pad_add_fusion.scalar_ref, bf16[96,9,256]{2,1,0:T(8,128)(2,1)} %pad.24.src_ref, bf16[96,32,256]{2,1,0:T(8,128)(2,1)} %f_ref.5, bf16[96,32,256]{2,1,0:T(8,128)(2,1)} %f_ref.5, bf16[96,32,256]{2,1,0:T(8,128)(2,1)} %f_ref.5, ...), custom_call_target="tpu_custom_call" | custom-call | tf_op jit(solution)/shard_map/pallas_call | solution.py:172
  45.6 0.0 collective-permute-done.2.west_ref
  45.6 0.0 copy-start.2
  45.6 0.0 copy-done.1
  45.7 0.1 constant_dynamic-update-slice_fusion.4
  45.7 0.0 collective-permute-done.3.east_ref
  45.7 1.0 %slice.47 = bf16[320,256]{1,0:T(8,128)(2,1)S(1)} slice(bf16[1120,256]{1,0:T(8,128)(2,1)} %collective-permute-done.3.east_ref), slice={[800:1120], [0:256]} | slice | bytes 327680 | tf_op jit(solution)/shard_map/slice | solution.py:251
  46.8 0.0 collective-permute-done.4
  46.8 0.0 copy-done.2
  46.8 1.0 %pad.20.ext_ref = bf16[11,160,256]{2,1,0:T(8,128)(2,1)} pad(bf16[10,160,256]{2,1,0:T(8,128)(2,1)S(1)} %constant_dynamic-update-slice_fusion.2, bf16[]{:T(256)} %constant.8.clone.1), padding=0_1x0_0x0_0 | pad | bytes 1720322 | tf_op jit(solution)/shard_map/jit(_pad)/pad | solution.py:254
  47.8 7.8 %shard_map.56.prev_ref = bf16[96,32,256]{2,1,0:T(8,128)(2,1)} custom-call(s32[2]{0:T(128)} %pad_add_fusion.scalar_ref, bf16[96,9,256]{2,1,0:T(8,128)(2,1)} %pad.24.src_ref, bf16[96,32,256]{2,1,0:T(8,128)(2,1)} %f_ref.5, bf16[96,32,256]{2,1,0:T(8,128)(2,1)} %f_ref.5, bf16[96,32,256]{2,1,0:T(8,128)(2,1)} %f_ref.5, ...), custom_call_target="tpu_custom_call", output_to_operand_aliasing={{}: (10, {})} | custom-call | tf_op jit(solution)/shard_map/pallas_call | solution.py:172
  55.6 3.0 %shard_map.57 = bf16[96,32,256]{2,1,0:T(8,128)(2,1)} custom-call(s32[2]{0:T(128)} %pad_add_fusion.scalar_ref, bf16[11,160,256]{2,1,0:T(8,128)(2,1)} %pad.20.ext_ref, bf16[8,9,512]{2,1,0:T(8,128)(2,1)} %pad.22.src_ref, bf16[96,32,256]{2,1,0:T(8,128)(2,1)} %f_ref.5, bf16[9,256,256]{2,1,0:T(8,128)(2,1)} %w_ref.1, ...), custom_call_target="tpu_custom_call", output_to_operand_aliasing={{}: (5, {})} | custom-call | tf_op jit(solution)/shard_map/pallas_call | solution.py:197
  (10 shorter events, 0.1 us)
Async XLA Ops:
  0.0 11.3 %copy-start = (bf16[96,32,256]{2,1,0:T(8,128)(2,1)S(1)}, bf16[96,32,256]{2,1,0:T(8,128)(2,1)}, u32[]{:S(2)}) copy-start(bf16[96,32,256]{2,1,0:T(8,128)(2,1)} %f_ref.5) | copy-start | bytes 4718596
  0.0 11.2 %copy-start.7 = (s32[96]{0:T(128)S(1)}, s32[96]{0:T(128)}, u32[]{:S(2)}) copy-start(s32[96]{0:T(128)} %param.8) | copy-start | bytes 1156
  0.9 10.4 %collective-permute-start.5 = (bf16[1,32,256]{2,1,0:T(8,128)(2,1)S(1)}, bf16[1,32,256]{2,1,0:T(8,128)(2,1)S(1)}, u32[]{:S(2)}, u32[]{:S(2)}) collective-permute-start(bf16[1,32,256]{2,1,0:T(8,128)(2,1)S(1)} %get-tuple-element.11), channel_id=1, source_target_pairs={{0,32},{32,64},{64,96},{96,128},{128,160},{160,192},{192,224},{1,3... | collective-permute-start | bytes 49160 | tf_op jit(solution)/shard_map/ppermute | solution.py:223
  4.1 12.7 %collective-permute-start.1 = (bf16[1,32,256]{2,1,0:T(8,128)(2,1)S(1)}, bf16[1,32,256]{2,1,0:T(8,128)(2,1)S(1)}, u32[]{:S(2)}, u32[]{:S(2)}) collective-permute-start(bf16[1,32,256]{2,1,0:T(8,128)(2,1)S(1)} %get-tuple-element.12), channel_id=1, source_target_pairs={{32,0},{64,32},{96,64},{128,96},{160,128},{192,160},{224,192},{33,... | collective-permute-start | bytes 49160 | tf_op jit(solution)/shard_map/ppermute | solution.py:224
  9.3 17.2 %collective-permute-start = (bf16[10,32,256]{2,1,0:T(8,128)(2,1)S(1)}, bf16[10,32,256]{2,1,0:T(8,128)(2,1)}, u32[]{:S(2)}, u32[]{:S(2)}) collective-permute-start(bf16[10,32,256]{2,1,0:T(8,128)(2,1)S(1)} %fusion.2), channel_id=1, source_target_pairs={{30,0},{31,1},{0,2},{1,3},{2,4},{3,5},{4,6},{5,7},{6,8},{7,9},{8,1... | collective-permute-start | bytes 491528 | tf_op jit(solution)/shard_map/ppermute | solution.py:19
  11.3 0.6 %copy-start.5 = (bf16[1,32,256]{2,1,0:T(8,128)(2,1)}, bf16[1,32,256]{2,1,0:T(8,128)(2,1)S(1)}, u32[]{:S(2)}) copy-start(bf16[1,32,256]{2,1,0:T(8,128)(2,1)S(1)} %collective-permute-done.5.north_ref) | copy-start | bytes 49156
  12.9 19.3 %collective-permute-start.6 = (bf16[800,256]{1,0:T(8,128)(2,1)}, bf16[800,256]{1,0:T(8,128)(2,1)}, u32[]{:S(2)}, u32[]{:S(2)}) collective-permute-start(bf16[800,256]{1,0:T(8,128)(2,1)} %bitcast.9), channel_id=1, source_target_pairs={{31,0},{0,1},{1,2},{2,3},{3,4},{4,5},{5,6},{6,7},{7,8},{8,9},{9,10... | collective-permute-start | bytes 1228808 | tf_op jit(solution)/shard_map/ppermute | solution.py:19
  16.7 21.0 %collective-permute-start.7 = (bf16[800,256]{1,0:T(8,128)(2,1)}, bf16[800,256]{1,0:T(8,128)(2,1)}, u32[]{:S(2)}, u32[]{:S(2)}) collective-permute-start(bf16[800,256]{1,0:T(8,128)(2,1)} %bitcast.10), channel_id=1, source_target_pairs={{1,0},{2,1},{3,2},{4,3},{5,4},{6,5},{7,6},{8,7},{9,8},{10,9},{11,1... | collective-permute-start | bytes 1228808 | tf_op jit(solution)/shard_map/ppermute | solution.py:19
  16.8 1.2 %copy-start.6 = (bf16[1,32,256]{2,1,0:T(8,128)(2,1)}, bf16[1,32,256]{2,1,0:T(8,128)(2,1)S(1)}, u32[]{:S(2)}) copy-start(bf16[1,32,256]{2,1,0:T(8,128)(2,1)S(1)} %collective-permute-done.1.south_ref) | copy-start | bytes 49156
  16.8 4.4 %copy-start.3 = (f32[96,3,129]{0,2,1:T(8,128)S(1)}, f32[96,3,129]{0,2,1:T(8,128)}, u32[]{:S(2)}) copy-start(f32[96,3,129]{0,2,1:T(8,128)} %param.6) | copy-start | bytes 445828
  16.8 4.4 %copy-start.4 = (s32[96,3,129]{0,2,1:T(8,128)S(1)}, s32[96,3,129]{0,2,1:T(8,128)}, u32[]{:S(2)}) copy-start(s32[96,3,129]{0,2,1:T(8,128)} %param.7) | copy-start | bytes 445828
  17.9 27.6 %collective-permute-start.2 = (bf16[1120,256]{1,0:T(8,128)(2,1)}, bf16[1120,256]{1,0:T(8,128)(2,1)S(1)}, u32[]{:S(2)}, u32[]{:S(2)}) collective-permute-start(bf16[1120,256]{1,0:T(8,128)(2,1)} %get-tuple-element.14), channel_id=1, source_target_pairs={{31,0},{0,1},{1,2},{2,3},{3,4},{4,5},{5,6},{6,7},{7,8},{8,9},{9,10... | collective-permute-start | bytes 1720328 | tf_op jit(solution)/shard_map/ppermute | solution.py:19
  21.6 24.1 %collective-permute-start.3 = (bf16[1120,256]{1,0:T(8,128)(2,1)}, bf16[1120,256]{1,0:T(8,128)(2,1)}, u32[]{:S(2)}, u32[]{:S(2)}) collective-permute-start(bf16[1120,256]{1,0:T(8,128)(2,1)} %get-tuple-element.13), channel_id=1, source_target_pairs={{1,0},{2,1},{3,2},{4,3},{5,4},{6,5},{7,6},{8,7},{9,8},{10,9},{11,1... | collective-permute-start | bytes 1720328 | tf_op jit(solution)/shard_map/ppermute | solution.py:19
  26.5 20.3 %collective-permute-start.4 = (bf16[10,32,256]{2,1,0:T(8,128)(2,1)S(1)}, bf16[10,32,256]{2,1,0:T(8,128)(2,1)S(1)}, u32[]{:S(2)}, u32[]{:S(2)}) collective-permute-start(bf16[10,32,256]{2,1,0:T(8,128)(2,1)S(1)} %fusion.2), channel_id=1, source_target_pairs={{2,0},{3,1},{4,2},{5,3},{6,4},{7,5},{8,6},{9,7},{10,8},{11,9},{12,... | collective-permute-start | bytes 491528 | tf_op jit(solution)/shard_map/ppermute | solution.py:19
  37.7 7.9 %copy-start.1 = (bf16[96,32,256]{2,1,0:T(8,128)(2,1)S(1)}, bf16[96,32,256]{2,1,0:T(8,128)(2,1)}, u32[]{:S(2)}) copy-start(bf16[96,32,256]{2,1,0:T(8,128)(2,1)} %f_ref.5) | copy-start | bytes 4718596
  45.6 1.2 %copy-start.2 = (bf16[1120,256]{1,0:T(8,128)(2,1)}, bf16[1120,256]{1,0:T(8,128)(2,1)S(1)}, u32[]{:S(2)}) copy-start(bf16[1120,256]{1,0:T(8,128)(2,1)S(1)} %collective-permute-done.2.west_ref) | copy-start | bytes 1720324

commit v16 on v15

--- a/solution.py
+++ b/solution.py
@@ -119,10 +119,13 @@
     conv_block(ext_scr, src_ref, f_ref, w_ref, o_ref, conv_scr, 0, wait_weights)
 
 
-def wide_kernel(scalar_ref, ext_ref, src_ref, f_ref, w_ref, prev_ref, o_ref, conv_scr):
+def wide_kernel(scalar_ref, ext_ref, src_ref, f_ref, w_hbm, prev_ref, o_ref, conv_scr, w_ref,
+                w_sem):
     @pl.when(scalar_ref[1] != 0)
     def _():
-        conv_block(ext_ref, src_ref, f_ref, w_ref, o_ref, conv_scr, 0)
+        weights = pltpu.make_async_copy(w_hbm, w_ref, w_sem)
+        weights.start()
+        conv_block(ext_ref, src_ref, f_ref, w_ref, o_ref, conv_scr, 0, weights.wait)
 
     @pl.when(scalar_ref[1] == 0)
     def _():
@@ -188,11 +191,15 @@
             full_spec(extended.shape),
             pl.BlockSpec((BLOCK,) + sources.shape[1:], lambda i, s: (i, 0, 0)),
             pl.BlockSpec((BLOCK, columns, channels), row_map),
-            full_spec(mix_weight.shape),
+            pl.BlockSpec(memory_space=pl.ANY),
             pl.BlockSpec((BLOCK, columns, channels), row_map),
         ],
         out_specs=pl.BlockSpec((BLOCK, columns, channels), row_map),
-        scratch_shapes=[pltpu.VMEM((count, BLOCK * columns, channels), jnp.bfloat16)],
+        scratch_shapes=[
+            pltpu.VMEM((count, BLOCK * columns, channels), jnp.bfloat16),
+            pltpu.VMEM(mix_weight.shape, mix_weight.dtype),
+            pltpu.SemaphoreType.DMA(()),
+        ],
     )
     return pl.pallas_call(
         wide_kernel, grid_spec=grid_spec,

time: 59.5 us -> 59.6 us (level)
  the two profiles are of different devices: /device:TPU:3 before, /device:TPU:1 now
where the time goes in v16:
time: 59.6 us; the launch traced here: 59.2 us
  Pallas kernels  20.3 us (34%)
  starting transfers between devices  19.8 us (33%)
  local copies, waits for them, and re-layouts  9.51 us (16%)
  waiting for transfers between devices  5.9 us (10%)
  other arithmetic  3.29 us (6%)
    pallas_call x2, Pallas kernels, near_call(): pl.pallas_call(functools.partial(near_kernel, first=first, lowest=lowest,...  15.6 us
    ppermute x6, starting transfers between devices, shifted(): return lax.ppermute(block, axis, route)  14.5 us
    ppermute x6, waiting for transfers between devices, shifted(): return lax.ppermute(block, axis, route)  5.9 us
    pallas_call x1, Pallas kernels, wide_call(): pl.pallas_call(wide_kernel, grid_spec=grid_spec, out_shape=jax.ShapeDtype...  4.67 us
    ppermute x1, starting transfers between devices, body(): north = lax.ppermute(features[lat_rows - 1:], 'lat', up)  4.02 us
    pad x2, local copies, waits for them, and re-layouts, flat_sources(): return jnp.pad(flat, ((0, 0), (0, 0), (0, lanes - offsets * span)))  1.75 us
    reshape x2, local copies, waits for them, and re-layouts, flat_sources(): flat = flat.reshape(rows, count, offsets * span)  1.65 us
    unnamed x20, local copies, waits for them, and re-layouts  1.31 us
  transfers between devices with their start and end apart: 8, of which 1 were waited for; matrix products, arithmetic and copies ran while one was open for 18% of the time, Pallas kernels for 13%

profile of v16, /device:TPU:1, one launch (start us, length us, event | category | flops | bytes accessed | tf_op | source)
XLA Modules:
  0.0 59.2 jit_solution(16041368390481708768)
XLA Ops:
  0.0 0.0 copy-start
  0.0 0.0 copy-start.7
  0.0 0.9 %fusion.5 = (bf16[1,32,256]{2,1,0:T(8,128)(2,1)S(1)}, bf16[1,32,256]{2,1,0:T(8,128)(2,1)S(1)}) fusion(bf16[96,32,256]{2,1,0:T(8,128)(2,1)} %f_ref.5), kind=kLoop, calls=%fused_computation.26 | loop fusion | bytes 65536 | tf_op jit(solution)/shard_map/slice | solution.py:230
  0.9 4.0 %collective-permute-start.5 = (bf16[1,32,256]{2,1,0:T(8,128)(2,1)S(1)}, bf16[1,32,256]{2,1,0:T(8,128)(2,1)S(1)}, u32[]{:S(2)}, u32[]{:S(2)}) collective-permute-start(bf16[1,32,256]{2,1,0:T(8,128)(2,1)S(1)} %get-tuple-element.11), channel_id=1, source_target_pairs={{0,32},{32,64},{64,96},{96,128},{128,160},{160,192},{192,224},{1,3... | collective-permute-start | bytes 49160 | tf_op jit(solution)/shard_map/ppermute | solution.py:230
  4.9 1.3 %collective-permute-start.1 = (bf16[1,32,256]{2,1,0:T(8,128)(2,1)S(1)}, bf16[1,32,256]{2,1,0:T(8,128)(2,1)S(1)}, u32[]{:S(2)}, u32[]{:S(2)}) collective-permute-start(bf16[1,32,256]{2,1,0:T(8,128)(2,1)S(1)} %get-tuple-element.12), channel_id=1, source_target_pairs={{32,0},{64,32},{96,64},{128,96},{160,128},{192,160},{224,192},{33,... | collective-permute-start | bytes 49160 | tf_op jit(solution)/shard_map/ppermute | solution.py:231
  6.2 1.0 %fusion.2 = bf16[10,32,256]{2,1,0:T(8,128)(2,1)S(1)} fusion(s32[]{:T(128)} %select_n.10, bf16[1,32,256]{2,1,0:T(8,128)(2,1)S(1)} %broadcast_in_dim.10, bf16[96,32,256]{2,1,0:T(8,128)(2,1)} %f_ref.5), kind=kLoop, calls=%fused_computation.9 | loop fusion | flops 163840 | bytes 1753092 | tf_op jit(solution)/shard_map/concatenate | solution.py:225
  7.2 2.8 %collective-permute-start = (bf16[10,32,256]{2,1,0:T(8,128)(2,1)S(1)}, bf16[10,32,256]{2,1,0:T(8,128)(2,1)}, u32[]{:S(2)}, u32[]{:S(2)}) collective-permute-start(bf16[10,32,256]{2,1,0:T(8,128)(2,1)S(1)} %fusion.2), channel_id=1, source_target_pairs={{30,0},{31,1},{0,2},{1,3},{2,4},{3,5},{4,6},{5,7},{6,8},{7,9},{8,1... | collective-permute-start | bytes 491528 | tf_op jit(solution)/shard_map/ppermute | solution.py:19
  10.0 0.0 copy-done.7
  10.0 0.1 broadcast_compare_fusion
  10.1 0.0 collective-permute-done.5.north_ref
  10.1 0.0 copy-start.5
  10.2 0.0 copy-done
  10.2 0.2 constant_dynamic-update-slice_fusion.7
  10.4 0.3 copy-done.5
  10.7 1.0 %fusion.3 = (bf16[50,16,256]{2,1,0:T(8,128)(2,1)}, bf16[50,16,256]{2,1,0:T(8,128)(2,1)}) fusion(bf16[97,32,256]{2,1,0:T(8,128)(2,1)S(1)} %get-tuple-element.9), kind=kLoop, calls=%fused_computation.24 | loop fusion | bytes 1638400 | tf_op jit(solution)/shard_map/slice | solution.py:237
  11.7 2.7 %collective-permute-start.6 = (bf16[800,256]{1,0:T(8,128)(2,1)}, bf16[800,256]{1,0:T(8,128)(2,1)}, u32[]{:S(2)}, u32[]{:S(2)}) collective-permute-start(bf16[800,256]{1,0:T(8,128)(2,1)} %bitcast.9), channel_id=1, source_target_pairs={{31,0},{0,1},{1,2},{2,3},{3,4},{4,5},{5,6},{6,7},{7,8},{8,9},{9,10... | collective-permute-start | bytes 1228808 | tf_op jit(solution)/shard_map/ppermute | solution.py:19
  14.4 0.0 collective-permute-start.7
  14.4 0.0 collective-permute-done.1.south_ref
  14.4 0.0 copy-start.6
  14.4 0.0 copy-start.3
  14.4 0.0 copy-start.4
  14.4 0.1 fusion.4
  14.5 1.1 %pad_maximum_fusion = (bf16[1120,256]{1,0:T(8,128)(2,1)}, bf16[1120,256]{1,0:T(8,128)(2,1)}) fusion(bf16[320,256]{1,0:T(8,128)(2,1)S(1)} %bitcast.15, bf16[800,256]{1,0:T(8,128)(2,1)S(1)} %bitcast.13, bf16[800,256]{1,0:T(8,128)(2,1)S(1)} %bitcast.14), kind=kLoop, calls=%fused_computation.6 | loop fusion | flops 2007040 | bytes 2129920 | tf_op jit(solution)/shard_map/concatenate | solution.py:240
  15.6 0.0 copy-done.6
  15.6 3.2 %collective-permute-start.2 = (bf16[1120,256]{1,0:T(8,128)(2,1)}, bf16[1120,256]{1,0:T(8,128)(2,1)S(1)}, u32[]{:S(2)}, u32[]{:S(2)}) collective-permute-start(bf16[1120,256]{1,0:T(8,128)(2,1)} %get-tuple-element.14), channel_id=1, source_target_pairs={{31,0},{0,1},{1,2},{2,3},{3,4},{4,5},{5,6},{6,7},{7,8},{8,9},{9,10... | collective-permute-start | bytes 1720328 | tf_op jit(solution)/shard_map/ppermute | solution.py:19
  18.8 0.0 copy-done.3
  18.8 0.0 copy-done.4
  18.8 0.4 multiply_convert_fusion
  19.3 0.7 %collective-permute-start.3 = (bf16[1120,256]{1,0:T(8,128)(2,1)}, bf16[1120,256]{1,0:T(8,128)(2,1)}, u32[]{:S(2)}, u32[]{:S(2)}) collective-permute-start(bf16[1120,256]{1,0:T(8,128)(2,1)} %get-tuple-element.13), channel_id=1, source_target_pairs={{1,0},{2,1},{3,2},{4,3},{5,4},{6,5},{7,6},{8,7},{9,8},{10,9},{11,1... | collective-permute-start | bytes 1720328 | tf_op jit(solution)/shard_map/ppermute | solution.py:19
  20.0 0.3 constant_dynamic-slice_fusion
  20.4 0.1 pad.23
  20.5 1.0 %copy.12 = bf16[96,9,192]{2,1,0:T(8,128)(2,1)S(1)} copy(bf16[96,9,192]{0,2,1:T(8,128)(2,1)S(1)} %bitcast.12) | data formatting | bytes 663552 | tf_op jit(solution)/shard_map/reshape | solution.py:45
  21.5 1.1 %pad.24.src_ref = bf16[96,9,256]{2,1,0:T(8,128)(2,1)} pad(bf16[96,9,192]{2,1,0:T(8,128)(2,1)S(1)} %copy.12, bf16[]{:T(256)} %constant.8.clone.1), padding=0_0x0_0x0_64 | pad | bytes 774146 | tf_op jit(solution)/shard_map/jit(_pad)/pad | solution.py:46
  22.6 0.2 pad.21
  22.8 0.6 %copy.11 = bf16[8,9,480]{2,1,0:T(8,128)(2,1)S(1)} copy(bf16[8,9,480]{0,2,1:T(8,128)(2,1)S(1)} %bitcast.11) | data formatting | bytes 138240 | tf_op jit(solution)/shard_map/reshape | solution.py:45
  23.4 0.7 %pad.22.src_ref = bf16[8,9,512]{2,1,0:T(8,128)(2,1)} pad(bf16[8,9,480]{2,1,0:T(8,128)(2,1)S(1)} %copy.11, bf16[]{:T(256)} %constant.8.clone.1), padding=0_0x0_0x0_32 | pad | bytes 142850 | tf_op jit(solution)/shard_map/jit(_pad)/pad | solution.py:46
  24.1 0.6 %pad_add_fusion.scalar_ref = s32[2]{0:T(128)} fusion(s32[1]{0:T(128)} %bitcast.1, s32[1]{0:T(128)} %bitcast), kind=kLoop, calls=%fused_computation.22 | loop fusion | flops 2 | bytes 16 | tf_op jit(solution)/shard_map/stack | solution.py:221
  24.8 0.0 collective-permute-done
  24.8 5.0 %collective-permute-start.4 = (bf16[10,32,256]{2,1,0:T(8,128)(2,1)S(1)}, bf16[10,32,256]{2,1,0:T(8,128)(2,1)S(1)}, u32[]{:S(2)}, u32[]{:S(2)}) collective-permute-start(bf16[10,32,256]{2,1,0:T(8,128)(2,1)S(1)} %fusion.2), channel_id=1, source_target_pairs={{2,0},{3,1},{4,2},{5,3},{6,4},{7,5},{8,6},{9,7},{10,8},{11,9},{12,... | collective-permute-start | bytes 491528 | tf_op jit(solution)/shard_map/ppermute | solution.py:19
  29.7 0.9 %constant_dynamic-update-slice_fusion.6 = bf16[10,160,256]{2,1,0:T(8,128)(2,1)S(1)} fusion(bf16[10,32,256]{2,1,0:T(8,128)(2,1)} %collective-permute-done), kind=kLoop, calls=%fused_computation.17 | loop fusion | bytes 327680
  30.7 0.0 collective-permute-done.6.west_ref
  30.7 5.9 %collective-permute-done.7.east_ref = bf16[800,256]{1,0:T(8,128)(2,1)} collective-permute-done((bf16[800,256]{1,0:T(8,128)(2,1)}, bf16[800,256]{1,0:T(8,128)(2,1)}, u32[]{:S(2)}, u32[]{:S(2)}) %collective-permute-start.7) | collective-permute-done | bytes 409632 | tf_op jit(solution)/shard_map/ppermute | solution.py:19
  36.6 0.0 copy-start.1
  36.6 7.8 %shard_map.55.rest_0_ = bf16[96,32,256]{2,1,0:T(8,128)(2,1)} custom-call(s32[2]{0:T(128)} %pad_add_fusion.scalar_ref, bf16[96,9,256]{2,1,0:T(8,128)(2,1)} %pad.24.src_ref, bf16[96,32,256]{2,1,0:T(8,128)(2,1)} %f_ref.5, bf16[96,32,256]{2,1,0:T(8,128)(2,1)} %f_ref.5, bf16[96,32,256]{2,1,0:T(8,128)(2,1)} %f_ref.5, ...), custom_call_target="tpu_custom_call" | custom-call | tf_op jit(solution)/shard_map/pallas_call | solution.py:175
  44.4 0.0 collective-permute-done.2.west_ref
  44.4 0.0 copy-start.2
  44.5 0.0 copy-done.1
  44.5 0.1 constant_dynamic-update-slice_fusion.4
  44.6 0.0 collective-permute-done.3.east_ref
  44.6 1.0 %slice.47 = bf16[320,256]{1,0:T(8,128)(2,1)S(1)} slice(bf16[1120,256]{1,0:T(8,128)(2,1)} %collective-permute-done.3.east_ref), slice={[800:1120], [0:256]} | slice | bytes 327680 | tf_op jit(solution)/shard_map/slice | solution.py:258
  45.6 0.0 collective-permute-done.4
  45.6 0.0 copy-done.2
  45.6 1.0 %pad.20.ext_ref = bf16[11,160,256]{2,1,0:T(8,128)(2,1)} pad(bf16[10,160,256]{2,1,0:T(8,128)(2,1)S(1)} %constant_dynamic-update-slice_fusion.2, bf16[]{:T(256)} %constant.8.clone.1), padding=0_1x0_0x0_0 | pad | bytes 1720322 | tf_op jit(solution)/shard_map/jit(_pad)/pad | solution.py:261
  46.6 7.8 %shard_map.56.prev_ref = bf16[96,32,256]{2,1,0:T(8,128)(2,1)} custom-call(s32[2]{0:T(128)} %pad_add_fusion.scalar_ref, bf16[96,9,256]{2,1,0:T(8,128)(2,1)} %pad.24.src_ref, bf16[96,32,256]{2,1,0:T(8,128)(2,1)} %f_ref.5, bf16[96,32,256]{2,1,0:T(8,128)(2,1)} %f_ref.5, bf16[96,32,256]{2,1,0:T(8,128)(2,1)} %f_ref.5, ...), custom_call_target="tpu_custom_call", output_to_operand_aliasing={{}: (10, {})} | custom-call | tf_op jit(solution)/shard_map/pallas_call | solution.py:175
  54.4 4.7 %shard_map.57 = bf16[96,32,256]{2,1,0:T(8,128)(2,1)} custom-call(s32[2]{0:T(128)} %pad_add_fusion.scalar_ref, bf16[11,160,256]{2,1,0:T(8,128)(2,1)} %pad.20.ext_ref, bf16[8,9,512]{2,1,0:T(8,128)(2,1)} %pad.22.src_ref, bf16[96,32,256]{2,1,0:T(8,128)(2,1)} %f_ref.5, bf16[9,256,256]{2,1,0:T(8,128)(2,1)} %w_hbm.5, ...), custom_call_target="tpu_custom_call", output_to_operand_aliasing={{}: (5, {})} | custom-call | tf_op jit(solution)/shard_map/pallas_call | solution.py:204
  (10 shorter events, 0.1 us)
Async XLA Ops:
  0.0 10.2 %copy-start = (bf16[96,32,256]{2,1,0:T(8,128)(2,1)S(1)}, bf16[96,32,256]{2,1,0:T(8,128)(2,1)}, u32[]{:S(2)}) copy-start(bf16[96,32,256]{2,1,0:T(8,128)(2,1)} %f_ref.5) | copy-start | bytes 4718596
  0.0 10.0 %copy-start.7 = (s32[96]{0:T(128)S(1)}, s32[96]{0:T(128)}, u32[]{:S(2)}) copy-start(s32[96]{0:T(128)} %param.8) | copy-start | bytes 1156
  0.9 9.3 %collective-permute-start.5 = (bf16[1,32,256]{2,1,0:T(8,128)(2,1)S(1)}, bf16[1,32,256]{2,1,0:T(8,128)(2,1)S(1)}, u32[]{:S(2)}, u32[]{:S(2)}) collective-permute-start(bf16[1,32,256]{2,1,0:T(8,128)(2,1)S(1)} %get-tuple-element.11), channel_id=1, source_target_pairs={{0,32},{32,64},{64,96},{96,128},{128,160},{160,192},{192,224},{1,3... | collective-permute-start | bytes 49160 | tf_op jit(solution)/shard_map/ppermute | solution.py:230
  4.9 9.5 %collective-permute-start.1 = (bf16[1,32,256]{2,1,0:T(8,128)(2,1)S(1)}, bf16[1,32,256]{2,1,0:T(8,128)(2,1)S(1)}, u32[]{:S(2)}, u32[]{:S(2)}) collective-permute-start(bf16[1,32,256]{2,1,0:T(8,128)(2,1)S(1)} %get-tuple-element.12), channel_id=1, source_target_pairs={{32,0},{64,32},{96,64},{128,96},{160,128},{192,160},{224,192},{33,... | collective-permute-start | bytes 49160 | tf_op jit(solution)/shard_map/ppermute | solution.py:231
  7.2 17.6 %collective-permute-start = (bf16[10,32,256]{2,1,0:T(8,128)(2,1)S(1)}, bf16[10,32,256]{2,1,0:T(8,128)(2,1)}, u32[]{:S(2)}, u32[]{:S(2)}) collective-permute-start(bf16[10,32,256]{2,1,0:T(8,128)(2,1)S(1)} %fusion.2), channel_id=1, source_target_pairs={{30,0},{31,1},{0,2},{1,3},{2,4},{3,5},{4,6},{5,7},{6,8},{7,9},{8,1... | collective-permute-start | bytes 491528 | tf_op jit(solution)/shard_map/ppermute | solution.py:19
  10.1 0.6 %copy-start.5 = (bf16[1,32,256]{2,1,0:T(8,128)(2,1)}, bf16[1,32,256]{2,1,0:T(8,128)(2,1)S(1)}, u32[]{:S(2)}) copy-start(bf16[1,32,256]{2,1,0:T(8,128)(2,1)S(1)} %collective-permute-done.5.north_ref) | copy-start | bytes 49156
  11.7 19.0 %collective-permute-start.6 = (bf16[800,256]{1,0:T(8,128)(2,1)}, bf16[800,256]{1,0:T(8,128)(2,1)}, u32[]{:S(2)}, u32[]{:S(2)}) collective-permute-start(bf16[800,256]{1,0:T(8,128)(2,1)} %bitcast.9), channel_id=1, source_target_pairs={{31,0},{0,1},{1,2},{2,3},{3,4},{4,5},{5,6},{6,7},{7,8},{8,9},{9,10... | collective-permute-start | bytes 1228808 | tf_op jit(solution)/shard_map/ppermute | solution.py:19
  14.4 22.2 %collective-permute-start.7 = (bf16[800,256]{1,0:T(8,128)(2,1)}, bf16[800,256]{1,0:T(8,128)(2,1)}, u32[]{:S(2)}, u32[]{:S(2)}) collective-permute-start(bf16[800,256]{1,0:T(8,128)(2,1)} %bitcast.10), channel_id=1, source_target_pairs={{1,0},{2,1},{3,2},{4,3},{5,4},{6,5},{7,6},{8,7},{9,8},{10,9},{11,1... | collective-permute-start | bytes 1228808 | tf_op jit(solution)/shard_map/ppermute | solution.py:19
  14.4 1.2 %copy-start.6 = (bf16[1,32,256]{2,1,0:T(8,128)(2,1)}, bf16[1,32,256]{2,1,0:T(8,128)(2,1)S(1)}, u32[]{:S(2)}) copy-start(bf16[1,32,256]{2,1,0:T(8,128)(2,1)S(1)} %collective-permute-done.1.south_ref) | copy-start | bytes 49156
  14.4 4.4 %copy-start.3 = (f32[96,3,129]{0,2,1:T(8,128)S(1)}, f32[96,3,129]{0,2,1:T(8,128)}, u32[]{:S(2)}) copy-start(f32[96,3,129]{0,2,1:T(8,128)} %param.6) | copy-start | bytes 445828
  14.4 4.4 %copy-start.4 = (s32[96,3,129]{0,2,1:T(8,128)S(1)}, s32[96,3,129]{0,2,1:T(8,128)}, u32[]{:S(2)}) copy-start(s32[96,3,129]{0,2,1:T(8,128)} %param.7) | copy-start | bytes 445828
  15.6 28.8 %collective-permute-start.2 = (bf16[1120,256]{1,0:T(8,128)(2,1)}, bf16[1120,256]{1,0:T(8,128)(2,1)S(1)}, u32[]{:S(2)}, u32[]{:S(2)}) collective-permute-start(bf16[1120,256]{1,0:T(8,128)(2,1)} %get-tuple-element.14), channel_id=1, source_target_pairs={{31,0},{0,1},{1,2},{2,3},{3,4},{4,5},{5,6},{6,7},{7,8},{8,9},{9,10... | collective-permute-start | bytes 1720328 | tf_op jit(solution)/shard_map/ppermute | solution.py:19
  19.3 25.3 %collective-permute-start.3 = (bf16[1120,256]{1,0:T(8,128)(2,1)}, bf16[1120,256]{1,0:T(8,128)(2,1)}, u32[]{:S(2)}, u32[]{:S(2)}) collective-permute-start(bf16[1120,256]{1,0:T(8,128)(2,1)} %get-tuple-element.13), channel_id=1, source_target_pairs={{1,0},{2,1},{3,2},{4,3},{5,4},{6,5},{7,6},{8,7},{9,8},{10,9},{11,1... | collective-permute-start | bytes 1720328 | tf_op jit(solution)/shard_map/ppermute | solution.py:19
  24.8 20.8 %collective-permute-start.4 = (bf16[10,32,256]{2,1,0:T(8,128)(2,1)S(1)}, bf16[10,32,256]{2,1,0:T(8,128)(2,1)S(1)}, u32[]{:S(2)}, u32[]{:S(2)}) collective-permute-start(bf16[10,32,256]{2,1,0:T(8,128)(2,1)S(1)} %fusion.2), channel_id=1, source_target_pairs={{2,0},{3,1},{4,2},{5,3},{6,4},{7,5},{8,6},{9,7},{10,8},{11,9},{12,... | collective-permute-start | bytes 491528 | tf_op jit(solution)/shard_map/ppermute | solution.py:19
  36.6 7.9 %copy-start.1 = (bf16[96,32,256]{2,1,0:T(8,128)(2,1)S(1)}, bf16[96,32,256]{2,1,0:T(8,128)(2,1)}, u32[]{:S(2)}) copy-start(bf16[96,32,256]{2,1,0:T(8,128)(2,1)} %f_ref.5) | copy-start | bytes 4718596
  44.4 1.2 %copy-start.2 = (bf16[1120,256]{1,0:T(8,128)(2,1)}, bf16[1120,256]{1,0:T(8,128)(2,1)S(1)}, u32[]{:S(2)}) copy-start(bf16[1120,256]{1,0:T(8,128)(2,1)S(1)} %collective-permute-done.2.west_ref) | copy-start | bytes 1720324

commit v17 on v15

--- a/solution.py
+++ b/solution.py
@@ -10,7 +10,7 @@
 POLAR = 8
 NEAR = 16
 BLOCK = 8
-NEAR_BLOCK = 24
+NEAR_BLOCK = 48
 
 
 def shifted(block, axis, distance):

time: 59.5 us -> 58.4 us (0.982)
  Pallas kernels: 18.6 us -> 17.6 us
    pallas_call x2, Pallas kernels: 15.6 us -> 14.6 us  [near_call(): pl.pallas_call(functools.partial(near_kernel, first=first, lowest=lowest,...]
where the time goes in v17:
time: 58.4 us; the launch traced here: 57.5 us
  starting transfers between devices  21.2 us (36%)
  Pallas kernels  17.6 us (30%)
  local copies, waits for them, and re-layouts  9.51 us (16%)
  waiting for transfers between devices  5.62 us (10%)
  other arithmetic  3.29 us (6%)
    pallas_call x2, Pallas kernels, near_call(): pl.pallas_call(functools.partial(near_kernel, first=first, lowest=lowest,...  14.6 us
    ppermute x6, starting transfers between devices, shifted(): return lax.ppermute(block, axis, route)  13.8 us
    ppermute x6, waiting for transfers between devices, shifted(): return lax.ppermute(block, axis, route)  5.62 us
    ppermute x1, starting transfers between devices, body(): south = lax.ppermute(features[:1], 'lat', down)  4.19 us
    ppermute x1, starting transfers between devices, body(): north = lax.ppermute(features[lat_rows - 1:], 'lat', up)  3.19 us
    pallas_call x1, Pallas kernels, wide_call(): pl.pallas_call(wide_kernel, grid_spec=grid_spec, out_shape=jax.ShapeDtype...  2.97 us
    pad x2, local copies, waits for them, and re-layouts, flat_sources(): return jnp.pad(flat, ((0, 0), (0, 0), (0, lanes - offsets * span)))  1.75 us
    reshape x2, local copies, waits for them, and re-layouts, flat_sources(): flat = flat.reshape(rows, count, offsets * span)  1.65 us
  transfers between devices with their start and end apart: 8, of which 1 were waited for; matrix products, arithmetic and copies ran while one was open for 18% of the time, Pallas kernels for 13%

profile of v17, /device:TPU:3, one launch (start us, length us, event | category | flops | bytes accessed | tf_op | source)
XLA Modules:
  0.0 57.5 jit_solution(16242004716574910101)
XLA Ops:
  0.0 0.0 copy-start
  0.0 0.0 copy-start.7
  0.0 0.9 %fusion.5 = (bf16[1,32,256]{2,1,0:T(8,128)(2,1)S(1)}, bf16[1,32,256]{2,1,0:T(8,128)(2,1)S(1)}) fusion(bf16[96,32,256]{2,1,0:T(8,128)(2,1)} %f_ref.5), kind=kLoop, calls=%fused_computation.26 | loop fusion | bytes 65536 | tf_op jit(solution)/shard_map/slice | solution.py:223
  0.9 3.2 %collective-permute-start.5 = (bf16[1,32,256]{2,1,0:T(8,128)(2,1)S(1)}, bf16[1,32,256]{2,1,0:T(8,128)(2,1)S(1)}, u32[]{:S(2)}, u32[]{:S(2)}) collective-permute-start(bf16[1,32,256]{2,1,0:T(8,128)(2,1)S(1)} %get-tuple-element.11), channel_id=1, source_target_pairs={{0,32},{32,64},{64,96},{96,128},{128,160},{160,192},{192,224},{1,3... | collective-permute-start | bytes 49160 | tf_op jit(solution)/shard_map/ppermute | solution.py:223
  4.1 4.2 %collective-permute-start.1 = (bf16[1,32,256]{2,1,0:T(8,128)(2,1)S(1)}, bf16[1,32,256]{2,1,0:T(8,128)(2,1)S(1)}, u32[]{:S(2)}, u32[]{:S(2)}) collective-permute-start(bf16[1,32,256]{2,1,0:T(8,128)(2,1)S(1)} %get-tuple-element.12), channel_id=1, source_target_pairs={{32,0},{64,32},{96,64},{128,96},{160,128},{192,160},{224,192},{33,... | collective-permute-start | bytes 49160 | tf_op jit(solution)/shard_map/ppermute | solution.py:224
  8.3 1.0 %fusion.2 = bf16[10,32,256]{2,1,0:T(8,128)(2,1)S(1)} fusion(s32[]{:T(128)} %select_n.10, bf16[1,32,256]{2,1,0:T(8,128)(2,1)S(1)} %broadcast_in_dim.10, bf16[96,32,256]{2,1,0:T(8,128)(2,1)} %f_ref.5), kind=kLoop, calls=%fused_computation.9 | loop fusion | flops 163840 | bytes 1753092 | tf_op jit(solution)/shard_map/concatenate | solution.py:218
  9.3 1.9 %collective-permute-start = (bf16[10,32,256]{2,1,0:T(8,128)(2,1)S(1)}, bf16[10,32,256]{2,1,0:T(8,128)(2,1)}, u32[]{:S(2)}, u32[]{:S(2)}) collective-permute-start(bf16[10,32,256]{2,1,0:T(8,128)(2,1)S(1)} %fusion.2), channel_id=1, source_target_pairs={{30,0},{31,1},{0,2},{1,3},{2,4},{3,5},{4,6},{5,7},{6,8},{7,9},{8,1... | collective-permute-start | bytes 491528 | tf_op jit(solution)/shard_map/ppermute | solution.py:19
  11.2 0.0 copy-done.7
  11.2 0.1 broadcast_compare_fusion
  11.3 0.0 collective-permute-done.5.north_ref
  11.3 0.0 copy-start.5
  11.3 0.0 copy-done
  11.3 0.2 constant_dynamic-update-slice_fusion.7
  11.6 0.3 copy-done.5
  11.9 1.0 %fusion.3 = (bf16[50,16,256]{2,1,0:T(8,128)(2,1)}, bf16[50,16,256]{2,1,0:T(8,128)(2,1)}) fusion(bf16[97,32,256]{2,1,0:T(8,128)(2,1)S(1)} %get-tuple-element.9), kind=kLoop, calls=%fused_computation.24 | loop fusion | bytes 1638400 | tf_op jit(solution)/shard_map/slice | solution.py:230
  12.9 3.9 %collective-permute-start.6 = (bf16[800,256]{1,0:T(8,128)(2,1)}, bf16[800,256]{1,0:T(8,128)(2,1)}, u32[]{:S(2)}, u32[]{:S(2)}) collective-permute-start(bf16[800,256]{1,0:T(8,128)(2,1)} %bitcast.9), channel_id=1, source_target_pairs={{31,0},{0,1},{1,2},{2,3},{3,4},{4,5},{5,6},{6,7},{7,8},{8,9},{9,10... | collective-permute-start | bytes 1228808 | tf_op jit(solution)/shard_map/ppermute | solution.py:19
  16.7 0.0 collective-permute-start.7
  16.7 0.0 collective-permute-done.1.south_ref
  16.8 0.0 copy-start.6
  16.8 0.0 copy-start.3
  16.8 0.0 copy-start.4
  16.8 0.1 fusion.4
  16.9 1.1 %pad_maximum_fusion = (bf16[1120,256]{1,0:T(8,128)(2,1)}, bf16[1120,256]{1,0:T(8,128)(2,1)}) fusion(bf16[320,256]{1,0:T(8,128)(2,1)S(1)} %bitcast.15, bf16[800,256]{1,0:T(8,128)(2,1)S(1)} %bitcast.13, bf16[800,256]{1,0:T(8,128)(2,1)S(1)} %bitcast.14), kind=kLoop, calls=%fused_computation.6 | loop fusion | flops 2007040 | bytes 2129920 | tf_op jit(solution)/shard_map/concatenate | solution.py:233
  17.9 0.0 copy-done.6
  17.9 3.2 %collective-permute-start.2 = (bf16[1120,256]{1,0:T(8,128)(2,1)}, bf16[1120,256]{1,0:T(8,128)(2,1)S(1)}, u32[]{:S(2)}, u32[]{:S(2)}) collective-permute-start(bf16[1120,256]{1,0:T(8,128)(2,1)} %get-tuple-element.14), channel_id=1, source_target_pairs={{31,0},{0,1},{1,2},{2,3},{3,4},{4,5},{5,6},{6,7},{7,8},{8,9},{9,10... | collective-permute-start | bytes 1720328 | tf_op jit(solution)/shard_map/ppermute | solution.py:19
  21.2 0.0 copy-done.3
  21.2 0.0 copy-done.4
  21.2 0.4 multiply_convert_fusion
  21.6 0.1 collective-permute-start.3
  21.7 0.3 constant_dynamic-slice_fusion
  22.1 0.1 pad.23
  22.2 1.0 %copy.12 = bf16[96,9,192]{2,1,0:T(8,128)(2,1)S(1)} copy(bf16[96,9,192]{0,2,1:T(8,128)(2,1)S(1)} %bitcast.12) | data formatting | bytes 663552 | tf_op jit(solution)/shard_map/reshape | solution.py:45
  23.2 1.1 %pad.24.src_ref = bf16[96,9,256]{2,1,0:T(8,128)(2,1)} pad(bf16[96,9,192]{2,1,0:T(8,128)(2,1)S(1)} %copy.12, bf16[]{:T(256)} %constant.8.clone.1), padding=0_0x0_0x0_64 | pad | bytes 774146 | tf_op jit(solution)/shard_map/jit(_pad)/pad | solution.py:46
  24.3 0.2 pad.21
  24.5 0.6 %copy.11 = bf16[8,9,480]{2,1,0:T(8,128)(2,1)S(1)} copy(bf16[8,9,480]{0,2,1:T(8,128)(2,1)S(1)} %bitcast.11) | data formatting | bytes 138240 | tf_op jit(solution)/shard_map/reshape | solution.py:45
  25.1 0.7 %pad.22.src_ref = bf16[8,9,512]{2,1,0:T(8,128)(2,1)} pad(bf16[8,9,480]{2,1,0:T(8,128)(2,1)S(1)} %copy.11, bf16[]{:T(256)} %constant.8.clone.1), padding=0_0x0_0x0_32 | pad | bytes 142850 | tf_op jit(solution)/shard_map/jit(_pad)/pad | solution.py:46
  25.8 0.6 %pad_add_fusion.scalar_ref = s32[2]{0:T(128)} fusion(s32[1]{0:T(128)} %bitcast.1, s32[1]{0:T(128)} %bitcast), kind=kLoop, calls=%fused_computation.22 | loop fusion | flops 2 | bytes 16 | tf_op jit(solution)/shard_map/stack | solution.py:214
  26.5 0.0 collective-permute-done
  26.5 4.7 %collective-permute-start.4 = (bf16[10,32,256]{2,1,0:T(8,128)(2,1)S(1)}, bf16[10,32,256]{2,1,0:T(8,128)(2,1)S(1)}, u32[]{:S(2)}, u32[]{:S(2)}) collective-permute-start(bf16[10,32,256]{2,1,0:T(8,128)(2,1)S(1)} %fusion.2), channel_id=1, source_target_pairs={{2,0},{3,1},{4,2},{5,3},{6,4},{7,5},{8,6},{9,7},{10,8},{11,9},{12,... | collective-permute-start | bytes 491528 | tf_op jit(solution)/shard_map/ppermute | solution.py:19
  31.2 0.9 %constant_dynamic-update-slice_fusion.6 = bf16[10,160,256]{2,1,0:T(8,128)(2,1)S(1)} fusion(bf16[10,32,256]{2,1,0:T(8,128)(2,1)} %collective-permute-done), kind=kLoop, calls=%fused_computation.17 | loop fusion | bytes 327680
  32.1 0.0 collective-permute-done.6.west_ref
  32.1 5.6 %collective-permute-done.7.east_ref = bf16[800,256]{1,0:T(8,128)(2,1)} collective-permute-done((bf16[800,256]{1,0:T(8,128)(2,1)}, bf16[800,256]{1,0:T(8,128)(2,1)}, u32[]{:S(2)}, u32[]{:S(2)}) %collective-permute-start.7) | collective-permute-done | bytes 409632 | tf_op jit(solution)/shard_map/ppermute | solution.py:19
  37.7 0.0 copy-start.1
  37.7 7.3 %shard_map.55.rest_0_ = bf16[96,32,256]{2,1,0:T(8,128)(2,1)} custom-call(s32[2]{0:T(128)} %pad_add_fusion.scalar_ref, bf16[96,9,256]{2,1,0:T(8,128)(2,1)} %pad.24.src_ref, bf16[96,32,256]{2,1,0:T(8,128)(2,1)} %f_ref.5, bf16[96,32,256]{2,1,0:T(8,128)(2,1)} %f_ref.5, bf16[96,32,256]{2,1,0:T(8,128)(2,1)} %f_ref.5, ...), custom_call_target="tpu_custom_call" | custom-call | tf_op jit(solution)/shard_map/pallas_call | solution.py:172
  45.0 0.0 collective-permute-done.2.west_ref
  45.1 0.0 copy-start.2
  45.1 0.0 copy-done.1
  45.1 0.1 constant_dynamic-update-slice_fusion.4
  45.2 0.0 collective-permute-done.3.east_ref
  45.2 1.0 %slice.47 = bf16[320,256]{1,0:T(8,128)(2,1)S(1)} slice(bf16[1120,256]{1,0:T(8,128)(2,1)} %collective-permute-done.3.east_ref), slice={[800:1120], [0:256]} | slice | bytes 327680 | tf_op jit(solution)/shard_map/slice | solution.py:251
  46.2 0.0 collective-permute-done.4
  46.3 0.0 copy-done.2
  46.3 1.0 %pad.20.ext_ref = bf16[11,160,256]{2,1,0:T(8,128)(2,1)} pad(bf16[10,160,256]{2,1,0:T(8,128)(2,1)S(1)} %constant_dynamic-update-slice_fusion.2, bf16[]{:T(256)} %constant.8.clone.1), padding=0_1x0_0x0_0 | pad | bytes 1720322 | tf_op jit(solution)/shard_map/jit(_pad)/pad | solution.py:254
  47.3 7.3 %shard_map.56.prev_ref = bf16[96,32,256]{2,1,0:T(8,128)(2,1)} custom-call(s32[2]{0:T(128)} %pad_add_fusion.scalar_ref, bf16[96,9,256]{2,1,0:T(8,128)(2,1)} %pad.24.src_ref, bf16[96,32,256]{2,1,0:T(8,128)(2,1)} %f_ref.5, bf16[96,32,256]{2,1,0:T(8,128)(2,1)} %f_ref.5, bf16[96,32,256]{2,1,0:T(8,128)(2,1)} %f_ref.5, ...), custom_call_target="tpu_custom_call", output_to_operand_aliasing={{}: (10, {})} | custom-call | tf_op jit(solution)/shard_map/pallas_call | solution.py:172
  54.5 3.0 %shard_map.57 = bf16[96,32,256]{2,1,0:T(8,128)(2,1)} custom-call(s32[2]{0:T(128)} %pad_add_fusion.scalar_ref, bf16[11,160,256]{2,1,0:T(8,128)(2,1)} %pad.20.ext_ref, bf16[8,9,512]{2,1,0:T(8,128)(2,1)} %pad.22.src_ref, bf16[96,32,256]{2,1,0:T(8,128)(2,1)} %f_ref.5, bf16[9,256,256]{2,1,0:T(8,128)(2,1)} %w_ref.1, ...), custom_call_target="tpu_custom_call", output_to_operand_aliasing={{}: (5, {})} | custom-call | tf_op jit(solution)/shard_map/pallas_call | solution.py:197
  (10 shorter events, 0.1 us)
Async XLA Ops:
  0.0 11.3 %copy-start = (bf16[96,32,256]{2,1,0:T(8,128)(2,1)S(1)}, bf16[96,32,256]{2,1,0:T(8,128)(2,1)}, u32[]{:S(2)}) copy-start(bf16[96,32,256]{2,1,0:T(8,128)(2,1)} %f_ref.5) | copy-start | bytes 4718596
  0.0 11.2 %copy-start.7 = (s32[96]{0:T(128)S(1)}, s32[96]{0:T(128)}, u32[]{:S(2)}) copy-start(s32[96]{0:T(128)} %param.8) | copy-start | bytes 1156
  0.9 10.4 %collective-permute-start.5 = (bf16[1,32,256]{2,1,0:T(8,128)(2,1)S(1)}, bf16[1,32,256]{2,1,0:T(8,128)(2,1)S(1)}, u32[]{:S(2)}, u32[]{:S(2)}) collective-permute-start(bf16[1,32,256]{2,1,0:T(8,128)(2,1)S(1)} %get-tuple-element.11), channel_id=1, source_target_pairs={{0,32},{32,64},{64,96},{96,128},{128,160},{160,192},{192,224},{1,3... | collective-permute-start | bytes 49160 | tf_op jit(solution)/shard_map/ppermute | solution.py:223
  4.1 12.7 %collective-permute-start.1 = (bf16[1,32,256]{2,1,0:T(8,128)(2,1)S(1)}, bf16[1,32,256]{2,1,0:T(8,128)(2,1)S(1)}, u32[]{:S(2)}, u32[]{:S(2)}) collective-permute-start(bf16[1,32,256]{2,1,0:T(8,128)(2,1)S(1)} %get-tuple-element.12), channel_id=1, source_target_pairs={{32,0},{64,32},{96,64},{128,96},{160,128},{192,160},{224,192},{33,... | collective-permute-start | bytes 49160 | tf_op jit(solution)/shard_map/ppermute | solution.py:224
  9.3 17.2 %collective-permute-start = (bf16[10,32,256]{2,1,0:T(8,128)(2,1)S(1)}, bf16[10,32,256]{2,1,0:T(8,128)(2,1)}, u32[]{:S(2)}, u32[]{:S(2)}) collective-permute-start(bf16[10,32,256]{2,1,0:T(8,128)(2,1)S(1)} %fusion.2), channel_id=1, source_target_pairs={{30,0},{31,1},{0,2},{1,3},{2,4},{3,5},{4,6},{5,7},{6,8},{7,9},{8,1... | collective-permute-start | bytes 491528 | tf_op jit(solution)/shard_map/ppermute | solution.py:19
  11.3 0.6 %copy-start.5 = (bf16[1,32,256]{2,1,0:T(8,128)(2,1)}, bf16[1,32,256]{2,1,0:T(8,128)(2,1)S(1)}, u32[]{:S(2)}) copy-start(bf16[1,32,256]{2,1,0:T(8,128)(2,1)S(1)} %collective-permute-done.5.north_ref) | copy-start | bytes 49156
  12.9 19.3 %collective-permute-start.6 = (bf16[800,256]{1,0:T(8,128)(2,1)}, bf16[800,256]{1,0:T(8,128)(2,1)}, u32[]{:S(2)}, u32[]{:S(2)}) collective-permute-start(bf16[800,256]{1,0:T(8,128)(2,1)} %bitcast.9), channel_id=1, source_target_pairs={{31,0},{0,1},{1,2},{2,3},{3,4},{4,5},{5,6},{6,7},{7,8},{8,9},{9,10... | collective-permute-start | bytes 1228808 | tf_op jit(solution)/shard_map/ppermute | solution.py:19
  16.7 21.0 %collective-permute-start.7 = (bf16[800,256]{1,0:T(8,128)(2,1)}, bf16[800,256]{1,0:T(8,128)(2,1)}, u32[]{:S(2)}, u32[]{:S(2)}) collective-permute-start(bf16[800,256]{1,0:T(8,128)(2,1)} %bitcast.10), channel_id=1, source_target_pairs={{1,0},{2,1},{3,2},{4,3},{5,4},{6,5},{7,6},{8,7},{9,8},{10,9},{11,1... | collective-permute-start | bytes 1228808 | tf_op jit(solution)/shard_map/ppermute | solution.py:19
  16.8 1.2 %copy-start.6 = (bf16[1,32,256]{2,1,0:T(8,128)(2,1)}, bf16[1,32,256]{2,1,0:T(8,128)(2,1)S(1)}, u32[]{:S(2)}) copy-start(bf16[1,32,256]{2,1,0:T(8,128)(2,1)S(1)} %collective-permute-done.1.south_ref) | copy-start | bytes 49156
  16.8 4.4 %copy-start.3 = (f32[96,3,129]{0,2,1:T(8,128)S(1)}, f32[96,3,129]{0,2,1:T(8,128)}, u32[]{:S(2)}) copy-start(f32[96,3,129]{0,2,1:T(8,128)} %param.6) | copy-start | bytes 445828
  16.8 4.4 %copy-start.4 = (s32[96,3,129]{0,2,1:T(8,128)S(1)}, s32[96,3,129]{0,2,1:T(8,128)}, u32[]{:S(2)}) copy-start(s32[96,3,129]{0,2,1:T(8,128)} %param.7) | copy-start | bytes 445828
  17.9 27.1 %collective-permute-start.2 = (bf16[1120,256]{1,0:T(8,128)(2,1)}, bf16[1120,256]{1,0:T(8,128)(2,1)S(1)}, u32[]{:S(2)}, u32[]{:S(2)}) collective-permute-start(bf16[1120,256]{1,0:T(8,128)(2,1)} %get-tuple-element.14), channel_id=1, source_target_pairs={{31,0},{0,1},{1,2},{2,3},{3,4},{4,5},{5,6},{6,7},{7,8},{8,9},{9,10... | collective-permute-start | bytes 1720328 | tf_op jit(solution)/shard_map/ppermute | solution.py:19
  21.6 23.6 %collective-permute-start.3 = (bf16[1120,256]{1,0:T(8,128)(2,1)}, bf16[1120,256]{1,0:T(8,128)(2,1)}, u32[]{:S(2)}, u32[]{:S(2)}) collective-permute-start(bf16[1120,256]{1,0:T(8,128)(2,1)} %get-tuple-element.13), channel_id=1, source_target_pairs={{1,0},{2,1},{3,2},{4,3},{5,4},{6,5},{7,6},{8,7},{9,8},{10,9},{11,1... | collective-permute-start | bytes 1720328 | tf_op jit(solution)/shard_map/ppermute | solution.py:19
  26.5 19.8 %collective-permute-start.4 = (bf16[10,32,256]{2,1,0:T(8,128)(2,1)S(1)}, bf16[10,32,256]{2,1,0:T(8,128)(2,1)S(1)}, u32[]{:S(2)}, u32[]{:S(2)}) collective-permute-start(bf16[10,32,256]{2,1,0:T(8,128)(2,1)S(1)} %fusion.2), channel_id=1, source_target_pairs={{2,0},{3,1},{4,2},{5,3},{6,4},{7,5},{8,6},{9,7},{10,8},{11,9},{12,... | collective-permute-start | bytes 491528 | tf_op jit(solution)/shard_map/ppermute | solution.py:19
  37.7 7.4 %copy-start.1 = (bf16[96,32,256]{2,1,0:T(8,128)(2,1)S(1)}, bf16[96,32,256]{2,1,0:T(8,128)(2,1)}, u32[]{:S(2)}) copy-start(bf16[96,32,256]{2,1,0:T(8,128)(2,1)} %f_ref.5) | copy-start | bytes 4718596
  45.1 1.2 %copy-start.2 = (bf16[1120,256]{1,0:T(8,128)(2,1)}, bf16[1120,256]{1,0:T(8,128)(2,1)S(1)}, u32[]{:S(2)}) copy-start(bf16[1120,256]{1,0:T(8,128)(2,1)S(1)} %collective-permute-done.2.west_ref) | copy-start | bytes 1720324

commit v18 on v17

--- a/solution.py
+++ b/solution.py
@@ -10,7 +10,7 @@
 POLAR = 8
 NEAR = 16
 BLOCK = 8
-NEAR_BLOCK = 48
+NEAR_BLOCK = 32
 
 
 def shifted(block, axis, distance):
@@ -223,7 +223,7 @@
     north = lax.ppermute(features[lat_rows - 1 :], "lat", up)
     south = lax.ppermute(features[:1], "lat", down)
     padded = jnp.concatenate([north, features, south], axis=0)
-    half = lat_rows // 2
+    half = lat_rows // 3
     head = padded[: half + 2]
     tail = padded[half:]
     head_west = shifted(head[:, columns - NEAR :].reshape(-1, channels), "lon", 1)

time: 58.4 us -> 67.4 us (1.15)
  the two profiles are of different devices: /device:TPU:3 before, /device:TPU:102 now
where the time goes in v18:
time: 67.4 us; the launch traced here: 67 us
  starting transfers between devices  19.8 us (29%)
  Pallas kernels  17.9 us (27%)
  waiting for transfers between devices  14.5 us (22%)
  local copies, waits for them, and re-layouts  9.49 us (14%)
  other arithmetic  5.03 us (7%)
    pallas_call x2, Pallas kernels, near_call(): pl.pallas_call(functools.partial(near_kernel, first=first, lowest=lowest,...  15 us
    ppermute x6, waiting for transfers between devices, shifted(): return lax.ppermute(block, axis, route)  14.5 us
    ppermute x6, starting transfers between devices, shifted(): return lax.ppermute(block, axis, route)  11.9 us
    ppermute x1, starting transfers between devices, body(): south = lax.ppermute(features[:1], 'lat', down)  4.47 us
    ppermute x1, starting transfers between devices, body(): north = lax.ppermute(features[lat_rows - 1:], 'lat', up)  3.47 us
    pallas_call x1, Pallas kernels, wide_call(): pl.pallas_call(wide_kernel, grid_spec=grid_spec, out_shape=jax.ShapeDtype...  2.97 us
    concatenate x1, other arithmetic, body(): jnp.concatenate([tail[:, :NEAR].reshape(-1, channels), flat_window])  2.15 us
    pad x2, local copies, waits for them, and re-layouts, flat_sources(): return jnp.pad(flat, ((0, 0), (0, 0), (0, lanes - offsets * span)))  1.77 us
  transfers between devices with their start and end apart: 8, of which 1 were waited for; matrix products, arithmetic and copies ran while one was open for 19% of the time, Pallas kernels for 9%

profile of v18, /device:TPU:102, one launch (start us, length us, event | category | flops | bytes accessed | tf_op | source)
XLA Modules:
  0.0 67.0 jit_solution(4324220525551976733)
XLA Ops:
  0.0 0.0 copy-start
  0.0 0.0 copy-start.7
  0.0 0.9 %fusion.5 = (bf16[1,32,256]{2,1,0:T(8,128)(2,1)S(1)}, bf16[1,32,256]{2,1,0:T(8,128)(2,1)S(1)}) fusion(bf16[96,32,256]{2,1,0:T(8,128)(2,1)} %f_ref.5), kind=kLoop, calls=%fused_computation.26 | loop fusion | bytes 65536 | tf_op jit(solution)/shard_map/slice | solution.py:223
  0.9 3.5 %collective-permute-start.5 = (bf16[1,32,256]{2,1,0:T(8,128)(2,1)S(1)}, bf16[1,32,256]{2,1,0:T(8,128)(2,1)S(1)}, u32[]{:S(2)}, u32[]{:S(2)}) collective-permute-start(bf16[1,32,256]{2,1,0:T(8,128)(2,1)S(1)} %get-tuple-element.11), channel_id=1, source_target_pairs={{0,32},{32,64},{64,96},{96,128},{128,160},{160,192},{192,224},{1,3... | collective-permute-start | bytes 49160 | tf_op jit(solution)/shard_map/ppermute | solution.py:223
  4.4 4.5 %collective-permute-start.1 = (bf16[1,32,256]{2,1,0:T(8,128)(2,1)S(1)}, bf16[1,32,256]{2,1,0:T(8,128)(2,1)S(1)}, u32[]{:S(2)}, u32[]{:S(2)}) collective-permute-start(bf16[1,32,256]{2,1,0:T(8,128)(2,1)S(1)} %get-tuple-element.12), channel_id=1, source_target_pairs={{32,0},{64,32},{96,64},{128,96},{160,128},{192,160},{224,192},{33,... | collective-permute-start | bytes 49160 | tf_op jit(solution)/shard_map/ppermute | solution.py:224
  8.9 1.6 %fusion.2 = bf16[10,32,256]{2,1,0:T(8,128)(2,1)} fusion(s32[]{:T(128)} %select_n.10, bf16[1,32,256]{2,1,0:T(8,128)(2,1)S(1)} %broadcast_in_dim.10, bf16[96,32,256]{2,1,0:T(8,128)(2,1)} %f_ref.5), kind=kLoop, calls=%fused_computation.9 | loop fusion | flops 163840 | bytes 1753092 | tf_op jit(solution)/shard_map/concatenate | solution.py:218
  10.5 4.0 %collective-permute-start = (bf16[10,32,256]{2,1,0:T(8,128)(2,1)}, bf16[10,32,256]{2,1,0:T(8,128)(2,1)}, u32[]{:S(2)}, u32[]{:S(2)}) collective-permute-start(bf16[10,32,256]{2,1,0:T(8,128)(2,1)} %fusion.2), channel_id=1, source_target_pairs={{30,0},{31,1},{0,2},{1,3},{2,4},{3,5},{4,6},{5,7},{6,8},{7,9},{8,1... | collective-permute-start | bytes 491528 | tf_op jit(solution)/shard_map/ppermute | solution.py:19
  14.5 0.0 copy-done.7
  14.5 0.1 broadcast_compare_fusion
  14.6 0.0 collective-permute-done.5.north_ref
  14.6 0.0 copy-start.5
  14.6 0.0 copy-done
  14.6 0.4 constant_dynamic-update-slice_fusion.7
  15.0 0.2 copy-done.5
  15.2 0.0 collective-permute-done.1.south_ref
  15.2 0.0 copy-start.6
  15.2 0.1 fusion.4
  15.3 0.0 copy-start.3
  15.3 0.0 copy-start.4
  15.3 2.1 %pad_maximum_fusion = (bf16[1376,256]{1,0:T(8,128)(2,1)}, bf16[1376,256]{1,0:T(8,128)(2,1)}) fusion(bf16[320,256]{1,0:T(8,128)(2,1)} %bitcast.3, bf16[1056,256]{1,0:T(8,128)(2,1)S(1)} %bitcast.12, bf16[1056,256]{1,0:T(8,128)(2,1)S(1)} %bitcast.13), kind=kLoop, calls=%fused_computation.6 | loop fusion | flops 2465792 | bytes 2654208 | tf_op jit(solution)/shard_map/concatenate | solution.py:233
  17.4 0.0 copy-done.6
  17.4 0.0 collective-permute-start.2
  17.4 0.0 copy-done.3
  17.4 0.0 copy-done.4
  17.5 0.4 multiply_convert_fusion
  17.9 3.3 %collective-permute-start.3 = (bf16[1376,256]{1,0:T(8,128)(2,1)}, bf16[1376,256]{1,0:T(8,128)(2,1)}, u32[]{:S(2)}, u32[]{:S(2)}) collective-permute-start(bf16[1376,256]{1,0:T(8,128)(2,1)} %get-tuple-element.13), channel_id=1, source_target_pairs={{1,0},{2,1},{3,2},{4,3},{5,4},{6,5},{7,6},{8,7},{9,8},{10,9},{11,1... | collective-permute-start | bytes 2113544 | tf_op jit(solution)/shard_map/ppermute | solution.py:19
  21.2 0.9 %fusion.3 = (bf16[34,16,256]{2,1,0:T(8,128)(2,1)}, bf16[34,16,256]{2,1,0:T(8,128)(2,1)}) fusion(bf16[97,32,256]{2,1,0:T(8,128)(2,1)S(1)} %get-tuple-element.9), kind=kLoop, calls=%fused_computation.24 | loop fusion | bytes 1114112 | tf_op jit(solution)/shard_map/slice | solution.py:230
  22.1 0.0 collective-permute-start.6
  22.1 3.2 %collective-permute-start.7 = (bf16[544,256]{1,0:T(8,128)(2,1)}, bf16[544,256]{1,0:T(8,128)(2,1)}, u32[]{:S(2)}, u32[]{:S(2)}) collective-permute-start(bf16[544,256]{1,0:T(8,128)(2,1)} %bitcast.10), channel_id=1, source_target_pairs={{1,0},{2,1},{3,2},{4,3},{5,4},{6,5},{7,6},{8,7},{9,8},{10,9},{11,1... | collective-permute-start | bytes 835592 | tf_op jit(solution)/shard_map/ppermute | solution.py:19
  25.3 0.3 constant_dynamic-slice_fusion
  25.7 0.1 pad.23
  25.8 1.0 %copy.12 = bf16[96,9,192]{2,1,0:T(8,128)(2,1)S(1)} copy(bf16[96,9,192]{0,2,1:T(8,128)(2,1)S(1)} %bitcast.14) | data formatting | bytes 663552 | tf_op jit(solution)/shard_map/reshape | solution.py:45
  26.8 1.1 %pad.24.src_ref = bf16[96,9,256]{2,1,0:T(8,128)(2,1)} pad(bf16[96,9,192]{2,1,0:T(8,128)(2,1)S(1)} %copy.12, bf16[]{:T(256)} %constant.8.clone.1), padding=0_0x0_0x0_64 | pad | bytes 774146 | tf_op jit(solution)/shard_map/jit(_pad)/pad | solution.py:46
  27.9 0.2 pad.21
  28.1 0.6 copy.11
  28.8 0.7 %pad.22.src_ref = bf16[8,9,512]{2,1,0:T(8,128)(2,1)} pad(bf16[8,9,480]{2,1,0:T(8,128)(2,1)S(1)} %copy.11, bf16[]{:T(256)} %constant.8.clone.1), padding=0_0x0_0x0_32 | pad | bytes 142850 | tf_op jit(solution)/shard_map/jit(_pad)/pad | solution.py:46
  29.4 0.6 pad_add_fusion.scalar_ref
  30.1 0.0 collective-permute-done
  30.1 1.4 %collective-permute-start.4 = (bf16[10,32,256]{2,1,0:T(8,128)(2,1)}, bf16[10,32,256]{2,1,0:T(8,128)(2,1)S(1)}, u32[]{:S(2)}, u32[]{:S(2)}) collective-permute-start(bf16[10,32,256]{2,1,0:T(8,128)(2,1)} %fusion.2), channel_id=1, source_target_pairs={{2,0},{3,1},{4,2},{5,3},{6,4},{7,5},{8,6},{9,7},{10,8},{11,9},{12,... | collective-permute-start | bytes 491528 | tf_op jit(solution)/shard_map/ppermute | solution.py:19
  31.5 0.9 %constant_dynamic-update-slice_fusion.6 = bf16[10,160,256]{2,1,0:T(8,128)(2,1)S(1)} fusion(bf16[10,32,256]{2,1,0:T(8,128)(2,1)} %collective-permute-done), kind=kLoop, calls=%fused_computation.17 | loop fusion | bytes 327680
  32.4 14.4 %collective-permute-done.6.west_ref = bf16[544,256]{1,0:T(8,128)(2,1)} collective-permute-done((bf16[544,256]{1,0:T(8,128)(2,1)}, bf16[544,256]{1,0:T(8,128)(2,1)}, u32[]{:S(2)}, u32[]{:S(2)}) %collective-permute-start.6) | collective-permute-done | bytes 278560 | tf_op jit(solution)/shard_map/ppermute | solution.py:19
  46.8 0.0 collective-permute-done.7.east_ref
  46.8 0.0 copy-start.1
  46.8 5.8 %shard_map.55.rest_0_ = bf16[96,32,256]{2,1,0:T(8,128)(2,1)} custom-call(s32[2]{0:T(128)} %pad_add_fusion.scalar_ref, bf16[96,9,256]{2,1,0:T(8,128)(2,1)} %pad.24.src_ref, bf16[96,32,256]{2,1,0:T(8,128)(2,1)} %f_ref.5, bf16[96,32,256]{2,1,0:T(8,128)(2,1)} %f_ref.5, bf16[96,32,256]{2,1,0:T(8,128)(2,1)} %f_ref.5, ...), custom_call_target="tpu_custom_call" | custom-call | tf_op jit(solution)/shard_map/pallas_call | solution.py:172
  52.6 0.0 collective-permute-done.2.west_ref
  52.6 0.0 copy-start.2
  52.7 0.0 copy-done.1
  52.7 0.1 constant_dynamic-update-slice_fusion.4
  52.8 0.0 collective-permute-done.3.east_ref
  52.8 1.0 %slice.47 = bf16[320,256]{1,0:T(8,128)(2,1)S(1)} slice(bf16[1376,256]{1,0:T(8,128)(2,1)} %collective-permute-done.3.east_ref), slice={[1056:1376], [0:256]} | slice | bytes 327680 | tf_op jit(solution)/shard_map/slice | solution.py:251
  53.8 0.0 collective-permute-done.4
  53.9 0.0 copy-done.2
  53.9 1.0 %pad.20.ext_ref = bf16[11,160,256]{2,1,0:T(8,128)(2,1)} pad(bf16[10,160,256]{2,1,0:T(8,128)(2,1)S(1)} %constant_dynamic-update-slice_fusion.2, bf16[]{:T(256)} %constant.8.clone.1), padding=0_1x0_0x0_0 | pad | bytes 1720322 | tf_op jit(solution)/shard_map/jit(_pad)/pad | solution.py:254
  54.9 9.2 %shard_map.56.prev_ref = bf16[96,32,256]{2,1,0:T(8,128)(2,1)} custom-call(s32[2]{0:T(128)} %pad_add_fusion.scalar_ref, bf16[96,9,256]{2,1,0:T(8,128)(2,1)} %pad.24.src_ref, bf16[96,32,256]{2,1,0:T(8,128)(2,1)} %f_ref.5, bf16[96,32,256]{2,1,0:T(8,128)(2,1)} %f_ref.5, bf16[96,32,256]{2,1,0:T(8,128)(2,1)} %f_ref.5, ...), custom_call_target="tpu_custom_call", output_to_operand_aliasing={{}: (10, {})} | custom-call | tf_op jit(solution)/shard_map/pallas_call | solution.py:172
  64.1 3.0 %shard_map.57 = bf16[96,32,256]{2,1,0:T(8,128)(2,1)} custom-call(s32[2]{0:T(128)} %pad_add_fusion.scalar_ref, bf16[11,160,256]{2,1,0:T(8,128)(2,1)} %pad.20.ext_ref, bf16[8,9,512]{2,1,0:T(8,128)(2,1)} %pad.22.src_ref, bf16[96,32,256]{2,1,0:T(8,128)(2,1)} %f_ref.5, bf16[9,256,256]{2,1,0:T(8,128)(2,1)} %w_ref.1, ...), custom_call_target="tpu_custom_call", output_to_operand_aliasing={{}: (5, {})} | custom-call | tf_op jit(solution)/shard_map/pallas_call | solution.py:197
  (10 shorter events, 0.1 us)
Async XLA Ops:
  0.0 14.6 %copy-start = (bf16[96,32,256]{2,1,0:T(8,128)(2,1)S(1)}, bf16[96,32,256]{2,1,0:T(8,128)(2,1)}, u32[]{:S(2)}) copy-start(bf16[96,32,256]{2,1,0:T(8,128)(2,1)} %f_ref.5) | copy-start | bytes 4718596
  0.0 14.5 %copy-start.7 = (s32[96]{0:T(128)S(1)}, s32[96]{0:T(128)}, u32[]{:S(2)}) copy-start(s32[96]{0:T(128)} %param.8) | copy-start | bytes 1156
  0.9 13.7 %collective-permute-start.5 = (bf16[1,32,256]{2,1,0:T(8,128)(2,1)S(1)}, bf16[1,32,256]{2,1,0:T(8,128)(2,1)S(1)}, u32[]{:S(2)}, u32[]{:S(2)}) collective-permute-start(bf16[1,32,256]{2,1,0:T(8,128)(2,1)S(1)} %get-tuple-element.11), channel_id=1, source_target_pairs={{0,32},{32,64},{64,96},{96,128},{128,160},{160,192},{192,224},{1,3... | collective-permute-start | bytes 49160 | tf_op jit(solution)/shard_map/ppermute | solution.py:223
  4.4 10.8 %collective-permute-start.1 = (bf16[1,32,256]{2,1,0:T(8,128)(2,1)S(1)}, bf16[1,32,256]{2,1,0:T(8,128)(2,1)S(1)}, u32[]{:S(2)}, u32[]{:S(2)}) collective-permute-start(bf16[1,32,256]{2,1,0:T(8,128)(2,1)S(1)} %get-tuple-element.12), channel_id=1, source_target_pairs={{32,0},{64,32},{96,64},{128,96},{160,128},{192,160},{224,192},{33,... | collective-permute-start | bytes 49160 | tf_op jit(solution)/shard_map/ppermute | solution.py:224
  10.5 19.6 %collective-permute-start = (bf16[10,32,256]{2,1,0:T(8,128)(2,1)}, bf16[10,32,256]{2,1,0:T(8,128)(2,1)}, u32[]{:S(2)}, u32[]{:S(2)}) collective-permute-start(bf16[10,32,256]{2,1,0:T(8,128)(2,1)} %fusion.2), channel_id=1, source_target_pairs={{30,0},{31,1},{0,2},{1,3},{2,4},{3,5},{4,6},{5,7},{6,8},{7,9},{8,1... | collective-permute-start | bytes 491528 | tf_op jit(solution)/shard_map/ppermute | solution.py:19
  14.6 0.6 copy-start.5
  15.2 2.3 %copy-start.6 = (bf16[1,32,256]{2,1,0:T(8,128)(2,1)}, bf16[1,32,256]{2,1,0:T(8,128)(2,1)S(1)}, u32[]{:S(2)}) copy-start(bf16[1,32,256]{2,1,0:T(8,128)(2,1)S(1)} %collective-permute-done.1.south_ref) | copy-start | bytes 49156
  15.3 2.2 %copy-start.3 = (f32[96,3,129]{0,2,1:T(8,128)S(1)}, f32[96,3,129]{0,2,1:T(8,128)}, u32[]{:S(2)}) copy-start(f32[96,3,129]{0,2,1:T(8,128)} %param.6) | copy-start | bytes 445828
  15.3 2.2 %copy-start.4 = (s32[96,3,129]{0,2,1:T(8,128)S(1)}, s32[96,3,129]{0,2,1:T(8,128)}, u32[]{:S(2)}) copy-start(s32[96,3,129]{0,2,1:T(8,128)} %param.7) | copy-start | bytes 445828
  17.4 35.2 %collective-permute-start.2 = (bf16[1376,256]{1,0:T(8,128)(2,1)}, bf16[1376,256]{1,0:T(8,128)(2,1)S(1)}, u32[]{:S(2)}, u32[]{:S(2)}) collective-permute-start(bf16[1376,256]{1,0:T(8,128)(2,1)} %get-tuple-element.14), channel_id=1, source_target_pairs={{31,0},{0,1},{1,2},{2,3},{3,4},{4,5},{5,6},{6,7},{7,8},{8,9},{9,10... | collective-permute-start | bytes 2113544 | tf_op jit(solution)/shard_map/ppermute | solution.py:19
  17.9 34.9 %collective-permute-start.3 = (bf16[1376,256]{1,0:T(8,128)(2,1)}, bf16[1376,256]{1,0:T(8,128)(2,1)}, u32[]{:S(2)}, u32[]{:S(2)}) collective-permute-start(bf16[1376,256]{1,0:T(8,128)(2,1)} %get-tuple-element.13), channel_id=1, source_target_pairs={{1,0},{2,1},{3,2},{4,3},{5,4},{6,5},{7,6},{8,7},{9,8},{10,9},{11,1... | collective-permute-start | bytes 2113544 | tf_op jit(solution)/shard_map/ppermute | solution.py:19
  22.1 24.8 %collective-permute-start.6 = (bf16[544,256]{1,0:T(8,128)(2,1)}, bf16[544,256]{1,0:T(8,128)(2,1)}, u32[]{:S(2)}, u32[]{:S(2)}) collective-permute-start(bf16[544,256]{1,0:T(8,128)(2,1)} %bitcast.9), channel_id=1, source_target_pairs={{31,0},{0,1},{1,2},{2,3},{3,4},{4,5},{5,6},{6,7},{7,8},{8,9},{9,10... | collective-permute-start | bytes 835592 | tf_op jit(solution)/shard_map/ppermute | solution.py:19
  22.1 24.8 %collective-permute-start.7 = (bf16[544,256]{1,0:T(8,128)(2,1)}, bf16[544,256]{1,0:T(8,128)(2,1)}, u32[]{:S(2)}, u32[]{:S(2)}) collective-permute-start(bf16[544,256]{1,0:T(8,128)(2,1)} %bitcast.10), channel_id=1, source_target_pairs={{1,0},{2,1},{3,2},{4,3},{5,4},{6,5},{7,6},{8,7},{9,8},{10,9},{11,1... | collective-permute-start | bytes 835592 | tf_op jit(solution)/shard_map/ppermute | solution.py:19
  30.1 23.7 %collective-permute-start.4 = (bf16[10,32,256]{2,1,0:T(8,128)(2,1)}, bf16[10,32,256]{2,1,0:T(8,128)(2,1)S(1)}, u32[]{:S(2)}, u32[]{:S(2)}) collective-permute-start(bf16[10,32,256]{2,1,0:T(8,128)(2,1)} %fusion.2), channel_id=1, source_target_pairs={{2,0},{3,1},{4,2},{5,3},{6,4},{7,5},{8,6},{9,7},{10,8},{11,9},{12,... | collective-permute-start | bytes 491528 | tf_op jit(solution)/shard_map/ppermute | solution.py:19
  46.8 5.8 %copy-start.1 = (bf16[96,32,256]{2,1,0:T(8,128)(2,1)S(1)}, bf16[96,32,256]{2,1,0:T(8,128)(2,1)}, u32[]{:S(2)}) copy-start(bf16[96,32,256]{2,1,0:T(8,128)(2,1)} %f_ref.5) | copy-start | bytes 4718596
  52.6 1.2 %copy-start.2 = (bf16[1376,256]{1,0:T(8,128)(2,1)}, bf16[1376,256]{1,0:T(8,128)(2,1)S(1)}, u32[]{:S(2)}) copy-start(bf16[1376,256]{1,0:T(8,128)(2,1)S(1)} %collective-permute-done.2.west_ref) | copy-start | bytes 2113540
